TPU v7x, 32 devices: a whole 2x2x4 slice. The times are simulated.
32 devices in a mesh: dp: 4 (over x, core), seq: 2 (over y), head: 4 (over z).
Axes of the slice: x: 2, y: 2, z: 4, core: 2. Of those that a mesh axis runs over, the one named last changes fastest.
Arguments:
- embed: bfloat16 [4, 1024, 1536], P('dp', 'seq', 'head'), may hold values from -6 to 6
- donor_pos: int32 [4, 256], P('dp', 'seq'), may hold values from -1 to 1023, as said below
- acceptor_pos: int32 [4, 256], P('dp', 'seq'), may hold values from -1 to 1023, as said below
- target: bfloat16 [4, 256, 256], P('dp', 'seq'), may hold values from 0 to 4
- donor_w: bfloat16 [1536, 384], P('head'), may hold values from -0.15625 to 0.15625
- acceptor_w: bfloat16 [1536, 384], P('head'), may hold values from -0.15625 to 0.15625
Outputs:
- grad_embed: bfloat16 [4, 1024, 1536], P('dp', 'seq', 'head')
- grad_donor_w: float32 [1536, 384], P('head', 'seq')
- grad_acceptor_w: float32 [1536, 384], P('head', 'seq')
Inputs may be any that keep to these rules, and one draw needn't show every extreme that they name: `donor_pos`: slots k * 128 to (k + 1) * 128 - 1 belong to slab k: they hold one or more positions of k * 512 to (k + 1) * 512 - 1 first, then -1 in the remaining slots. Positions may repeat. `acceptor_pos`: as for donor_pos, drawn independently.
All inputs are finite; a program needn't handle non-finite values.
Results may differ from a plain program's by a relative error of at most 0.02.
Values may be sent and summed in bfloat16 or wider, within the bound.
No kernel may reach another device: no remote copies, remote signals or barrier semaphores. Data moves between devices by JAX's collectives and lax.ppermute only.
A program may use at most 64 MiB of HBM per device.

v0:
```python
import math

import jax
import jax.numpy as jnp
from jax import lax
from jax.sharding import PartitionSpec as P


def site_match(positions, slab_rows, slab_index):
    local_pos = positions - slab_index * slab_rows
    return local_pos[:, :, None] == jnp.arange(slab_rows, dtype=jnp.int32)[None, None, :]


def pair_slope(scores, target, donor_at, acceptor_at):
    allowed = (donor_at[:, :, None] >= 0) & (acceptor_at[:, None, :] > donor_at[:, :, None])
    rate = jax.nn.softplus(scores) + 1.0
    return jnp.where(
        allowed, (1.0 - target.astype(jnp.float32) / rate) * jax.nn.sigmoid(scores), 0.0
    ).astype(jnp.bfloat16)


def place_rows(match_bf, values):
    upper = values.astype(jnp.bfloat16)
    lower = (values - upper.astype(jnp.float32)).astype(jnp.bfloat16)
    placed = jnp.einsum("bnr,bnc->brc", match_bf, upper, preferred_element_type=jnp.float32)
    return placed + jnp.einsum("bnr,bnc->brc", match_bf, lower, preferred_element_type=jnp.float32)


def shards(embed, donor_pos, acceptor_pos, target, donor_w, acceptor_w):
    slab_rows = embed.shape[1]
    slab_sites = donor_pos.shape[1]
    heads = lax.axis_size("head")
    quarter = slab_sites // heads
    width = donor_w.shape[1]
    scale = 1.0 / math.sqrt(width)
    slab_index = lax.axis_index("seq")
    head_index = lax.axis_index("head")
    donor_match = site_match(donor_pos, slab_rows, slab_index).astype(jnp.bfloat16)
    acceptor_match = site_match(acceptor_pos, slab_rows, slab_index).astype(jnp.bfloat16)
    donor_rows = jnp.einsum(
        "bnr,brc->bnc", donor_match, embed, preferred_element_type=jnp.float32
    ).astype(jnp.bfloat16)
    acceptor_rows = jnp.einsum(
        "bnr,brc->bnc", acceptor_match, embed, preferred_element_type=jnp.float32
    ).astype(jnp.bfloat16)
    donor_part = jnp.einsum("bnc,cp->bnp", donor_rows, donor_w, preferred_element_type=jnp.float32)
    acceptor_part = jnp.einsum(
        "bnc,cp->bnp", acceptor_rows, acceptor_w, preferred_element_type=jnp.float32
    )
    donor_sum, acceptor_sum = (
        lax.psum_scatter(
            donor_part.astype(jnp.bfloat16), "head", scatter_dimension=1, tiled=True
        ).astype(jnp.float32),
        lax.psum_scatter(
            acceptor_part.astype(jnp.bfloat16), "head", scatter_dimension=1, tiled=True
        ).astype(jnp.float32),
    )
    donor_feat = donor_sum.astype(jnp.bfloat16)
    acceptor_feat = acceptor_sum.astype(jnp.bfloat16)
    acceptor_here = lax.dynamic_slice_in_dim(acceptor_pos, head_index * quarter, quarter, 1)
    donor_here = lax.dynamic_slice_in_dim(donor_pos, head_index * quarter, quarter, 1)
    target_here = lax.dynamic_slice_in_dim(target, head_index * quarter, quarter, 1)
    every_feat, every_pos = (
        lax.all_gather(acceptor_feat, ("seq", "head"), axis=1, tiled=True),
        lax.all_gather(acceptor_here, ("seq", "head"), axis=1, tiled=True),
    )
    scores = (
        jnp.einsum("bqp,bap->bqa", donor_feat, every_feat, preferred_element_type=jnp.float32)
        * scale
    )
    slope = pair_slope(scores, target_here, donor_here, every_pos)
    donor_grad = (
        jnp.einsum("bqa,bap->bqp", slope, every_feat, preferred_element_type=jnp.float32) * scale
    ).astype(jnp.bfloat16)
    summed = lax.psum_scatter(
        (
            jnp.einsum("bqa,bqp->abp", slope, donor_feat, preferred_element_type=jnp.float32)
            * scale
        ).astype(jnp.bfloat16),
        ("seq", "head"),
        scatter_dimension=0,
        tiled=True,
    ).astype(jnp.float32)
    acceptor_grad = jnp.transpose(summed, (1, 0, 2)).astype(jnp.bfloat16)
    slab_donor_grad, slab_acceptor_grad = (
        lax.all_gather(donor_grad, "head", axis=1, tiled=True),
        lax.all_gather(acceptor_grad, "head", axis=1, tiled=True),
    )
    donor_site = jnp.einsum(
        "bnp,cp->bnc", slab_donor_grad, donor_w, preferred_element_type=jnp.float32
    )
    acceptor_site = jnp.einsum(
        "bnp,cp->bnc", slab_acceptor_grad, acceptor_w, preferred_element_type=jnp.float32
    )
    row_grad = place_rows(donor_match, donor_site) + place_rows(acceptor_match, acceptor_site)
    local_dw = jnp.einsum(
        "bnc,bnp->cp", donor_rows, slab_donor_grad, preferred_element_type=jnp.float32
    )
    local_aw = jnp.einsum(
        "bnc,bnp->cp", acceptor_rows, slab_acceptor_grad, preferred_element_type=jnp.float32
    )
    slab_dw, slab_aw = (
        lax.psum_scatter(
            local_dw.astype(jnp.bfloat16), "seq", scatter_dimension=1, tiled=True
        ).astype(jnp.float32),
        lax.psum_scatter(
            local_aw.astype(jnp.bfloat16), "seq", scatter_dimension=1, tiled=True
        ).astype(jnp.float32),
    )
    grad_dw, grad_aw = (
        lax.psum(slab_dw.astype(jnp.bfloat16), "dp").astype(jnp.float32),
        lax.psum(slab_aw.astype(jnp.bfloat16), "dp").astype(jnp.float32),
    )
    return (row_grad.astype(jnp.bfloat16), grad_dw, grad_aw)


def solution(mesh):
    in_specs = (
        P("dp", "seq", "head"),
        P("dp", "seq"),
        P("dp", "seq"),
        P("dp", "seq", None),
        P("head", None),
        P("head", None),
    )
    out_specs = (P("dp", "seq", "head"), P("head", "seq"), P("head", "seq"))
    return jax.shard_map(shards, mesh=mesh, in_specs=in_specs, out_specs=out_specs, check_vma=False)
```

profile of v0, /device:TPU:0, one launch (start us, length us, event | category | flops | bytes accessed | tf_op | source)
XLA Modules:
  0.0 209.6 jit_solution(6092293367804286707)
XLA Ops:
  7.2 0.7 subtract_bitcast_fusion
  8.5 0.9 fusion.6
  9.7 0.6 copy-done.1
  10.3 0.8 fusion.5
  11.2 0.6 copy-done.5
  11.9 0.6 fusion.51
  13.0 0.6 copy-done.6
  13.8 13.0 %all-reduce = s32[256]{0:T(256)S(1)} all-reduce(s32[256]{0:T(256)S(1)} %fusion.49), channel_id=1, replica_groups=mesh['dp'=4,'seq'=2,'head'=4] {'seq','head'}, use_global_device_ids=true, to_apply=%add | all-reduce | flops 256 | bytes 2048
  27.6 5.1 %reduce-scatter.7.cloned.1.call-done = bf16[1,32,384]{2,1,0:T(8,128)(2,1)} async-done(((bf16[1,128,384]{2,1,0:T(8,128)(2,1)}), bf16[1,32,384]{2,1,0:T(8,128)(2,1)}) %reduce-scatter.7.cloned.1.call-update) | async-done | bytes 24592 | tf_op jit(solution)/shard_map/reduce_scatter | solution.py:54
  32.7 31.2 %all_gather.13 = bf16[1,256,384]{2,1,0:T(8,128)(2,1)S(1)} all-gather(bf16[1,32,384]{2,1,0:T(8,128)(2,1)} %reduce-scatter.7.cloned.1.call-done), channel_id=1, replica_groups=mesh['dp'=4,'seq'=2,'head'=4] {'seq','head'}, dimensions={1}, use_global_device_ids=true | all-gather | bytes 221184 | tf_op jit(solution)/shard_map/all_gather | solution.py:64
  63.9 1.0 fusion.42
  65.1 0.6 copy-done.4
  65.9 1.1 copy.9
  67.0 13.7 %all-gather = bf16[128,384]{1,0:T(8,128)(2,1)S(1)} all-gather(bf16[32,384]{1,0:T(8,128)(2,1)S(1)} %fusion.7), channel_id=2, replica_groups=mesh['dp'=4,'seq'=2,'head'=4] {'head'}, dimensions={0}, use_global_device_ids=true | all-gather | bytes 122880 | tf_op jit(solution)/shard_map/all_gather | solution.py:86
  80.9 1.0 convolution_convert_fusion.1
  82.4 54.5 %all-reduce.6.cloned.1.call-done = bf16[256,1,384]{2,1,0:T(2,128)(2,1)} async-done(((bf16[256,1,384]{2,1,0:T(2,128)(2,1)}), bf16[256,1,384]{2,1,0:T(2,128)(2,1)}) %all-reduce.6.cloned.1.call-update) | async-done | bytes 196624
  136.9 0.8 constant_dynamic-slice_fusion.2
  137.8 13.4 %all-gather.1 = bf16[128,1,384]{2,0,1:T(8,128)(2,1)S(1)} all-gather(bf16[32,1,384]{2,0,1:T(8,128)(2,1)S(1)} %copy.10), channel_id=3, replica_groups=mesh['dp'=4,'seq'=2,'head'=4] {'head'}, dimensions={0}, use_global_device_ids=true | all-gather | bytes 122880 | tf_op jit(solution)/shard_map/all_gather | solution.py:87
  151.1 1.0 convolution_convert_fusion
  153.2 12.4 %reduce-scatter.11.cloned.1.call-done = bf16[384,192]{0,1:T(8,128)(2,1)} async-done(((bf16[384,384]{0,1:T(8,128)(2,1)}), bf16[384,192]{0,1:T(8,128)(2,1)}) %reduce-scatter.11.cloned.1.call-update) | async-done | bytes 147472 | tf_op jit(solution)/shard_map/reduce_scatter | solution.py:106
  165.7 1.1 fusion.2
  166.8 33.5 %all-reduce.8.cloned.1.call-done = (bf16[384,192]{0,1:T(8,128)(2,1)}, bf16[384,192]{0,1:T(8,128)(2,1)}) async-done(((bf16[384,192]{0,1:T(8,128)(2,1)}, bf16[384,192]{0,1:T(8,128)(2,1)}), (bf16[384,192]{0,1:T(8,128)(2,1)}, bf16[384,192]{0,1:T(8,128)(2,1)})) %all-reduce.8.cloned.1.call-update) | async-done | bytes 294928 | tf_op jit(solution)/shard_map/psum | solution.py:111
  200.3 1.7 convert_element_type.129
  202.0 0.7 convert_element_type.131
  (40 shorter events, 3.4 us)
Async XLA Ops:
  7.2 1.0 copy-start
  7.2 1.3 copy-start.2
  7.2 25.5 %reduce-scatter.7.cloned.1.call-start = ((), (), s32[]{:S(2)}) async-start(), calls=%async_computation.5 | async-start | bytes 122880 | tf_op jit(solution)/shard_map/reduce_scatter | solution.py:54
  8.4 0.9 copy-start.7
  9.3 1.0 copy-start.1
  9.3 54.6 %reduce-scatter.5.cloned.1.call-start = ((), (), s32[]{:S(2)}) async-start(), calls=%async_computation.4 | async-start | bytes 122880 | tf_op jit(solution)/shard_map/reduce_scatter | solution.py:51
  11.1 125.8 %all-reduce.6.cloned.1.call-start = ((), (), s32[]{:S(2)}) async-start(), calls=%async_computation.8 | async-start | bytes 786432
  11.2 0.7 copy-start.5
  13.0 0.7 copy-start.6
  64.9 0.7 copy-start.4
  67.0 86.3 %reduce-scatter.9.cloned.1.call-start = ((), (), s32[]{:S(2)}) async-start(), calls=%async_computation.6 | async-start | bytes 442368 | tf_op jit(solution)/shard_map/reduce_scatter | solution.py:103
  81.9 83.7 %reduce-scatter.11.cloned.1.call-start = ((), (), s32[]{:S(2)}) async-start(), calls=%async_computation.7 | async-start | bytes 442368 | tf_op jit(solution)/shard_map/reduce_scatter | solution.py:106
  152.2 48.2 %all-reduce.8.cloned.1.call-start = ((), (), s32[]{:S(2)}) async-start(), calls=%async_computation.9 | async-start | bytes 589824 | tf_op jit(solution)/shard_map/psum | solution.py:111
  200.3 1.7 copy-start.3
Sparse Core Ops, SparseCore 0:
  10.8 21.8 reduce-scatter.6
  35.6 17.3 reduce-scatter.4
  67.1 69.7 all-reduce.5
  139.7 11.0 reduce-scatter.8
  153.5 12.0 reduce-scatter.10
  168.0 32.3 all-reduce.7
where the time goes:
time: 210 us
  waiting for transfers between devices  106 us (50%)
  blocking collectives  71.2 us (34%)
  between operations  15.5 us (7%)
  matrix products  8.33 us (4%)
  local copies, waits for them, and re-layouts  5.36 us (3%)
  other arithmetic  3.22 us (2%)
    unnamed x7, waiting for transfers between devices  54.6 us
    psum x1, waiting for transfers between devices, shards(): lax.psum(slab_dw.astype(jnp.bfloat16), 'dp').astype(jnp.float32)  33.5 us
    all_gather x1, blocking collectives, shards(): lax.all_gather(acceptor_feat, ('seq', 'head'), axis=1, tiled=True)  31.2 us
    all_gather x1, blocking collectives, shards(): lax.all_gather(donor_grad, 'head', axis=1, tiled=True)  13.7 us
    all_gather x1, blocking collectives, shards(): lax.all_gather(acceptor_grad, 'head', axis=1, tiled=True)  13.4 us
    unnamed x1, blocking collectives  13 us
    reduce_scatter x1, waiting for transfers between devices, shards(): lax.psum_scatter(local_aw.astype(jnp.bfloat16), 'seq', scatter_dimension=...  12.4 us
    reduce_scatter x1, waiting for transfers between devices, shards(): lax.psum_scatter(acceptor_part.astype(jnp.bfloat16), 'head', scatter_dime...  5.12 us
  transfers between devices with their start and end apart: 6, of which 4 were waited for; matrix products, arithmetic and copies ran while one was open for 4% of the time, Pallas kernels for 0%

commit v1 on v0

v1 whole, which is shorter than its diff:
```python
import math

import jax
import jax.numpy as jnp
from jax import lax
from jax.sharding import PartitionSpec as P


def site_match(positions, slab_rows, slab_index):
    local_pos = positions - slab_index * slab_rows
    return local_pos[:, :, None] == jnp.arange(slab_rows, dtype=jnp.int32)[None, None, :]


def pair_slope(scores, target, allowed):
    rate = jax.nn.softplus(scores) + 1.0
    return jnp.where(
        allowed, (1.0 - target.astype(jnp.float32) / rate) * jax.nn.sigmoid(scores), 0.0
    ).astype(jnp.bfloat16)


def place_rows(match_bf, values):
    upper = values.astype(jnp.bfloat16)
    lower = (values - upper.astype(jnp.float32)).astype(jnp.bfloat16)
    placed = jnp.einsum("bnr,bnc->brc", match_bf, upper, preferred_element_type=jnp.float32)
    return placed + jnp.einsum("bnr,bnc->brc", match_bf, lower, preferred_element_type=jnp.float32)


def shards(embed, donor_pos, acceptor_pos, target, donor_w, acceptor_w):
    batch, slab_rows, _ = embed.shape
    slab_sites = donor_pos.shape[1]
    width = donor_w.shape[1]
    scale = 1.0 / math.sqrt(width)
    n_seq = lax.axis_size("seq")
    n_head = lax.axis_size("head")
    slab = lax.axis_index("seq")
    sites = slab_sites * n_seq

    target_all = lax.all_gather(target, "seq", axis=1, tiled=True)

    donor_match = site_match(donor_pos, slab_rows, slab).astype(jnp.bfloat16)
    acceptor_match = site_match(acceptor_pos, slab_rows, slab).astype(jnp.bfloat16)
    donor_rows = jnp.einsum(
        "bnr,brc->bnc", donor_match, embed, preferred_element_type=jnp.float32
    ).astype(jnp.bfloat16)
    acceptor_rows = jnp.einsum(
        "bnr,brc->bnc", acceptor_match, embed, preferred_element_type=jnp.float32
    ).astype(jnp.bfloat16)
    donor_part = jnp.einsum(
        "bnc,cp->bnp", donor_rows, donor_w, preferred_element_type=jnp.float32
    ).astype(jnp.bfloat16)
    acceptor_part = jnp.einsum(
        "bnc,cp->bnp", acceptor_rows, acceptor_w, preferred_element_type=jnp.float32
    ).astype(jnp.bfloat16)

    assert slab_sites <= width
    flags = jnp.zeros((batch, 8, width), jnp.bfloat16)
    flags = flags.at[:, 0, :slab_sites].set((donor_pos >= 0).astype(jnp.bfloat16))
    flags = flags.at[:, 1, :slab_sites].set((acceptor_pos >= 0).astype(jnp.bfloat16))
    packed = jnp.concatenate([donor_part, acceptor_part, flags], axis=1)
    gathered = lax.all_gather(packed, ("seq", "head"), axis=1, tiled=False)
    gathered = gathered.reshape(batch, n_seq, n_head, 2 * slab_sites + 8, width)

    donor_total = jnp.zeros((batch, n_seq, slab_sites, width), jnp.float32)
    acceptor_total = jnp.zeros((batch, n_seq, slab_sites, width), jnp.float32)
    for h in range(n_head):
        donor_total = donor_total + gathered[:, :, h, :slab_sites].astype(jnp.float32)
        acceptor_total = acceptor_total + gathered[:, :, h, slab_sites : 2 * slab_sites].astype(
            jnp.float32
        )
    donor_feat_all = donor_total.astype(jnp.bfloat16).reshape(batch, sites, width)
    acceptor_feat_all = acceptor_total.astype(jnp.bfloat16).reshape(batch, sites, width)
    donor_ok_all = (gathered[:, :, 0, 2 * slab_sites, :slab_sites] > 0).reshape(batch, sites)
    acceptor_ok_all = (gathered[:, :, 0, 2 * slab_sites + 1, :slab_sites] > 0).reshape(batch, sites)

    site_slab = jnp.arange(sites, dtype=jnp.int32) // slab_sites
    big = jnp.int32(1 << 30)
    acceptor_tiled = jnp.tile(acceptor_pos, (1, n_seq))
    acceptor_eff = jnp.where(
        site_slab[None, :] == slab,
        acceptor_tiled,
        jnp.where(
            (site_slab[None, :] > slab) & acceptor_ok_all, (slab + 1) * slab_rows, -1
        ),
    )
    donor_tiled = jnp.tile(donor_pos, (1, n_seq))
    donor_eff = jnp.where(
        site_slab[None, :] == slab,
        donor_tiled,
        jnp.where(
            site_slab[None, :] > slab,
            big,
            jnp.where(donor_ok_all, slab * slab_rows - 1, -1),
        ),
    )

    donor_feat = lax.dynamic_slice_in_dim(donor_feat_all, slab * slab_sites, slab_sites, 1)
    acceptor_feat = lax.dynamic_slice_in_dim(acceptor_feat_all, slab * slab_sites, slab_sites, 1)

    scores_row = (
        jnp.einsum("bip,bjp->bij", donor_feat, acceptor_feat_all, preferred_element_type=jnp.float32)
        * scale
    )
    allowed_row = (donor_pos[:, :, None] >= 0) & (acceptor_eff[:, None, :] > donor_pos[:, :, None])
    slope_row = pair_slope(scores_row, target, allowed_row)
    donor_grad = (
        jnp.einsum("bij,bjp->bip", slope_row, acceptor_feat_all, preferred_element_type=jnp.float32)
        * scale
    ).astype(jnp.bfloat16)

    target_col = lax.dynamic_slice_in_dim(target_all, slab * slab_sites, slab_sites, 2)
    scores_col = (
        jnp.einsum("bip,bjp->bij", donor_feat_all, acceptor_feat, preferred_element_type=jnp.float32)
        * scale
    )
    allowed_col = (donor_eff[:, :, None] >= 0) & (acceptor_pos[:, None, :] > donor_eff[:, :, None])
    slope_col = pair_slope(scores_col, target_col, allowed_col)
    acceptor_grad = (
        jnp.einsum("bij,bip->bjp", slope_col, donor_feat_all, preferred_element_type=jnp.float32)
        * scale
    ).astype(jnp.bfloat16)

    donor_site = jnp.einsum("bnp,cp->bnc", donor_grad, donor_w, preferred_element_type=jnp.float32)
    acceptor_site = jnp.einsum(
        "bnp,cp->bnc", acceptor_grad, acceptor_w, preferred_element_type=jnp.float32
    )
    row_grad = place_rows(donor_match, donor_site) + place_rows(acceptor_match, acceptor_site)

    local_dw = jnp.einsum("bnc,bnp->cp", donor_rows, donor_grad, preferred_element_type=jnp.float32)
    local_aw = jnp.einsum(
        "bnc,bnp->cp", acceptor_rows, acceptor_grad, preferred_element_type=jnp.float32
    )
    summed = lax.psum(jnp.stack([local_dw, local_aw]).astype(jnp.bfloat16), ("dp", "seq"))
    part = width // n_seq
    mine = lax.dynamic_slice_in_dim(summed, slab * part, part, 2).astype(jnp.float32)
    return (row_grad.astype(jnp.bfloat16), mine[0], mine[1])


def solution(mesh):
    in_specs = (
        P("dp", "seq", "head"),
        P("dp", "seq"),
        P("dp", "seq"),
        P("dp", "seq", None),
        P("head", None),
        P("head", None),
    )
    out_specs = (P("dp", "seq", "head"), P("head", "seq"), P("head", "seq"))
    return jax.shard_map(shards, mesh=mesh, in_specs=in_specs, out_specs=out_specs, check_vma=False)
```

time: 210 us -> 130 us (0.62)
  blocking collectives: 71.2 us -> 5.86 us
  waiting for transfers between devices: 106 us -> 93.8 us
  other arithmetic: 3.22 us -> 5.94 us
  local copies, waits for them, and re-layouts: 5.36 us -> 2.75 us
    unnamed x7 -> x2, waiting for transfers between devices: 54.6 us -> 0.03 us
    all_gather x3 -> x1, blocking collectives: 58.2 us -> 5.86 us  [shards(): target_all = lax.all_gather(target, 'seq', axis=1, tiled=True)]
    all_gather x0 -> x1, waiting for transfers between devices: none -> 41.4 us  [shards(): gathered = lax.all_gather(packed, ('seq', 'head'), axis=1, tiled=False)]
    psum x1, waiting for transfers between devices: 33.5 us -> 52.4 us  [shards(): lax.psum(jnp.stack([local_dw, local_aw]).astype(jnp.bfloat16), ('dp', 'se...]
    reduce_scatter x4 -> x0, waiting for transfers between devices: 17.5 us -> none  [the longest x1 12.4 us: shards(): lax.psum_scatter(local_aw.astype(jnp.bfloat16), 'seq', scatter_dimension=...]
    unnamed x1 -> x0, blocking collectives: 13 us -> none
    another operation x0 -> x3, other arithmetic: none -> 3.3 us
    unnamed x20 -> x14, local copies, waits for them, and re-layouts: 4.28 us -> 1.77 us
  transfers between devices with their start and end apart: 6 -> 2, of which waited for: 4 -> 2; matrix products, arithmetic and copies ran while one was open for 4% -> 1% of each run, Pallas kernels for 0% -> 0%
where the time goes in v1:
time: 130 us
  waiting for transfers between devices  93.8 us (72%)
  between operations  14.2 us (11%)
  matrix products  7.21 us (6%)
  other arithmetic  5.94 us (5%)
  blocking collectives  5.86 us (5%)
  local copies, waits for them, and re-layouts  2.75 us (2%)
    psum x1, waiting for transfers between devices, shards(): lax.psum(jnp.stack([local_dw, local_aw]).astype(jnp.bfloat16), ('dp', 'se...  52.4 us
    all_gather x1, waiting for transfers between devices, shards(): gathered = lax.all_gather(packed, ('seq', 'head'), axis=1, tiled=False)  41.4 us
    all_gather x1, blocking collectives, shards(): target_all = lax.all_gather(target, 'seq', axis=1, tiled=True)  5.86 us
  transfers between devices with their start and end apart: 2, of which 2 were waited for; matrix products, arithmetic and copies ran while one was open for 1% of the time, Pallas kernels for 0%

profile of v1, /device:TPU:0, one launch (start us, length us, event | category | flops | bytes accessed | tf_op | source)
XLA Modules:
  0.0 129.9 jit_solution(11049242850485408550)
XLA Ops:
  7.3 0.7 compare_bitcast_fusion
  8.0 0.7 subtract_bitcast_fusion
  8.7 0.3 convolution_convert_fusion.3
  8.9 0.3 convolution_convert_fusion.5
  9.2 1.2 fusion.8
  10.4 1.2 fusion.7
  11.8 0.7 pad_maximum_fusion.1
  12.6 5.9 %all_gather.11 = bf16[1,256,256]{2,1,0:T(8,128)(2,1)S(1)} all-gather(bf16[1,128,256]{2,1,0:T(8,128)(2,1)S(1)} %copy-done.3), channel_id=1, replica_groups=mesh['dp'=4,'seq'=2,'head'=4] {'seq'}, dimensions={1}, use_global_device_ids=true | all-gather | bytes 196608 | tf_op jit(solution)/shard_map/all_gather | solution.py:38
  18.4 41.4 %all-gather.3.cloned.1.call-done = bf16[8,264,384]{2,1,0:T(8,128)(2,1)} async-done(((bf16[1,264,384]{2,1,0:T(8,128)(2,1)}), bf16[8,264,384]{2,1,0:T(8,128)(2,1)}) %all-gather.3.cloned.1.call-update) | async-done | bytes 1622032 | tf_op jit(solution)/shard_map/all_gather | solution.py:60
  59.8 1.7 %add_convert_fusion.1 = (bf16[1,2,1,128,384]{4,3,2,1,0:T(8,128)(2,1)S(1)}, bf16[1,2,1,128,384]{4,3,2,1,0:T(8,128)(2,1)S(1)}) fusion(bf16[1,2,4,264,384]{4,3,2,1,0:T(8,128)(2,1)} %bitcast.139), kind=kLoop, calls=%fused_computation.28 | loop fusion | flops 1572864 | bytes 1966080 | tf_op jit(solution)/shard_map/convert.9
  61.5 0.8 fusion.91
  62.3 0.6 fusion.6
  63.1 0.3 fusion.4
  63.4 0.5 fusion.5
  64.2 0.3 fusion.3
  64.4 0.4 fusion.12
  64.8 0.4 convolution_add_fusion.1
  65.2 0.9 pad_maximum_fusion
  66.1 0.4 fusion.11
  66.5 1.1 fusion.2
  67.6 52.4 %all-reduce.3.cloned.1.call-done = bf16[2,384,384]{2,1,0:T(8,128)(2,1)} async-done(((bf16[2,384,384]{2,1,0:T(8,128)(2,1)}), bf16[2,384,384]{2,1,0:T(8,128)(2,1)}) %all-reduce.3.cloned.1.call-update) | async-done | bytes 589840 | tf_op jit(solution)/shard_map/psum | solution.py:132
  120.0 1.2 dynamic-slice_convert_fusion
  121.3 0.9 copy.17
  122.2 0.9 copy.18
  (24 shorter events, 0.9 us)
Async XLA Ops:
  7.2 1.5 %copy-start = (bf16[1,512,384]{2,1,0:T(8,128)(2,1)S(1)}, bf16[1,512,384]{2,1,0:T(8,128)(2,1)}, u32[]{:S(2)}) copy-start(bf16[1,512,384]{2,1,0:T(8,128)(2,1)} %param.10) | copy-start | bytes 1179652
  7.2 11.2 %copy-start.5 = (s32[1,128]{1,0:T(1,128)S(1)}, s32[1,128]{1,0:T(1,128)}, u32[]{:S(2)}) copy-start(s32[1,128]{1,0:T(1,128)} %param.11) | copy-start | bytes 1540
  7.2 5.4 %copy-start.3 = (bf16[1,128,256]{2,1,0:T(8,128)(2,1)S(1)}, bf16[1,128,256]{2,1,0:T(8,128)(2,1)}, u32[]{:S(2)}) copy-start(bf16[1,128,256]{2,1,0:T(8,128)(2,1)} %param.13) | copy-start | bytes 196612
  7.2 52.6 %all-gather.3.cloned.1.call-start = ((), (), s32[]{:S(2)}) async-start(), calls=%async_computation.1 | async-start | bytes 1824768 | tf_op jit(solution)/shard_map/all_gather | solution.py:60
  10.4 51.9 %copy-start.4 = (s32[1,128]{1,0:T(1,128)S(1)}, s32[1,128]{1,0:T(1,128)}, u32[]{:S(2)}) copy-start(s32[1,128]{1,0:T(1,128)} %param.12) | copy-start | bytes 1540
  12.5 107.5 %all-reduce.3.cloned.1.call-start = ((), (), s32[]{:S(2)}) async-start(), calls=%async_computation | async-start | bytes 1179648 | tf_op jit(solution)/shard_map/psum | solution.py:132
  59.8 3.0 %copy-start.1 = (bf16[384,384]{1,0:T(8,128)(2,1)S(1)}, bf16[384,384]{1,0:T(8,128)(2,1)}, u32[]{:S(2)}) copy-start(bf16[384,384]{1,0:T(8,128)(2,1)} %param.15) | copy-start | bytes 884740
  62.8 1.1 copy-start.2
Sparse Core Ops, SparseCore 0:
  12.6 47.1 all-gather.2
  66.2 53.7 all-reduce.2

commit v2 on v1

--- a/solution.py
+++ b/solution.py
@@ -25,6 +25,16 @@
     return placed + jnp.einsum("bnr,bnc->brc", match_bf, lower, preferred_element_type=jnp.float32)
 
 
+def gather_by_permute(x, axes, count, me):
+    pieces = [x]
+    for k in range(1, count):
+        perm = [(i, (i + k) % count) for i in range(count)]
+        pieces.append(lax.ppermute(x, axes, perm))
+    by_offset = jnp.stack(pieces)
+    order = (me - jnp.arange(count, dtype=jnp.int32)) % count
+    return jnp.take(by_offset, order, axis=0)
+
+
 def shards(embed, donor_pos, acceptor_pos, target, donor_w, acceptor_w):
     batch, slab_rows, _ = embed.shape
     slab_sites = donor_pos.shape[1]
@@ -35,7 +45,8 @@
     slab = lax.axis_index("seq")
     sites = slab_sites * n_seq
 
-    target_all = lax.all_gather(target, "seq", axis=1, tiled=True)
+    target_all = gather_by_permute(target, ("seq",), n_seq, slab)
+    target_all = jnp.moveaxis(target_all, 0, 1).reshape(batch, sites, target.shape[2])
 
     donor_match = site_match(donor_pos, slab_rows, slab).astype(jnp.bfloat16)
     acceptor_match = site_match(acceptor_pos, slab_rows, slab).astype(jnp.bfloat16)
@@ -57,8 +68,9 @@
     flags = flags.at[:, 0, :slab_sites].set((donor_pos >= 0).astype(jnp.bfloat16))
     flags = flags.at[:, 1, :slab_sites].set((acceptor_pos >= 0).astype(jnp.bfloat16))
     packed = jnp.concatenate([donor_part, acceptor_part, flags], axis=1)
-    gathered = lax.all_gather(packed, ("seq", "head"), axis=1, tiled=False)
-    gathered = gathered.reshape(batch, n_seq, n_head, 2 * slab_sites + 8, width)
+    me = slab * n_head + lax.axis_index("head")
+    gathered = gather_by_permute(packed, ("seq", "head"), n_seq * n_head, me)
+    gathered = jnp.moveaxis(gathered, 0, 1).reshape(batch, n_seq, n_head, 2 * slab_sites + 8, width)
 
     donor_total = jnp.zeros((batch, n_seq, slab_sites, width), jnp.float32)
     acceptor_total = jnp.zeros((batch, n_seq, slab_sites, width), jnp.float32)
@@ -129,9 +141,22 @@
     local_aw = jnp.einsum(
         "bnc,bnp->cp", acceptor_rows, acceptor_grad, preferred_element_type=jnp.float32
     )
-    summed = lax.psum(jnp.stack([local_dw, local_aw]).astype(jnp.bfloat16), ("dp", "seq"))
     part = width // n_seq
-    mine = lax.dynamic_slice_in_dim(summed, slab * part, part, 2).astype(jnp.float32)
+    blocks = jnp.stack([local_dw, local_aw]).astype(jnp.bfloat16)
+    mine = lax.dynamic_slice_in_dim(blocks, slab * part, part, 2).astype(jnp.float32)
+    for k in range(1, n_seq):
+        dest = (slab + k) % n_seq
+        outgoing = lax.dynamic_slice_in_dim(blocks, dest * part, part, 2)
+        perm = [(i, (i + k) % n_seq) for i in range(n_seq)]
+        mine = mine + lax.ppermute(outgoing, "seq", perm).astype(jnp.float32)
+    n_dp = lax.axis_size("dp")
+    assert n_dp & (n_dp - 1) == 0
+    bit = 1
+    while bit < n_dp:
+        held = mine.astype(jnp.bfloat16)
+        perm = [(i, i ^ bit) for i in range(n_dp)]
+        mine = held.astype(jnp.float32) + lax.ppermute(held, "dp", perm).astype(jnp.float32)
+        bit *= 2
     return (row_grad.astype(jnp.bfloat16), mine[0], mine[1])
 
 

time: 130 us -> 77.9 us (0.60)
  the two profiles are of different devices: /device:TPU:0 before, /device:TPU:8 now
where the time goes in v2:
time: 77.9 us; the launch traced here: 77.6 us
  waiting for transfers between devices  37.3 us (48%)
  starting transfers between devices  21.2 us (27%)
  local copies, waits for them, and re-layouts  7.65 us (10%)
  matrix products  7.26 us (9%)
  other arithmetic  3.21 us (4%)
  between operations  1.03 us (1%)
    ppermute x8, waiting for transfers between devices, gather_by_permute(): pieces.append(lax.ppermute(x, axes, perm))  23.4 us
    ppermute x8, starting transfers between devices, gather_by_permute(): pieces.append(lax.ppermute(x, axes, perm))  18.1 us
    ppermute x2, waiting for transfers between devices, shards(): lax.ppermute(held, 'dp', perm).astype(jnp.float32)  6.98 us
    ppermute x1, waiting for transfers between devices, shards(): mine = mine + lax.ppermute(outgoing, 'seq', perm).astype(jnp.float32)  6.92 us
    gather x2, local copies, waits for them, and re-layouts, gather_by_permute(): return jnp.take(by_offset, order, axis=0)  3.55 us
    unnamed x22, local copies, waits for them, and re-layouts  2.97 us
    ppermute x2, starting transfers between devices, shards(): lax.ppermute(held, 'dp', perm).astype(jnp.float32)  1.63 us
  transfers between devices with their start and end apart: 11, of which 7 were waited for; matrix products, arithmetic and copies ran while one was open for 8% of the time, Pallas kernels for 0%

profile of v2, /device:TPU:8, one launch (start us, length us, event | category | flops | bytes accessed | tf_op | source)
XLA Modules:
  0.0 77.6 jit_solution(247829318418919535)
XLA Ops:
  0.7 0.7 compare_bitcast_fusion
  2.6 1.2 %fusion.7 = bf16[1,128,384]{2,1,0:T(8,128)(2,1)S(1)} fusion(bf16[128,384]{1,0:T(8,128)(2,1)S(1)} %convolution_convert_fusion.5, bf16[384,384]{1,0:T(8,128)(2,1)} %param.14), kind=kOutput, calls=%fused_computation.22 | convolution fusion | flops 37797888 | bytes 491520 | tf_op jit(solution)/shard_map/bnc,cp->bnp/dot_general | solution.py:59
  3.8 1.2 %fusion.8 = bf16[1,128,384]{2,1,0:T(8,128)(2,1)S(1)} fusion(bf16[128,384]{1,0:T(8,128)(2,1)S(1)} %convolution_convert_fusion.3, bf16[384,384]{1,0:T(8,128)(2,1)} %param.15), kind=kOutput, calls=%fused_computation.23 | convolution fusion | flops 37797888 | bytes 491520 | tf_op jit(solution)/shard_map/bnc,cp->bnp/dot_general | solution.py:62
  5.2 1.6 %collective-permute-start = (bf16[1,264,384]{2,1,0:T(8,128)(2,1)S(1)}, bf16[1,264,384]{2,1,0:T(8,128)(2,1)S(1)}, u32[]{:S(2)}, u32[]{:S(2)}) collective-permute-start(bf16[1,264,384]{2,1,0:T(8,128)(2,1)S(1)} %pad_maximum_fusion), channel_id=1, source_target_pairs={{0,1},{1,2},{2,3},{3,4},{4,5},{5,6},{6,7},{7,0},{8,9},{9,10},{10,1... | collective-permute-start | bytes 608264 | tf_op jit(solution)/shard_map/ppermute | solution.py:32
  6.8 2.2 %collective-permute-start.1 = (bf16[1,264,384]{2,1,0:T(8,128)(2,1)S(1)}, bf16[1,264,384]{2,1,0:T(8,128)(2,1)S(1)}, u32[]{:S(2)}, u32[]{:S(2)}) collective-permute-start(bf16[1,264,384]{2,1,0:T(8,128)(2,1)S(1)} %pad_maximum_fusion), channel_id=1, source_target_pairs={{0,2},{1,3},{2,4},{3,5},{4,6},{5,7},{6,0},{7,1},{8,10},{9,11},{10,... | collective-permute-start | bytes 608264 | tf_op jit(solution)/shard_map/ppermute | solution.py:32
  9.0 1.8 %collective-permute-start.2 = (bf16[1,264,384]{2,1,0:T(8,128)(2,1)S(1)}, bf16[1,264,384]{2,1,0:T(8,128)(2,1)S(1)}, u32[]{:S(2)}, u32[]{:S(2)}) collective-permute-start(bf16[1,264,384]{2,1,0:T(8,128)(2,1)S(1)} %pad_maximum_fusion), channel_id=1, source_target_pairs={{0,3},{1,4},{2,5},{3,6},{4,7},{5,0},{6,1},{7,2},{8,11},{9,12},{10,... | collective-permute-start | bytes 608264 | tf_op jit(solution)/shard_map/ppermute | solution.py:32
  11.4 1.5 %collective-permute-start.7 = (bf16[1,128,256]{2,1,0:T(8,128)(2,1)S(1)}, bf16[1,128,256]{2,1,0:T(8,128)(2,1)}, u32[]{:S(2)}, u32[]{:S(2)}) collective-permute-start(bf16[1,128,256]{2,1,0:T(8,128)(2,1)S(1)} %copy-done.5), channel_id=1, source_target_pairs={{0,4},{4,0},{1,5},{5,1},{2,6},{6,2},{3,7},{7,3},{8,12},{12,8},{9,1... | collective-permute-start | bytes 196616 | tf_op jit(solution)/shard_map/ppermute | solution.py:32
  13.1 9.5 %collective-permute-done.7 = bf16[1,128,256]{2,1,0:T(8,128)(2,1)} collective-permute-done((bf16[1,128,256]{2,1,0:T(8,128)(2,1)S(1)}, bf16[1,128,256]{2,1,0:T(8,128)(2,1)}, u32[]{:S(2)}, u32[]{:S(2)}) %collective-permute-start.7) | collective-permute-done | bytes 65568 | tf_op jit(solution)/shard_map/ppermute | solution.py:32
  22.7 0.9 %maximum_bitcast_fusion = bf16[2,128,256]{2,1,0:T(8,128)(2,1)S(1)} fusion(bf16[1,1,128,256]{3,2,1,0:T(8,128)(2,1)} %bitcast.33, bf16[1,1,128,256]{3,2,1,0:T(8,128)(2,1)S(1)} %bitcast.168), kind=kLoop, calls=%fused_computation.72 | loop fusion | flops 65536 | bytes 262144 | tf_op jit(solution)/shard_map/stack | solution.py:33
  23.5 1.2 %gather_fusion.1 = bf16[2,128,256]{2,1,0:T(8,128)(2,1)} fusion(bf16[2,128,256]{2,1,0:T(8,128)(2,1)S(1)} %maximum_bitcast_fusion, s32[1024]{0:T(1024)S(1)} %pad_clamp_fusion), kind=kCustom, calls=%fused_computation.1 | custom fusion | bytes 262152 | tf_op jit(solution)/shard_map/jit(_take)/gather | solution.py:35
  24.7 10.4 %collective-permute-start.5 = (bf16[1,264,384]{2,1,0:T(8,128)(2,1)S(1)}, bf16[1,264,384]{2,1,0:T(8,128)(2,1)S(1)}, u32[]{:S(2)}, u32[]{:S(2)}) collective-permute-start(bf16[1,264,384]{2,1,0:T(8,128)(2,1)S(1)} %pad_maximum_fusion), channel_id=1, source_target_pairs={{0,6},{1,7},{2,0},{3,1},{4,2},{5,3},{6,4},{7,5},{8,14},{9,15},{10,... | collective-permute-start | bytes 608264 | tf_op jit(solution)/shard_map/ppermute | solution.py:32
  35.4 1.2 %collective-permute-done.4 = bf16[1,264,384]{2,1,0:T(8,128)(2,1)} collective-permute-done((bf16[1,264,384]{2,1,0:T(8,128)(2,1)S(1)}, bf16[1,264,384]{2,1,0:T(8,128)(2,1)}, u32[]{:S(2)}, u32[]{:S(2)}) %collective-permute-start.4) | collective-permute-done | bytes 202784 | tf_op jit(solution)/shard_map/ppermute | solution.py:32
  36.6 1.0 %bitcast_dynamic-update-slice_fusion.2 = bf16[8,1,264,384]{3,2,1,0:T(8,128)(2,1)S(1)} fusion(bf16[8,1,264,384]{3,2,1,0:T(8,128)(2,1)S(1)} %bitcast_dynamic-update-slice_fusion.3, bf16[1,264,384]{2,1,0:T(8,128)(2,1)} %collective-permute-done.4), kind=kLoop, calls=%fused_computation.52 | loop fusion | bytes 405504
  37.6 9.5 %collective-permute-done.5 = bf16[1,264,384]{2,1,0:T(8,128)(2,1)S(1)} collective-permute-done((bf16[1,264,384]{2,1,0:T(8,128)(2,1)S(1)}, bf16[1,264,384]{2,1,0:T(8,128)(2,1)S(1)}, u32[]{:S(2)}, u32[]{:S(2)}) %collective-permute-start.5) | collective-permute-done | bytes 202784 | tf_op jit(solution)/shard_map/ppermute | solution.py:32
  47.1 3.1 %collective-permute-done.6 = bf16[1,264,384]{2,1,0:T(8,128)(2,1)S(1)} collective-permute-done((bf16[1,264,384]{2,1,0:T(8,128)(2,1)S(1)}, bf16[1,264,384]{2,1,0:T(8,128)(2,1)S(1)}, u32[]{:S(2)}, u32[]{:S(2)}) %collective-permute-start.6) | collective-permute-done | bytes 202784 | tf_op jit(solution)/shard_map/ppermute | solution.py:32
  50.2 1.2 %copy-done.1 = bf16[8,1,264,384]{3,2,1,0:T(8,128)(2,1)} copy-done((bf16[8,1,264,384]{3,2,1,0:T(8,128)(2,1)}, bf16[8,1,264,384]{3,2,1,0:T(8,128)(2,1)S(1)}, u32[]{:S(2)}) %copy-start.1) | copy-done | bytes 1622040
  51.4 2.3 %gather_fusion = bf16[8,264,384]{2,1,0:T(8,128)(2,1)S(1)} fusion(bf16[8,264,384]{2,1,0:T(8,128)(2,1)} %bitcast.162, s32[1024]{0:T(1024)S(1)} %pad_clamp_fusion.1), kind=kCustom, calls=%fused_computation | custom fusion | bytes 3244064 | tf_op jit(solution)/shard_map/jit(_take)/gather | solution.py:35
  56.7 1.5 %collective-permute-start.8 = (bf16[2,384,192]{1,2,0:T(8,128)(2,1)S(1)}, bf16[2,384,192]{1,2,0:T(8,128)(2,1)S(1)}, u32[]{:S(2)}, u32[]{:S(2)}) collective-permute-start(bf16[2,384,192]{1,2,0:T(8,128)(2,1)S(1)} %fusion.11), channel_id=1, source_target_pairs={{0,4},{4,0},{1,5},{5,1},{2,6},{6,2},{3,7},{7,3},{8,12},{12,8},{9,1... | collective-permute-start | bytes 884744 | tf_op jit(solution)/shard_map/ppermute | solution.py:151
  58.8 6.9 %collective-permute-done.8 = bf16[2,384,192]{1,2,0:T(8,128)(2,1)S(1)} collective-permute-done((bf16[2,384,192]{1,2,0:T(8,128)(2,1)S(1)}, bf16[2,384,192]{1,2,0:T(8,128)(2,1)S(1)}, u32[]{:S(2)}, u32[]{:S(2)}) %collective-permute-start.8) | collective-permute-done | bytes 294944 | tf_op jit(solution)/shard_map/ppermute | solution.py:151
  66.5 0.9 %collective-permute-done.9 = bf16[2,384,192]{1,2,0:T(8,128)(2,1)S(1)} collective-permute-done((bf16[2,384,192]{1,2,0:T(8,128)(2,1)S(1)}, bf16[2,384,192]{1,2,0:T(8,128)(2,1)S(1)}, u32[]{:S(2)}, u32[]{:S(2)}) %collective-permute-start.9) | collective-permute-done | bytes 294944 | tf_op jit(solution)/shard_map/ppermute | solution.py:158
  67.5 1.6 %collective-permute-start.10 = (bf16[2,384,192]{1,2,0:T(8,128)(2,1)S(1)}, bf16[2,384,192]{1,2,0:T(8,128)(2,1)S(1)}, u32[]{:S(2)}, u32[]{:S(2)}) collective-permute-start(bf16[2,384,192]{1,2,0:T(8,128)(2,1)S(1)} %add_convert_fusion), channel_id=1, source_target_pairs={{0,16},{8,24},{16,0},{24,8},{1,17},{9,25},{17,1},{25,9},{2,18},{10... | collective-permute-start | bytes 884744 | tf_op jit(solution)/shard_map/ppermute | solution.py:158
  69.5 1.1 %fusion.2 = bf16[1,512,384]{2,1,0:T(8,128)(2,1)} fusion(f32[512,384]{1,0:T(8,128)S(1)} %convolution_add_fusion.1, f32[512,384]{1,0:T(8,128)S(1)} %fusion.13, s32[128]{0:T(128)S(1)} %get-tuple-element.33, f32[128,384]{1,0:T(8,128)S(1)} %fusion.98), kind=kOutput, calls=%fused_computation.9 | convolution fusion | flops 51183616 | bytes 2163200 | tf_op jit(solution)/shard_map/bnr,bnc->brc/dot_general | solution.py:25
  70.6 6.0 %collective-permute-done.10 = bf16[2,384,192]{1,2,0:T(8,128)(2,1)S(1)} collective-permute-done((bf16[2,384,192]{1,2,0:T(8,128)(2,1)S(1)}, bf16[2,384,192]{1,2,0:T(8,128)(2,1)S(1)}, u32[]{:S(2)}, u32[]{:S(2)}) %collective-permute-start.10) | collective-permute-done | bytes 294944 | tf_op jit(solution)/shard_map/ppermute | solution.py:158
  76.7 0.9 %slice_bitcast_fusion = (f32[384,192]{0,1:T(8,128)}, f32[384,192]{0,1:T(8,128)}) fusion(f32[2,384,192]{1,2,0:T(8,128)S(1)} %convert_add_fusion), kind=kLoop, calls=%fused_computation.39 | loop fusion | bytes 1179648 | tf_op jit(solution)/shard_map/squeeze | solution.py:160
  (63 shorter events, 7.2 us)
Async XLA Ops:
  0.6 1.5 %copy-start = (bf16[1,512,384]{2,1,0:T(8,128)(2,1)S(1)}, bf16[1,512,384]{2,1,0:T(8,128)(2,1)}, u32[]{:S(2)}) copy-start(bf16[1,512,384]{2,1,0:T(8,128)(2,1)} %param.10) | copy-start | bytes 1179652
  0.6 12.3 %copy-start.6 = (s32[1,128]{1,0:T(1,128)S(1)}, s32[1,128]{1,0:T(1,128)}, u32[]{:S(2)}) copy-start(s32[1,128]{1,0:T(1,128)} %param.11) | copy-start | bytes 1540
  0.7 10.7 %copy-start.5 = (bf16[1,128,256]{2,1,0:T(8,128)(2,1)S(1)}, bf16[1,128,256]{2,1,0:T(8,128)(2,1)}, u32[]{:S(2)}) copy-start(bf16[1,128,256]{2,1,0:T(8,128)(2,1)} %param.13) | copy-start | bytes 196612
  5.2 19.5 %collective-permute-start = (bf16[1,264,384]{2,1,0:T(8,128)(2,1)S(1)}, bf16[1,264,384]{2,1,0:T(8,128)(2,1)S(1)}, u32[]{:S(2)}, u32[]{:S(2)}) collective-permute-start(bf16[1,264,384]{2,1,0:T(8,128)(2,1)S(1)} %pad_maximum_fusion), channel_id=1, source_target_pairs={{0,1},{1,2},{2,3},{3,4},{4,5},{5,6},{6,7},{7,0},{8,9},{9,10},{10,1... | collective-permute-start | bytes 608264 | tf_op jit(solution)/shard_map/ppermute | solution.py:32
  6.8 28.3 %collective-permute-start.1 = (bf16[1,264,384]{2,1,0:T(8,128)(2,1)S(1)}, bf16[1,264,384]{2,1,0:T(8,128)(2,1)S(1)}, u32[]{:S(2)}, u32[]{:S(2)}) collective-permute-start(bf16[1,264,384]{2,1,0:T(8,128)(2,1)S(1)} %pad_maximum_fusion), channel_id=1, source_target_pairs={{0,2},{1,3},{2,4},{3,5},{4,6},{5,7},{6,0},{7,1},{8,10},{9,11},{10,... | collective-permute-start | bytes 608264 | tf_op jit(solution)/shard_map/ppermute | solution.py:32
  9.0 26.2 %collective-permute-start.2 = (bf16[1,264,384]{2,1,0:T(8,128)(2,1)S(1)}, bf16[1,264,384]{2,1,0:T(8,128)(2,1)S(1)}, u32[]{:S(2)}, u32[]{:S(2)}) collective-permute-start(bf16[1,264,384]{2,1,0:T(8,128)(2,1)S(1)} %pad_maximum_fusion), channel_id=1, source_target_pairs={{0,3},{1,4},{2,5},{3,6},{4,7},{5,0},{6,1},{7,2},{8,11},{9,12},{10,... | collective-permute-start | bytes 608264 | tf_op jit(solution)/shard_map/ppermute | solution.py:32
  10.8 24.5 %collective-permute-start.3 = (bf16[1,264,384]{2,1,0:T(8,128)(2,1)S(1)}, bf16[1,264,384]{2,1,0:T(8,128)(2,1)S(1)}, u32[]{:S(2)}, u32[]{:S(2)}) collective-permute-start(bf16[1,264,384]{2,1,0:T(8,128)(2,1)S(1)} %pad_maximum_fusion), channel_id=1, source_target_pairs={{0,4},{1,5},{2,6},{3,7},{4,0},{5,1},{6,2},{7,3},{8,12},{9,13},{10,... | collective-permute-start | bytes 608264 | tf_op jit(solution)/shard_map/ppermute | solution.py:32
  11.4 11.3 %collective-permute-start.7 = (bf16[1,128,256]{2,1,0:T(8,128)(2,1)S(1)}, bf16[1,128,256]{2,1,0:T(8,128)(2,1)}, u32[]{:S(2)}, u32[]{:S(2)}) collective-permute-start(bf16[1,128,256]{2,1,0:T(8,128)(2,1)S(1)} %copy-done.5), channel_id=1, source_target_pairs={{0,4},{4,0},{1,5},{5,1},{2,6},{6,2},{3,7},{7,3},{8,12},{12,8},{9,1... | collective-permute-start | bytes 196616 | tf_op jit(solution)/shard_map/ppermute | solution.py:32
  22.7 14.0 %collective-permute-start.4 = (bf16[1,264,384]{2,1,0:T(8,128)(2,1)S(1)}, bf16[1,264,384]{2,1,0:T(8,128)(2,1)}, u32[]{:S(2)}, u32[]{:S(2)}) collective-permute-start(bf16[1,264,384]{2,1,0:T(8,128)(2,1)S(1)} %pad_maximum_fusion), channel_id=1, source_target_pairs={{0,5},{1,6},{2,7},{3,0},{4,1},{5,2},{6,3},{7,4},{8,13},{9,14},{10,... | collective-permute-start | bytes 608264 | tf_op jit(solution)/shard_map/ppermute | solution.py:32
  24.7 22.3 %collective-permute-start.5 = (bf16[1,264,384]{2,1,0:T(8,128)(2,1)S(1)}, bf16[1,264,384]{2,1,0:T(8,128)(2,1)S(1)}, u32[]{:S(2)}, u32[]{:S(2)}) collective-permute-start(bf16[1,264,384]{2,1,0:T(8,128)(2,1)S(1)} %pad_maximum_fusion), channel_id=1, source_target_pairs={{0,6},{1,7},{2,0},{3,1},{4,2},{5,3},{6,4},{7,5},{8,14},{9,15},{10,... | collective-permute-start | bytes 608264 | tf_op jit(solution)/shard_map/ppermute | solution.py:32
  35.2 15.0 %collective-permute-start.6 = (bf16[1,264,384]{2,1,0:T(8,128)(2,1)S(1)}, bf16[1,264,384]{2,1,0:T(8,128)(2,1)S(1)}, u32[]{:S(2)}, u32[]{:S(2)}) collective-permute-start(bf16[1,264,384]{2,1,0:T(8,128)(2,1)S(1)} %pad_maximum_fusion), channel_id=1, source_target_pairs={{0,7},{1,0},{2,1},{3,2},{4,3},{5,4},{6,5},{7,6},{8,15},{9,8},{10,9... | collective-permute-start | bytes 608264 | tf_op jit(solution)/shard_map/ppermute | solution.py:32
  50.2 1.2 %copy-start.1 = (bf16[8,1,264,384]{3,2,1,0:T(8,128)(2,1)}, bf16[8,1,264,384]{3,2,1,0:T(8,128)(2,1)S(1)}, u32[]{:S(2)}) copy-start(bf16[8,1,264,384]{3,2,1,0:T(8,128)(2,1)S(1)} %bitcast_dynamic-update-slice_fusion) | copy-start | bytes 4866052
  54.0 0.9 %copy-start.4 = (bf16[2,128,256]{2,1,0:T(8,128)(2,1)S(1)}, bf16[2,128,256]{2,1,0:T(8,128)(2,1)}, u32[]{:S(2)}) copy-start(bf16[2,128,256]{2,1,0:T(8,128)(2,1)} %gather_fusion.1) | copy-start | bytes 393220
  54.0 0.9 %copy-start.7 = (s32[1,128]{1,0:T(1,128)S(1)}, s32[1,128]{1,0:T(1,128)}, u32[]{:S(2)}) copy-start(s32[1,128]{1,0:T(1,128)} %param.12) | copy-start | bytes 1540
  55.8 2.4 %copy-start.2 = (bf16[384,384]{1,0:T(8,128)(2,1)S(1)}, bf16[384,384]{1,0:T(8,128)(2,1)}, u32[]{:S(2)}) copy-start(bf16[384,384]{1,0:T(8,128)(2,1)} %param.14) | copy-start | bytes 884740
  56.6 9.2 %copy-start.3 = (bf16[384,384]{1,0:T(8,128)(2,1)S(1)}, bf16[384,384]{1,0:T(8,128)(2,1)}, u32[]{:S(2)}) copy-start(bf16[384,384]{1,0:T(8,128)(2,1)} %param.15) | copy-start | bytes 884740
  56.7 9.0 %collective-permute-start.8 = (bf16[2,384,192]{1,2,0:T(8,128)(2,1)S(1)}, bf16[2,384,192]{1,2,0:T(8,128)(2,1)S(1)}, u32[]{:S(2)}, u32[]{:S(2)}) collective-permute-start(bf16[2,384,192]{1,2,0:T(8,128)(2,1)S(1)} %fusion.11), channel_id=1, source_target_pairs={{0,4},{4,0},{1,5},{5,1},{2,6},{6,2},{3,7},{7,3},{8,12},{12,8},{9,1... | collective-permute-start | bytes 884744 | tf_op jit(solution)/shard_map/ppermute | solution.py:151
  65.8 1.6 %collective-permute-start.9 = (bf16[2,384,192]{1,2,0:T(8,128)(2,1)S(1)}, bf16[2,384,192]{1,2,0:T(8,128)(2,1)S(1)}, u32[]{:S(2)}, u32[]{:S(2)}) collective-permute-start(bf16[2,384,192]{1,2,0:T(8,128)(2,1)S(1)} %add_convert_fusion.1), channel_id=1, source_target_pairs={{0,8},{8,0},{16,24},{24,16},{1,9},{9,1},{17,25},{25,17},{2,10},{10... | collective-permute-start | bytes 884744 | tf_op jit(solution)/shard_map/ppermute | solution.py:158
  67.5 9.1 %collective-permute-start.10 = (bf16[2,384,192]{1,2,0:T(8,128)(2,1)S(1)}, bf16[2,384,192]{1,2,0:T(8,128)(2,1)S(1)}, u32[]{:S(2)}, u32[]{:S(2)}) collective-permute-start(bf16[2,384,192]{1,2,0:T(8,128)(2,1)S(1)} %add_convert_fusion), channel_id=1, source_target_pairs={{0,16},{8,24},{16,0},{24,8},{1,17},{9,25},{17,1},{25,9},{2,18},{10... | collective-permute-start | bytes 884744 | tf_op jit(solution)/shard_map/ppermute | solution.py:158

commit v3 on v2

--- a/solution.py
+++ b/solution.py
@@ -45,8 +45,21 @@
     slab = lax.axis_index("seq")
     sites = slab_sites * n_seq
 
-    target_all = gather_by_permute(target, ("seq",), n_seq, slab)
-    target_all = jnp.moveaxis(target_all, 0, 1).reshape(batch, sites, target.shape[2])
+    head = lax.axis_index("head")
+    me = slab * n_head + head
+
+    target_col = jnp.zeros((batch, sites, slab_sites), target.dtype)
+    own_cols = lax.dynamic_slice_in_dim(target, slab * slab_sites, slab_sites, 2)
+    target_col = lax.dynamic_update_slice_in_dim(target_col, own_cols, slab * slab_sites, 1)
+    for k in range(1, n_seq):
+        outgoing = lax.dynamic_slice_in_dim(
+            target, jnp.minimum(slab + k, n_seq - 1) * slab_sites, slab_sites, 2
+        )
+        perm = [(i, i + k) for i in range(n_seq - k)]
+        arrived = lax.ppermute(outgoing, "seq", perm)
+        source = jnp.maximum(slab - k, 0)
+        placed = lax.dynamic_update_slice_in_dim(target_col, arrived, source * slab_sites, 1)
+        target_col = jnp.where(slab >= k, placed, target_col)
 
     donor_match = site_match(donor_pos, slab_rows, slab).astype(jnp.bfloat16)
     acceptor_match = site_match(acceptor_pos, slab_rows, slab).astype(jnp.bfloat16)
@@ -63,26 +76,34 @@
         "bnc,cp->bnp", acceptor_rows, acceptor_w, preferred_element_type=jnp.float32
     ).astype(jnp.bfloat16)
 
+    both = 2 * slab_sites
+    assert both % n_head == 0
+    quarter = both // n_head
+    parts = jnp.concatenate([donor_part, acceptor_part], axis=1)
+    pieces = [lax.dynamic_slice_in_dim(parts, head * quarter, quarter, 1)]
+    for k in range(1, n_head):
+        outgoing = lax.dynamic_slice_in_dim(parts, ((head + k) % n_head) * quarter, quarter, 1)
+        perm = [(i, (i + k) % n_head) for i in range(n_head)]
+        pieces.append(lax.ppermute(outgoing, "head", perm))
+    by_offset = jnp.stack(pieces)
+    by_head = jnp.take(by_offset, (head - jnp.arange(n_head, dtype=jnp.int32)) % n_head, axis=0)
+    total = jnp.zeros((batch, quarter, width), jnp.float32)
+    for h in range(n_head):
+        total = total + by_head[h].astype(jnp.float32)
+    feat_quarter = total.astype(jnp.bfloat16)
+
     assert slab_sites <= width
     flags = jnp.zeros((batch, 8, width), jnp.bfloat16)
     flags = flags.at[:, 0, :slab_sites].set((donor_pos >= 0).astype(jnp.bfloat16))
     flags = flags.at[:, 1, :slab_sites].set((acceptor_pos >= 0).astype(jnp.bfloat16))
-    packed = jnp.concatenate([donor_part, acceptor_part, flags], axis=1)
-    me = slab * n_head + lax.axis_index("head")
+    packed = jnp.concatenate([feat_quarter, flags], axis=1)
     gathered = gather_by_permute(packed, ("seq", "head"), n_seq * n_head, me)
-    gathered = jnp.moveaxis(gathered, 0, 1).reshape(batch, n_seq, n_head, 2 * slab_sites + 8, width)
-
-    donor_total = jnp.zeros((batch, n_seq, slab_sites, width), jnp.float32)
-    acceptor_total = jnp.zeros((batch, n_seq, slab_sites, width), jnp.float32)
-    for h in range(n_head):
-        donor_total = donor_total + gathered[:, :, h, :slab_sites].astype(jnp.float32)
-        acceptor_total = acceptor_total + gathered[:, :, h, slab_sites : 2 * slab_sites].astype(
-            jnp.float32
-        )
-    donor_feat_all = donor_total.astype(jnp.bfloat16).reshape(batch, sites, width)
-    acceptor_feat_all = acceptor_total.astype(jnp.bfloat16).reshape(batch, sites, width)
-    donor_ok_all = (gathered[:, :, 0, 2 * slab_sites, :slab_sites] > 0).reshape(batch, sites)
-    acceptor_ok_all = (gathered[:, :, 0, 2 * slab_sites + 1, :slab_sites] > 0).reshape(batch, sites)
+    gathered = jnp.moveaxis(gathered, 0, 1).reshape(batch, n_seq, n_head, quarter + 8, width)
+    feats = gathered[:, :, :, :quarter].reshape(batch, n_seq, both, width)
+    donor_feat_all = feats[:, :, :slab_sites].reshape(batch, sites, width)
+    acceptor_feat_all = feats[:, :, slab_sites:].reshape(batch, sites, width)
+    donor_ok_all = (gathered[:, :, 0, quarter, :slab_sites] > 0).reshape(batch, sites)
+    acceptor_ok_all = (gathered[:, :, 0, quarter + 1, :slab_sites] > 0).reshape(batch, sites)
 
     site_slab = jnp.arange(sites, dtype=jnp.int32) // slab_sites
     big = jnp.int32(1 << 30)
@@ -119,7 +140,6 @@
         * scale
     ).astype(jnp.bfloat16)
 
-    target_col = lax.dynamic_slice_in_dim(target_all, slab * slab_sites, slab_sites, 2)
     scores_col = (
         jnp.einsum("bip,bjp->bij", donor_feat_all, acceptor_feat, preferred_element_type=jnp.float32)
         * scale
@@ -141,22 +161,31 @@
     local_aw = jnp.einsum(
         "bnc,bnp->cp", acceptor_rows, acceptor_grad, preferred_element_type=jnp.float32
     )
+    n_dp = lax.axis_size("dp")
+    assert n_dp & (n_dp - 1) == 0 and n_dp >= 2
+    dp = lax.axis_index("dp")
+    pair = dp % 2
+    channels = local_dw.shape[0]
+    half = channels // 2
     part = width // n_seq
     blocks = jnp.stack([local_dw, local_aw]).astype(jnp.bfloat16)
-    mine = lax.dynamic_slice_in_dim(blocks, slab * part, part, 2).astype(jnp.float32)
+    mine = lax.dynamic_slice_in_dim(blocks, pair * half, half, 1).astype(jnp.float32)
+    outgoing = lax.dynamic_slice_in_dim(blocks, (1 - pair) * half, half, 1)
+    mine = mine + lax.ppermute(outgoing, "dp", [(i, i ^ 1) for i in range(n_dp)]).astype(jnp.float32)
+    held = mine.astype(jnp.bfloat16)
+    mine = lax.dynamic_slice_in_dim(held, slab * part, part, 2).astype(jnp.float32)
     for k in range(1, n_seq):
-        dest = (slab + k) % n_seq
-        outgoing = lax.dynamic_slice_in_dim(blocks, dest * part, part, 2)
+        outgoing = lax.dynamic_slice_in_dim(held, ((slab + k) % n_seq) * part, part, 2)
         perm = [(i, (i + k) % n_seq) for i in range(n_seq)]
         mine = mine + lax.ppermute(outgoing, "seq", perm).astype(jnp.float32)
-    n_dp = lax.axis_size("dp")
-    assert n_dp & (n_dp - 1) == 0
-    bit = 1
+    bit = 2
     while bit < n_dp:
         held = mine.astype(jnp.bfloat16)
         perm = [(i, i ^ bit) for i in range(n_dp)]
         mine = held.astype(jnp.float32) + lax.ppermute(held, "dp", perm).astype(jnp.float32)
         bit *= 2
+    other = lax.ppermute(mine, "dp", [(i, i ^ 1) for i in range(n_dp)])
+    mine = jnp.where(pair == 0, jnp.concatenate([mine, other], 1), jnp.concatenate([other, mine], 1))
     return (row_grad.astype(jnp.bfloat16), mine[0], mine[1])
 
 

time: 77.9 us -> 54 us (0.69)
  the two profiles are of different devices: /device:TPU:8 before, /device:TPU:0 now
where the time goes in v3:
time: 54 us; the launch traced here: 53.8 us
  starting transfers between devices  25.3 us (47%)
  waiting for transfers between devices  14.9 us (28%)
  local copies, waits for them, and re-layouts  5.54 us (10%)
  matrix products  5.28 us (10%)
  other arithmetic  1.53 us (3%)
  between operations  1.21 us (2%)
    ppermute x7, starting transfers between devices, gather_by_permute(): pieces.append(lax.ppermute(x, axes, perm))  13 us
    ppermute x3, starting transfers between devices, shards(): pieces.append(lax.ppermute(outgoing, 'head', perm))  6.11 us
    ppermute x1, waiting for transfers between devices, shards(): mine = mine + lax.ppermute(outgoing, 'seq', perm).astype(jnp.float32)  5.51 us
    ppermute x1, waiting for transfers between devices, shards(): lax.ppermute(held, 'dp', perm).astype(jnp.float32)  4.4 us
    unnamed x20, local copies, waits for them, and re-layouts  3.54 us
    ppermute x1, starting transfers between devices, shards(): arrived = lax.ppermute(outgoing, 'seq', perm)  3.43 us
    ppermute x7, waiting for transfers between devices, gather_by_permute(): pieces.append(lax.ppermute(x, axes, perm))  2.7 us
    ppermute x1, starting transfers between devices, shards(): lax.ppermute(held, 'dp', perm).astype(jnp.float32)  1.55 us
  transfers between devices with their start and end apart: 15, of which 7 were waited for; matrix products, arithmetic and copies ran while one was open for 6% of the time, Pallas kernels for 0%

profile of v3, /device:TPU:0, one launch (start us, length us, event | category | flops | bytes accessed | tf_op | source)
XLA Modules:
  0.0 53.8 jit_solution(3556221660394997809)
XLA Ops:
  0.7 0.7 %copy-done.4 = s32[1,128]{1,0:T(1,128)S(1)} copy-done((s32[1,128]{1,0:T(1,128)S(1)}, s32[1,128]{1,0:T(1,128)}, u32[]{:S(2)}) %copy-start.4) | copy-done | bytes 536
  2.2 0.7 %copy-done.1 = bf16[384,384]{1,0:T(8,128)(2,1)S(1)} copy-done((bf16[384,384]{1,0:T(8,128)(2,1)S(1)}, bf16[384,384]{1,0:T(8,128)(2,1)}, u32[]{:S(2)}) %copy-start.1) | copy-done | bytes 294936
  3.8 5.1 %collective-permute-start.2 = (bf16[1,64,384]{2,1,0:T(8,128)(2,1)S(1)}, bf16[1,64,384]{2,1,0:T(8,128)(2,1)S(1)}, u32[]{:S(2)}, u32[]{:S(2)}) collective-permute-start(bf16[1,64,384]{2,1,0:T(8,128)(2,1)S(1)} %get-tuple-element.45), channel_id=1, source_target_pairs={{0,3},{1,0},{2,1},{3,2},{4,7},{5,4},{6,5},{7,6},{8,11},{9,8},{10,9... | collective-permute-start | bytes 147464 | tf_op jit(solution)/shard_map/ppermute | solution.py:87
  8.9 1.0 %collective-permute-start = (bf16[1,64,384]{2,1,0:T(8,128)(2,1)S(1)}, bf16[1,64,384]{2,1,0:T(8,128)(2,1)S(1)}, u32[]{:S(2)}, u32[]{:S(2)}) collective-permute-start(bf16[1,64,384]{2,1,0:T(8,128)(2,1)S(1)} %get-tuple-element.43), channel_id=1, source_target_pairs={{0,1},{1,2},{2,3},{3,0},{4,5},{5,6},{6,7},{7,4},{8,9},{9,10},{10,1... | collective-permute-start | bytes 147464 | tf_op jit(solution)/shard_map/ppermute | solution.py:87
  10.0 3.4 %collective-permute-start.10 = (bf16[1,128,128]{2,1,0:T(8,128)(2,1)S(1)}, bf16[1,128,128]{2,1,0:T(8,128)(2,1)S(1)}, u32[]{:S(2)}, u32[]{:S(2)}) collective-permute-start(bf16[1,128,128]{2,1,0:T(8,128)(2,1)S(1)} %get-tuple-element.46), channel_id=1, source_target_pairs={{0,4},{1,5},{2,6},{3,7},{8,12},{9,13},{10,14},{11,15},{16,20},{17,... | collective-permute-start | bytes 98312 | tf_op jit(solution)/shard_map/ppermute | solution.py:59
  13.8 1.2 %collective-permute-done.10 = bf16[1,128,128]{2,1,0:T(8,128)(2,1)S(1)} collective-permute-done((bf16[1,128,128]{2,1,0:T(8,128)(2,1)S(1)}, bf16[1,128,128]{2,1,0:T(8,128)(2,1)S(1)}, u32[]{:S(2)}, u32[]{:S(2)}) %collective-permute-start.10) | collective-permute-done | bytes 32800 | tf_op jit(solution)/shard_map/ppermute | solution.py:59
  15.1 0.6 %gather_fusion = bf16[4,64,384]{2,1,0:T(8,128)(2,1)S(1)} fusion(bf16[4,64,384]{2,1,0:T(8,128)(2,1)S(1)} %maximum_bitcast_fusion, s32[1024]{0:T(1024)S(1)} %pad_clamp_fusion.1), kind=kCustom, calls=%fused_computation | custom fusion | bytes 393232 | tf_op jit(solution)/shard_map/jit(_take)/gather | solution.py:89
  15.8 2.5 %collective-permute-start.3 = (bf16[1,72,384]{2,1,0:T(8,128)(2,1)S(1)}, bf16[1,72,384]{2,1,0:T(8,128)(2,1)S(1)}, u32[]{:S(2)}, u32[]{:S(2)}) collective-permute-start(bf16[1,72,384]{2,1,0:T(8,128)(2,1)S(1)} %pad_maximum_fusion), channel_id=1, source_target_pairs={{0,1},{1,2},{2,3},{3,4},{4,5},{5,6},{6,7},{7,0},{8,9},{9,10},{10,1... | collective-permute-start | bytes 165896 | tf_op jit(solution)/shard_map/ppermute | solution.py:32
  18.4 0.9 %collective-permute-start.4 = (bf16[1,72,384]{2,1,0:T(8,128)(2,1)S(1)}, bf16[1,72,384]{2,1,0:T(8,128)(2,1)S(1)}, u32[]{:S(2)}, u32[]{:S(2)}) collective-permute-start(bf16[1,72,384]{2,1,0:T(8,128)(2,1)S(1)} %pad_maximum_fusion), channel_id=1, source_target_pairs={{0,2},{1,3},{2,4},{3,5},{4,6},{5,7},{6,0},{7,1},{8,10},{9,11},{10,... | collective-permute-start | bytes 165896 | tf_op jit(solution)/shard_map/ppermute | solution.py:32
  19.3 3.3 %collective-permute-start.5 = (bf16[1,72,384]{2,1,0:T(8,128)(2,1)S(1)}, bf16[1,72,384]{2,1,0:T(8,128)(2,1)S(1)}, u32[]{:S(2)}, u32[]{:S(2)}) collective-permute-start(bf16[1,72,384]{2,1,0:T(8,128)(2,1)S(1)} %pad_maximum_fusion), channel_id=1, source_target_pairs={{0,3},{1,4},{2,5},{3,6},{4,7},{5,0},{6,1},{7,2},{8,11},{9,12},{10,... | collective-permute-start | bytes 165896 | tf_op jit(solution)/shard_map/ppermute | solution.py:32
  22.6 2.0 %collective-permute-start.7 = (bf16[1,72,384]{2,1,0:T(8,128)(2,1)S(1)}, bf16[1,72,384]{2,1,0:T(8,128)(2,1)S(1)}, u32[]{:S(2)}, u32[]{:S(2)}) collective-permute-start(bf16[1,72,384]{2,1,0:T(8,128)(2,1)S(1)} %pad_maximum_fusion), channel_id=1, source_target_pairs={{0,5},{1,6},{2,7},{3,0},{4,1},{5,2},{6,3},{7,4},{8,13},{9,14},{10,... | collective-permute-start | bytes 165896 | tf_op jit(solution)/shard_map/ppermute | solution.py:32
  24.5 2.9 %collective-permute-start.8 = (bf16[1,72,384]{2,1,0:T(8,128)(2,1)S(1)}, bf16[1,72,384]{2,1,0:T(8,128)(2,1)S(1)}, u32[]{:S(2)}, u32[]{:S(2)}) collective-permute-start(bf16[1,72,384]{2,1,0:T(8,128)(2,1)S(1)} %pad_maximum_fusion), channel_id=1, source_target_pairs={{0,6},{1,7},{2,0},{3,1},{4,2},{5,3},{6,4},{7,5},{8,14},{9,15},{10,... | collective-permute-start | bytes 165896 | tf_op jit(solution)/shard_map/ppermute | solution.py:32
  27.5 1.4 %collective-permute-start.9 = (bf16[1,72,384]{2,1,0:T(8,128)(2,1)S(1)}, bf16[1,72,384]{2,1,0:T(8,128)(2,1)S(1)}, u32[]{:S(2)}, u32[]{:S(2)}) collective-permute-start(bf16[1,72,384]{2,1,0:T(8,128)(2,1)S(1)} %pad_maximum_fusion), channel_id=1, source_target_pairs={{0,7},{1,0},{2,1},{3,2},{4,3},{5,4},{6,5},{7,6},{8,15},{9,8},{10,9... | collective-permute-start | bytes 165896 | tf_op jit(solution)/shard_map/ppermute | solution.py:32
  29.0 1.2 %collective-permute-done.8 = bf16[1,72,384]{2,1,0:T(8,128)(2,1)S(1)} collective-permute-done((bf16[1,72,384]{2,1,0:T(8,128)(2,1)S(1)}, bf16[1,72,384]{2,1,0:T(8,128)(2,1)S(1)}, u32[]{:S(2)}, u32[]{:S(2)}) %collective-permute-start.8) | collective-permute-done | bytes 55328 | tf_op jit(solution)/shard_map/ppermute | solution.py:32
  30.2 1.5 %collective-permute-done.9 = bf16[1,72,384]{2,1,0:T(8,128)(2,1)S(1)} collective-permute-done((bf16[1,72,384]{2,1,0:T(8,128)(2,1)S(1)}, bf16[1,72,384]{2,1,0:T(8,128)(2,1)S(1)}, u32[]{:S(2)}, u32[]{:S(2)}) %collective-permute-start.9) | collective-permute-done | bytes 55328 | tf_op jit(solution)/shard_map/ppermute | solution.py:32
  31.7 0.6 %gather_fusion.1 = bf16[8,72,384]{2,1,0:T(8,128)(2,1)S(1)} fusion(bf16[8,72,384]{2,1,0:T(8,128)(2,1)S(1)} %bitcast.179, s32[1024]{0:T(1024)S(1)} %pad_clamp_fusion), kind=kCustom, calls=%fused_computation.1 | custom fusion | bytes 884768 | tf_op jit(solution)/shard_map/jit(_take)/gather | solution.py:35
  35.6 0.9 %collective-permute-done.11 = bf16[2,192,384]{2,1,0:T(8,128)(2,1)S(1)} collective-permute-done((bf16[2,192,384]{2,1,0:T(8,128)(2,1)S(1)}, bf16[2,192,384]{2,1,0:T(8,128)(2,1)S(1)}, u32[]{:S(2)}, u32[]{:S(2)}) %collective-permute-start.11) | collective-permute-done | bytes 294944 | tf_op jit(solution)/shard_map/ppermute | solution.py:174
  36.8 1.1 %collective-permute-start.12 = (bf16[2,192,192]{2,1,0:T(8,128)(2,1)S(1)}, bf16[2,192,192]{2,1,0:T(8,128)(2,1)S(1)}, u32[]{:S(2)}, u32[]{:S(2)}) collective-permute-start(bf16[2,192,192]{2,1,0:T(8,128)(2,1)S(1)} %constant_dynamic-slice_fusion.1), channel_id=1, source_target_pairs={{0,4},{4,0},{1,5},{5,1},{2,6},{6,2},{3,7},{7,3},{8,12},{12,8},{9,1... | collective-permute-start | bytes 442376 | tf_op jit(solution)/shard_map/ppermute | solution.py:180
  38.3 5.5 %collective-permute-done.12 = bf16[2,192,192]{2,1,0:T(8,128)(2,1)S(1)} collective-permute-done((bf16[2,192,192]{2,1,0:T(8,128)(2,1)S(1)}, bf16[2,192,192]{2,1,0:T(8,128)(2,1)S(1)}, u32[]{:S(2)}, u32[]{:S(2)}) %collective-permute-start.12) | collective-permute-done | bytes 147488 | tf_op jit(solution)/shard_map/ppermute | solution.py:180
  44.0 1.6 %collective-permute-start.13 = (bf16[2,192,192]{2,1,0:T(8,128)(2,1)S(1)}, bf16[2,192,192]{2,1,0:T(8,128)(2,1)S(1)}, u32[]{:S(2)}, u32[]{:S(2)}) collective-permute-start(bf16[2,192,192]{2,1,0:T(8,128)(2,1)S(1)} %add_convert_fusion.1), channel_id=1, source_target_pairs={{0,16},{8,24},{16,0},{24,8},{1,17},{9,25},{17,1},{25,9},{2,18},{10... | collective-permute-start | bytes 442376 | tf_op jit(solution)/shard_map/ppermute | solution.py:185
  45.7 4.4 %collective-permute-done.13 = bf16[2,192,192]{2,1,0:T(8,128)(2,1)S(1)} collective-permute-done((bf16[2,192,192]{2,1,0:T(8,128)(2,1)S(1)}, bf16[2,192,192]{2,1,0:T(8,128)(2,1)S(1)}, u32[]{:S(2)}, u32[]{:S(2)}) %collective-permute-start.13) | collective-permute-done | bytes 147488 | tf_op jit(solution)/shard_map/ppermute | solution.py:185
  50.7 1.1 %fusion.2 = bf16[1,512,384]{2,1,0:T(8,128)(2,1)} fusion(f32[512,384]{1,0:T(8,128)S(1)} %convolution_add_fusion.1, f32[512,384]{1,0:T(8,128)S(1)} %fusion.13, s32[128]{0:T(128)S(1)} %get-tuple-element.48, f32[128,384]{1,0:T(8,128)S(1)} %fusion.108), kind=kOutput, calls=%fused_computation.8 | convolution fusion | flops 51183616 | bytes 2163200 | tf_op jit(solution)/shard_map/bnr,bnc->brc/dot_general | solution.py:25
  52.1 0.9 %copy.16 = f32[384,192]{0,1:T(8,128)} copy(f32[384,192]{1,0:T(8,128)S(1)} %get-tuple-element.39) | data formatting | bytes 589824
  53.0 0.9 %copy.17 = f32[384,192]{0,1:T(8,128)} copy(f32[384,192]{1,0:T(8,128)S(1)} %get-tuple-element.38) | data formatting | bytes 589824
  (76 shorter events, 7.3 us)
Async XLA Ops:
  0.6 1.0 %copy-start = (bf16[1,512,384]{2,1,0:T(8,128)(2,1)S(1)}, bf16[1,512,384]{2,1,0:T(8,128)(2,1)}, u32[]{:S(2)}) copy-start(bf16[1,512,384]{2,1,0:T(8,128)(2,1)} %param.10) | copy-start | bytes 1179652
  0.7 0.7 %copy-start.4 = (s32[1,128]{1,0:T(1,128)S(1)}, s32[1,128]{1,0:T(1,128)}, u32[]{:S(2)}) copy-start(s32[1,128]{1,0:T(1,128)} %param.11) | copy-start | bytes 1540
  0.7 0.7 %copy-start.5 = (s32[1,128]{1,0:T(1,128)S(1)}, s32[1,128]{1,0:T(1,128)}, u32[]{:S(2)}) copy-start(s32[1,128]{1,0:T(1,128)} %param.12) | copy-start | bytes 1540
  1.9 1.0 %copy-start.1 = (bf16[384,384]{1,0:T(8,128)(2,1)S(1)}, bf16[384,384]{1,0:T(8,128)(2,1)}, u32[]{:S(2)}) copy-start(bf16[384,384]{1,0:T(8,128)(2,1)} %param.14) | copy-start | bytes 884740
  2.2 1.0 %copy-start.2 = (bf16[384,384]{1,0:T(8,128)(2,1)S(1)}, bf16[384,384]{1,0:T(8,128)(2,1)}, u32[]{:S(2)}) copy-start(bf16[384,384]{1,0:T(8,128)(2,1)} %param.15) | copy-start | bytes 884740
  3.8 6.1 %copy-start.3 = (bf16[1,128,256]{2,1,0:T(8,128)(2,1)S(1)}, bf16[1,128,256]{2,1,0:T(8,128)(2,1)}, u32[]{:S(2)}) copy-start(bf16[1,128,256]{2,1,0:T(8,128)(2,1)} %param.13) | copy-start | bytes 196612
  3.8 11.2 %collective-permute-start.2 = (bf16[1,64,384]{2,1,0:T(8,128)(2,1)S(1)}, bf16[1,64,384]{2,1,0:T(8,128)(2,1)S(1)}, u32[]{:S(2)}, u32[]{:S(2)}) collective-permute-start(bf16[1,64,384]{2,1,0:T(8,128)(2,1)S(1)} %get-tuple-element.45), channel_id=1, source_target_pairs={{0,3},{1,0},{2,1},{3,2},{4,7},{5,4},{6,5},{7,6},{8,11},{9,8},{10,9... | collective-permute-start | bytes 147464 | tf_op jit(solution)/shard_map/ppermute | solution.py:87
  8.9 6.1 %collective-permute-start.1 = (bf16[1,64,384]{2,1,0:T(8,128)(2,1)S(1)}, bf16[1,64,384]{2,1,0:T(8,128)(2,1)S(1)}, u32[]{:S(2)}, u32[]{:S(2)}) collective-permute-start(bf16[1,64,384]{2,1,0:T(8,128)(2,1)S(1)} %get-tuple-element.44), channel_id=1, source_target_pairs={{0,2},{1,3},{2,0},{3,1},{4,6},{5,7},{6,4},{7,5},{8,10},{9,11},{10,... | collective-permute-start | bytes 147464 | tf_op jit(solution)/shard_map/ppermute | solution.py:87
  8.9 6.1 %collective-permute-start = (bf16[1,64,384]{2,1,0:T(8,128)(2,1)S(1)}, bf16[1,64,384]{2,1,0:T(8,128)(2,1)S(1)}, u32[]{:S(2)}, u32[]{:S(2)}) collective-permute-start(bf16[1,64,384]{2,1,0:T(8,128)(2,1)S(1)} %get-tuple-element.43), channel_id=1, source_target_pairs={{0,1},{1,2},{2,3},{3,0},{4,5},{5,6},{6,7},{7,4},{8,9},{9,10},{10,1... | collective-permute-start | bytes 147464 | tf_op jit(solution)/shard_map/ppermute | solution.py:87
  10.0 5.0 %collective-permute-start.10 = (bf16[1,128,128]{2,1,0:T(8,128)(2,1)S(1)}, bf16[1,128,128]{2,1,0:T(8,128)(2,1)S(1)}, u32[]{:S(2)}, u32[]{:S(2)}) collective-permute-start(bf16[1,128,128]{2,1,0:T(8,128)(2,1)S(1)} %get-tuple-element.46), channel_id=1, source_target_pairs={{0,4},{1,5},{2,6},{3,7},{8,12},{9,13},{10,14},{11,15},{16,20},{17,... | collective-permute-start | bytes 98312 | tf_op jit(solution)/shard_map/ppermute | solution.py:59
  15.8 8.7 %collective-permute-start.3 = (bf16[1,72,384]{2,1,0:T(8,128)(2,1)S(1)}, bf16[1,72,384]{2,1,0:T(8,128)(2,1)S(1)}, u32[]{:S(2)}, u32[]{:S(2)}) collective-permute-start(bf16[1,72,384]{2,1,0:T(8,128)(2,1)S(1)} %pad_maximum_fusion), channel_id=1, source_target_pairs={{0,1},{1,2},{2,3},{3,4},{4,5},{5,6},{6,7},{7,0},{8,9},{9,10},{10,1... | collective-permute-start | bytes 165896 | tf_op jit(solution)/shard_map/ppermute | solution.py:32
  18.4 9.1 %collective-permute-start.4 = (bf16[1,72,384]{2,1,0:T(8,128)(2,1)S(1)}, bf16[1,72,384]{2,1,0:T(8,128)(2,1)S(1)}, u32[]{:S(2)}, u32[]{:S(2)}) collective-permute-start(bf16[1,72,384]{2,1,0:T(8,128)(2,1)S(1)} %pad_maximum_fusion), channel_id=1, source_target_pairs={{0,2},{1,3},{2,4},{3,5},{4,6},{5,7},{6,0},{7,1},{8,10},{9,11},{10,... | collective-permute-start | bytes 165896 | tf_op jit(solution)/shard_map/ppermute | solution.py:32
  19.3 9.6 %collective-permute-start.5 = (bf16[1,72,384]{2,1,0:T(8,128)(2,1)S(1)}, bf16[1,72,384]{2,1,0:T(8,128)(2,1)S(1)}, u32[]{:S(2)}, u32[]{:S(2)}) collective-permute-start(bf16[1,72,384]{2,1,0:T(8,128)(2,1)S(1)} %pad_maximum_fusion), channel_id=1, source_target_pairs={{0,3},{1,4},{2,5},{3,6},{4,7},{5,0},{6,1},{7,2},{8,11},{9,12},{10,... | collective-permute-start | bytes 165896 | tf_op jit(solution)/shard_map/ppermute | solution.py:32
  22.6 6.4 %collective-permute-start.6 = (bf16[1,72,384]{2,1,0:T(8,128)(2,1)S(1)}, bf16[1,72,384]{2,1,0:T(8,128)(2,1)S(1)}, u32[]{:S(2)}, u32[]{:S(2)}) collective-permute-start(bf16[1,72,384]{2,1,0:T(8,128)(2,1)S(1)} %pad_maximum_fusion), channel_id=1, source_target_pairs={{0,4},{1,5},{2,6},{3,7},{4,0},{5,1},{6,2},{7,3},{8,12},{9,13},{10,... | collective-permute-start | bytes 165896 | tf_op jit(solution)/shard_map/ppermute | solution.py:32
  22.6 6.4 %collective-permute-start.7 = (bf16[1,72,384]{2,1,0:T(8,128)(2,1)S(1)}, bf16[1,72,384]{2,1,0:T(8,128)(2,1)S(1)}, u32[]{:S(2)}, u32[]{:S(2)}) collective-permute-start(bf16[1,72,384]{2,1,0:T(8,128)(2,1)S(1)} %pad_maximum_fusion), channel_id=1, source_target_pairs={{0,5},{1,6},{2,7},{3,0},{4,1},{5,2},{6,3},{7,4},{8,13},{9,14},{10,... | collective-permute-start | bytes 165896 | tf_op jit(solution)/shard_map/ppermute | solution.py:32
  24.5 5.6 %collective-permute-start.8 = (bf16[1,72,384]{2,1,0:T(8,128)(2,1)S(1)}, bf16[1,72,384]{2,1,0:T(8,128)(2,1)S(1)}, u32[]{:S(2)}, u32[]{:S(2)}) collective-permute-start(bf16[1,72,384]{2,1,0:T(8,128)(2,1)S(1)} %pad_maximum_fusion), channel_id=1, source_target_pairs={{0,6},{1,7},{2,0},{3,1},{4,2},{5,3},{6,4},{7,5},{8,14},{9,15},{10,... | collective-permute-start | bytes 165896 | tf_op jit(solution)/shard_map/ppermute | solution.py:32
  27.5 4.2 %collective-permute-start.9 = (bf16[1,72,384]{2,1,0:T(8,128)(2,1)S(1)}, bf16[1,72,384]{2,1,0:T(8,128)(2,1)S(1)}, u32[]{:S(2)}, u32[]{:S(2)}) collective-permute-start(bf16[1,72,384]{2,1,0:T(8,128)(2,1)S(1)} %pad_maximum_fusion), channel_id=1, source_target_pairs={{0,7},{1,0},{2,1},{3,2},{4,3},{5,4},{6,5},{7,6},{8,15},{9,8},{10,9... | collective-permute-start | bytes 165896 | tf_op jit(solution)/shard_map/ppermute | solution.py:32
  34.9 1.6 %collective-permute-start.11 = (bf16[2,192,384]{2,1,0:T(8,128)(2,1)S(1)}, bf16[2,192,384]{2,1,0:T(8,128)(2,1)S(1)}, u32[]{:S(2)}, u32[]{:S(2)}) collective-permute-start(bf16[2,192,384]{2,1,0:T(8,128)(2,1)S(1)} %fusion.11), channel_id=1, source_target_pairs={{0,8},{8,0},{16,24},{24,16},{1,9},{9,1},{17,25},{25,17},{2,10},{10... | collective-permute-start | bytes 884744 | tf_op jit(solution)/shard_map/ppermute | solution.py:174
  36.8 7.0 %collective-permute-start.12 = (bf16[2,192,192]{2,1,0:T(8,128)(2,1)S(1)}, bf16[2,192,192]{2,1,0:T(8,128)(2,1)S(1)}, u32[]{:S(2)}, u32[]{:S(2)}) collective-permute-start(bf16[2,192,192]{2,1,0:T(8,128)(2,1)S(1)} %constant_dynamic-slice_fusion.1), channel_id=1, source_target_pairs={{0,4},{4,0},{1,5},{5,1},{2,6},{6,2},{3,7},{7,3},{8,12},{12,8},{9,1... | collective-permute-start | bytes 442376 | tf_op jit(solution)/shard_map/ppermute | solution.py:180
  44.0 6.2 %collective-permute-start.13 = (bf16[2,192,192]{2,1,0:T(8,128)(2,1)S(1)}, bf16[2,192,192]{2,1,0:T(8,128)(2,1)S(1)}, u32[]{:S(2)}, u32[]{:S(2)}) collective-permute-start(bf16[2,192,192]{2,1,0:T(8,128)(2,1)S(1)} %add_convert_fusion.1), channel_id=1, source_target_pairs={{0,16},{8,24},{16,0},{24,8},{1,17},{9,25},{17,1},{25,9},{2,18},{10... | collective-permute-start | bytes 442376 | tf_op jit(solution)/shard_map/ppermute | solution.py:185
  50.2 1.8 %collective-permute-start.14 = (f32[2,192,192]{2,1,0:T(8,128)S(1)}, f32[2,192,192]{2,1,0:T(8,128)S(1)}, u32[]{:S(2)}, u32[]{:S(2)}) collective-permute-start(f32[2,192,192]{2,1,0:T(8,128)S(1)} %convert_add_fusion), channel_id=1, source_target_pairs={{0,8},{8,0},{16,24},{24,16},{1,9},{9,1},{17,25},{25,17},{2,10},{10... | collective-permute-start | bytes 884744 | tf_op jit(solution)/shard_map/ppermute | solution.py:187

commit v4 on v3

--- a/solution.py
+++ b/solution.py
@@ -80,13 +80,10 @@
     assert both % n_head == 0
     quarter = both // n_head
     parts = jnp.concatenate([donor_part, acceptor_part], axis=1)
-    pieces = [lax.dynamic_slice_in_dim(parts, head * quarter, quarter, 1)]
-    for k in range(1, n_head):
-        outgoing = lax.dynamic_slice_in_dim(parts, ((head + k) % n_head) * quarter, quarter, 1)
-        perm = [(i, (i + k) % n_head) for i in range(n_head)]
-        pieces.append(lax.ppermute(outgoing, "head", perm))
-    by_offset = jnp.stack(pieces)
-    by_head = jnp.take(by_offset, (head - jnp.arange(n_head, dtype=jnp.int32)) % n_head, axis=0)
+    by_head = lax.all_to_all(
+        parts.reshape(batch, n_head, quarter, width), "head", 1, 1, tiled=False
+    )
+    by_head = jnp.moveaxis(by_head, 1, 0)
     total = jnp.zeros((batch, quarter, width), jnp.float32)
     for h in range(n_head):
         total = total + by_head[h].astype(jnp.float32)
@@ -97,8 +94,10 @@
     flags = flags.at[:, 0, :slab_sites].set((donor_pos >= 0).astype(jnp.bfloat16))
     flags = flags.at[:, 1, :slab_sites].set((acceptor_pos >= 0).astype(jnp.bfloat16))
     packed = jnp.concatenate([feat_quarter, flags], axis=1)
-    gathered = gather_by_permute(packed, ("seq", "head"), n_seq * n_head, me)
-    gathered = jnp.moveaxis(gathered, 0, 1).reshape(batch, n_seq, n_head, quarter + 8, width)
+    count = n_seq * n_head
+    copies = jnp.broadcast_to(packed[:, None], (batch, count) + packed.shape[1:])
+    gathered = lax.all_to_all(copies, ("seq", "head"), 1, 1, tiled=False)
+    gathered = gathered.reshape(batch, n_seq, n_head, quarter + 8, width)
     feats = gathered[:, :, :, :quarter].reshape(batch, n_seq, both, width)
     donor_feat_all = feats[:, :, :slab_sites].reshape(batch, sites, width)
     acceptor_feat_all = feats[:, :, slab_sites:].reshape(batch, sites, width)

time: 54 us -> 57.4 us (1.063)
  waiting for transfers between devices: 14.9 us -> 27 us
  starting transfers between devices: 25.3 us -> 16.2 us
  local copies, waits for them, and re-layouts: 5.54 us -> 6.24 us
    ppermute x10 -> x0, starting transfers between devices: 19.1 us -> none  [the longest x7 13 us: gather_by_permute(): pieces.append(lax.ppermute(x, axes, perm))]
    all_to_all x0 -> x2, waiting for transfers between devices: none -> 14 us  [the longest x1 7.31 us: shards(): lax.all_to_all(parts.reshape(batch, n_head, quarter, width), 'head', 1, 1...]
    all_to_all x0 -> x2, starting transfers between devices: none -> 9.97 us  [the longest x1 6.32 us: shards(): lax.all_to_all(parts.reshape(batch, n_head, quarter, width), 'head', 1, 1...]
    ppermute x10 -> x0, waiting for transfers between devices: 2.71 us -> none  [the longest x7 2.7 us: gather_by_permute(): pieces.append(lax.ppermute(x, axes, perm))]
    unnamed x20 -> x14, local copies, waits for them, and re-layouts: 3.54 us -> 4.97 us
    gather x2 -> x0, local copies, waits for them, and re-layouts: 1.24 us -> none  [the longest x1 0.65 us: gather_by_permute(): return jnp.take(by_offset, order, axis=0)]
    broadcast_in_dim x0 -> x1, local copies, waits for them, and re-layouts: none -> 0.81 us  [shards(): jnp.broadcast_to(packed[:, None], (batch, count) + packed.shape[1:])]
    concatenate x1, other arithmetic: 0.01 us -> 0.7 us  [shards(): parts = jnp.concatenate([donor_part, acceptor_part], axis=1)]
  transfers between devices with their start and end apart: 15 -> 7, of which waited for: 7 -> 7; matrix products, arithmetic and copies ran while one was open for 6% -> 5% of each run, Pallas kernels for 0% -> 0%
where the time goes in v4:
time: 57.4 us; the launch traced here: 56.9 us
  waiting for transfers between devices  27 us (47%)
  starting transfers between devices  16.2 us (28%)
  local copies, waits for them, and re-layouts  6.24 us (11%)
  matrix products  5.28 us (9%)
  other arithmetic  1.21 us (2%)
  between operations  0.96 us (2%)
    all_to_all x1, waiting for transfers between devices, shards(): lax.all_to_all(parts.reshape(batch, n_head, quarter, width), 'head', 1, 1...  7.31 us
    all_to_all x1, waiting for transfers between devices, shards(): gathered = lax.all_to_all(copies, ('seq', 'head'), 1, 1, tiled=False)  6.65 us
    all_to_all x1, starting transfers between devices, shards(): lax.all_to_all(parts.reshape(batch, n_head, quarter, width), 'head', 1, 1...  6.32 us
    ppermute x1, waiting for transfers between devices, shards(): mine = mine + lax.ppermute(outgoing, 'seq', perm).astype(jnp.float32)  6 us
    unnamed x14, local copies, waits for them, and re-layouts  4.97 us
    ppermute x1, waiting for transfers between devices, shards(): lax.ppermute(held, 'dp', perm).astype(jnp.float32)  4.39 us
    ppermute x1, starting transfers between devices, shards(): arrived = lax.ppermute(outgoing, 'seq', perm)  3.93 us
    all_to_all x1, starting transfers between devices, shards(): gathered = lax.all_to_all(copies, ('seq', 'head'), 1, 1, tiled=False)  3.65 us
  transfers between devices with their start and end apart: 7, of which 7 were waited for; matrix products, arithmetic and copies ran while one was open for 5% of the time, Pallas kernels for 0%

profile of v4, /device:TPU:0, one launch (start us, length us, event | category | flops | bytes accessed | tf_op | source)
XLA Modules:
  0.0 56.9 jit_solution(3503655639135972750)
XLA Ops:
  0.7 0.7 %copy-done.4 = s32[1,128]{1,0:T(1,128)S(1)} copy-done((s32[1,128]{1,0:T(1,128)S(1)}, s32[1,128]{1,0:T(1,128)}, u32[]{:S(2)}) %copy-start.4) | copy-done | bytes 536
  2.2 0.7 %copy-done.2 = bf16[384,384]{1,0:T(8,128)(2,1)S(1)} copy-done((bf16[384,384]{1,0:T(8,128)(2,1)S(1)}, bf16[384,384]{1,0:T(8,128)(2,1)}, u32[]{:S(2)}) %copy-start.2) | copy-done | bytes 294936
  3.1 0.7 %copy-done.1 = bf16[384,384]{1,0:T(8,128)(2,1)S(1)} copy-done((bf16[384,384]{1,0:T(8,128)(2,1)S(1)}, bf16[384,384]{1,0:T(8,128)(2,1)}, u32[]{:S(2)}) %copy-start.1) | copy-done | bytes 294936
  4.1 0.7 %pad_maximum_fusion = bf16[1,256,384]{2,1,0:T(8,128)(2,1)} fusion(bf16[1,128,384]{2,1,0:T(8,128)(2,1)S(1)} %fusion.8, bf16[1,128,384]{2,1,0:T(8,128)(2,1)S(1)} %fusion.7), kind=kLoop, calls=%fused_computation.45 | loop fusion | flops 393216 | bytes 393216 | tf_op jit(solution)/shard_map/concatenate | solution.py:82
  4.8 6.3 %all-to-all-start = ((bf16[1,4,64,384]{3,2,0,1:T(8,128)(2,1)}), bf16[1,4,64,384]{3,2,0,1:T(8,128)(2,1)S(1)}, u32[]{:S(2)}, u32[]{:S(2)}) async-start(bf16[1,4,64,384]{3,2,0,1:T(8,128)(2,1)} %bitcast.11), calls=%async_computation | async-start | bytes 393216 | tf_op jit(solution)/shard_map/all_to_all | solution.py:83
  11.3 7.3 %all-to-all-done = bf16[1,4,64,384]{3,2,0,1:T(8,128)(2,1)S(1)} async-done(((bf16[1,4,64,384]{3,2,0,1:T(8,128)(2,1)}), bf16[1,4,64,384]{3,2,0,1:T(8,128)(2,1)S(1)}, u32[]{:S(2)}, u32[]{:S(2)}) %all-to-all-start) | async-done | bytes 196640 | tf_op jit(solution)/shard_map/all_to_all | solution.py:83
  18.7 0.8 %broadcast_in_dim.27 = bf16[1,8,72,384]{3,2,0,1:T(8,128)(2,1)} broadcast(bf16[72,384]{1,0:T(8,128)(2,1)S(1)} %maximum_bitcast_fusion), dimensions={2,3} | broadcast | bytes 497664 | tf_op jit(solution)/shard_map/broadcast_in_dim | solution.py:98
  19.5 3.6 %all-to-all-start.1 = ((bf16[1,8,72,384]{3,2,0,1:T(8,128)(2,1)}), bf16[1,8,72,384]{3,2,0,1:T(8,128)(2,1)S(1)}, u32[]{:S(2)}, u32[]{:S(2)}) async-start(bf16[1,8,72,384]{3,2,0,1:T(8,128)(2,1)} %broadcast_in_dim.27), calls=%async_computation.1 | async-start | bytes 884736 | tf_op jit(solution)/shard_map/all_to_all | solution.py:99
  23.1 0.8 %copy-done.3 = bf16[1,128,256]{2,1,0:T(8,128)(2,1)S(1)} copy-done((bf16[1,128,256]{2,1,0:T(8,128)(2,1)S(1)}, bf16[1,128,256]{2,1,0:T(8,128)(2,1)}, u32[]{:S(2)}) %copy-start.3) | copy-done | bytes 65560
  24.0 3.9 %collective-permute-start = (bf16[1,128,128]{2,1,0:T(8,128)(2,1)S(1)}, bf16[1,128,128]{2,1,0:T(8,128)(2,1)S(1)}, u32[]{:S(2)}, u32[]{:S(2)}) collective-permute-start(bf16[1,128,128]{2,1,0:T(8,128)(2,1)S(1)} %get-tuple-element.45), channel_id=1, source_target_pairs={{0,4},{1,5},{2,6},{3,7},{8,12},{9,13},{10,14},{11,15},{16,20},{17,... | collective-permute-start | bytes 98312 | tf_op jit(solution)/shard_map/ppermute | solution.py:59
  28.0 1.5 %collective-permute-done = bf16[1,128,128]{2,1,0:T(8,128)(2,1)S(1)} collective-permute-done((bf16[1,128,128]{2,1,0:T(8,128)(2,1)S(1)}, bf16[1,128,128]{2,1,0:T(8,128)(2,1)S(1)}, u32[]{:S(2)}, u32[]{:S(2)}) %collective-permute-start) | collective-permute-done | bytes 32800 | tf_op jit(solution)/shard_map/ppermute | solution.py:59
  29.5 6.7 %all-to-all-done.1 = bf16[1,8,72,384]{3,2,0,1:T(8,128)(2,1)S(1)} async-done(((bf16[1,8,72,384]{3,2,0,1:T(8,128)(2,1)}), bf16[1,8,72,384]{3,2,0,1:T(8,128)(2,1)S(1)}, u32[]{:S(2)}, u32[]{:S(2)}) %all-to-all-start.1) | async-done | bytes 442400 | tf_op jit(solution)/shard_map/all_to_all | solution.py:99
  36.3 0.5 fusion.5
  37.1 0.6 fusion.6
  38.3 0.4 fusion.14
  38.7 0.9 %collective-permute-done.1 = bf16[2,192,384]{2,1,0:T(8,128)(2,1)S(1)} collective-permute-done((bf16[2,192,384]{2,1,0:T(8,128)(2,1)S(1)}, bf16[2,192,384]{2,1,0:T(8,128)(2,1)S(1)}, u32[]{:S(2)}, u32[]{:S(2)}) %collective-permute-start.1) | collective-permute-done | bytes 294944 | tf_op jit(solution)/shard_map/ppermute | solution.py:173
  39.9 0.6 %collective-permute-start.2 = (bf16[2,192,192]{2,1,0:T(8,128)(2,1)S(1)}, bf16[2,192,192]{2,1,0:T(8,128)(2,1)S(1)}, u32[]{:S(2)}, u32[]{:S(2)}) collective-permute-start(bf16[2,192,192]{2,1,0:T(8,128)(2,1)S(1)} %constant_dynamic-slice_fusion.1), channel_id=1, source_target_pairs={{0,4},{4,0},{1,5},{5,1},{2,6},{6,2},{3,7},{7,3},{8,12},{12,8},{9,1... | collective-permute-start | bytes 442376 | tf_op jit(solution)/shard_map/ppermute | solution.py:179
  40.5 0.4 convolution_add_fusion.1
  40.9 6.0 %collective-permute-done.2 = bf16[2,192,192]{2,1,0:T(8,128)(2,1)S(1)} collective-permute-done((bf16[2,192,192]{2,1,0:T(8,128)(2,1)S(1)}, bf16[2,192,192]{2,1,0:T(8,128)(2,1)S(1)}, u32[]{:S(2)}, u32[]{:S(2)}) %collective-permute-start.2) | collective-permute-done | bytes 147488 | tf_op jit(solution)/shard_map/ppermute | solution.py:179
  47.0 1.6 %collective-permute-start.3 = (bf16[2,192,192]{2,1,0:T(8,128)(2,1)S(1)}, bf16[2,192,192]{2,1,0:T(8,128)(2,1)S(1)}, u32[]{:S(2)}, u32[]{:S(2)}) collective-permute-start(bf16[2,192,192]{2,1,0:T(8,128)(2,1)S(1)} %add_convert_fusion.1), channel_id=1, source_target_pairs={{0,16},{8,24},{16,0},{24,8},{1,17},{9,25},{17,1},{25,9},{2,18},{10... | collective-permute-start | bytes 442376 | tf_op jit(solution)/shard_map/ppermute | solution.py:184
  48.8 4.4 %collective-permute-done.3 = bf16[2,192,192]{2,1,0:T(8,128)(2,1)S(1)} collective-permute-done((bf16[2,192,192]{2,1,0:T(8,128)(2,1)S(1)}, bf16[2,192,192]{2,1,0:T(8,128)(2,1)S(1)}, u32[]{:S(2)}, u32[]{:S(2)}) %collective-permute-start.3) | collective-permute-done | bytes 147488 | tf_op jit(solution)/shard_map/ppermute | solution.py:184
  53.7 1.1 %fusion.2 = bf16[1,512,384]{2,1,0:T(8,128)(2,1)} fusion(f32[512,384]{1,0:T(8,128)S(1)} %convolution_add_fusion.1, f32[512,384]{1,0:T(8,128)S(1)} %fusion.13, s32[128]{0:T(128)S(1)} %get-tuple-element.47, f32[128,384]{1,0:T(8,128)S(1)} %fusion.93), kind=kOutput, calls=%fused_computation.6 | convolution fusion | flops 51183616 | bytes 2163200 | tf_op jit(solution)/shard_map/bnr,bnc->brc/dot_general | solution.py:25
  55.2 0.9 %copy.16 = f32[384,192]{0,1:T(8,128)} copy(f32[384,192]{1,0:T(8,128)S(1)} %get-tuple-element.42) | data formatting | bytes 589824
  56.0 0.9 %copy.17 = f32[384,192]{0,1:T(8,128)} copy(f32[384,192]{1,0:T(8,128)S(1)} %get-tuple-element.41) | data formatting | bytes 589824
  (44 shorter events, 3.9 us)
Async XLA Ops:
  0.6 1.0 %copy-start = (bf16[1,512,384]{2,1,0:T(8,128)(2,1)S(1)}, bf16[1,512,384]{2,1,0:T(8,128)(2,1)}, u32[]{:S(2)}) copy-start(bf16[1,512,384]{2,1,0:T(8,128)(2,1)} %param.10) | copy-start | bytes 1179652
  0.7 0.7 %copy-start.4 = (s32[1,128]{1,0:T(1,128)S(1)}, s32[1,128]{1,0:T(1,128)}, u32[]{:S(2)}) copy-start(s32[1,128]{1,0:T(1,128)} %param.11) | copy-start | bytes 1540
  0.7 0.7 %copy-start.5 = (s32[1,128]{1,0:T(1,128)S(1)}, s32[1,128]{1,0:T(1,128)}, u32[]{:S(2)}) copy-start(s32[1,128]{1,0:T(1,128)} %param.12) | copy-start | bytes 1540
  1.9 1.0 %copy-start.2 = (bf16[384,384]{1,0:T(8,128)(2,1)S(1)}, bf16[384,384]{1,0:T(8,128)(2,1)}, u32[]{:S(2)}) copy-start(bf16[384,384]{1,0:T(8,128)(2,1)} %param.15) | copy-start | bytes 884740
  2.9 1.0 %copy-start.1 = (bf16[384,384]{1,0:T(8,128)(2,1)S(1)}, bf16[384,384]{1,0:T(8,128)(2,1)}, u32[]{:S(2)}) copy-start(bf16[384,384]{1,0:T(8,128)(2,1)} %param.14) | copy-start | bytes 884740
  4.8 13.8 %all-to-all-start = ((bf16[1,4,64,384]{3,2,0,1:T(8,128)(2,1)}), bf16[1,4,64,384]{3,2,0,1:T(8,128)(2,1)S(1)}, u32[]{:S(2)}, u32[]{:S(2)}) async-start(bf16[1,4,64,384]{3,2,0,1:T(8,128)(2,1)} %bitcast.11), calls=%async_computation | async-start | bytes 393216 | tf_op jit(solution)/shard_map/all_to_all | solution.py:83
  19.5 16.7 %all-to-all-start.1 = ((bf16[1,8,72,384]{3,2,0,1:T(8,128)(2,1)}), bf16[1,8,72,384]{3,2,0,1:T(8,128)(2,1)S(1)}, u32[]{:S(2)}, u32[]{:S(2)}) async-start(bf16[1,8,72,384]{3,2,0,1:T(8,128)(2,1)} %broadcast_in_dim.27), calls=%async_computation.1 | async-start | bytes 884736 | tf_op jit(solution)/shard_map/all_to_all | solution.py:99
  23.1 0.8 %copy-start.3 = (bf16[1,128,256]{2,1,0:T(8,128)(2,1)S(1)}, bf16[1,128,256]{2,1,0:T(8,128)(2,1)}, u32[]{:S(2)}) copy-start(bf16[1,128,256]{2,1,0:T(8,128)(2,1)} %param.13) | copy-start | bytes 196612
  24.0 5.5 %collective-permute-start = (bf16[1,128,128]{2,1,0:T(8,128)(2,1)S(1)}, bf16[1,128,128]{2,1,0:T(8,128)(2,1)S(1)}, u32[]{:S(2)}, u32[]{:S(2)}) collective-permute-start(bf16[1,128,128]{2,1,0:T(8,128)(2,1)S(1)} %get-tuple-element.45), channel_id=1, source_target_pairs={{0,4},{1,5},{2,6},{3,7},{8,12},{9,13},{10,14},{11,15},{16,20},{17,... | collective-permute-start | bytes 98312 | tf_op jit(solution)/shard_map/ppermute | solution.py:59
  38.0 1.6 %collective-permute-start.1 = (bf16[2,192,384]{2,1,0:T(8,128)(2,1)S(1)}, bf16[2,192,384]{2,1,0:T(8,128)(2,1)S(1)}, u32[]{:S(2)}, u32[]{:S(2)}) collective-permute-start(bf16[2,192,384]{2,1,0:T(8,128)(2,1)S(1)} %fusion.11), channel_id=1, source_target_pairs={{0,8},{8,0},{16,24},{24,16},{1,9},{9,1},{17,25},{25,17},{2,10},{10... | collective-permute-start | bytes 884744 | tf_op jit(solution)/shard_map/ppermute | solution.py:173
  39.9 7.0 %collective-permute-start.2 = (bf16[2,192,192]{2,1,0:T(8,128)(2,1)S(1)}, bf16[2,192,192]{2,1,0:T(8,128)(2,1)S(1)}, u32[]{:S(2)}, u32[]{:S(2)}) collective-permute-start(bf16[2,192,192]{2,1,0:T(8,128)(2,1)S(1)} %constant_dynamic-slice_fusion.1), channel_id=1, source_target_pairs={{0,4},{4,0},{1,5},{5,1},{2,6},{6,2},{3,7},{7,3},{8,12},{12,8},{9,1... | collective-permute-start | bytes 442376 | tf_op jit(solution)/shard_map/ppermute | solution.py:179
  47.0 6.2 %collective-permute-start.3 = (bf16[2,192,192]{2,1,0:T(8,128)(2,1)S(1)}, bf16[2,192,192]{2,1,0:T(8,128)(2,1)S(1)}, u32[]{:S(2)}, u32[]{:S(2)}) collective-permute-start(bf16[2,192,192]{2,1,0:T(8,128)(2,1)S(1)} %add_convert_fusion.1), channel_id=1, source_target_pairs={{0,16},{8,24},{16,0},{24,8},{1,17},{9,25},{17,1},{25,9},{2,18},{10... | collective-permute-start | bytes 442376 | tf_op jit(solution)/shard_map/ppermute | solution.py:184
  53.2 1.8 %collective-permute-start.4 = (f32[2,192,192]{2,1,0:T(8,128)S(1)}, f32[2,192,192]{2,1,0:T(8,128)S(1)}, u32[]{:S(2)}, u32[]{:S(2)}) collective-permute-start(f32[2,192,192]{2,1,0:T(8,128)S(1)} %convert_add_fusion), channel_id=1, source_target_pairs={{0,8},{8,0},{16,24},{24,16},{1,9},{9,1},{17,25},{25,17},{2,10},{10... | collective-permute-start | bytes 884744 | tf_op jit(solution)/shard_map/ppermute | solution.py:186

commit v5 on v3

--- a/solution.py
+++ b/solution.py
@@ -3,6 +3,7 @@
 import jax
 import jax.numpy as jnp
 from jax import lax
+from jax.experimental.layout import Layout, with_layout_constraint
 from jax.sharding import PartitionSpec as P
 
 
@@ -25,10 +26,10 @@
     return placed + jnp.einsum("bnr,bnc->brc", match_bf, lower, preferred_element_type=jnp.float32)
 
 
-def gather_by_permute(x, axes, count, me):
+def gather_by_permute(x, axes, count, me, keep=lambda i, j: True):
     pieces = [x]
     for k in range(1, count):
-        perm = [(i, (i + k) % count) for i in range(count)]
+        perm = [(i, (i + k) % count) for i in range(count) if keep(i, (i + k) % count)]
         pieces.append(lax.ppermute(x, axes, perm))
     by_offset = jnp.stack(pieces)
     order = (me - jnp.arange(count, dtype=jnp.int32)) % count
@@ -97,13 +98,18 @@
     flags = flags.at[:, 0, :slab_sites].set((donor_pos >= 0).astype(jnp.bfloat16))
     flags = flags.at[:, 1, :slab_sites].set((acceptor_pos >= 0).astype(jnp.bfloat16))
     packed = jnp.concatenate([feat_quarter, flags], axis=1)
-    gathered = gather_by_permute(packed, ("seq", "head"), n_seq * n_head, me)
+    keep = lambda i, j: (
+        i // n_head == j // n_head
+        or (i // n_head < j // n_head and (i % n_head) * quarter < slab_sites)
+        or (i // n_head > j // n_head and (i % n_head) * quarter >= slab_sites)
+    )
+    gathered = gather_by_permute(packed, ("seq", "head"), n_seq * n_head, me, keep)
     gathered = jnp.moveaxis(gathered, 0, 1).reshape(batch, n_seq, n_head, quarter + 8, width)
     feats = gathered[:, :, :, :quarter].reshape(batch, n_seq, both, width)
     donor_feat_all = feats[:, :, :slab_sites].reshape(batch, sites, width)
     acceptor_feat_all = feats[:, :, slab_sites:].reshape(batch, sites, width)
     donor_ok_all = (gathered[:, :, 0, quarter, :slab_sites] > 0).reshape(batch, sites)
-    acceptor_ok_all = (gathered[:, :, 0, quarter + 1, :slab_sites] > 0).reshape(batch, sites)
+    acceptor_ok_all = (gathered[:, :, n_head - 1, quarter + 1, :slab_sites] > 0).reshape(batch, sites)
 
     site_slab = jnp.arange(sites, dtype=jnp.int32) // slab_sites
     big = jnp.int32(1 << 30)
@@ -157,25 +163,25 @@
     )
     row_grad = place_rows(donor_match, donor_site) + place_rows(acceptor_match, acceptor_site)
 
-    local_dw = jnp.einsum("bnc,bnp->cp", donor_rows, donor_grad, preferred_element_type=jnp.float32)
+    local_dw = jnp.einsum("bnc,bnp->pc", donor_rows, donor_grad, preferred_element_type=jnp.float32)
     local_aw = jnp.einsum(
-        "bnc,bnp->cp", acceptor_rows, acceptor_grad, preferred_element_type=jnp.float32
+        "bnc,bnp->pc", acceptor_rows, acceptor_grad, preferred_element_type=jnp.float32
     )
     n_dp = lax.axis_size("dp")
     assert n_dp & (n_dp - 1) == 0 and n_dp >= 2
     dp = lax.axis_index("dp")
     pair = dp % 2
-    channels = local_dw.shape[0]
+    channels = local_dw.shape[1]
     half = channels // 2
     part = width // n_seq
     blocks = jnp.stack([local_dw, local_aw]).astype(jnp.bfloat16)
-    mine = lax.dynamic_slice_in_dim(blocks, pair * half, half, 1).astype(jnp.float32)
-    outgoing = lax.dynamic_slice_in_dim(blocks, (1 - pair) * half, half, 1)
+    mine = lax.dynamic_slice_in_dim(blocks, pair * half, half, 2).astype(jnp.float32)
+    outgoing = lax.dynamic_slice_in_dim(blocks, (1 - pair) * half, half, 2)
     mine = mine + lax.ppermute(outgoing, "dp", [(i, i ^ 1) for i in range(n_dp)]).astype(jnp.float32)
     held = mine.astype(jnp.bfloat16)
-    mine = lax.dynamic_slice_in_dim(held, slab * part, part, 2).astype(jnp.float32)
+    mine = lax.dynamic_slice_in_dim(held, slab * part, part, 1).astype(jnp.float32)
     for k in range(1, n_seq):
-        outgoing = lax.dynamic_slice_in_dim(held, ((slab + k) % n_seq) * part, part, 2)
+        outgoing = lax.dynamic_slice_in_dim(held, ((slab + k) % n_seq) * part, part, 1)
         perm = [(i, (i + k) % n_seq) for i in range(n_seq)]
         mine = mine + lax.ppermute(outgoing, "seq", perm).astype(jnp.float32)
     bit = 2
@@ -185,8 +191,12 @@
         mine = held.astype(jnp.float32) + lax.ppermute(held, "dp", perm).astype(jnp.float32)
         bit *= 2
     other = lax.ppermute(mine, "dp", [(i, i ^ 1) for i in range(n_dp)])
-    mine = jnp.where(pair == 0, jnp.concatenate([mine, other], 1), jnp.concatenate([other, mine], 1))
-    return (row_grad.astype(jnp.bfloat16), mine[0], mine[1])
+    mine = jnp.where(pair == 0, jnp.concatenate([mine, other], 2), jnp.concatenate([other, mine], 2))
+    mine = jnp.swapaxes(mine, 1, 2)
+    column_major = Layout(major_to_minor=(1, 0))
+    grad_dw = with_layout_constraint(mine[0], column_major)
+    grad_aw = with_layout_constraint(mine[1], column_major)
+    return (row_grad.astype(jnp.bfloat16), grad_dw, grad_aw)
 
 
 def solution(mesh):

time: 54 us -> 62.9 us (1.16)
  starting transfers between devices: 25.3 us -> 33.6 us
  waiting for transfers between devices: 14.9 us -> 16 us
  local copies, waits for them, and re-layouts: 5.54 us -> 4.5 us
    ppermute x7, starting transfers between devices: 13 us -> 22.3 us  [gather_by_permute(): pieces.append(lax.ppermute(x, axes, perm))]
    unnamed x20 -> x18, local copies, waits for them, and re-layouts: 3.54 us -> 1.81 us
    ppermute x1, starting transfers between devices: 1.11 us -> 0.07 us  [shards(): mine = mine + lax.ppermute(outgoing, 'seq', perm).astype(jnp.float32)]
    ppermute x1, waiting for transfers between devices: 5.51 us -> 6.54 us  [shards(): mine = mine + lax.ppermute(outgoing, 'seq', perm).astype(jnp.float32)]
    squeeze x1, local copies, waits for them, and re-layouts: 0.05 us -> 0.85 us  [shards(): grad_aw = with_layout_constraint(mine[1], column_major)]
  transfers between devices with their start and end apart: 15 -> 15, of which waited for: 7 -> 7; matrix products, arithmetic and copies ran while one was open for 6% -> 5% of each run, Pallas kernels for 0% -> 0%
where the time goes in v5:
time: 62.9 us; the launch traced here: 62.6 us
  starting transfers between devices  33.6 us (53%)
  waiting for transfers between devices  16 us (25%)
  matrix products  5.27 us (8%)
  local copies, waits for them, and re-layouts  4.5 us (7%)
  other arithmetic  1.92 us (3%)
  between operations  1.28 us (2%)
    ppermute x7, starting transfers between devices, gather_by_permute(): pieces.append(lax.ppermute(x, axes, perm))  22.3 us
    ppermute x1, waiting for transfers between devices, shards(): mine = mine + lax.ppermute(outgoing, 'seq', perm).astype(jnp.float32)  6.54 us
    ppermute x3, starting transfers between devices, shards(): pieces.append(lax.ppermute(outgoing, 'head', perm))  6.11 us
    ppermute x1, waiting for transfers between devices, shards(): lax.ppermute(held, 'dp', perm).astype(jnp.float32)  4.39 us
    ppermute x1, starting transfers between devices, shards(): arrived = lax.ppermute(outgoing, 'seq', perm)  3.43 us
    ppermute x7, waiting for transfers between devices, gather_by_permute(): pieces.append(lax.ppermute(x, axes, perm))  2.56 us
    unnamed x18, local copies, waits for them, and re-layouts  1.81 us
    ppermute x1, starting transfers between devices, shards(): lax.ppermute(held, 'dp', perm).astype(jnp.float32)  1.56 us
  transfers between devices with their start and end apart: 15, of which 7 were waited for; matrix products, arithmetic and copies ran while one was open for 5% of the time, Pallas kernels for 0%

profile of v5, /device:TPU:0, one launch (start us, length us, event | category | flops | bytes accessed | tf_op | source)
XLA Modules:
  0.0 62.6 jit_solution(2313080167006866629)
XLA Ops:
  0.7 0.7 %copy-done.4 = s32[1,128]{1,0:T(1,128)S(1)} copy-done((s32[1,128]{1,0:T(1,128)S(1)}, s32[1,128]{1,0:T(1,128)}, u32[]{:S(2)}) %copy-start.4) | copy-done | bytes 536
  2.2 0.7 %copy-done.1 = bf16[384,384]{1,0:T(8,128)(2,1)S(1)} copy-done((bf16[384,384]{1,0:T(8,128)(2,1)S(1)}, bf16[384,384]{1,0:T(8,128)(2,1)}, u32[]{:S(2)}) %copy-start.1) | copy-done | bytes 294936
  3.8 5.1 %collective-permute-start.2 = (bf16[1,64,384]{2,1,0:T(8,128)(2,1)S(1)}, bf16[1,64,384]{2,1,0:T(8,128)(2,1)S(1)}, u32[]{:S(2)}, u32[]{:S(2)}) collective-permute-start(bf16[1,64,384]{2,1,0:T(8,128)(2,1)S(1)} %get-tuple-element.36), channel_id=1, source_target_pairs={{0,3},{1,0},{2,1},{3,2},{4,7},{5,4},{6,5},{7,6},{8,11},{9,8},{10,9... | collective-permute-start | bytes 147464 | tf_op jit(solution)/shard_map/ppermute | solution.py:88
  8.9 1.0 %collective-permute-start = (bf16[1,64,384]{2,1,0:T(8,128)(2,1)S(1)}, bf16[1,64,384]{2,1,0:T(8,128)(2,1)S(1)}, u32[]{:S(2)}, u32[]{:S(2)}) collective-permute-start(bf16[1,64,384]{2,1,0:T(8,128)(2,1)S(1)} %get-tuple-element.34), channel_id=1, source_target_pairs={{0,1},{1,2},{2,3},{3,0},{4,5},{5,6},{6,7},{7,4},{8,9},{9,10},{10,1... | collective-permute-start | bytes 147464 | tf_op jit(solution)/shard_map/ppermute | solution.py:88
  10.0 3.4 %collective-permute-start.10 = (bf16[1,128,128]{2,1,0:T(8,128)(2,1)S(1)}, bf16[1,128,128]{2,1,0:T(8,128)(2,1)S(1)}, u32[]{:S(2)}, u32[]{:S(2)}) collective-permute-start(bf16[1,128,128]{2,1,0:T(8,128)(2,1)S(1)} %get-tuple-element.37), channel_id=1, source_target_pairs={{0,4},{1,5},{2,6},{3,7},{8,12},{9,13},{10,14},{11,15},{16,20},{17,... | collective-permute-start | bytes 98312 | tf_op jit(solution)/shard_map/ppermute | solution.py:60
  13.8 1.2 %collective-permute-done.10 = bf16[1,128,128]{2,1,0:T(8,128)(2,1)S(1)} collective-permute-done((bf16[1,128,128]{2,1,0:T(8,128)(2,1)S(1)}, bf16[1,128,128]{2,1,0:T(8,128)(2,1)S(1)}, u32[]{:S(2)}, u32[]{:S(2)}) %collective-permute-start.10) | collective-permute-done | bytes 32800 | tf_op jit(solution)/shard_map/ppermute | solution.py:60
  15.1 0.6 gather_fusion
  15.8 4.4 %collective-permute-start.3 = (bf16[1,72,384]{2,1,0:T(8,128)(2,1)S(1)}, bf16[1,72,384]{2,1,0:T(8,128)(2,1)S(1)}, u32[]{:S(2)}, u32[]{:S(2)}) collective-permute-start(bf16[1,72,384]{2,1,0:T(8,128)(2,1)S(1)} %pad_maximum_fusion), channel_id=1, source_target_pairs={{0,1},{1,2},{2,3},{4,5},{5,6},{6,7},{7,0},{8,9},{9,10},{10,11},{12... | collective-permute-start | bytes 165896 | tf_op jit(solution)/shard_map/ppermute | solution.py:33
  20.2 2.8 %collective-permute-start.4 = (bf16[1,72,384]{2,1,0:T(8,128)(2,1)S(1)}, bf16[1,72,384]{2,1,0:T(8,128)(2,1)S(1)}, u32[]{:S(2)}, u32[]{:S(2)}) collective-permute-start(bf16[1,72,384]{2,1,0:T(8,128)(2,1)S(1)} %pad_maximum_fusion), channel_id=1, source_target_pairs={{0,2},{1,3},{4,6},{5,7},{6,0},{7,1},{8,10},{9,11},{12,14},{13,15},... | collective-permute-start | bytes 165896 | tf_op jit(solution)/shard_map/ppermute | solution.py:33
  23.1 1.3 %collective-permute-start.5 = (bf16[1,72,384]{2,1,0:T(8,128)(2,1)S(1)}, bf16[1,72,384]{2,1,0:T(8,128)(2,1)S(1)}, u32[]{:S(2)}, u32[]{:S(2)}) collective-permute-start(bf16[1,72,384]{2,1,0:T(8,128)(2,1)S(1)} %pad_maximum_fusion), channel_id=1, source_target_pairs={{0,3},{1,4},{4,7},{6,1},{7,2},{8,11},{9,12},{12,15},{14,9},{15,10}... | collective-permute-start | bytes 165896 | tf_op jit(solution)/shard_map/ppermute | solution.py:33
  24.4 5.5 %collective-permute-start.6 = (bf16[1,72,384]{2,1,0:T(8,128)(2,1)S(1)}, bf16[1,72,384]{2,1,0:T(8,128)(2,1)S(1)}, u32[]{:S(2)}, u32[]{:S(2)}) collective-permute-start(bf16[1,72,384]{2,1,0:T(8,128)(2,1)S(1)} %pad_maximum_fusion), channel_id=1, source_target_pairs={{0,4},{1,5},{6,2},{7,3},{8,12},{9,13},{14,10},{15,11},{16,20},{17,... | collective-permute-start | bytes 165896 | tf_op jit(solution)/shard_map/ppermute | solution.py:33
  29.8 1.9 %collective-permute-start.7 = (bf16[1,72,384]{2,1,0:T(8,128)(2,1)S(1)}, bf16[1,72,384]{2,1,0:T(8,128)(2,1)S(1)}, u32[]{:S(2)}, u32[]{:S(2)}) collective-permute-start(bf16[1,72,384]{2,1,0:T(8,128)(2,1)S(1)} %pad_maximum_fusion), channel_id=1, source_target_pairs={{0,5},{1,6},{3,0},{6,3},{7,4},{8,13},{9,14},{11,8},{14,11},{15,12}... | collective-permute-start | bytes 165896 | tf_op jit(solution)/shard_map/ppermute | solution.py:33
  31.8 1.9 %collective-permute-start.8 = (bf16[1,72,384]{2,1,0:T(8,128)(2,1)S(1)}, bf16[1,72,384]{2,1,0:T(8,128)(2,1)S(1)}, u32[]{:S(2)}, u32[]{:S(2)}) collective-permute-start(bf16[1,72,384]{2,1,0:T(8,128)(2,1)S(1)} %pad_maximum_fusion), channel_id=1, source_target_pairs={{0,6},{1,7},{2,0},{3,1},{6,4},{7,5},{8,14},{9,15},{10,8},{11,9},{1... | collective-permute-start | bytes 165896 | tf_op jit(solution)/shard_map/ppermute | solution.py:33
  33.7 4.5 %collective-permute-start.9 = (bf16[1,72,384]{2,1,0:T(8,128)(2,1)S(1)}, bf16[1,72,384]{2,1,0:T(8,128)(2,1)S(1)}, u32[]{:S(2)}, u32[]{:S(2)}) collective-permute-start(bf16[1,72,384]{2,1,0:T(8,128)(2,1)S(1)} %pad_maximum_fusion), channel_id=1, source_target_pairs={{0,7},{1,0},{2,1},{3,2},{5,4},{6,5},{7,6},{8,15},{9,8},{10,9},{11,... | collective-permute-start | bytes 165896 | tf_op jit(solution)/shard_map/ppermute | solution.py:33
  38.4 1.2 %collective-permute-done.8 = bf16[1,72,384]{2,1,0:T(8,128)(2,1)S(1)} collective-permute-done((bf16[1,72,384]{2,1,0:T(8,128)(2,1)S(1)}, bf16[1,72,384]{2,1,0:T(8,128)(2,1)S(1)}, u32[]{:S(2)}, u32[]{:S(2)}) %collective-permute-start.8) | collective-permute-done | bytes 55328 | tf_op jit(solution)/shard_map/ppermute | solution.py:33
  39.6 1.3 %collective-permute-done.9 = bf16[1,72,384]{2,1,0:T(8,128)(2,1)S(1)} collective-permute-done((bf16[1,72,384]{2,1,0:T(8,128)(2,1)S(1)}, bf16[1,72,384]{2,1,0:T(8,128)(2,1)S(1)}, u32[]{:S(2)}, u32[]{:S(2)}) %collective-permute-start.9) | collective-permute-done | bytes 55328 | tf_op jit(solution)/shard_map/ppermute | solution.py:33
  41.0 0.6 %gather_fusion.1 = bf16[8,72,384]{2,1,0:T(8,128)(2,1)S(1)} fusion(bf16[8,72,384]{2,1,0:T(8,128)(2,1)S(1)} %bitcast.181, s32[1024]{0:T(1024)S(1)} %pad_clamp_fusion), kind=kCustom, calls=%fused_computation.1 | custom fusion | bytes 884768 | tf_op jit(solution)/shard_map/jit(_take)/gather | solution.py:36
  43.3 0.6 fusion.6
  45.0 1.1 %collective-permute-done.11 = bf16[2,384,192]{2,1,0:T(8,128)(2,1)S(1)} collective-permute-done((bf16[2,384,192]{2,1,0:T(8,128)(2,1)S(1)}, bf16[2,384,192]{2,1,0:T(8,128)(2,1)S(1)}, u32[]{:S(2)}, u32[]{:S(2)}) %collective-permute-start.11) | collective-permute-done | bytes 294944 | tf_op jit(solution)/shard_map/ppermute | solution.py:180
  46.8 6.5 %collective-permute-done.12 = bf16[2,192,192]{2,1,0:T(8,128)(2,1)S(1)} collective-permute-done((bf16[2,192,192]{2,1,0:T(8,128)(2,1)S(1)}, bf16[2,192,192]{2,1,0:T(8,128)(2,1)S(1)}, u32[]{:S(2)}, u32[]{:S(2)}) %collective-permute-start.12) | collective-permute-done | bytes 147488 | tf_op jit(solution)/shard_map/ppermute | solution.py:186
  53.4 1.6 %collective-permute-start.13 = (bf16[2,192,192]{2,1,0:T(8,128)(2,1)S(1)}, bf16[2,192,192]{2,1,0:T(8,128)(2,1)S(1)}, u32[]{:S(2)}, u32[]{:S(2)}) collective-permute-start(bf16[2,192,192]{2,1,0:T(8,128)(2,1)S(1)} %add_convert_fusion.1), channel_id=1, source_target_pairs={{0,16},{8,24},{16,0},{24,8},{1,17},{9,25},{17,1},{25,9},{2,18},{10... | collective-permute-start | bytes 442376 | tf_op jit(solution)/shard_map/ppermute | solution.py:191
  55.2 4.4 %collective-permute-done.13 = bf16[2,192,192]{2,1,0:T(8,128)(2,1)S(1)} collective-permute-done((bf16[2,192,192]{2,1,0:T(8,128)(2,1)S(1)}, bf16[2,192,192]{2,1,0:T(8,128)(2,1)S(1)}, u32[]{:S(2)}, u32[]{:S(2)}) %collective-permute-start.13) | collective-permute-done | bytes 147488 | tf_op jit(solution)/shard_map/ppermute | solution.py:191
  60.1 1.1 %fusion.2 = bf16[1,512,384]{2,1,0:T(8,128)(2,1)} fusion(f32[512,384]{1,0:T(8,128)S(1)} %convolution_add_fusion.1, f32[512,384]{1,0:T(8,128)S(1)} %fusion.14, s32[128]{0:T(128)S(1)} %get-tuple-element.39, f32[128,384]{1,0:T(8,128)S(1)} %fusion.109), kind=kOutput, calls=%fused_computation.8 | convolution fusion | flops 51183616 | bytes 2163200 | tf_op jit(solution)/shard_map/bnr,bnc->brc/dot_general | solution.py:26
  61.7 0.9 %slice_bitcast_fusion = (f32[384,192]{0,1:T(8,128)}, f32[384,192]{0,1:T(8,128)}) fusion(f32[2,384,192]{1,2,0:T(8,128)S(1)} %fusion.9), kind=kLoop, calls=%fused_computation.39 | loop fusion | bytes 1179648 | tf_op jit(solution)/shard_map/squeeze | solution.py:198
  (74 shorter events, 7.0 us)
Async XLA Ops:
  0.6 1.0 %copy-start = (bf16[1,512,384]{2,1,0:T(8,128)(2,1)S(1)}, bf16[1,512,384]{2,1,0:T(8,128)(2,1)}, u32[]{:S(2)}) copy-start(bf16[1,512,384]{2,1,0:T(8,128)(2,1)} %param.10) | copy-start | bytes 1179652
  0.7 0.7 %copy-start.4 = (s32[1,128]{1,0:T(1,128)S(1)}, s32[1,128]{1,0:T(1,128)}, u32[]{:S(2)}) copy-start(s32[1,128]{1,0:T(1,128)} %param.11) | copy-start | bytes 1540
  0.7 0.7 %copy-start.5 = (s32[1,128]{1,0:T(1,128)S(1)}, s32[1,128]{1,0:T(1,128)}, u32[]{:S(2)}) copy-start(s32[1,128]{1,0:T(1,128)} %param.12) | copy-start | bytes 1540
  1.9 1.0 %copy-start.1 = (bf16[384,384]{1,0:T(8,128)(2,1)S(1)}, bf16[384,384]{1,0:T(8,128)(2,1)}, u32[]{:S(2)}) copy-start(bf16[384,384]{1,0:T(8,128)(2,1)} %param.14) | copy-start | bytes 884740
  2.2 1.0 %copy-start.2 = (bf16[384,384]{1,0:T(8,128)(2,1)S(1)}, bf16[384,384]{1,0:T(8,128)(2,1)}, u32[]{:S(2)}) copy-start(bf16[384,384]{1,0:T(8,128)(2,1)} %param.15) | copy-start | bytes 884740
  3.8 6.1 %copy-start.3 = (bf16[1,128,256]{2,1,0:T(8,128)(2,1)S(1)}, bf16[1,128,256]{2,1,0:T(8,128)(2,1)}, u32[]{:S(2)}) copy-start(bf16[1,128,256]{2,1,0:T(8,128)(2,1)} %param.13) | copy-start | bytes 196612
  3.8 11.2 %collective-permute-start.2 = (bf16[1,64,384]{2,1,0:T(8,128)(2,1)S(1)}, bf16[1,64,384]{2,1,0:T(8,128)(2,1)S(1)}, u32[]{:S(2)}, u32[]{:S(2)}) collective-permute-start(bf16[1,64,384]{2,1,0:T(8,128)(2,1)S(1)} %get-tuple-element.36), channel_id=1, source_target_pairs={{0,3},{1,0},{2,1},{3,2},{4,7},{5,4},{6,5},{7,6},{8,11},{9,8},{10,9... | collective-permute-start | bytes 147464 | tf_op jit(solution)/shard_map/ppermute | solution.py:88
  8.9 6.1 %collective-permute-start.1 = (bf16[1,64,384]{2,1,0:T(8,128)(2,1)S(1)}, bf16[1,64,384]{2,1,0:T(8,128)(2,1)S(1)}, u32[]{:S(2)}, u32[]{:S(2)}) collective-permute-start(bf16[1,64,384]{2,1,0:T(8,128)(2,1)S(1)} %get-tuple-element.35), channel_id=1, source_target_pairs={{0,2},{1,3},{2,0},{3,1},{4,6},{5,7},{6,4},{7,5},{8,10},{9,11},{10,... | collective-permute-start | bytes 147464 | tf_op jit(solution)/shard_map/ppermute | solution.py:88
  8.9 6.1 %collective-permute-start = (bf16[1,64,384]{2,1,0:T(8,128)(2,1)S(1)}, bf16[1,64,384]{2,1,0:T(8,128)(2,1)S(1)}, u32[]{:S(2)}, u32[]{:S(2)}) collective-permute-start(bf16[1,64,384]{2,1,0:T(8,128)(2,1)S(1)} %get-tuple-element.34), channel_id=1, source_target_pairs={{0,1},{1,2},{2,3},{3,0},{4,5},{5,6},{6,7},{7,4},{8,9},{9,10},{10,1... | collective-permute-start | bytes 147464 | tf_op jit(solution)/shard_map/ppermute | solution.py:88
  10.0 5.0 %collective-permute-start.10 = (bf16[1,128,128]{2,1,0:T(8,128)(2,1)S(1)}, bf16[1,128,128]{2,1,0:T(8,128)(2,1)S(1)}, u32[]{:S(2)}, u32[]{:S(2)}) collective-permute-start(bf16[1,128,128]{2,1,0:T(8,128)(2,1)S(1)} %get-tuple-element.37), channel_id=1, source_target_pairs={{0,4},{1,5},{2,6},{3,7},{8,12},{9,13},{10,14},{11,15},{16,20},{17,... | collective-permute-start | bytes 98312 | tf_op jit(solution)/shard_map/ppermute | solution.py:60
  15.8 15.9 %collective-permute-start.3 = (bf16[1,72,384]{2,1,0:T(8,128)(2,1)S(1)}, bf16[1,72,384]{2,1,0:T(8,128)(2,1)S(1)}, u32[]{:S(2)}, u32[]{:S(2)}) collective-permute-start(bf16[1,72,384]{2,1,0:T(8,128)(2,1)S(1)} %pad_maximum_fusion), channel_id=1, source_target_pairs={{0,1},{1,2},{2,3},{4,5},{5,6},{6,7},{7,0},{8,9},{9,10},{10,11},{12... | collective-permute-start | bytes 165896 | tf_op jit(solution)/shard_map/ppermute | solution.py:33
  20.2 13.5 %collective-permute-start.4 = (bf16[1,72,384]{2,1,0:T(8,128)(2,1)S(1)}, bf16[1,72,384]{2,1,0:T(8,128)(2,1)S(1)}, u32[]{:S(2)}, u32[]{:S(2)}) collective-permute-start(bf16[1,72,384]{2,1,0:T(8,128)(2,1)S(1)} %pad_maximum_fusion), channel_id=1, source_target_pairs={{0,2},{1,3},{4,6},{5,7},{6,0},{7,1},{8,10},{9,11},{12,14},{13,15},... | collective-permute-start | bytes 165896 | tf_op jit(solution)/shard_map/ppermute | solution.py:33
  23.1 15.2 %collective-permute-start.5 = (bf16[1,72,384]{2,1,0:T(8,128)(2,1)S(1)}, bf16[1,72,384]{2,1,0:T(8,128)(2,1)S(1)}, u32[]{:S(2)}, u32[]{:S(2)}) collective-permute-start(bf16[1,72,384]{2,1,0:T(8,128)(2,1)S(1)} %pad_maximum_fusion), channel_id=1, source_target_pairs={{0,3},{1,4},{4,7},{6,1},{7,2},{8,11},{9,12},{12,15},{14,9},{15,10}... | collective-permute-start | bytes 165896 | tf_op jit(solution)/shard_map/ppermute | solution.py:33
  24.4 14.0 %collective-permute-start.6 = (bf16[1,72,384]{2,1,0:T(8,128)(2,1)S(1)}, bf16[1,72,384]{2,1,0:T(8,128)(2,1)S(1)}, u32[]{:S(2)}, u32[]{:S(2)}) collective-permute-start(bf16[1,72,384]{2,1,0:T(8,128)(2,1)S(1)} %pad_maximum_fusion), channel_id=1, source_target_pairs={{0,4},{1,5},{6,2},{7,3},{8,12},{9,13},{14,10},{15,11},{16,20},{17,... | collective-permute-start | bytes 165896 | tf_op jit(solution)/shard_map/ppermute | solution.py:33
  29.8 8.5 %collective-permute-start.7 = (bf16[1,72,384]{2,1,0:T(8,128)(2,1)S(1)}, bf16[1,72,384]{2,1,0:T(8,128)(2,1)S(1)}, u32[]{:S(2)}, u32[]{:S(2)}) collective-permute-start(bf16[1,72,384]{2,1,0:T(8,128)(2,1)S(1)} %pad_maximum_fusion), channel_id=1, source_target_pairs={{0,5},{1,6},{3,0},{6,3},{7,4},{8,13},{9,14},{11,8},{14,11},{15,12}... | collective-permute-start | bytes 165896 | tf_op jit(solution)/shard_map/ppermute | solution.py:33
  31.8 7.9 %collective-permute-start.8 = (bf16[1,72,384]{2,1,0:T(8,128)(2,1)S(1)}, bf16[1,72,384]{2,1,0:T(8,128)(2,1)S(1)}, u32[]{:S(2)}, u32[]{:S(2)}) collective-permute-start(bf16[1,72,384]{2,1,0:T(8,128)(2,1)S(1)} %pad_maximum_fusion), channel_id=1, source_target_pairs={{0,6},{1,7},{2,0},{3,1},{6,4},{7,5},{8,14},{9,15},{10,8},{11,9},{1... | collective-permute-start | bytes 165896 | tf_op jit(solution)/shard_map/ppermute | solution.py:33
  33.7 7.2 %collective-permute-start.9 = (bf16[1,72,384]{2,1,0:T(8,128)(2,1)S(1)}, bf16[1,72,384]{2,1,0:T(8,128)(2,1)S(1)}, u32[]{:S(2)}, u32[]{:S(2)}) collective-permute-start(bf16[1,72,384]{2,1,0:T(8,128)(2,1)S(1)} %pad_maximum_fusion), channel_id=1, source_target_pairs={{0,7},{1,0},{2,1},{3,2},{5,4},{6,5},{7,6},{8,15},{9,8},{10,9},{11,... | collective-permute-start | bytes 165896 | tf_op jit(solution)/shard_map/ppermute | solution.py:33
  44.3 1.8 %collective-permute-start.11 = (bf16[2,384,192]{2,1,0:T(8,128)(2,1)S(1)}, bf16[2,384,192]{2,1,0:T(8,128)(2,1)S(1)}, u32[]{:S(2)}, u32[]{:S(2)}) collective-permute-start(bf16[2,384,192]{2,1,0:T(8,128)(2,1)S(1)} %fusion.10), channel_id=1, source_target_pairs={{0,8},{8,0},{16,24},{24,16},{1,9},{9,1},{17,25},{25,17},{2,10},{10... | collective-permute-start | bytes 884744 | tf_op jit(solution)/shard_map/ppermute | solution.py:180
  46.4 7.0 %collective-permute-start.12 = (bf16[2,192,192]{2,1,0:T(8,128)(2,1)S(1)}, bf16[2,192,192]{2,1,0:T(8,128)(2,1)S(1)}, u32[]{:S(2)}, u32[]{:S(2)}) collective-permute-start(bf16[2,192,192]{2,1,0:T(8,128)(2,1)S(1)} %constant_dynamic-slice_fusion.1), channel_id=1, source_target_pairs={{0,4},{4,0},{1,5},{5,1},{2,6},{6,2},{3,7},{7,3},{8,12},{12,8},{9,1... | collective-permute-start | bytes 442376 | tf_op jit(solution)/shard_map/ppermute | solution.py:186
  53.4 6.2 %collective-permute-start.13 = (bf16[2,192,192]{2,1,0:T(8,128)(2,1)S(1)}, bf16[2,192,192]{2,1,0:T(8,128)(2,1)S(1)}, u32[]{:S(2)}, u32[]{:S(2)}) collective-permute-start(bf16[2,192,192]{2,1,0:T(8,128)(2,1)S(1)} %add_convert_fusion.1), channel_id=1, source_target_pairs={{0,16},{8,24},{16,0},{24,8},{1,17},{9,25},{17,1},{25,9},{2,18},{10... | collective-permute-start | bytes 442376 | tf_op jit(solution)/shard_map/ppermute | solution.py:191
  59.7 1.8 %collective-permute-start.14 = (f32[2,192,192]{2,1,0:T(8,128)S(1)}, f32[2,192,192]{2,1,0:T(8,128)S(1)}, u32[]{:S(2)}, u32[]{:S(2)}) collective-permute-start(f32[2,192,192]{2,1,0:T(8,128)S(1)} %convert_add_fusion), channel_id=1, source_target_pairs={{0,8},{8,0},{16,24},{24,16},{1,9},{9,1},{17,25},{25,17},{2,10},{10... | collective-permute-start | bytes 884744 | tf_op jit(solution)/shard_map/ppermute | solution.py:193

commit v6 on v5

--- a/solution.py
+++ b/solution.py
@@ -26,10 +26,10 @@
     return placed + jnp.einsum("bnr,bnc->brc", match_bf, lower, preferred_element_type=jnp.float32)
 
 
-def gather_by_permute(x, axes, count, me, keep=lambda i, j: True):
+def gather_by_permute(x, axes, count, me):
     pieces = [x]
     for k in range(1, count):
-        perm = [(i, (i + k) % count) for i in range(count) if keep(i, (i + k) % count)]
+        perm = [(i, (i + k) % count) for i in range(count)]
         pieces.append(lax.ppermute(x, axes, perm))
     by_offset = jnp.stack(pieces)
     order = (me - jnp.arange(count, dtype=jnp.int32)) % count
@@ -93,23 +93,52 @@
         total = total + by_head[h].astype(jnp.float32)
     feat_quarter = total.astype(jnp.bfloat16)
 
+    slab_feats = gather_by_permute(feat_quarter, ("head",), n_head, head)
+    slab_feats = jnp.moveaxis(slab_feats, 0, 1).reshape(batch, both, width)
+    own_donor = slab_feats[:, :slab_sites]
+    own_acceptor = slab_feats[:, slab_sites:]
+
     assert slab_sites <= width
     flags = jnp.zeros((batch, 8, width), jnp.bfloat16)
     flags = flags.at[:, 0, :slab_sites].set((donor_pos >= 0).astype(jnp.bfloat16))
     flags = flags.at[:, 1, :slab_sites].set((acceptor_pos >= 0).astype(jnp.bfloat16))
-    packed = jnp.concatenate([feat_quarter, flags], axis=1)
-    keep = lambda i, j: (
-        i // n_head == j // n_head
-        or (i // n_head < j // n_head and (i % n_head) * quarter < slab_sites)
-        or (i // n_head > j // n_head and (i % n_head) * quarter >= slab_sites)
-    )
-    gathered = gather_by_permute(packed, ("seq", "head"), n_seq * n_head, me, keep)
-    gathered = jnp.moveaxis(gathered, 0, 1).reshape(batch, n_seq, n_head, quarter + 8, width)
-    feats = gathered[:, :, :, :quarter].reshape(batch, n_seq, both, width)
-    donor_feat_all = feats[:, :, :slab_sites].reshape(batch, sites, width)
-    acceptor_feat_all = feats[:, :, slab_sites:].reshape(batch, sites, width)
-    donor_ok_all = (gathered[:, :, 0, quarter, :slab_sites] > 0).reshape(batch, sites)
-    acceptor_ok_all = (gathered[:, :, n_head - 1, quarter + 1, :slab_sites] > 0).reshape(batch, sites)
+    donor_feat_all = jnp.zeros((batch, sites, width), jnp.bfloat16)
+    acceptor_feat_all = jnp.zeros((batch, sites, width), jnp.bfloat16)
+    donor_feat_all = lax.dynamic_update_slice_in_dim(donor_feat_all, own_donor, slab * slab_sites, 1)
+    acceptor_feat_all = lax.dynamic_update_slice_in_dim(
+        acceptor_feat_all, own_acceptor, slab * slab_sites, 1
+    )
+    donor_ok_all = jnp.zeros((batch, sites), jnp.bool_)
+    acceptor_ok_all = jnp.zeros((batch, sites), jnp.bool_)
+    for k in range(1, n_seq):
+        sent = jnp.where(slab + k < n_seq, own_donor, own_acceptor)
+        perm = [(i, (i + k) % n_seq) for i in range(n_seq)]
+        arrived = lax.ppermute(jnp.concatenate([sent, flags], axis=1), "seq", perm)
+        source = (slab - k) % n_seq
+        earlier = slab >= k
+        feat_in = arrived[:, :slab_sites]
+        donor_feat_all = jnp.where(
+            earlier,
+            lax.dynamic_update_slice_in_dim(donor_feat_all, feat_in, source * slab_sites, 1),
+            donor_feat_all,
+        )
+        acceptor_feat_all = jnp.where(
+            earlier,
+            acceptor_feat_all,
+            lax.dynamic_update_slice_in_dim(acceptor_feat_all, feat_in, source * slab_sites, 1),
+        )
+        donor_in = arrived[:, slab_sites, :slab_sites] > 0
+        acceptor_in = arrived[:, slab_sites + 1, :slab_sites] > 0
+        donor_ok_all = jnp.where(
+            earlier,
+            lax.dynamic_update_slice_in_dim(donor_ok_all, donor_in, source * slab_sites, 1),
+            donor_ok_all,
+        )
+        acceptor_ok_all = jnp.where(
+            earlier,
+            acceptor_ok_all,
+            lax.dynamic_update_slice_in_dim(acceptor_ok_all, acceptor_in, source * slab_sites, 1),
+        )
 
     site_slab = jnp.arange(sites, dtype=jnp.int32) // slab_sites
     big = jnp.int32(1 << 30)
@@ -132,8 +161,8 @@
         ),
     )
 
-    donor_feat = lax.dynamic_slice_in_dim(donor_feat_all, slab * slab_sites, slab_sites, 1)
-    acceptor_feat = lax.dynamic_slice_in_dim(acceptor_feat_all, slab * slab_sites, slab_sites, 1)
+    donor_feat = own_donor
+    acceptor_feat = own_acceptor
 
     scores_row = (
         jnp.einsum("bip,bjp->bij", donor_feat, acceptor_feat_all, preferred_element_type=jnp.float32)

time: 62.9 us -> 52.6 us (0.84)
  starting transfers between devices: 33.6 us -> 19.7 us
  waiting for transfers between devices: 16 us -> 20.4 us
    ppermute x7 -> x3, starting transfers between devices: 22.3 us -> 3.99 us  [gather_by_permute(): pieces.append(lax.ppermute(x, axes, perm))]
    ppermute x7 -> x3, waiting for transfers between devices: 2.56 us -> 5.85 us  [gather_by_permute(): pieces.append(lax.ppermute(x, axes, perm))]
    ppermute x0 -> x1, waiting for transfers between devices: none -> 2.55 us  [shards(): arrived = lax.ppermute(jnp.concatenate([sent, flags], axis=1), 'seq', perm)]
    ppermute x0 -> x1, starting transfers between devices: none -> 2.38 us  [shards(): arrived = lax.ppermute(jnp.concatenate([sent, flags], axis=1), 'seq', perm)]
    ppermute x1, starting transfers between devices: 0.07 us -> 2.09 us  [shards(): mine = mine + lax.ppermute(outgoing, 'seq', perm).astype(jnp.float32)]
    ppermute x1, waiting for transfers between devices: 6.54 us -> 4.81 us  [shards(): mine = mine + lax.ppermute(outgoing, 'seq', perm).astype(jnp.float32)]
    unnamed x18 -> x14, local copies, waits for them, and re-layouts: 1.81 us -> 1.78 us
  transfers between devices with their start and end apart: 15 -> 12, of which waited for: 7 -> 9; matrix products, arithmetic and copies ran while one was open for 5% -> 6% of each run, Pallas kernels for 0% -> 0%
where the time goes in v6:
time: 52.6 us; the launch traced here: 52.4 us
  waiting for transfers between devices  20.4 us (39%)
  starting transfers between devices  19.7 us (37%)
  matrix products  5.26 us (10%)
  local copies, waits for them, and re-layouts  4.11 us (8%)
  other arithmetic  1.7 us (3%)
  between operations  1.2 us (2%)
    ppermute x3, starting transfers between devices, shards(): pieces.append(lax.ppermute(outgoing, 'head', perm))  6.11 us
    ppermute x3, waiting for transfers between devices, gather_by_permute(): pieces.append(lax.ppermute(x, axes, perm))  5.85 us
    ppermute x1, waiting for transfers between devices, shards(): mine = mine + lax.ppermute(outgoing, 'seq', perm).astype(jnp.float32)  4.81 us
    ppermute x1, waiting for transfers between devices, shards(): lax.ppermute(held, 'dp', perm).astype(jnp.float32)  4.71 us
    ppermute x3, starting transfers between devices, gather_by_permute(): pieces.append(lax.ppermute(x, axes, perm))  3.99 us
    ppermute x1, starting transfers between devices, shards(): arrived = lax.ppermute(outgoing, 'seq', perm)  3.43 us
    ppermute x1, waiting for transfers between devices, shards(): arrived = lax.ppermute(jnp.concatenate([sent, flags], axis=1), 'seq', perm)  2.55 us
    ppermute x1, starting transfers between devices, shards(): arrived = lax.ppermute(jnp.concatenate([sent, flags], axis=1), 'seq', perm)  2.38 us
  transfers between devices with their start and end apart: 12, of which 9 were waited for; matrix products, arithmetic and copies ran while one was open for 6% of the time, Pallas kernels for 0%

profile of v6, /device:TPU:0, one launch (start us, length us, event | category | flops | bytes accessed | tf_op | source)
XLA Modules:
  0.0 52.4 jit_solution(4830175733638598314)
XLA Ops:
  0.7 0.7 %copy-done.4 = s32[1,128]{1,0:T(1,128)S(1)} copy-done((s32[1,128]{1,0:T(1,128)S(1)}, s32[1,128]{1,0:T(1,128)}, u32[]{:S(2)}) %copy-start.4) | copy-done | bytes 536
  2.2 0.7 %copy-done.1 = bf16[384,384]{1,0:T(8,128)(2,1)S(1)} copy-done((bf16[384,384]{1,0:T(8,128)(2,1)S(1)}, bf16[384,384]{1,0:T(8,128)(2,1)}, u32[]{:S(2)}) %copy-start.1) | copy-done | bytes 294936
  3.8 5.1 %collective-permute-start.2 = (bf16[1,64,384]{2,1,0:T(8,128)(2,1)S(1)}, bf16[1,64,384]{2,1,0:T(8,128)(2,1)S(1)}, u32[]{:S(2)}, u32[]{:S(2)}) collective-permute-start(bf16[1,64,384]{2,1,0:T(8,128)(2,1)S(1)} %get-tuple-element.35), channel_id=1, source_target_pairs={{0,3},{1,0},{2,1},{3,2},{4,7},{5,4},{6,5},{7,6},{8,11},{9,8},{10,9... | collective-permute-start | bytes 147464 | tf_op jit(solution)/shard_map/ppermute | solution.py:88
  8.9 1.0 %collective-permute-start = (bf16[1,64,384]{2,1,0:T(8,128)(2,1)S(1)}, bf16[1,64,384]{2,1,0:T(8,128)(2,1)S(1)}, u32[]{:S(2)}, u32[]{:S(2)}) collective-permute-start(bf16[1,64,384]{2,1,0:T(8,128)(2,1)S(1)} %get-tuple-element.33), channel_id=1, source_target_pairs={{0,1},{1,2},{2,3},{3,0},{4,5},{5,6},{6,7},{7,4},{8,9},{9,10},{10,1... | collective-permute-start | bytes 147464 | tf_op jit(solution)/shard_map/ppermute | solution.py:88
  10.0 3.4 %collective-permute-start.7 = (bf16[1,128,128]{2,1,0:T(8,128)(2,1)S(1)}, bf16[1,128,128]{2,1,0:T(8,128)(2,1)S(1)}, u32[]{:S(2)}, u32[]{:S(2)}) collective-permute-start(bf16[1,128,128]{2,1,0:T(8,128)(2,1)S(1)} %get-tuple-element.38), channel_id=1, source_target_pairs={{0,4},{1,5},{2,6},{3,7},{8,12},{9,13},{10,14},{11,15},{16,20},{17,... | collective-permute-start | bytes 98312 | tf_op jit(solution)/shard_map/ppermute | solution.py:60
  13.8 1.2 %collective-permute-done.7 = bf16[1,128,128]{2,1,0:T(8,128)(2,1)S(1)} collective-permute-done((bf16[1,128,128]{2,1,0:T(8,128)(2,1)S(1)}, bf16[1,128,128]{2,1,0:T(8,128)(2,1)S(1)}, u32[]{:S(2)}, u32[]{:S(2)}) %collective-permute-start.7) | collective-permute-done | bytes 32800 | tf_op jit(solution)/shard_map/ppermute | solution.py:60
  15.1 0.6 %gather_fusion = bf16[4,64,384]{2,1,0:T(8,128)(2,1)S(1)} fusion(bf16[4,64,384]{2,1,0:T(8,128)(2,1)S(1)} %maximum_bitcast_fusion, s32[1024]{0:T(1024)S(1)} %pad_clamp_fusion), kind=kCustom, calls=%fused_computation.clone | custom fusion | bytes 393232 | tf_op jit(solution)/shard_map/jit(_take)/gather | solution.py:90
  15.8 2.9 %collective-permute-start.5 = (bf16[1,64,384]{2,1,0:T(8,128)(2,1)S(1)}, bf16[1,64,384]{2,1,0:T(8,128)(2,1)S(1)}, u32[]{:S(2)}, u32[]{:S(2)}) collective-permute-start(bf16[1,64,384]{2,1,0:T(8,128)(2,1)S(1)} %fusion.109), channel_id=1, source_target_pairs={{0,3},{1,0},{2,1},{3,2},{4,7},{5,4},{6,5},{7,6},{8,11},{9,8},{10,9... | collective-permute-start | bytes 147464 | tf_op jit(solution)/shard_map/ppermute | solution.py:33
  18.7 1.1 %collective-permute-start.4 = (bf16[1,64,384]{2,1,0:T(8,128)(2,1)S(1)}, bf16[1,64,384]{2,1,0:T(8,128)(2,1)S(1)}, u32[]{:S(2)}, u32[]{:S(2)}) collective-permute-start(bf16[1,64,384]{2,1,0:T(8,128)(2,1)S(1)} %fusion.109), channel_id=1, source_target_pairs={{0,2},{1,3},{2,0},{3,1},{4,6},{5,7},{6,4},{7,5},{8,10},{9,11},{10,... | collective-permute-start | bytes 147464 | tf_op jit(solution)/shard_map/ppermute | solution.py:33
  19.8 0.6 %collective-permute-done.5 = bf16[1,64,384]{2,1,0:T(8,128)(2,1)S(1)} collective-permute-done((bf16[1,64,384]{2,1,0:T(8,128)(2,1)S(1)}, bf16[1,64,384]{2,1,0:T(8,128)(2,1)S(1)}, u32[]{:S(2)}, u32[]{:S(2)}) %collective-permute-start.5) | collective-permute-done | bytes 49184 | tf_op jit(solution)/shard_map/ppermute | solution.py:33
  20.4 3.2 %collective-permute-done.4 = bf16[1,64,384]{2,1,0:T(8,128)(2,1)S(1)} collective-permute-done((bf16[1,64,384]{2,1,0:T(8,128)(2,1)S(1)}, bf16[1,64,384]{2,1,0:T(8,128)(2,1)S(1)}, u32[]{:S(2)}, u32[]{:S(2)}) %collective-permute-start.4) | collective-permute-done | bytes 49184 | tf_op jit(solution)/shard_map/ppermute | solution.py:33
  23.7 2.0 %collective-permute-done.3 = bf16[1,64,384]{2,1,0:T(8,128)(2,1)S(1)} collective-permute-done((bf16[1,64,384]{2,1,0:T(8,128)(2,1)S(1)}, bf16[1,64,384]{2,1,0:T(8,128)(2,1)S(1)}, u32[]{:S(2)}, u32[]{:S(2)}) %collective-permute-start.3) | collective-permute-done | bytes 49184 | tf_op jit(solution)/shard_map/ppermute | solution.py:33
  25.7 0.6 %gather_fusion.1 = bf16[4,64,384]{2,1,0:T(8,128)(2,1)S(1)} fusion(bf16[4,64,384]{2,1,0:T(8,128)(2,1)S(1)} %maximum_bitcast_fusion.1, s32[1024]{0:T(1024)S(1)} %pad_clamp_fusion), kind=kCustom, calls=%fused_computation.1.clone | custom fusion | bytes 393232 | tf_op jit(solution)/shard_map/jit(_take)/gather | solution.py:36
  26.5 2.4 %collective-permute-start.6 = (bf16[1,136,384]{2,1,0:T(8,128)(2,1)S(1)}, bf16[1,136,384]{2,1,0:T(8,128)(2,1)S(1)}, u32[]{:S(2)}, u32[]{:S(2)}) collective-permute-start(bf16[1,136,384]{2,1,0:T(8,128)(2,1)S(1)} %pad_maximum_fusion), channel_id=1, source_target_pairs={{0,4},{4,0},{1,5},{5,1},{2,6},{6,2},{3,7},{7,3},{8,12},{12,8},{9,1... | collective-permute-start | bytes 313352 | tf_op jit(solution)/shard_map/ppermute | solution.py:116
  29.0 2.5 %collective-permute-done.6 = bf16[1,136,384]{2,1,0:T(8,128)(2,1)S(1)} collective-permute-done((bf16[1,136,384]{2,1,0:T(8,128)(2,1)S(1)}, bf16[1,136,384]{2,1,0:T(8,128)(2,1)S(1)}, u32[]{:S(2)}, u32[]{:S(2)}) %collective-permute-start.6) | collective-permute-done | bytes 104480 | tf_op jit(solution)/shard_map/ppermute | solution.py:116
  31.8 0.5 %fusion.5 = bf16[128,384]{1,0:T(8,128)(2,1)S(1)} fusion(bf16[256,384]{1,0:T(8,128)(2,1)S(1)} %get-tuple-element.37, bf16[1,128,256]{2,1,0:T(8,128)(2,1)S(1)} %copy-done.3, bf16[1,256,384]{2,1,0:T(8,128)(2,1)S(1)} %bitcast.162, s32[256]{0:T(256)S(1)} %bitcast.178, s32[128]{0:T(128)S(1)} %bitcast.173, pred[128]{0:T(512)(128)(4,1)S(1)} %broadcast_compare_fusion.1), kind=kOutput, calls=%fused_computation.13 | convolution fusion | flops 51052544 | bytes 657408 | tf_op jit(solution)/shard_map/bij,bjp->bip/dot_general | solution.py:174
  32.6 0.5 %fusion.6 = bf16[128,384]{1,0:T(8,128)(2,1)S(1)} fusion(bf16[256,384]{1,0:T(8,128)(2,1)S(1)} %get-tuple-element.36, bf16[1,256,128]{2,1,0:T(8,128)(2,1)S(1)} %select_dynamic-update-slice_fusion, bf16[1,256,384]{2,1,0:T(8,128)(2,1)S(1)} %bitcast.163, s32[128]{0:T(128)S(1)} %bitcast.175, s32[256]{0:T(256)S(1)} %bitcast.177, ...), kind=kOutput, calls=%fused_computation.14 | convolution fusion | flops 51052544 | bytes 657408 | tf_op jit(solution)/shard_map/bij,bip->bjp/dot_general | solution.py:185
  34.3 1.1 %collective-permute-done.8 = bf16[2,384,192]{2,1,0:T(8,128)(2,1)S(1)} collective-permute-done((bf16[2,384,192]{2,1,0:T(8,128)(2,1)S(1)}, bf16[2,384,192]{2,1,0:T(8,128)(2,1)S(1)}, u32[]{:S(2)}, u32[]{:S(2)}) %collective-permute-start.8) | collective-permute-done | bytes 294944 | tf_op jit(solution)/shard_map/ppermute | solution.py:209
  35.6 2.1 %collective-permute-start.9 = (bf16[2,192,192]{2,1,0:T(8,128)(2,1)S(1)}, bf16[2,192,192]{2,1,0:T(8,128)(2,1)S(1)}, u32[]{:S(2)}, u32[]{:S(2)}) collective-permute-start(bf16[2,192,192]{2,1,0:T(8,128)(2,1)S(1)} %constant_dynamic-slice_fusion.1), channel_id=1, source_target_pairs={{0,4},{4,0},{1,5},{5,1},{2,6},{6,2},{3,7},{7,3},{8,12},{12,8},{9,1... | collective-permute-start | bytes 442376 | tf_op jit(solution)/shard_map/ppermute | solution.py:215
  38.1 4.8 %collective-permute-done.9 = bf16[2,192,192]{2,1,0:T(8,128)(2,1)S(1)} collective-permute-done((bf16[2,192,192]{2,1,0:T(8,128)(2,1)S(1)}, bf16[2,192,192]{2,1,0:T(8,128)(2,1)S(1)}, u32[]{:S(2)}, u32[]{:S(2)}) %collective-permute-start.9) | collective-permute-done | bytes 147488 | tf_op jit(solution)/shard_map/ppermute | solution.py:215
  43.0 1.6 %collective-permute-start.10 = (bf16[2,192,192]{2,1,0:T(8,128)(2,1)S(1)}, bf16[2,192,192]{2,1,0:T(8,128)(2,1)S(1)}, u32[]{:S(2)}, u32[]{:S(2)}) collective-permute-start(bf16[2,192,192]{2,1,0:T(8,128)(2,1)S(1)} %add_convert_fusion.1), channel_id=1, source_target_pairs={{0,16},{8,24},{16,0},{24,8},{1,17},{9,25},{17,1},{25,9},{2,18},{10... | collective-permute-start | bytes 442376 | tf_op jit(solution)/shard_map/ppermute | solution.py:220
  44.7 4.7 %collective-permute-done.10 = bf16[2,192,192]{2,1,0:T(8,128)(2,1)S(1)} collective-permute-done((bf16[2,192,192]{2,1,0:T(8,128)(2,1)S(1)}, bf16[2,192,192]{2,1,0:T(8,128)(2,1)S(1)}, u32[]{:S(2)}, u32[]{:S(2)}) %collective-permute-start.10) | collective-permute-done | bytes 147488 | tf_op jit(solution)/shard_map/ppermute | solution.py:220
  50.0 1.1 %fusion.2 = bf16[1,512,384]{2,1,0:T(8,128)(2,1)} fusion(f32[512,384]{1,0:T(8,128)S(1)} %convolution_add_fusion.1, f32[512,384]{1,0:T(8,128)S(1)} %fusion.14, s32[128]{0:T(128)S(1)} %get-tuple-element.40, f32[128,384]{1,0:T(8,128)S(1)} %fusion.92), kind=kOutput, calls=%fused_computation.8 | convolution fusion | flops 51183616 | bytes 2163200 | tf_op jit(solution)/shard_map/bnr,bnc->brc/dot_general | solution.py:26
  51.6 0.9 %slice_bitcast_fusion = (f32[384,192]{0,1:T(8,128)}, f32[384,192]{0,1:T(8,128)}) fusion(f32[2,384,192]{1,2,0:T(8,128)S(1)} %fusion.9), kind=kLoop, calls=%fused_computation.38 | loop fusion | bytes 1179648 | tf_op jit(solution)/shard_map/squeeze | solution.py:227
  (70 shorter events, 5.8 us)
Async XLA Ops:
  0.6 1.0 %copy-start = (bf16[1,512,384]{2,1,0:T(8,128)(2,1)S(1)}, bf16[1,512,384]{2,1,0:T(8,128)(2,1)}, u32[]{:S(2)}) copy-start(bf16[1,512,384]{2,1,0:T(8,128)(2,1)} %param.12) | copy-start | bytes 1179652
  0.7 0.7 %copy-start.4 = (s32[1,128]{1,0:T(1,128)S(1)}, s32[1,128]{1,0:T(1,128)}, u32[]{:S(2)}) copy-start(s32[1,128]{1,0:T(1,128)} %param.13) | copy-start | bytes 1540
  0.7 0.7 %copy-start.5 = (s32[1,128]{1,0:T(1,128)S(1)}, s32[1,128]{1,0:T(1,128)}, u32[]{:S(2)}) copy-start(s32[1,128]{1,0:T(1,128)} %param.14) | copy-start | bytes 1540
  1.9 1.0 %copy-start.1 = (bf16[384,384]{1,0:T(8,128)(2,1)S(1)}, bf16[384,384]{1,0:T(8,128)(2,1)}, u32[]{:S(2)}) copy-start(bf16[384,384]{1,0:T(8,128)(2,1)} %param.16) | copy-start | bytes 884740
  2.2 1.0 %copy-start.2 = (bf16[384,384]{1,0:T(8,128)(2,1)S(1)}, bf16[384,384]{1,0:T(8,128)(2,1)}, u32[]{:S(2)}) copy-start(bf16[384,384]{1,0:T(8,128)(2,1)} %param.17) | copy-start | bytes 884740
  3.8 6.1 %copy-start.3 = (bf16[1,128,256]{2,1,0:T(8,128)(2,1)S(1)}, bf16[1,128,256]{2,1,0:T(8,128)(2,1)}, u32[]{:S(2)}) copy-start(bf16[1,128,256]{2,1,0:T(8,128)(2,1)} %param.15) | copy-start | bytes 196612
  3.8 11.2 %collective-permute-start.2 = (bf16[1,64,384]{2,1,0:T(8,128)(2,1)S(1)}, bf16[1,64,384]{2,1,0:T(8,128)(2,1)S(1)}, u32[]{:S(2)}, u32[]{:S(2)}) collective-permute-start(bf16[1,64,384]{2,1,0:T(8,128)(2,1)S(1)} %get-tuple-element.35), channel_id=1, source_target_pairs={{0,3},{1,0},{2,1},{3,2},{4,7},{5,4},{6,5},{7,6},{8,11},{9,8},{10,9... | collective-permute-start | bytes 147464 | tf_op jit(solution)/shard_map/ppermute | solution.py:88
  8.9 6.1 %collective-permute-start.1 = (bf16[1,64,384]{2,1,0:T(8,128)(2,1)S(1)}, bf16[1,64,384]{2,1,0:T(8,128)(2,1)S(1)}, u32[]{:S(2)}, u32[]{:S(2)}) collective-permute-start(bf16[1,64,384]{2,1,0:T(8,128)(2,1)S(1)} %get-tuple-element.34), channel_id=1, source_target_pairs={{0,2},{1,3},{2,0},{3,1},{4,6},{5,7},{6,4},{7,5},{8,10},{9,11},{10,... | collective-permute-start | bytes 147464 | tf_op jit(solution)/shard_map/ppermute | solution.py:88
  8.9 6.1 %collective-permute-start = (bf16[1,64,384]{2,1,0:T(8,128)(2,1)S(1)}, bf16[1,64,384]{2,1,0:T(8,128)(2,1)S(1)}, u32[]{:S(2)}, u32[]{:S(2)}) collective-permute-start(bf16[1,64,384]{2,1,0:T(8,128)(2,1)S(1)} %get-tuple-element.33), channel_id=1, source_target_pairs={{0,1},{1,2},{2,3},{3,0},{4,5},{5,6},{6,7},{7,4},{8,9},{9,10},{10,1... | collective-permute-start | bytes 147464 | tf_op jit(solution)/shard_map/ppermute | solution.py:88
  10.0 5.0 %collective-permute-start.7 = (bf16[1,128,128]{2,1,0:T(8,128)(2,1)S(1)}, bf16[1,128,128]{2,1,0:T(8,128)(2,1)S(1)}, u32[]{:S(2)}, u32[]{:S(2)}) collective-permute-start(bf16[1,128,128]{2,1,0:T(8,128)(2,1)S(1)} %get-tuple-element.38), channel_id=1, source_target_pairs={{0,4},{1,5},{2,6},{3,7},{8,12},{9,13},{10,14},{11,15},{16,20},{17,... | collective-permute-start | bytes 98312 | tf_op jit(solution)/shard_map/ppermute | solution.py:60
  15.8 4.6 %collective-permute-start.5 = (bf16[1,64,384]{2,1,0:T(8,128)(2,1)S(1)}, bf16[1,64,384]{2,1,0:T(8,128)(2,1)S(1)}, u32[]{:S(2)}, u32[]{:S(2)}) collective-permute-start(bf16[1,64,384]{2,1,0:T(8,128)(2,1)S(1)} %fusion.109), channel_id=1, source_target_pairs={{0,3},{1,0},{2,1},{3,2},{4,7},{5,4},{6,5},{7,6},{8,11},{9,8},{10,9... | collective-permute-start | bytes 147464 | tf_op jit(solution)/shard_map/ppermute | solution.py:33
  18.7 5.0 %collective-permute-start.4 = (bf16[1,64,384]{2,1,0:T(8,128)(2,1)S(1)}, bf16[1,64,384]{2,1,0:T(8,128)(2,1)S(1)}, u32[]{:S(2)}, u32[]{:S(2)}) collective-permute-start(bf16[1,64,384]{2,1,0:T(8,128)(2,1)S(1)} %fusion.109), channel_id=1, source_target_pairs={{0,2},{1,3},{2,0},{3,1},{4,6},{5,7},{6,4},{7,5},{8,10},{9,11},{10,... | collective-permute-start | bytes 147464 | tf_op jit(solution)/shard_map/ppermute | solution.py:33
  19.8 5.9 %collective-permute-start.3 = (bf16[1,64,384]{2,1,0:T(8,128)(2,1)S(1)}, bf16[1,64,384]{2,1,0:T(8,128)(2,1)S(1)}, u32[]{:S(2)}, u32[]{:S(2)}) collective-permute-start(bf16[1,64,384]{2,1,0:T(8,128)(2,1)S(1)} %fusion.109), channel_id=1, source_target_pairs={{0,1},{1,2},{2,3},{3,0},{4,5},{5,6},{6,7},{7,4},{8,9},{9,10},{10,1... | collective-permute-start | bytes 147464 | tf_op jit(solution)/shard_map/ppermute | solution.py:33
  26.5 5.0 %collective-permute-start.6 = (bf16[1,136,384]{2,1,0:T(8,128)(2,1)S(1)}, bf16[1,136,384]{2,1,0:T(8,128)(2,1)S(1)}, u32[]{:S(2)}, u32[]{:S(2)}) collective-permute-start(bf16[1,136,384]{2,1,0:T(8,128)(2,1)S(1)} %pad_maximum_fusion), channel_id=1, source_target_pairs={{0,4},{4,0},{1,5},{5,1},{2,6},{6,2},{3,7},{7,3},{8,12},{12,8},{9,1... | collective-permute-start | bytes 313352 | tf_op jit(solution)/shard_map/ppermute | solution.py:116
  33.6 1.8 %collective-permute-start.8 = (bf16[2,384,192]{2,1,0:T(8,128)(2,1)S(1)}, bf16[2,384,192]{2,1,0:T(8,128)(2,1)S(1)}, u32[]{:S(2)}, u32[]{:S(2)}) collective-permute-start(bf16[2,384,192]{2,1,0:T(8,128)(2,1)S(1)} %fusion.10), channel_id=1, source_target_pairs={{0,8},{8,0},{16,24},{24,16},{1,9},{9,1},{17,25},{25,17},{2,10},{10... | collective-permute-start | bytes 884744 | tf_op jit(solution)/shard_map/ppermute | solution.py:209
  35.6 7.3 %collective-permute-start.9 = (bf16[2,192,192]{2,1,0:T(8,128)(2,1)S(1)}, bf16[2,192,192]{2,1,0:T(8,128)(2,1)S(1)}, u32[]{:S(2)}, u32[]{:S(2)}) collective-permute-start(bf16[2,192,192]{2,1,0:T(8,128)(2,1)S(1)} %constant_dynamic-slice_fusion.1), channel_id=1, source_target_pairs={{0,4},{4,0},{1,5},{5,1},{2,6},{6,2},{3,7},{7,3},{8,12},{12,8},{9,1... | collective-permute-start | bytes 442376 | tf_op jit(solution)/shard_map/ppermute | solution.py:215
  43.0 6.5 %collective-permute-start.10 = (bf16[2,192,192]{2,1,0:T(8,128)(2,1)S(1)}, bf16[2,192,192]{2,1,0:T(8,128)(2,1)S(1)}, u32[]{:S(2)}, u32[]{:S(2)}) collective-permute-start(bf16[2,192,192]{2,1,0:T(8,128)(2,1)S(1)} %add_convert_fusion.1), channel_id=1, source_target_pairs={{0,16},{8,24},{16,0},{24,8},{1,17},{9,25},{17,1},{25,9},{2,18},{10... | collective-permute-start | bytes 442376 | tf_op jit(solution)/shard_map/ppermute | solution.py:220
  49.5 1.8 %collective-permute-start.11 = (f32[2,192,192]{2,1,0:T(8,128)S(1)}, f32[2,192,192]{2,1,0:T(8,128)S(1)}, u32[]{:S(2)}, u32[]{:S(2)}) collective-permute-start(f32[2,192,192]{2,1,0:T(8,128)S(1)} %convert_add_fusion), channel_id=1, source_target_pairs={{0,8},{8,0},{16,24},{24,16},{1,9},{9,1},{17,25},{25,17},{2,10},{10... | collective-permute-start | bytes 884744 | tf_op jit(solution)/shard_map/ppermute | solution.py:222

commit v7 on v6

--- a/solution.py
+++ b/solution.py
@@ -81,19 +81,22 @@
     assert both % n_head == 0
     quarter = both // n_head
     parts = jnp.concatenate([donor_part, acceptor_part], axis=1)
+    assert n_head & (n_head - 1) == 0
     pieces = [lax.dynamic_slice_in_dim(parts, head * quarter, quarter, 1)]
     for k in range(1, n_head):
-        outgoing = lax.dynamic_slice_in_dim(parts, ((head + k) % n_head) * quarter, quarter, 1)
-        perm = [(i, (i + k) % n_head) for i in range(n_head)]
-        pieces.append(lax.ppermute(outgoing, "head", perm))
-    by_offset = jnp.stack(pieces)
-    by_head = jnp.take(by_offset, (head - jnp.arange(n_head, dtype=jnp.int32)) % n_head, axis=0)
+        outgoing = lax.dynamic_slice_in_dim(parts, (head ^ k) * quarter, quarter, 1)
+        pieces.append(lax.ppermute(outgoing, "head", [(i, i ^ k) for i in range(n_head)]))
+    by_partner = jnp.stack(pieces)
+    by_head = jnp.take(by_partner, head ^ jnp.arange(n_head, dtype=jnp.int32), axis=0)
     total = jnp.zeros((batch, quarter, width), jnp.float32)
     for h in range(n_head):
         total = total + by_head[h].astype(jnp.float32)
     feat_quarter = total.astype(jnp.bfloat16)
 
-    slab_feats = gather_by_permute(feat_quarter, ("head",), n_head, head)
+    pieces = [feat_quarter]
+    for k in range(1, n_head):
+        pieces.append(lax.ppermute(feat_quarter, "head", [(i, i ^ k) for i in range(n_head)]))
+    slab_feats = jnp.take(jnp.stack(pieces), head ^ jnp.arange(n_head, dtype=jnp.int32), axis=0)
     slab_feats = jnp.moveaxis(slab_feats, 0, 1).reshape(batch, both, width)
     own_donor = slab_feats[:, :slab_sites]
     own_acceptor = slab_feats[:, slab_sites:]

time: 52.6 us -> 51.2 us (0.973)
  waiting for transfers between devices: 20.4 us -> 18.8 us
    ppermute x6, waiting for transfers between devices: 5.86 us -> 4.18 us  [the longest x3 4.17 us: shards(): lax.ppermute(feat_quarter, 'head', [(i, i ^ k) for i in range(n_head)])]
  transfers between devices with their start and end apart: 12 -> 12, of which waited for: 9 -> 8; matrix products, arithmetic and copies ran while one was open for 6% -> 6% of each run, Pallas kernels for 0% -> 0%
where the time goes in v7:
time: 51.2 us; the launch traced here: 51 us
  starting transfers between devices  19.9 us (39%)
  waiting for transfers between devices  18.8 us (37%)
  matrix products  5.26 us (10%)
  local copies, waits for them, and re-layouts  4.14 us (8%)
  other arithmetic  1.69 us (3%)
  between operations  1.19 us (2%)
    ppermute x3, starting transfers between devices, shards(): lax.ppermute(outgoing, 'head', [(i, i ^ k) for i in range(n_head)])  5.76 us
    ppermute x1, waiting for transfers between devices, shards(): mine = mine + lax.ppermute(outgoing, 'seq', perm).astype(jnp.float32)  4.81 us
    ppermute x1, waiting for transfers between devices, shards(): lax.ppermute(held, 'dp', perm).astype(jnp.float32)  4.71 us
    ppermute x3, starting transfers between devices, shards(): lax.ppermute(feat_quarter, 'head', [(i, i ^ k) for i in range(n_head)])  4.45 us
    ppermute x3, waiting for transfers between devices, shards(): lax.ppermute(feat_quarter, 'head', [(i, i ^ k) for i in range(n_head)])  4.17 us
    ppermute x1, starting transfers between devices, shards(): arrived = lax.ppermute(outgoing, 'seq', perm)  3.57 us
    ppermute x1, waiting for transfers between devices, shards(): arrived = lax.ppermute(jnp.concatenate([sent, flags], axis=1), 'seq', perm)  2.55 us
    ppermute x1, starting transfers between devices, shards(): arrived = lax.ppermute(jnp.concatenate([sent, flags], axis=1), 'seq', perm)  2.38 us
  transfers between devices with their start and end apart: 12, of which 8 were waited for; matrix products, arithmetic and copies ran while one was open for 6% of the time, Pallas kernels for 0%

profile of v7, /device:TPU:0, one launch (start us, length us, event | category | flops | bytes accessed | tf_op | source)
XLA Modules:
  0.0 51.0 jit_solution(5636647215134152841)
XLA Ops:
  0.7 0.7 %copy-done.4 = s32[1,128]{1,0:T(1,128)S(1)} copy-done((s32[1,128]{1,0:T(1,128)S(1)}, s32[1,128]{1,0:T(1,128)}, u32[]{:S(2)}) %copy-start.4) | copy-done | bytes 536
  2.2 0.7 %copy-done.1 = bf16[384,384]{1,0:T(8,128)(2,1)S(1)} copy-done((bf16[384,384]{1,0:T(8,128)(2,1)S(1)}, bf16[384,384]{1,0:T(8,128)(2,1)}, u32[]{:S(2)}) %copy-start.1) | copy-done | bytes 294936
  3.8 5.1 %collective-permute-start.2 = (bf16[1,64,384]{2,1,0:T(8,128)(2,1)S(1)}, bf16[1,64,384]{2,1,0:T(8,128)(2,1)S(1)}, u32[]{:S(2)}, u32[]{:S(2)}) collective-permute-start(bf16[1,64,384]{2,1,0:T(8,128)(2,1)S(1)} %get-tuple-element.35), channel_id=1, source_target_pairs={{0,3},{1,2},{2,1},{3,0},{4,7},{5,6},{6,5},{7,4},{8,11},{9,10},{10,... | collective-permute-start | bytes 147464 | tf_op jit(solution)/shard_map/ppermute | solution.py:88
  8.9 0.6 %collective-permute-start = (bf16[1,64,384]{2,1,0:T(8,128)(2,1)S(1)}, bf16[1,64,384]{2,1,0:T(8,128)(2,1)S(1)}, u32[]{:S(2)}, u32[]{:S(2)}) collective-permute-start(bf16[1,64,384]{2,1,0:T(8,128)(2,1)S(1)} %get-tuple-element.33), channel_id=1, source_target_pairs={{0,1},{1,0},{2,3},{3,2},{4,5},{5,4},{6,7},{7,6},{8,9},{9,8},{10,11... | collective-permute-start | bytes 147464 | tf_op jit(solution)/shard_map/ppermute | solution.py:88
  9.6 3.6 %collective-permute-start.7 = (bf16[1,128,128]{2,1,0:T(8,128)(2,1)S(1)}, bf16[1,128,128]{2,1,0:T(8,128)(2,1)S(1)}, u32[]{:S(2)}, u32[]{:S(2)}) collective-permute-start(bf16[1,128,128]{2,1,0:T(8,128)(2,1)S(1)} %get-tuple-element.38), channel_id=1, source_target_pairs={{0,4},{1,5},{2,6},{3,7},{8,12},{9,13},{10,14},{11,15},{16,20},{17,... | collective-permute-start | bytes 98312 | tf_op jit(solution)/shard_map/ppermute | solution.py:60
  13.6 1.2 %collective-permute-done.7 = bf16[1,128,128]{2,1,0:T(8,128)(2,1)S(1)} collective-permute-done((bf16[1,128,128]{2,1,0:T(8,128)(2,1)S(1)}, bf16[1,128,128]{2,1,0:T(8,128)(2,1)S(1)}, u32[]{:S(2)}, u32[]{:S(2)}) %collective-permute-start.7) | collective-permute-done | bytes 32800 | tf_op jit(solution)/shard_map/ppermute | solution.py:60
  14.9 0.6 %gather_fusion = bf16[4,64,384]{2,1,0:T(8,128)(2,1)S(1)} fusion(bf16[4,64,384]{2,1,0:T(8,128)(2,1)S(1)} %maximum_bitcast_fusion, s32[1024]{0:T(1024)S(1)} %pad_clamp_fusion), kind=kCustom, calls=%fused_computation.clone | custom fusion | bytes 393232 | tf_op jit(solution)/shard_map/jit(_take)/gather | solution.py:90
  15.6 3.7 %collective-permute-start.5 = (bf16[1,64,384]{2,1,0:T(8,128)(2,1)S(1)}, bf16[1,64,384]{2,1,0:T(8,128)(2,1)S(1)}, u32[]{:S(2)}, u32[]{:S(2)}) collective-permute-start(bf16[1,64,384]{2,1,0:T(8,128)(2,1)S(1)} %fusion.108), channel_id=1, source_target_pairs={{0,3},{1,2},{2,1},{3,0},{4,7},{5,6},{6,5},{7,4},{8,11},{9,10},{10,... | collective-permute-start | bytes 147464 | tf_op jit(solution)/shard_map/ppermute | solution.py:98
  19.3 0.8 %collective-permute-start.3 = (bf16[1,64,384]{2,1,0:T(8,128)(2,1)S(1)}, bf16[1,64,384]{2,1,0:T(8,128)(2,1)S(1)}, u32[]{:S(2)}, u32[]{:S(2)}) collective-permute-start(bf16[1,64,384]{2,1,0:T(8,128)(2,1)S(1)} %fusion.108), channel_id=1, source_target_pairs={{0,1},{1,0},{2,3},{3,2},{4,5},{5,4},{6,7},{7,6},{8,9},{9,8},{10,11... | collective-permute-start | bytes 147464 | tf_op jit(solution)/shard_map/ppermute | solution.py:98
  20.1 1.6 %collective-permute-done.5 = bf16[1,64,384]{2,1,0:T(8,128)(2,1)S(1)} collective-permute-done((bf16[1,64,384]{2,1,0:T(8,128)(2,1)S(1)}, bf16[1,64,384]{2,1,0:T(8,128)(2,1)S(1)}, u32[]{:S(2)}, u32[]{:S(2)}) %collective-permute-start.5) | collective-permute-done | bytes 49184 | tf_op jit(solution)/shard_map/ppermute | solution.py:98
  21.7 2.6 %collective-permute-done.4 = bf16[1,64,384]{2,1,0:T(8,128)(2,1)S(1)} collective-permute-done((bf16[1,64,384]{2,1,0:T(8,128)(2,1)S(1)}, bf16[1,64,384]{2,1,0:T(8,128)(2,1)S(1)}, u32[]{:S(2)}, u32[]{:S(2)}) %collective-permute-start.4) | collective-permute-done | bytes 49184 | tf_op jit(solution)/shard_map/ppermute | solution.py:98
  24.3 0.6 %gather_fusion.1 = bf16[4,64,384]{2,1,0:T(8,128)(2,1)S(1)} fusion(bf16[4,64,384]{2,1,0:T(8,128)(2,1)S(1)} %maximum_bitcast_fusion.1, s32[1024]{0:T(1024)S(1)} %pad_clamp_fusion), kind=kCustom, calls=%fused_computation.1.clone | custom fusion | bytes 393232 | tf_op jit(solution)/shard_map/jit(_take)/gather | solution.py:99
  25.1 2.4 %collective-permute-start.6 = (bf16[1,136,384]{2,1,0:T(8,128)(2,1)S(1)}, bf16[1,136,384]{2,1,0:T(8,128)(2,1)S(1)}, u32[]{:S(2)}, u32[]{:S(2)}) collective-permute-start(bf16[1,136,384]{2,1,0:T(8,128)(2,1)S(1)} %pad_maximum_fusion), channel_id=1, source_target_pairs={{0,4},{4,0},{1,5},{5,1},{2,6},{6,2},{3,7},{7,3},{8,12},{12,8},{9,1... | collective-permute-start | bytes 313352 | tf_op jit(solution)/shard_map/ppermute | solution.py:119
  27.6 2.5 %collective-permute-done.6 = bf16[1,136,384]{2,1,0:T(8,128)(2,1)S(1)} collective-permute-done((bf16[1,136,384]{2,1,0:T(8,128)(2,1)S(1)}, bf16[1,136,384]{2,1,0:T(8,128)(2,1)S(1)}, u32[]{:S(2)}, u32[]{:S(2)}) %collective-permute-start.6) | collective-permute-done | bytes 104480 | tf_op jit(solution)/shard_map/ppermute | solution.py:119
  30.3 0.5 %fusion.5 = bf16[128,384]{1,0:T(8,128)(2,1)S(1)} fusion(bf16[256,384]{1,0:T(8,128)(2,1)S(1)} %get-tuple-element.37, bf16[1,128,256]{2,1,0:T(8,128)(2,1)S(1)} %copy-done.3, bf16[1,256,384]{2,1,0:T(8,128)(2,1)S(1)} %bitcast.162, s32[256]{0:T(256)S(1)} %bitcast.178, s32[128]{0:T(128)S(1)} %bitcast.173, pred[128]{0:T(512)(128)(4,1)S(1)} %broadcast_compare_fusion.1), kind=kOutput, calls=%fused_computation.13 | convolution fusion | flops 51052544 | bytes 657408 | tf_op jit(solution)/shard_map/bij,bjp->bip/dot_general | solution.py:177
  31.1 0.5 %fusion.6 = bf16[128,384]{1,0:T(8,128)(2,1)S(1)} fusion(bf16[256,384]{1,0:T(8,128)(2,1)S(1)} %get-tuple-element.36, bf16[1,256,128]{2,1,0:T(8,128)(2,1)S(1)} %select_dynamic-update-slice_fusion, bf16[1,256,384]{2,1,0:T(8,128)(2,1)S(1)} %bitcast.163, s32[128]{0:T(128)S(1)} %bitcast.175, s32[256]{0:T(256)S(1)} %bitcast.177, ...), kind=kOutput, calls=%fused_computation.14 | convolution fusion | flops 51052544 | bytes 657408 | tf_op jit(solution)/shard_map/bij,bip->bjp/dot_general | solution.py:188
  32.8 1.1 %collective-permute-done.8 = bf16[2,384,192]{2,1,0:T(8,128)(2,1)S(1)} collective-permute-done((bf16[2,384,192]{2,1,0:T(8,128)(2,1)S(1)}, bf16[2,384,192]{2,1,0:T(8,128)(2,1)S(1)}, u32[]{:S(2)}, u32[]{:S(2)}) %collective-permute-start.8) | collective-permute-done | bytes 294944 | tf_op jit(solution)/shard_map/ppermute | solution.py:212
  34.2 2.1 %collective-permute-start.9 = (bf16[2,192,192]{2,1,0:T(8,128)(2,1)S(1)}, bf16[2,192,192]{2,1,0:T(8,128)(2,1)S(1)}, u32[]{:S(2)}, u32[]{:S(2)}) collective-permute-start(bf16[2,192,192]{2,1,0:T(8,128)(2,1)S(1)} %constant_dynamic-slice_fusion.1), channel_id=1, source_target_pairs={{0,4},{4,0},{1,5},{5,1},{2,6},{6,2},{3,7},{7,3},{8,12},{12,8},{9,1... | collective-permute-start | bytes 442376 | tf_op jit(solution)/shard_map/ppermute | solution.py:218
  36.3 0.4 convolution_add_fusion.1
  36.7 4.8 %collective-permute-done.9 = bf16[2,192,192]{2,1,0:T(8,128)(2,1)S(1)} collective-permute-done((bf16[2,192,192]{2,1,0:T(8,128)(2,1)S(1)}, bf16[2,192,192]{2,1,0:T(8,128)(2,1)S(1)}, u32[]{:S(2)}, u32[]{:S(2)}) %collective-permute-start.9) | collective-permute-done | bytes 147488 | tf_op jit(solution)/shard_map/ppermute | solution.py:218
  41.5 1.6 %collective-permute-start.10 = (bf16[2,192,192]{2,1,0:T(8,128)(2,1)S(1)}, bf16[2,192,192]{2,1,0:T(8,128)(2,1)S(1)}, u32[]{:S(2)}, u32[]{:S(2)}) collective-permute-start(bf16[2,192,192]{2,1,0:T(8,128)(2,1)S(1)} %add_convert_fusion.1), channel_id=1, source_target_pairs={{0,16},{8,24},{16,0},{24,8},{1,17},{9,25},{17,1},{25,9},{2,18},{10... | collective-permute-start | bytes 442376 | tf_op jit(solution)/shard_map/ppermute | solution.py:223
  43.3 4.7 %collective-permute-done.10 = bf16[2,192,192]{2,1,0:T(8,128)(2,1)S(1)} collective-permute-done((bf16[2,192,192]{2,1,0:T(8,128)(2,1)S(1)}, bf16[2,192,192]{2,1,0:T(8,128)(2,1)S(1)}, u32[]{:S(2)}, u32[]{:S(2)}) %collective-permute-start.10) | collective-permute-done | bytes 147488 | tf_op jit(solution)/shard_map/ppermute | solution.py:223
  48.5 1.1 %fusion.2 = bf16[1,512,384]{2,1,0:T(8,128)(2,1)} fusion(f32[512,384]{1,0:T(8,128)S(1)} %convolution_add_fusion.1, f32[512,384]{1,0:T(8,128)S(1)} %fusion.14, s32[128]{0:T(128)S(1)} %get-tuple-element.40, f32[128,384]{1,0:T(8,128)S(1)} %fusion.91), kind=kOutput, calls=%fused_computation.8 | convolution fusion | flops 51183616 | bytes 2163200 | tf_op jit(solution)/shard_map/bnr,bnc->brc/dot_general | solution.py:26
  50.1 0.9 %slice_bitcast_fusion = (f32[384,192]{0,1:T(8,128)}, f32[384,192]{0,1:T(8,128)}) fusion(f32[2,384,192]{1,2,0:T(8,128)S(1)} %fusion.9), kind=kLoop, calls=%fused_computation.38 | loop fusion | bytes 1179648 | tf_op jit(solution)/shard_map/squeeze | solution.py:230
  (70 shorter events, 5.5 us)
Async XLA Ops:
  0.6 1.0 %copy-start = (bf16[1,512,384]{2,1,0:T(8,128)(2,1)S(1)}, bf16[1,512,384]{2,1,0:T(8,128)(2,1)}, u32[]{:S(2)}) copy-start(bf16[1,512,384]{2,1,0:T(8,128)(2,1)} %param.12) | copy-start | bytes 1179652
  0.7 0.7 %copy-start.4 = (s32[1,128]{1,0:T(1,128)S(1)}, s32[1,128]{1,0:T(1,128)}, u32[]{:S(2)}) copy-start(s32[1,128]{1,0:T(1,128)} %param.13) | copy-start | bytes 1540
  0.7 0.7 %copy-start.5 = (s32[1,128]{1,0:T(1,128)S(1)}, s32[1,128]{1,0:T(1,128)}, u32[]{:S(2)}) copy-start(s32[1,128]{1,0:T(1,128)} %param.14) | copy-start | bytes 1540
  1.9 1.0 %copy-start.1 = (bf16[384,384]{1,0:T(8,128)(2,1)S(1)}, bf16[384,384]{1,0:T(8,128)(2,1)}, u32[]{:S(2)}) copy-start(bf16[384,384]{1,0:T(8,128)(2,1)} %param.16) | copy-start | bytes 884740
  2.2 1.0 %copy-start.2 = (bf16[384,384]{1,0:T(8,128)(2,1)S(1)}, bf16[384,384]{1,0:T(8,128)(2,1)}, u32[]{:S(2)}) copy-start(bf16[384,384]{1,0:T(8,128)(2,1)} %param.17) | copy-start | bytes 884740
  3.8 5.8 %copy-start.3 = (bf16[1,128,256]{2,1,0:T(8,128)(2,1)S(1)}, bf16[1,128,256]{2,1,0:T(8,128)(2,1)}, u32[]{:S(2)}) copy-start(bf16[1,128,256]{2,1,0:T(8,128)(2,1)} %param.15) | copy-start | bytes 196612
  3.8 11.0 %collective-permute-start.2 = (bf16[1,64,384]{2,1,0:T(8,128)(2,1)S(1)}, bf16[1,64,384]{2,1,0:T(8,128)(2,1)S(1)}, u32[]{:S(2)}, u32[]{:S(2)}) collective-permute-start(bf16[1,64,384]{2,1,0:T(8,128)(2,1)S(1)} %get-tuple-element.35), channel_id=1, source_target_pairs={{0,3},{1,2},{2,1},{3,0},{4,7},{5,6},{6,5},{7,4},{8,11},{9,10},{10,... | collective-permute-start | bytes 147464 | tf_op jit(solution)/shard_map/ppermute | solution.py:88
  8.9 5.9 %collective-permute-start.1 = (bf16[1,64,384]{2,1,0:T(8,128)(2,1)S(1)}, bf16[1,64,384]{2,1,0:T(8,128)(2,1)S(1)}, u32[]{:S(2)}, u32[]{:S(2)}) collective-permute-start(bf16[1,64,384]{2,1,0:T(8,128)(2,1)S(1)} %get-tuple-element.34), channel_id=1, source_target_pairs={{0,2},{1,3},{2,0},{3,1},{4,6},{5,7},{6,4},{7,5},{8,10},{9,11},{10,... | collective-permute-start | bytes 147464 | tf_op jit(solution)/shard_map/ppermute | solution.py:88
  8.9 5.9 %collective-permute-start = (bf16[1,64,384]{2,1,0:T(8,128)(2,1)S(1)}, bf16[1,64,384]{2,1,0:T(8,128)(2,1)S(1)}, u32[]{:S(2)}, u32[]{:S(2)}) collective-permute-start(bf16[1,64,384]{2,1,0:T(8,128)(2,1)S(1)} %get-tuple-element.33), channel_id=1, source_target_pairs={{0,1},{1,0},{2,3},{3,2},{4,5},{5,4},{6,7},{7,6},{8,9},{9,8},{10,11... | collective-permute-start | bytes 147464 | tf_op jit(solution)/shard_map/ppermute | solution.py:88
  9.6 5.2 %collective-permute-start.7 = (bf16[1,128,128]{2,1,0:T(8,128)(2,1)S(1)}, bf16[1,128,128]{2,1,0:T(8,128)(2,1)S(1)}, u32[]{:S(2)}, u32[]{:S(2)}) collective-permute-start(bf16[1,128,128]{2,1,0:T(8,128)(2,1)S(1)} %get-tuple-element.38), channel_id=1, source_target_pairs={{0,4},{1,5},{2,6},{3,7},{8,12},{9,13},{10,14},{11,15},{16,20},{17,... | collective-permute-start | bytes 98312 | tf_op jit(solution)/shard_map/ppermute | solution.py:60
  15.6 6.1 %collective-permute-start.5 = (bf16[1,64,384]{2,1,0:T(8,128)(2,1)S(1)}, bf16[1,64,384]{2,1,0:T(8,128)(2,1)S(1)}, u32[]{:S(2)}, u32[]{:S(2)}) collective-permute-start(bf16[1,64,384]{2,1,0:T(8,128)(2,1)S(1)} %fusion.108), channel_id=1, source_target_pairs={{0,3},{1,2},{2,1},{3,0},{4,7},{5,6},{6,5},{7,4},{8,11},{9,10},{10,... | collective-permute-start | bytes 147464 | tf_op jit(solution)/shard_map/ppermute | solution.py:98
  19.3 5.0 %collective-permute-start.4 = (bf16[1,64,384]{2,1,0:T(8,128)(2,1)S(1)}, bf16[1,64,384]{2,1,0:T(8,128)(2,1)S(1)}, u32[]{:S(2)}, u32[]{:S(2)}) collective-permute-start(bf16[1,64,384]{2,1,0:T(8,128)(2,1)S(1)} %fusion.108), channel_id=1, source_target_pairs={{0,2},{1,3},{2,0},{3,1},{4,6},{5,7},{6,4},{7,5},{8,10},{9,11},{10,... | collective-permute-start | bytes 147464 | tf_op jit(solution)/shard_map/ppermute | solution.py:98
  19.3 5.0 %collective-permute-start.3 = (bf16[1,64,384]{2,1,0:T(8,128)(2,1)S(1)}, bf16[1,64,384]{2,1,0:T(8,128)(2,1)S(1)}, u32[]{:S(2)}, u32[]{:S(2)}) collective-permute-start(bf16[1,64,384]{2,1,0:T(8,128)(2,1)S(1)} %fusion.108), channel_id=1, source_target_pairs={{0,1},{1,0},{2,3},{3,2},{4,5},{5,4},{6,7},{7,6},{8,9},{9,8},{10,11... | collective-permute-start | bytes 147464 | tf_op jit(solution)/shard_map/ppermute | solution.py:98
  25.1 5.0 %collective-permute-start.6 = (bf16[1,136,384]{2,1,0:T(8,128)(2,1)S(1)}, bf16[1,136,384]{2,1,0:T(8,128)(2,1)S(1)}, u32[]{:S(2)}, u32[]{:S(2)}) collective-permute-start(bf16[1,136,384]{2,1,0:T(8,128)(2,1)S(1)} %pad_maximum_fusion), channel_id=1, source_target_pairs={{0,4},{4,0},{1,5},{5,1},{2,6},{6,2},{3,7},{7,3},{8,12},{12,8},{9,1... | collective-permute-start | bytes 313352 | tf_op jit(solution)/shard_map/ppermute | solution.py:119
  32.1 1.8 %collective-permute-start.8 = (bf16[2,384,192]{2,1,0:T(8,128)(2,1)S(1)}, bf16[2,384,192]{2,1,0:T(8,128)(2,1)S(1)}, u32[]{:S(2)}, u32[]{:S(2)}) collective-permute-start(bf16[2,384,192]{2,1,0:T(8,128)(2,1)S(1)} %fusion.10), channel_id=1, source_target_pairs={{0,8},{8,0},{16,24},{24,16},{1,9},{9,1},{17,25},{25,17},{2,10},{10... | collective-permute-start | bytes 884744 | tf_op jit(solution)/shard_map/ppermute | solution.py:212
  34.2 7.3 %collective-permute-start.9 = (bf16[2,192,192]{2,1,0:T(8,128)(2,1)S(1)}, bf16[2,192,192]{2,1,0:T(8,128)(2,1)S(1)}, u32[]{:S(2)}, u32[]{:S(2)}) collective-permute-start(bf16[2,192,192]{2,1,0:T(8,128)(2,1)S(1)} %constant_dynamic-slice_fusion.1), channel_id=1, source_target_pairs={{0,4},{4,0},{1,5},{5,1},{2,6},{6,2},{3,7},{7,3},{8,12},{12,8},{9,1... | collective-permute-start | bytes 442376 | tf_op jit(solution)/shard_map/ppermute | solution.py:218
  41.5 6.5 %collective-permute-start.10 = (bf16[2,192,192]{2,1,0:T(8,128)(2,1)S(1)}, bf16[2,192,192]{2,1,0:T(8,128)(2,1)S(1)}, u32[]{:S(2)}, u32[]{:S(2)}) collective-permute-start(bf16[2,192,192]{2,1,0:T(8,128)(2,1)S(1)} %add_convert_fusion.1), channel_id=1, source_target_pairs={{0,16},{8,24},{16,0},{24,8},{1,17},{9,25},{17,1},{25,9},{2,18},{10... | collective-permute-start | bytes 442376 | tf_op jit(solution)/shard_map/ppermute | solution.py:223
  48.1 1.8 %collective-permute-start.11 = (f32[2,192,192]{2,1,0:T(8,128)S(1)}, f32[2,192,192]{2,1,0:T(8,128)S(1)}, u32[]{:S(2)}, u32[]{:S(2)}) collective-permute-start(f32[2,192,192]{2,1,0:T(8,128)S(1)} %convert_add_fusion), channel_id=1, source_target_pairs={{0,8},{8,0},{16,24},{24,16},{1,9},{9,1},{17,25},{25,17},{2,10},{10... | collective-permute-start | bytes 884744 | tf_op jit(solution)/shard_map/ppermute | solution.py:225

commit v8 on v7

--- a/solution.py
+++ b/solution.py
@@ -101,6 +101,47 @@
     own_donor = slab_feats[:, :slab_sites]
     own_acceptor = slab_feats[:, slab_sites:]
 
+    n_dp = lax.axis_size("dp")
+    assert n_dp & (n_dp - 1) == 0 and n_dp >= 2
+    dp = lax.axis_index("dp")
+    pair = dp % 2
+    channels = embed.shape[2]
+    half = channels // 2
+    part = width // n_seq
+    if n_seq == 2:
+        target_own = lax.dynamic_slice_in_dim(target, slab * slab_sites, slab_sites, 2)
+        scores_own = (
+            jnp.einsum("bip,bjp->bij", own_donor, own_acceptor, preferred_element_type=jnp.float32)
+            * scale
+        )
+        allowed_own = (donor_pos[:, :, None] >= 0) & (acceptor_pos[:, None, :] > donor_pos[:, :, None])
+        slope_own = pair_slope(scores_own, target_own, allowed_own)
+        early_acceptor = (
+            jnp.einsum("bij,bip->bjp", slope_own, own_donor, preferred_element_type=jnp.float32) * scale
+        ).astype(jnp.bfloat16)
+        early_donor = (
+            jnp.einsum("bij,bjp->bip", slope_own, own_acceptor, preferred_element_type=jnp.float32)
+            * scale
+        ).astype(jnp.bfloat16)
+        first = slab == 0
+        grad_early = jnp.where(first, early_acceptor, early_donor)
+        rows_early = jnp.where(first, acceptor_rows, donor_rows)
+
+        def to_seq_partner(rows, grad):
+            local = jnp.einsum("bnc,bnp->pc", rows, grad, preferred_element_type=jnp.float32)
+            local = local.astype(jnp.bfloat16)
+            kept = lax.dynamic_slice_in_dim(local, pair * half, half, 1).astype(jnp.float32)
+            outgoing = lax.dynamic_slice_in_dim(local, (1 - pair) * half, half, 1)
+            kept = kept + lax.ppermute(outgoing, "dp", [(i, i ^ 1) for i in range(n_dp)]).astype(
+                jnp.float32
+            )
+            held = kept.astype(jnp.bfloat16)
+            own = lax.dynamic_slice_in_dim(held, slab * part, part, 0).astype(jnp.float32)
+            outgoing = lax.dynamic_slice_in_dim(held, (1 - slab) * part, part, 0)
+            return own, lax.ppermute(outgoing, "seq", [(0, 1), (1, 0)]).astype(jnp.float32)
+
+        own_early, from_early = to_seq_partner(rows_early, grad_early)
+
     assert slab_sites <= width
     flags = jnp.zeros((batch, 8, width), jnp.bfloat16)
     flags = flags.at[:, 0, :slab_sites].set((donor_pos >= 0).astype(jnp.bfloat16))
@@ -117,6 +158,8 @@
         sent = jnp.where(slab + k < n_seq, own_donor, own_acceptor)
         perm = [(i, (i + k) % n_seq) for i in range(n_seq)]
         arrived = lax.ppermute(jnp.concatenate([sent, flags], axis=1), "seq", perm)
+        if n_seq == 2:
+            arrived, from_early = lax.optimization_barrier((arrived, from_early))
         source = (slab - k) % n_seq
         earlier = slab >= k
         feat_in = arrived[:, :slab_sites]
@@ -189,33 +232,46 @@
         * scale
     ).astype(jnp.bfloat16)
 
+
+    if n_seq == 2:
+        first = slab == 0
+        grad_early = jnp.where(first, early_acceptor, early_donor)
+        rows_early = jnp.where(first, acceptor_rows, donor_rows)
+        grad_late = jnp.where(first, donor_grad, acceptor_grad)
+        rows_late = jnp.where(first, donor_rows, acceptor_rows)
+        donor_grad = jnp.where(first, grad_late, grad_early)
+        acceptor_grad = jnp.where(first, grad_early, grad_late)
+
+        own_late, from_late = to_seq_partner(rows_late, grad_late)
+        sum_early = own_early + from_late
+        sum_late = own_late + from_early
+        mine = jnp.stack(
+            [jnp.where(first, sum_late, sum_early), jnp.where(first, sum_early, sum_late)]
+        )
+    else:
+        local_dw = jnp.einsum(
+            "bnc,bnp->pc", donor_rows, donor_grad, preferred_element_type=jnp.float32
+        )
+        local_aw = jnp.einsum(
+            "bnc,bnp->pc", acceptor_rows, acceptor_grad, preferred_element_type=jnp.float32
+        )
+        blocks = jnp.stack([local_dw, local_aw]).astype(jnp.bfloat16)
+        mine = lax.dynamic_slice_in_dim(blocks, pair * half, half, 2).astype(jnp.float32)
+        outgoing = lax.dynamic_slice_in_dim(blocks, (1 - pair) * half, half, 2)
+        mine = mine + lax.ppermute(outgoing, "dp", [(i, i ^ 1) for i in range(n_dp)]).astype(
+            jnp.float32
+        )
+        held = mine.astype(jnp.bfloat16)
+        mine = lax.dynamic_slice_in_dim(held, slab * part, part, 1).astype(jnp.float32)
+        for k in range(1, n_seq):
+            outgoing = lax.dynamic_slice_in_dim(held, ((slab + k) % n_seq) * part, part, 1)
+            perm = [(i, (i + k) % n_seq) for i in range(n_seq)]
+            mine = mine + lax.ppermute(outgoing, "seq", perm).astype(jnp.float32)
     donor_site = jnp.einsum("bnp,cp->bnc", donor_grad, donor_w, preferred_element_type=jnp.float32)
     acceptor_site = jnp.einsum(
         "bnp,cp->bnc", acceptor_grad, acceptor_w, preferred_element_type=jnp.float32
     )
     row_grad = place_rows(donor_match, donor_site) + place_rows(acceptor_match, acceptor_site)
-
-    local_dw = jnp.einsum("bnc,bnp->pc", donor_rows, donor_grad, preferred_element_type=jnp.float32)
-    local_aw = jnp.einsum(
-        "bnc,bnp->pc", acceptor_rows, acceptor_grad, preferred_element_type=jnp.float32
-    )
-    n_dp = lax.axis_size("dp")
-    assert n_dp & (n_dp - 1) == 0 and n_dp >= 2
-    dp = lax.axis_index("dp")
-    pair = dp % 2
-    channels = local_dw.shape[1]
-    half = channels // 2
-    part = width // n_seq
-    blocks = jnp.stack([local_dw, local_aw]).astype(jnp.bfloat16)
-    mine = lax.dynamic_slice_in_dim(blocks, pair * half, half, 2).astype(jnp.float32)
-    outgoing = lax.dynamic_slice_in_dim(blocks, (1 - pair) * half, half, 2)
-    mine = mine + lax.ppermute(outgoing, "dp", [(i, i ^ 1) for i in range(n_dp)]).astype(jnp.float32)
-    held = mine.astype(jnp.bfloat16)
-    mine = lax.dynamic_slice_in_dim(held, slab * part, part, 1).astype(jnp.float32)
-    for k in range(1, n_seq):
-        outgoing = lax.dynamic_slice_in_dim(held, ((slab + k) % n_seq) * part, part, 1)
-        perm = [(i, (i + k) % n_seq) for i in range(n_seq)]
-        mine = mine + lax.ppermute(outgoing, "seq", perm).astype(jnp.float32)
     bit = 2
     while bit < n_dp:
         held = mine.astype(jnp.bfloat16)

time: 51.2 us -> 54.3 us (1.061)
  waiting for transfers between devices: 18.8 us -> 23.7 us
  starting transfers between devices: 19.9 us -> 16.8 us
  local copies, waits for them, and re-layouts: 4.14 us -> 4.91 us
  matrix products: 5.26 us -> 5.9 us
    ppermute x2 -> x4, waiting for transfers between devices: 5.9 us -> 11.5 us  [the longest x2 9.23 us: to_seq_partner(): lax.ppermute(outgoing, 'seq', [(0, 1), (1, 0)]).astype(jnp.float32)]
    ppermute x3, waiting for transfers between devices: 0.01 us -> 5.31 us  [shards(): lax.ppermute(outgoing, 'head', [(i, i ^ k) for i in range(n_head)])]
    ppermute x1, waiting for transfers between devices: 2.55 us -> 0.01 us  [shards(): arrived = lax.ppermute(jnp.concatenate([sent, flags], axis=1), 'seq', perm)]
    ppermute x1, starting transfers between devices: 2.38 us -> 0.07 us  [shards(): arrived = lax.ppermute(jnp.concatenate([sent, flags], axis=1), 'seq', perm)]
    ppermute x3, waiting for transfers between devices: 4.17 us -> 2.26 us  [shards(): lax.ppermute(feat_quarter, 'head', [(i, i ^ k) for i in range(n_head)])]
    ppermute x3, starting transfers between devices: 5.76 us -> 4.45 us  [shards(): lax.ppermute(outgoing, 'head', [(i, i ^ k) for i in range(n_head)])]
    ppermute x1, starting transfers between devices: 3.57 us -> 4.87 us  [shards(): arrived = lax.ppermute(outgoing, 'seq', perm)]
    ppermute x1, waiting for transfers between devices: 1.23 us -> 0.01 us  [shards(): arrived = lax.ppermute(outgoing, 'seq', perm)]
  transfers between devices with their start and end apart: 12 -> 14, of which waited for: 8 -> 10; matrix products, arithmetic and copies ran while one was open for 6% -> 8% of each run, Pallas kernels for 0% -> 0%
where the time goes in v8:
time: 54.3 us; the launch traced here: 54.1 us
  waiting for transfers between devices  23.7 us (44%)
  starting transfers between devices  16.8 us (31%)
  matrix products  5.9 us (11%)
  local copies, waits for them, and re-layouts  4.91 us (9%)
  other arithmetic  1.6 us (3%)
  between operations  1.23 us (2%)
    ppermute x2, waiting for transfers between devices, to_seq_partner(): lax.ppermute(outgoing, 'seq', [(0, 1), (1, 0)]).astype(jnp.float32)  9.23 us
    ppermute x3, waiting for transfers between devices, shards(): lax.ppermute(outgoing, 'head', [(i, i ^ k) for i in range(n_head)])  5.31 us
    ppermute x1, starting transfers between devices, shards(): arrived = lax.ppermute(outgoing, 'seq', perm)  4.87 us
    ppermute x3, starting transfers between devices, shards(): lax.ppermute(feat_quarter, 'head', [(i, i ^ k) for i in range(n_head)])  4.45 us
    ppermute x3, starting transfers between devices, shards(): lax.ppermute(outgoing, 'head', [(i, i ^ k) for i in range(n_head)])  4.45 us
    ppermute x1, waiting for transfers between devices, shards(): lax.ppermute(held, 'dp', perm).astype(jnp.float32)  4.38 us
    unnamed x14, local copies, waits for them, and re-layouts  2.31 us
    ppermute x2, waiting for transfers between devices, to_seq_partner(): lax.ppermute(outgoing, 'dp', [(i, i ^ 1) for i in range(n_dp)])  2.3 us
  transfers between devices with their start and end apart: 14, of which 10 were waited for; matrix products, arithmetic and copies ran while one was open for 8% of the time, Pallas kernels for 0%

profile of v8, /device:TPU:0, one launch (start us, length us, event | category | flops | bytes accessed | tf_op | source)
XLA Modules:
  0.0 54.1 jit_solution(3151923885612085034)
XLA Ops:
  0.7 0.9 %copy-done.3 = bf16[1,128,256]{2,1,0:T(8,128)(2,1)S(1)} copy-done((bf16[1,128,256]{2,1,0:T(8,128)(2,1)S(1)}, bf16[1,128,256]{2,1,0:T(8,128)(2,1)}, u32[]{:S(2)}) %copy-start.3) | copy-done | bytes 65560
  1.5 4.9 %collective-permute-start.9 = (bf16[1,128,128]{2,1,0:T(8,128)(2,1)S(1)}, bf16[1,128,128]{2,1,0:T(8,128)(2,1)S(1)}, u32[]{:S(2)}, u32[]{:S(2)}) collective-permute-start(bf16[1,128,128]{2,1,0:T(8,128)(2,1)S(1)} %get-tuple-element.44), channel_id=1, source_target_pairs={{0,4},{1,5},{2,6},{3,7},{8,12},{9,13},{10,14},{11,15},{16,20},{17,... | collective-permute-start | bytes 98312 | tf_op jit(solution)/shard_map/ppermute | solution.py:60
  6.5 0.6 %copy-done.4 = s32[1,128]{1,0:T(1,128)S(1)} copy-done((s32[1,128]{1,0:T(1,128)S(1)}, s32[1,128]{1,0:T(1,128)}, u32[]{:S(2)}) %copy-start.4) | copy-done | bytes 536
  7.7 0.6 %copy-done.1 = bf16[384,384]{1,0:T(8,128)(2,1)S(1)} copy-done((bf16[384,384]{1,0:T(8,128)(2,1)S(1)}, bf16[384,384]{1,0:T(8,128)(2,1)}, u32[]{:S(2)}) %copy-start.1) | copy-done | bytes 294936
  9.2 1.6 %collective-permute-start = (bf16[1,64,384]{2,1,0:T(8,128)(2,1)S(1)}, bf16[1,64,384]{2,1,0:T(8,128)(2,1)S(1)}, u32[]{:S(2)}, u32[]{:S(2)}) collective-permute-start(bf16[1,64,384]{2,1,0:T(8,128)(2,1)S(1)} %get-tuple-element.39), channel_id=1, source_target_pairs={{0,1},{1,0},{2,3},{3,2},{4,5},{5,4},{6,7},{7,6},{8,9},{9,8},{10,11... | collective-permute-start | bytes 147464 | tf_op jit(solution)/shard_map/ppermute | solution.py:88
  10.9 2.6 %collective-permute-start.1 = (bf16[1,64,384]{2,1,0:T(8,128)(2,1)S(1)}, bf16[1,64,384]{2,1,0:T(8,128)(2,1)S(1)}, u32[]{:S(2)}, u32[]{:S(2)}) collective-permute-start(bf16[1,64,384]{2,1,0:T(8,128)(2,1)S(1)} %get-tuple-element.40), channel_id=1, source_target_pairs={{0,2},{1,3},{2,0},{3,1},{4,6},{5,7},{6,4},{7,5},{8,10},{9,11},{10,... | collective-permute-start | bytes 147464 | tf_op jit(solution)/shard_map/ppermute | solution.py:88
  14.1 2.5 %collective-permute-done.1 = bf16[1,64,384]{2,1,0:T(8,128)(2,1)S(1)} collective-permute-done((bf16[1,64,384]{2,1,0:T(8,128)(2,1)S(1)}, bf16[1,64,384]{2,1,0:T(8,128)(2,1)S(1)}, u32[]{:S(2)}, u32[]{:S(2)}) %collective-permute-start.1) | collective-permute-done | bytes 49184 | tf_op jit(solution)/shard_map/ppermute | solution.py:88
  16.5 2.8 %collective-permute-done.2 = bf16[1,64,384]{2,1,0:T(8,128)(2,1)S(1)} collective-permute-done((bf16[1,64,384]{2,1,0:T(8,128)(2,1)S(1)}, bf16[1,64,384]{2,1,0:T(8,128)(2,1)S(1)}, u32[]{:S(2)}, u32[]{:S(2)}) %collective-permute-start.2) | collective-permute-done | bytes 49184 | tf_op jit(solution)/shard_map/ppermute | solution.py:88
  19.4 0.6 %gather_fusion = bf16[4,64,384]{2,1,0:T(8,128)(2,1)S(1)} fusion(bf16[4,64,384]{2,1,0:T(8,128)(2,1)S(1)} %maximum_bitcast_fusion, s32[1024]{0:T(1024)S(1)} %pad_clamp_fusion), kind=kCustom, calls=%fused_computation.clone | custom fusion | bytes 393232 | tf_op jit(solution)/shard_map/jit(_take)/gather | solution.py:90
  20.1 0.7 %collective-permute-start.5 = (bf16[1,64,384]{2,1,0:T(8,128)(2,1)S(1)}, bf16[1,64,384]{2,1,0:T(8,128)(2,1)S(1)}, u32[]{:S(2)}, u32[]{:S(2)}) collective-permute-start(bf16[1,64,384]{2,1,0:T(8,128)(2,1)S(1)} %fusion.144), channel_id=1, source_target_pairs={{0,3},{1,2},{2,1},{3,0},{4,7},{5,6},{6,5},{7,4},{8,11},{9,10},{10,... | collective-permute-start | bytes 147464 | tf_op jit(solution)/shard_map/ppermute | solution.py:98
  20.8 3.8 %collective-permute-start.3 = (bf16[1,64,384]{2,1,0:T(8,128)(2,1)S(1)}, bf16[1,64,384]{2,1,0:T(8,128)(2,1)S(1)}, u32[]{:S(2)}, u32[]{:S(2)}) collective-permute-start(bf16[1,64,384]{2,1,0:T(8,128)(2,1)S(1)} %fusion.144), channel_id=1, source_target_pairs={{0,1},{1,0},{2,3},{3,2},{4,5},{5,4},{6,7},{7,6},{8,9},{9,8},{10,11... | collective-permute-start | bytes 147464 | tf_op jit(solution)/shard_map/ppermute | solution.py:98
  24.6 1.6 %collective-permute-done.5 = bf16[1,64,384]{2,1,0:T(8,128)(2,1)S(1)} collective-permute-done((bf16[1,64,384]{2,1,0:T(8,128)(2,1)S(1)}, bf16[1,64,384]{2,1,0:T(8,128)(2,1)S(1)}, u32[]{:S(2)}, u32[]{:S(2)}) %collective-permute-start.5) | collective-permute-done | bytes 49184 | tf_op jit(solution)/shard_map/ppermute | solution.py:98
  26.2 0.7 %collective-permute-done.4 = bf16[1,64,384]{2,1,0:T(8,128)(2,1)S(1)} collective-permute-done((bf16[1,64,384]{2,1,0:T(8,128)(2,1)S(1)}, bf16[1,64,384]{2,1,0:T(8,128)(2,1)S(1)}, u32[]{:S(2)}, u32[]{:S(2)}) %collective-permute-start.4) | collective-permute-done | bytes 49184 | tf_op jit(solution)/shard_map/ppermute | solution.py:98
  26.9 0.6 %gather_fusion.1 = bf16[4,64,384]{2,1,0:T(8,128)(2,1)S(1)} fusion(bf16[4,64,384]{2,1,0:T(8,128)(2,1)S(1)} %maximum_bitcast_fusion.1, s32[1024]{0:T(1024)S(1)} %pad_clamp_fusion), kind=kCustom, calls=%fused_computation.1.clone | custom fusion | bytes 393232 | tf_op jit(solution)/shard_map/jit(_take)/gather | solution.py:99
  28.9 1.3 %collective-permute-done.7 = bf16[384,192]{1,0:T(8,128)(2,1)S(1)} collective-permute-done((bf16[384,192]{1,0:T(8,128)(2,1)S(1)}, bf16[384,192]{1,0:T(8,128)(2,1)S(1)}, u32[]{:S(2)}, u32[]{:S(2)}) %collective-permute-start.7) | collective-permute-done | bytes 147488 | tf_op jit(solution)/shard_map/ppermute | solution.py:135
  30.3 0.8 %collective-permute-start.8 = (bf16[192,192]{1,0:T(8,128)(2,1)S(1)}, bf16[192,192]{1,0:T(8,128)(2,1)S(1)}, u32[]{:S(2)}, u32[]{:S(2)}) collective-permute-start(bf16[192,192]{1,0:T(8,128)(2,1)S(1)} %constant_dynamic-slice_fusion.2), channel_id=1, source_target_pairs={{0,4},{4,0},{1,5},{5,1},{2,6},{6,2},{3,7},{7,3},{8,12},{12,8},{9,1... | collective-permute-start | bytes 221192 | tf_op jit(solution)/shard_map/ppermute | solution.py:141
  31.3 5.1 %collective-permute-done.8 = bf16[192,192]{1,0:T(8,128)(2,1)S(1)} collective-permute-done((bf16[192,192]{1,0:T(8,128)(2,1)S(1)}, bf16[192,192]{1,0:T(8,128)(2,1)S(1)}, u32[]{:S(2)}, u32[]{:S(2)}) %collective-permute-start.8) | collective-permute-done | bytes 73760 | tf_op jit(solution)/shard_map/ppermute | solution.py:141
  37.1 0.5 %fusion.10 = bf16[128,384]{1,0:T(8,128)(2,1)S(1)} fusion(bf16[128,384]{1,0:T(8,128)(2,1)S(1)} %fusion.3, bf16[256,384]{1,0:T(8,128)(2,1)S(1)} %get-tuple-element.42, bf16[1,256,128]{2,1,0:T(8,128)(2,1)S(1)} %select_dynamic-update-slice_fusion, pred[]{:T(512)S(6)} %eq.114, s32[128]{0:T(128)S(1)} %bitcast.220, s32[256]{0:T(256)S(1)} %bitcast.222, ...), kind=kOutput, calls=%fused_computation.26 | convolution fusion | flops 51101696 | bytes 755713 | tf_op jit(solution)/shard_map/bij,bip->bjp/dot_general | solution.py:231
  38.8 1.0 %collective-permute-done.10 = bf16[384,192]{1,0:T(8,128)(2,1)S(1)} collective-permute-done((bf16[384,192]{1,0:T(8,128)(2,1)S(1)}, bf16[384,192]{1,0:T(8,128)(2,1)S(1)}, u32[]{:S(2)}, u32[]{:S(2)}) %collective-permute-start.10) | collective-permute-done | bytes 147488 | tf_op jit(solution)/shard_map/ppermute | solution.py:135
  40.7 4.2 %collective-permute-done.11 = bf16[192,192]{1,0:T(8,128)(2,1)S(1)} collective-permute-done((bf16[192,192]{1,0:T(8,128)(2,1)S(1)}, bf16[192,192]{1,0:T(8,128)(2,1)S(1)}, u32[]{:S(2)}, u32[]{:S(2)}) %collective-permute-start.11) | collective-permute-done | bytes 73760 | tf_op jit(solution)/shard_map/ppermute | solution.py:141
  45.0 1.6 %collective-permute-start.12 = (bf16[2,192,192]{2,1,0:T(8,128)(2,1)S(1)}, bf16[2,192,192]{2,1,0:T(8,128)(2,1)S(1)}, u32[]{:S(2)}, u32[]{:S(2)}) collective-permute-start(bf16[2,192,192]{2,1,0:T(8,128)(2,1)S(1)} %pad_maximum_fusion), channel_id=1, source_target_pairs={{0,16},{8,24},{16,0},{24,8},{1,17},{9,25},{17,1},{25,9},{2,18},{10... | collective-permute-start | bytes 442376 | tf_op jit(solution)/shard_map/ppermute | solution.py:279
  46.8 4.4 %collective-permute-done.12 = bf16[2,192,192]{2,1,0:T(8,128)(2,1)S(1)} collective-permute-done((bf16[2,192,192]{2,1,0:T(8,128)(2,1)S(1)}, bf16[2,192,192]{2,1,0:T(8,128)(2,1)S(1)}, u32[]{:S(2)}, u32[]{:S(2)}) %collective-permute-start.12) | collective-permute-done | bytes 147488 | tf_op jit(solution)/shard_map/ppermute | solution.py:279
  51.7 1.1 %fusion.2 = bf16[1,512,384]{2,1,0:T(8,128)(2,1)} fusion(f32[512,384]{1,0:T(8,128)S(1)} %convolution_add_fusion.1, f32[512,384]{1,0:T(8,128)S(1)} %fusion.14, s32[128]{0:T(128)S(1)} %get-tuple-element.46, f32[128,384]{1,0:T(8,128)S(1)} %fusion.61), kind=kOutput, calls=%fused_computation.8 | convolution fusion | flops 51183616 | bytes 2163200 | tf_op jit(solution)/shard_map/bnr,bnc->brc/dot_general | solution.py:26
  53.3 0.9 %slice_bitcast_fusion = (f32[384,192]{0,1:T(8,128)}, f32[384,192]{0,1:T(8,128)}) fusion(f32[2,384,192]{1,2,0:T(8,128)S(1)} %fusion.11), kind=kLoop, calls=%fused_computation.37 | loop fusion | bytes 1179648 | tf_op jit(solution)/shard_map/squeeze | solution.py:286
  (82 shorter events, 7.6 us)
Async XLA Ops:
  0.6 6.5 %copy-start = (bf16[1,512,384]{2,1,0:T(8,128)(2,1)S(1)}, bf16[1,512,384]{2,1,0:T(8,128)(2,1)}, u32[]{:S(2)}) copy-start(bf16[1,512,384]{2,1,0:T(8,128)(2,1)} %param.12) | copy-start | bytes 1179652
  0.6 0.9 %copy-start.3 = (bf16[1,128,256]{2,1,0:T(8,128)(2,1)S(1)}, bf16[1,128,256]{2,1,0:T(8,128)(2,1)}, u32[]{:S(2)}) copy-start(bf16[1,128,256]{2,1,0:T(8,128)(2,1)} %param.15) | copy-start | bytes 196612
  1.5 12.5 %collective-permute-start.9 = (bf16[1,128,128]{2,1,0:T(8,128)(2,1)S(1)}, bf16[1,128,128]{2,1,0:T(8,128)(2,1)S(1)}, u32[]{:S(2)}, u32[]{:S(2)}) collective-permute-start(bf16[1,128,128]{2,1,0:T(8,128)(2,1)S(1)} %get-tuple-element.44), channel_id=1, source_target_pairs={{0,4},{1,5},{2,6},{3,7},{8,12},{9,13},{10,14},{11,15},{16,20},{17,... | collective-permute-start | bytes 98312 | tf_op jit(solution)/shard_map/ppermute | solution.py:60
  6.4 0.7 %copy-start.4 = (s32[1,128]{1,0:T(1,128)S(1)}, s32[1,128]{1,0:T(1,128)}, u32[]{:S(2)}) copy-start(s32[1,128]{1,0:T(1,128)} %param.13) | copy-start | bytes 1540
  6.5 0.7 %copy-start.5 = (s32[1,128]{1,0:T(1,128)S(1)}, s32[1,128]{1,0:T(1,128)}, u32[]{:S(2)}) copy-start(s32[1,128]{1,0:T(1,128)} %param.14) | copy-start | bytes 1540
  7.4 1.0 %copy-start.1 = (bf16[384,384]{1,0:T(8,128)(2,1)S(1)}, bf16[384,384]{1,0:T(8,128)(2,1)}, u32[]{:S(2)}) copy-start(bf16[384,384]{1,0:T(8,128)(2,1)} %param.16) | copy-start | bytes 884740
  7.7 1.0 %copy-start.2 = (bf16[384,384]{1,0:T(8,128)(2,1)S(1)}, bf16[384,384]{1,0:T(8,128)(2,1)}, u32[]{:S(2)}) copy-start(bf16[384,384]{1,0:T(8,128)(2,1)} %param.17) | copy-start | bytes 884740
  9.2 4.8 %collective-permute-start = (bf16[1,64,384]{2,1,0:T(8,128)(2,1)S(1)}, bf16[1,64,384]{2,1,0:T(8,128)(2,1)S(1)}, u32[]{:S(2)}, u32[]{:S(2)}) collective-permute-start(bf16[1,64,384]{2,1,0:T(8,128)(2,1)S(1)} %get-tuple-element.39), channel_id=1, source_target_pairs={{0,1},{1,0},{2,3},{3,2},{4,5},{5,4},{6,7},{7,6},{8,9},{9,8},{10,11... | collective-permute-start | bytes 147464 | tf_op jit(solution)/shard_map/ppermute | solution.py:88
  10.9 5.6 %collective-permute-start.1 = (bf16[1,64,384]{2,1,0:T(8,128)(2,1)S(1)}, bf16[1,64,384]{2,1,0:T(8,128)(2,1)S(1)}, u32[]{:S(2)}, u32[]{:S(2)}) collective-permute-start(bf16[1,64,384]{2,1,0:T(8,128)(2,1)S(1)} %get-tuple-element.40), channel_id=1, source_target_pairs={{0,2},{1,3},{2,0},{3,1},{4,6},{5,7},{6,4},{7,5},{8,10},{9,11},{10,... | collective-permute-start | bytes 147464 | tf_op jit(solution)/shard_map/ppermute | solution.py:88
  13.5 5.9 %collective-permute-start.2 = (bf16[1,64,384]{2,1,0:T(8,128)(2,1)S(1)}, bf16[1,64,384]{2,1,0:T(8,128)(2,1)S(1)}, u32[]{:S(2)}, u32[]{:S(2)}) collective-permute-start(bf16[1,64,384]{2,1,0:T(8,128)(2,1)S(1)} %get-tuple-element.41), channel_id=1, source_target_pairs={{0,3},{1,2},{2,1},{3,0},{4,7},{5,6},{6,5},{7,4},{8,11},{9,10},{10,... | collective-permute-start | bytes 147464 | tf_op jit(solution)/shard_map/ppermute | solution.py:88
  20.1 6.1 %collective-permute-start.5 = (bf16[1,64,384]{2,1,0:T(8,128)(2,1)S(1)}, bf16[1,64,384]{2,1,0:T(8,128)(2,1)S(1)}, u32[]{:S(2)}, u32[]{:S(2)}) collective-permute-start(bf16[1,64,384]{2,1,0:T(8,128)(2,1)S(1)} %fusion.144), channel_id=1, source_target_pairs={{0,3},{1,2},{2,1},{3,0},{4,7},{5,6},{6,5},{7,4},{8,11},{9,10},{10,... | collective-permute-start | bytes 147464 | tf_op jit(solution)/shard_map/ppermute | solution.py:98
  20.8 6.0 %collective-permute-start.4 = (bf16[1,64,384]{2,1,0:T(8,128)(2,1)S(1)}, bf16[1,64,384]{2,1,0:T(8,128)(2,1)S(1)}, u32[]{:S(2)}, u32[]{:S(2)}) collective-permute-start(bf16[1,64,384]{2,1,0:T(8,128)(2,1)S(1)} %fusion.144), channel_id=1, source_target_pairs={{0,2},{1,3},{2,0},{3,1},{4,6},{5,7},{6,4},{7,5},{8,10},{9,11},{10,... | collective-permute-start | bytes 147464 | tf_op jit(solution)/shard_map/ppermute | solution.py:98
  20.8 6.0 %collective-permute-start.3 = (bf16[1,64,384]{2,1,0:T(8,128)(2,1)S(1)}, bf16[1,64,384]{2,1,0:T(8,128)(2,1)S(1)}, u32[]{:S(2)}, u32[]{:S(2)}) collective-permute-start(bf16[1,64,384]{2,1,0:T(8,128)(2,1)S(1)} %fusion.144), channel_id=1, source_target_pairs={{0,1},{1,0},{2,3},{3,2},{4,5},{5,4},{6,7},{7,6},{8,9},{9,8},{10,11... | collective-permute-start | bytes 147464 | tf_op jit(solution)/shard_map/ppermute | solution.py:98
  28.7 1.5 %collective-permute-start.7 = (bf16[384,192]{1,0:T(8,128)(2,1)S(1)}, bf16[384,192]{1,0:T(8,128)(2,1)S(1)}, u32[]{:S(2)}, u32[]{:S(2)}) collective-permute-start(bf16[384,192]{1,0:T(8,128)(2,1)S(1)} %constant_dynamic-slice_fusion.3), channel_id=1, source_target_pairs={{0,8},{8,0},{16,24},{24,16},{1,9},{9,1},{17,25},{25,17},{2,10},{10... | collective-permute-start | bytes 442376 | tf_op jit(solution)/shard_map/ppermute | solution.py:135
  28.8 7.5 %collective-permute-start.6 = (bf16[1,136,384]{2,1,0:T(8,128)(2,1)S(1)}, bf16[1,136,384]{2,1,0:T(8,128)(2,1)S(1)}, u32[]{:S(2)}, u32[]{:S(2)}) collective-permute-start(bf16[1,136,384]{2,1,0:T(8,128)(2,1)S(1)} %pad_maximum_fusion.1), channel_id=1, source_target_pairs={{0,4},{4,0},{1,5},{5,1},{2,6},{6,2},{3,7},{7,3},{8,12},{12,8},{9,1... | collective-permute-start | bytes 313352 | tf_op jit(solution)/shard_map/ppermute | solution.py:160
  30.3 6.0 %collective-permute-start.8 = (bf16[192,192]{1,0:T(8,128)(2,1)S(1)}, bf16[192,192]{1,0:T(8,128)(2,1)S(1)}, u32[]{:S(2)}, u32[]{:S(2)}) collective-permute-start(bf16[192,192]{1,0:T(8,128)(2,1)S(1)} %constant_dynamic-slice_fusion.2), channel_id=1, source_target_pairs={{0,4},{4,0},{1,5},{5,1},{2,6},{6,2},{3,7},{7,3},{8,12},{12,8},{9,1... | collective-permute-start | bytes 221192 | tf_op jit(solution)/shard_map/ppermute | solution.py:141
  38.3 1.5 %collective-permute-start.10 = (bf16[384,192]{1,0:T(8,128)(2,1)S(1)}, bf16[384,192]{1,0:T(8,128)(2,1)S(1)}, u32[]{:S(2)}, u32[]{:S(2)}) collective-permute-start(bf16[384,192]{1,0:T(8,128)(2,1)S(1)} %constant_dynamic-slice_fusion), channel_id=1, source_target_pairs={{0,8},{8,0},{16,24},{24,16},{1,9},{9,1},{17,25},{25,17},{2,10},{10... | collective-permute-start | bytes 442376 | tf_op jit(solution)/shard_map/ppermute | solution.py:135
  40.0 4.9 %collective-permute-start.11 = (bf16[192,192]{1,0:T(8,128)(2,1)S(1)}, bf16[192,192]{1,0:T(8,128)(2,1)S(1)}, u32[]{:S(2)}, u32[]{:S(2)}) collective-permute-start(bf16[192,192]{1,0:T(8,128)(2,1)S(1)} %constant_dynamic-slice_fusion.4), channel_id=1, source_target_pairs={{0,4},{4,0},{1,5},{5,1},{2,6},{6,2},{3,7},{7,3},{8,12},{12,8},{9,1... | collective-permute-start | bytes 221192 | tf_op jit(solution)/shard_map/ppermute | solution.py:141
  45.0 6.2 %collective-permute-start.12 = (bf16[2,192,192]{2,1,0:T(8,128)(2,1)S(1)}, bf16[2,192,192]{2,1,0:T(8,128)(2,1)S(1)}, u32[]{:S(2)}, u32[]{:S(2)}) collective-permute-start(bf16[2,192,192]{2,1,0:T(8,128)(2,1)S(1)} %pad_maximum_fusion), channel_id=1, source_target_pairs={{0,16},{8,24},{16,0},{24,8},{1,17},{9,25},{17,1},{25,9},{2,18},{10... | collective-permute-start | bytes 442376 | tf_op jit(solution)/shard_map/ppermute | solution.py:279
  51.2 1.8 %collective-permute-start.13 = (f32[2,192,192]{2,1,0:T(8,128)S(1)}, f32[2,192,192]{2,1,0:T(8,128)S(1)}, u32[]{:S(2)}, u32[]{:S(2)}) collective-permute-start(f32[2,192,192]{2,1,0:T(8,128)S(1)} %convert_add_fusion), channel_id=1, source_target_pairs={{0,8},{8,0},{16,24},{24,16},{1,9},{9,1},{17,25},{25,17},{2,10},{10... | collective-permute-start | bytes 884744 | tf_op jit(solution)/shard_map/ppermute | solution.py:281

commit v9 on v8

--- a/solution.py
+++ b/solution.py
@@ -49,12 +49,32 @@
     head = lax.axis_index("head")
     me = slab * n_head + head
 
+    donor_match = site_match(donor_pos, slab_rows, slab).astype(jnp.bfloat16)
+    acceptor_match = site_match(acceptor_pos, slab_rows, slab).astype(jnp.bfloat16)
+    donor_rows = jnp.einsum(
+        "bnr,brc->bnc", donor_match, embed, preferred_element_type=jnp.float32
+    ).astype(jnp.bfloat16)
+    acceptor_rows = jnp.einsum(
+        "bnr,brc->bnc", acceptor_match, embed, preferred_element_type=jnp.float32
+    ).astype(jnp.bfloat16)
+    donor_part = jnp.einsum(
+        "bnc,cp->bnp", donor_rows, donor_w, preferred_element_type=jnp.float32
+    ).astype(jnp.bfloat16)
+    acceptor_part = jnp.einsum(
+        "bnc,cp->bnp", acceptor_rows, acceptor_w, preferred_element_type=jnp.float32
+    ).astype(jnp.bfloat16)
+
+    both = 2 * slab_sites
+    assert both % n_head == 0
+    quarter = both // n_head
+    parts = jnp.concatenate([donor_part, acceptor_part], axis=1)
+    parts, target_late = lax.optimization_barrier((parts, target))
     target_col = jnp.zeros((batch, sites, slab_sites), target.dtype)
     own_cols = lax.dynamic_slice_in_dim(target, slab * slab_sites, slab_sites, 2)
     target_col = lax.dynamic_update_slice_in_dim(target_col, own_cols, slab * slab_sites, 1)
     for k in range(1, n_seq):
         outgoing = lax.dynamic_slice_in_dim(
-            target, jnp.minimum(slab + k, n_seq - 1) * slab_sites, slab_sites, 2
+            target_late, jnp.minimum(slab + k, n_seq - 1) * slab_sites, slab_sites, 2
         )
         perm = [(i, i + k) for i in range(n_seq - k)]
         arrived = lax.ppermute(outgoing, "seq", perm)
@@ -62,25 +82,6 @@
         placed = lax.dynamic_update_slice_in_dim(target_col, arrived, source * slab_sites, 1)
         target_col = jnp.where(slab >= k, placed, target_col)
 
-    donor_match = site_match(donor_pos, slab_rows, slab).astype(jnp.bfloat16)
-    acceptor_match = site_match(acceptor_pos, slab_rows, slab).astype(jnp.bfloat16)
-    donor_rows = jnp.einsum(
-        "bnr,brc->bnc", donor_match, embed, preferred_element_type=jnp.float32
-    ).astype(jnp.bfloat16)
-    acceptor_rows = jnp.einsum(
-        "bnr,brc->bnc", acceptor_match, embed, preferred_element_type=jnp.float32
-    ).astype(jnp.bfloat16)
-    donor_part = jnp.einsum(
-        "bnc,cp->bnp", donor_rows, donor_w, preferred_element_type=jnp.float32
-    ).astype(jnp.bfloat16)
-    acceptor_part = jnp.einsum(
-        "bnc,cp->bnp", acceptor_rows, acceptor_w, preferred_element_type=jnp.float32
-    ).astype(jnp.bfloat16)
-
-    both = 2 * slab_sites
-    assert both % n_head == 0
-    quarter = both // n_head
-    parts = jnp.concatenate([donor_part, acceptor_part], axis=1)
     assert n_head & (n_head - 1) == 0
     pieces = [lax.dynamic_slice_in_dim(parts, head * quarter, quarter, 1)]
     for k in range(1, n_head):

time: 54.3 us -> 54.2 us (level)
  local copies, waits for them, and re-layouts: 4.91 us -> 5.92 us
  waiting for transfers between devices: 23.7 us -> 22.8 us
    ppermute x3, waiting for transfers between devices: 5.31 us -> 3.81 us  [shards(): lax.ppermute(outgoing, 'head', [(i, i ^ k) for i in range(n_head)])]
    unnamed x14, local copies, waits for them, and re-layouts: 2.31 us -> 3.28 us
    ppermute x3, waiting for transfers between devices: 2.26 us -> 2.92 us  [shards(): lax.ppermute(feat_quarter, 'head', [(i, i ^ k) for i in range(n_head)])]
  transfers between devices with their start and end apart: 14 -> 14, of which waited for: 10 -> 10; matrix products, arithmetic and copies ran while one was open for 8% -> 6% of each run, Pallas kernels for 0% -> 0%
where the time goes in v9:
time: 54.2 us; the launch traced here: 53.9 us
  waiting for transfers between devices  22.8 us (42%)
  starting transfers between devices  16.8 us (31%)
  local copies, waits for them, and re-layouts  5.92 us (11%)
  matrix products  5.9 us (11%)
  other arithmetic  1.27 us (2%)
  between operations  1.22 us (2%)
    ppermute x2, waiting for transfers between devices, to_seq_partner(): lax.ppermute(outgoing, 'seq', [(0, 1), (1, 0)]).astype(jnp.float32)  9.23 us
    ppermute x1, starting transfers between devices, shards(): arrived = lax.ppermute(outgoing, 'seq', perm)  4.86 us
    ppermute x3, starting transfers between devices, shards(): lax.ppermute(feat_quarter, 'head', [(i, i ^ k) for i in range(n_head)])  4.45 us
    ppermute x3, starting transfers between devices, shards(): lax.ppermute(outgoing, 'head', [(i, i ^ k) for i in range(n_head)])  4.45 us
    ppermute x1, waiting for transfers between devices, shards(): lax.ppermute(held, 'dp', perm).astype(jnp.float32)  4.39 us
    ppermute x3, waiting for transfers between devices, shards(): lax.ppermute(outgoing, 'head', [(i, i ^ k) for i in range(n_head)])  3.81 us
    unnamed x14, local copies, waits for them, and re-layouts  3.28 us
    ppermute x3, waiting for transfers between devices, shards(): lax.ppermute(feat_quarter, 'head', [(i, i ^ k) for i in range(n_head)])  2.92 us
  transfers between devices with their start and end apart: 14, of which 10 were waited for; matrix products, arithmetic and copies ran while one was open for 6% of the time, Pallas kernels for 0%

profile of v9, /device:TPU:0, one launch (start us, length us, event | category | flops | bytes accessed | tf_op | source)
XLA Modules:
  0.0 53.9 jit_solution(3139568724320850970)
XLA Ops:
  0.7 0.7 %copy-done.4 = s32[1,128]{1,0:T(1,128)S(1)} copy-done((s32[1,128]{1,0:T(1,128)S(1)}, s32[1,128]{1,0:T(1,128)}, u32[]{:S(2)}) %copy-start.4) | copy-done | bytes 536
  2.2 0.7 %copy-done.1 = bf16[384,384]{1,0:T(8,128)(2,1)S(1)} copy-done((bf16[384,384]{1,0:T(8,128)(2,1)S(1)}, bf16[384,384]{1,0:T(8,128)(2,1)}, u32[]{:S(2)}) %copy-start.1) | copy-done | bytes 294936
  3.1 0.7 %copy-done.2 = bf16[384,384]{1,0:T(8,128)(2,1)S(1)} copy-done((bf16[384,384]{1,0:T(8,128)(2,1)S(1)}, bf16[384,384]{1,0:T(8,128)(2,1)}, u32[]{:S(2)}) %copy-start.2) | copy-done | bytes 294936
  4.1 0.8 %copy-done.3 = bf16[1,128,256]{2,1,0:T(8,128)(2,1)S(1)} copy-done((bf16[1,128,256]{2,1,0:T(8,128)(2,1)S(1)}, bf16[1,128,256]{2,1,0:T(8,128)(2,1)}, u32[]{:S(2)}) %copy-start.3) | copy-done | bytes 65560
  4.9 4.9 %collective-permute-start.9 = (bf16[1,128,128]{2,1,0:T(8,128)(2,1)S(1)}, bf16[1,128,128]{2,1,0:T(8,128)(2,1)S(1)}, u32[]{:S(2)}, u32[]{:S(2)}) collective-permute-start(bf16[1,128,128]{2,1,0:T(8,128)(2,1)S(1)} %constant_dynamic-slice_fusion.1), channel_id=1, source_target_pairs={{0,4},{1,5},{2,6},{3,7},{8,12},{9,13},{10,14},{11,15},{16,20},{17,... | collective-permute-start | bytes 98312 | tf_op jit(solution)/shard_map/ppermute | solution.py:80
  9.9 3.7 %collective-permute-start.2 = (bf16[1,64,384]{2,1,0:T(8,128)(2,1)S(1)}, bf16[1,64,384]{2,1,0:T(8,128)(2,1)S(1)}, u32[]{:S(2)}, u32[]{:S(2)}) collective-permute-start(bf16[1,64,384]{2,1,0:T(8,128)(2,1)S(1)} %get-tuple-element.43), channel_id=1, source_target_pairs={{0,3},{1,2},{2,1},{3,0},{4,7},{5,6},{6,5},{7,4},{8,11},{9,10},{10,... | collective-permute-start | bytes 147464 | tf_op jit(solution)/shard_map/ppermute | solution.py:89
  13.5 0.8 %collective-permute-start = (bf16[1,64,384]{2,1,0:T(8,128)(2,1)S(1)}, bf16[1,64,384]{2,1,0:T(8,128)(2,1)S(1)}, u32[]{:S(2)}, u32[]{:S(2)}) collective-permute-start(bf16[1,64,384]{2,1,0:T(8,128)(2,1)S(1)} %get-tuple-element.45), channel_id=1, source_target_pairs={{0,1},{1,0},{2,3},{3,2},{4,5},{5,4},{6,7},{7,6},{8,9},{9,8},{10,11... | collective-permute-start | bytes 147464 | tf_op jit(solution)/shard_map/ppermute | solution.py:89
  14.7 1.6 %collective-permute-done.2 = bf16[1,64,384]{2,1,0:T(8,128)(2,1)S(1)} collective-permute-done((bf16[1,64,384]{2,1,0:T(8,128)(2,1)S(1)}, bf16[1,64,384]{2,1,0:T(8,128)(2,1)S(1)}, u32[]{:S(2)}, u32[]{:S(2)}) %collective-permute-start.2) | collective-permute-done | bytes 49184 | tf_op jit(solution)/shard_map/ppermute | solution.py:89
  16.3 2.2 %collective-permute-done.1 = bf16[1,64,384]{2,1,0:T(8,128)(2,1)S(1)} collective-permute-done((bf16[1,64,384]{2,1,0:T(8,128)(2,1)S(1)}, bf16[1,64,384]{2,1,0:T(8,128)(2,1)S(1)}, u32[]{:S(2)}, u32[]{:S(2)}) %collective-permute-start.1) | collective-permute-done | bytes 49184 | tf_op jit(solution)/shard_map/ppermute | solution.py:89
  18.6 0.6 %gather_fusion = bf16[4,64,384]{2,1,0:T(8,128)(2,1)S(1)} fusion(bf16[4,64,384]{2,1,0:T(8,128)(2,1)S(1)} %maximum_bitcast_fusion, s32[1024]{0:T(1024)S(1)} %pad_clamp_fusion), kind=kCustom, calls=%fused_computation.clone | custom fusion | bytes 393232 | tf_op jit(solution)/shard_map/jit(_take)/gather | solution.py:91
  19.3 1.9 %collective-permute-start.5 = (bf16[1,64,384]{2,1,0:T(8,128)(2,1)S(1)}, bf16[1,64,384]{2,1,0:T(8,128)(2,1)S(1)}, u32[]{:S(2)}, u32[]{:S(2)}) collective-permute-start(bf16[1,64,384]{2,1,0:T(8,128)(2,1)S(1)} %fusion.139), channel_id=1, source_target_pairs={{0,3},{1,2},{2,1},{3,0},{4,7},{5,6},{6,5},{7,4},{8,11},{9,10},{10,... | collective-permute-start | bytes 147464 | tf_op jit(solution)/shard_map/ppermute | solution.py:99
  21.5 2.3 %collective-permute-start.3 = (bf16[1,64,384]{2,1,0:T(8,128)(2,1)S(1)}, bf16[1,64,384]{2,1,0:T(8,128)(2,1)S(1)}, u32[]{:S(2)}, u32[]{:S(2)}) collective-permute-start(bf16[1,64,384]{2,1,0:T(8,128)(2,1)S(1)} %fusion.139), channel_id=1, source_target_pairs={{0,1},{1,0},{2,3},{3,2},{4,5},{5,4},{6,7},{7,6},{8,9},{9,8},{10,11... | collective-permute-start | bytes 147464 | tf_op jit(solution)/shard_map/ppermute | solution.py:99
  23.8 1.5 %collective-permute-done.5 = bf16[1,64,384]{2,1,0:T(8,128)(2,1)S(1)} collective-permute-done((bf16[1,64,384]{2,1,0:T(8,128)(2,1)S(1)}, bf16[1,64,384]{2,1,0:T(8,128)(2,1)S(1)}, u32[]{:S(2)}, u32[]{:S(2)}) %collective-permute-start.5) | collective-permute-done | bytes 49184 | tf_op jit(solution)/shard_map/ppermute | solution.py:99
  25.2 1.4 %collective-permute-done.4 = bf16[1,64,384]{2,1,0:T(8,128)(2,1)S(1)} collective-permute-done((bf16[1,64,384]{2,1,0:T(8,128)(2,1)S(1)}, bf16[1,64,384]{2,1,0:T(8,128)(2,1)S(1)}, u32[]{:S(2)}, u32[]{:S(2)}) %collective-permute-start.4) | collective-permute-done | bytes 49184 | tf_op jit(solution)/shard_map/ppermute | solution.py:99
  26.7 0.6 %gather_fusion.1 = bf16[4,64,384]{2,1,0:T(8,128)(2,1)S(1)} fusion(bf16[4,64,384]{2,1,0:T(8,128)(2,1)S(1)} %maximum_bitcast_fusion.1, s32[1024]{0:T(1024)S(1)} %pad_clamp_fusion), kind=kCustom, calls=%fused_computation.1.clone | custom fusion | bytes 393232 | tf_op jit(solution)/shard_map/jit(_take)/gather | solution.py:100
  28.7 1.3 %collective-permute-done.7 = bf16[384,192]{1,0:T(8,128)(2,1)S(1)} collective-permute-done((bf16[384,192]{1,0:T(8,128)(2,1)S(1)}, bf16[384,192]{1,0:T(8,128)(2,1)S(1)}, u32[]{:S(2)}, u32[]{:S(2)}) %collective-permute-start.7) | collective-permute-done | bytes 147488 | tf_op jit(solution)/shard_map/ppermute | solution.py:136
  30.1 0.8 %collective-permute-start.8 = (bf16[192,192]{1,0:T(8,128)(2,1)S(1)}, bf16[192,192]{1,0:T(8,128)(2,1)S(1)}, u32[]{:S(2)}, u32[]{:S(2)}) collective-permute-start(bf16[192,192]{1,0:T(8,128)(2,1)S(1)} %constant_dynamic-slice_fusion.3), channel_id=1, source_target_pairs={{0,4},{4,0},{1,5},{5,1},{2,6},{6,2},{3,7},{7,3},{8,12},{12,8},{9,1... | collective-permute-start | bytes 221192 | tf_op jit(solution)/shard_map/ppermute | solution.py:142
  31.1 5.1 %collective-permute-done.8 = bf16[192,192]{1,0:T(8,128)(2,1)S(1)} collective-permute-done((bf16[192,192]{1,0:T(8,128)(2,1)S(1)}, bf16[192,192]{1,0:T(8,128)(2,1)S(1)}, u32[]{:S(2)}, u32[]{:S(2)}) %collective-permute-start.8) | collective-permute-done | bytes 73760 | tf_op jit(solution)/shard_map/ppermute | solution.py:142
  38.6 1.0 %collective-permute-done.10 = bf16[384,192]{1,0:T(8,128)(2,1)S(1)} collective-permute-done((bf16[384,192]{1,0:T(8,128)(2,1)S(1)}, bf16[384,192]{1,0:T(8,128)(2,1)S(1)}, u32[]{:S(2)}, u32[]{:S(2)}) %collective-permute-start.10) | collective-permute-done | bytes 147488 | tf_op jit(solution)/shard_map/ppermute | solution.py:136
  40.5 4.2 %collective-permute-done.11 = bf16[192,192]{1,0:T(8,128)(2,1)S(1)} collective-permute-done((bf16[192,192]{1,0:T(8,128)(2,1)S(1)}, bf16[192,192]{1,0:T(8,128)(2,1)S(1)}, u32[]{:S(2)}, u32[]{:S(2)}) %collective-permute-start.11) | collective-permute-done | bytes 73760 | tf_op jit(solution)/shard_map/ppermute | solution.py:142
  44.8 1.6 %collective-permute-start.12 = (bf16[2,192,192]{2,1,0:T(8,128)(2,1)S(1)}, bf16[2,192,192]{2,1,0:T(8,128)(2,1)S(1)}, u32[]{:S(2)}, u32[]{:S(2)}) collective-permute-start(bf16[2,192,192]{2,1,0:T(8,128)(2,1)S(1)} %pad_maximum_fusion.1), channel_id=1, source_target_pairs={{0,16},{8,24},{16,0},{24,8},{1,17},{9,25},{17,1},{25,9},{2,18},{10... | collective-permute-start | bytes 442376 | tf_op jit(solution)/shard_map/ppermute | solution.py:280
  46.6 4.4 %collective-permute-done.12 = bf16[2,192,192]{2,1,0:T(8,128)(2,1)S(1)} collective-permute-done((bf16[2,192,192]{2,1,0:T(8,128)(2,1)S(1)}, bf16[2,192,192]{2,1,0:T(8,128)(2,1)S(1)}, u32[]{:S(2)}, u32[]{:S(2)}) %collective-permute-start.12) | collective-permute-done | bytes 147488 | tf_op jit(solution)/shard_map/ppermute | solution.py:280
  51.5 1.1 %fusion.2 = bf16[1,512,384]{2,1,0:T(8,128)(2,1)} fusion(f32[512,384]{1,0:T(8,128)S(1)} %convolution_add_fusion.1, f32[512,384]{1,0:T(8,128)S(1)} %fusion.14, s32[128]{0:T(128)S(1)} %get-tuple-element.48, f32[128,384]{1,0:T(8,128)S(1)} %fusion.61), kind=kOutput, calls=%fused_computation.8 | convolution fusion | flops 51183616 | bytes 2163200 | tf_op jit(solution)/shard_map/bnr,bnc->brc/dot_general | solution.py:26
  53.1 0.9 %slice_bitcast_fusion = (f32[384,192]{0,1:T(8,128)}, f32[384,192]{0,1:T(8,128)}) fusion(f32[2,384,192]{1,2,0:T(8,128)S(1)} %fusion.11), kind=kLoop, calls=%fused_computation.37 | loop fusion | bytes 1179648 | tf_op jit(solution)/shard_map/squeeze | solution.py:287
  (84 shorter events, 8.1 us)
Async XLA Ops:
  0.6 1.0 %copy-start = (bf16[1,512,384]{2,1,0:T(8,128)(2,1)S(1)}, bf16[1,512,384]{2,1,0:T(8,128)(2,1)}, u32[]{:S(2)}) copy-start(bf16[1,512,384]{2,1,0:T(8,128)(2,1)} %param.12) | copy-start | bytes 1179652
  0.7 0.7 %copy-start.4 = (s32[1,128]{1,0:T(1,128)S(1)}, s32[1,128]{1,0:T(1,128)}, u32[]{:S(2)}) copy-start(s32[1,128]{1,0:T(1,128)} %param.13) | copy-start | bytes 1540
  0.7 0.7 %copy-start.5 = (s32[1,128]{1,0:T(1,128)S(1)}, s32[1,128]{1,0:T(1,128)}, u32[]{:S(2)}) copy-start(s32[1,128]{1,0:T(1,128)} %param.14) | copy-start | bytes 1540
  1.9 1.0 %copy-start.1 = (bf16[384,384]{1,0:T(8,128)(2,1)S(1)}, bf16[384,384]{1,0:T(8,128)(2,1)}, u32[]{:S(2)}) copy-start(bf16[384,384]{1,0:T(8,128)(2,1)} %param.16) | copy-start | bytes 884740
  2.9 1.0 %copy-start.2 = (bf16[384,384]{1,0:T(8,128)(2,1)S(1)}, bf16[384,384]{1,0:T(8,128)(2,1)}, u32[]{:S(2)}) copy-start(bf16[384,384]{1,0:T(8,128)(2,1)} %param.17) | copy-start | bytes 884740
  4.1 0.8 %copy-start.3 = (bf16[1,128,256]{2,1,0:T(8,128)(2,1)S(1)}, bf16[1,128,256]{2,1,0:T(8,128)(2,1)}, u32[]{:S(2)}) copy-start(bf16[1,128,256]{2,1,0:T(8,128)(2,1)} %param.15) | copy-start | bytes 196612
  4.9 9.7 %collective-permute-start.9 = (bf16[1,128,128]{2,1,0:T(8,128)(2,1)S(1)}, bf16[1,128,128]{2,1,0:T(8,128)(2,1)S(1)}, u32[]{:S(2)}, u32[]{:S(2)}) collective-permute-start(bf16[1,128,128]{2,1,0:T(8,128)(2,1)S(1)} %constant_dynamic-slice_fusion.1), channel_id=1, source_target_pairs={{0,4},{1,5},{2,6},{3,7},{8,12},{9,13},{10,14},{11,15},{16,20},{17,... | collective-permute-start | bytes 98312 | tf_op jit(solution)/shard_map/ppermute | solution.py:80
  9.9 6.5 %collective-permute-start.2 = (bf16[1,64,384]{2,1,0:T(8,128)(2,1)S(1)}, bf16[1,64,384]{2,1,0:T(8,128)(2,1)S(1)}, u32[]{:S(2)}, u32[]{:S(2)}) collective-permute-start(bf16[1,64,384]{2,1,0:T(8,128)(2,1)S(1)} %get-tuple-element.43), channel_id=1, source_target_pairs={{0,3},{1,2},{2,1},{3,0},{4,7},{5,6},{6,5},{7,4},{8,11},{9,10},{10,... | collective-permute-start | bytes 147464 | tf_op jit(solution)/shard_map/ppermute | solution.py:89
  13.5 5.0 %collective-permute-start.1 = (bf16[1,64,384]{2,1,0:T(8,128)(2,1)S(1)}, bf16[1,64,384]{2,1,0:T(8,128)(2,1)S(1)}, u32[]{:S(2)}, u32[]{:S(2)}) collective-permute-start(bf16[1,64,384]{2,1,0:T(8,128)(2,1)S(1)} %get-tuple-element.44), channel_id=1, source_target_pairs={{0,2},{1,3},{2,0},{3,1},{4,6},{5,7},{6,4},{7,5},{8,10},{9,11},{10,... | collective-permute-start | bytes 147464 | tf_op jit(solution)/shard_map/ppermute | solution.py:89
  13.5 5.0 %collective-permute-start = (bf16[1,64,384]{2,1,0:T(8,128)(2,1)S(1)}, bf16[1,64,384]{2,1,0:T(8,128)(2,1)S(1)}, u32[]{:S(2)}, u32[]{:S(2)}) collective-permute-start(bf16[1,64,384]{2,1,0:T(8,128)(2,1)S(1)} %get-tuple-element.45), channel_id=1, source_target_pairs={{0,1},{1,0},{2,3},{3,2},{4,5},{5,4},{6,7},{7,6},{8,9},{9,8},{10,11... | collective-permute-start | bytes 147464 | tf_op jit(solution)/shard_map/ppermute | solution.py:89
  19.3 6.0 %collective-permute-start.5 = (bf16[1,64,384]{2,1,0:T(8,128)(2,1)S(1)}, bf16[1,64,384]{2,1,0:T(8,128)(2,1)S(1)}, u32[]{:S(2)}, u32[]{:S(2)}) collective-permute-start(bf16[1,64,384]{2,1,0:T(8,128)(2,1)S(1)} %fusion.139), channel_id=1, source_target_pairs={{0,3},{1,2},{2,1},{3,0},{4,7},{5,6},{6,5},{7,4},{8,11},{9,10},{10,... | collective-permute-start | bytes 147464 | tf_op jit(solution)/shard_map/ppermute | solution.py:99
  21.2 5.5 %collective-permute-start.4 = (bf16[1,64,384]{2,1,0:T(8,128)(2,1)S(1)}, bf16[1,64,384]{2,1,0:T(8,128)(2,1)S(1)}, u32[]{:S(2)}, u32[]{:S(2)}) collective-permute-start(bf16[1,64,384]{2,1,0:T(8,128)(2,1)S(1)} %fusion.139), channel_id=1, source_target_pairs={{0,2},{1,3},{2,0},{3,1},{4,6},{5,7},{6,4},{7,5},{8,10},{9,11},{10,... | collective-permute-start | bytes 147464 | tf_op jit(solution)/shard_map/ppermute | solution.py:99
  21.5 5.2 %collective-permute-start.3 = (bf16[1,64,384]{2,1,0:T(8,128)(2,1)S(1)}, bf16[1,64,384]{2,1,0:T(8,128)(2,1)S(1)}, u32[]{:S(2)}, u32[]{:S(2)}) collective-permute-start(bf16[1,64,384]{2,1,0:T(8,128)(2,1)S(1)} %fusion.139), channel_id=1, source_target_pairs={{0,1},{1,0},{2,3},{3,2},{4,5},{5,4},{6,7},{7,6},{8,9},{9,8},{10,11... | collective-permute-start | bytes 147464 | tf_op jit(solution)/shard_map/ppermute | solution.py:99
  28.5 1.5 %collective-permute-start.7 = (bf16[384,192]{1,0:T(8,128)(2,1)S(1)}, bf16[384,192]{1,0:T(8,128)(2,1)S(1)}, u32[]{:S(2)}, u32[]{:S(2)}) collective-permute-start(bf16[384,192]{1,0:T(8,128)(2,1)S(1)} %constant_dynamic-slice_fusion.4), channel_id=1, source_target_pairs={{0,8},{8,0},{16,24},{24,16},{1,9},{9,1},{17,25},{25,17},{2,10},{10... | collective-permute-start | bytes 442376 | tf_op jit(solution)/shard_map/ppermute | solution.py:136
  28.7 7.5 %collective-permute-start.6 = (bf16[1,136,384]{2,1,0:T(8,128)(2,1)S(1)}, bf16[1,136,384]{2,1,0:T(8,128)(2,1)S(1)}, u32[]{:S(2)}, u32[]{:S(2)}) collective-permute-start(bf16[1,136,384]{2,1,0:T(8,128)(2,1)S(1)} %pad_maximum_fusion.2), channel_id=1, source_target_pairs={{0,4},{4,0},{1,5},{5,1},{2,6},{6,2},{3,7},{7,3},{8,12},{12,8},{9,1... | collective-permute-start | bytes 313352 | tf_op jit(solution)/shard_map/ppermute | solution.py:161
  30.1 6.0 %collective-permute-start.8 = (bf16[192,192]{1,0:T(8,128)(2,1)S(1)}, bf16[192,192]{1,0:T(8,128)(2,1)S(1)}, u32[]{:S(2)}, u32[]{:S(2)}) collective-permute-start(bf16[192,192]{1,0:T(8,128)(2,1)S(1)} %constant_dynamic-slice_fusion.3), channel_id=1, source_target_pairs={{0,4},{4,0},{1,5},{5,1},{2,6},{6,2},{3,7},{7,3},{8,12},{12,8},{9,1... | collective-permute-start | bytes 221192 | tf_op jit(solution)/shard_map/ppermute | solution.py:142
  38.1 1.5 %collective-permute-start.10 = (bf16[384,192]{1,0:T(8,128)(2,1)S(1)}, bf16[384,192]{1,0:T(8,128)(2,1)S(1)}, u32[]{:S(2)}, u32[]{:S(2)}) collective-permute-start(bf16[384,192]{1,0:T(8,128)(2,1)S(1)} %constant_dynamic-slice_fusion), channel_id=1, source_target_pairs={{0,8},{8,0},{16,24},{24,16},{1,9},{9,1},{17,25},{25,17},{2,10},{10... | collective-permute-start | bytes 442376 | tf_op jit(solution)/shard_map/ppermute | solution.py:136
  39.8 4.9 %collective-permute-start.11 = (bf16[192,192]{1,0:T(8,128)(2,1)S(1)}, bf16[192,192]{1,0:T(8,128)(2,1)S(1)}, u32[]{:S(2)}, u32[]{:S(2)}) collective-permute-start(bf16[192,192]{1,0:T(8,128)(2,1)S(1)} %constant_dynamic-slice_fusion.2), channel_id=1, source_target_pairs={{0,4},{4,0},{1,5},{5,1},{2,6},{6,2},{3,7},{7,3},{8,12},{12,8},{9,1... | collective-permute-start | bytes 221192 | tf_op jit(solution)/shard_map/ppermute | solution.py:142
  44.8 6.2 %collective-permute-start.12 = (bf16[2,192,192]{2,1,0:T(8,128)(2,1)S(1)}, bf16[2,192,192]{2,1,0:T(8,128)(2,1)S(1)}, u32[]{:S(2)}, u32[]{:S(2)}) collective-permute-start(bf16[2,192,192]{2,1,0:T(8,128)(2,1)S(1)} %pad_maximum_fusion.1), channel_id=1, source_target_pairs={{0,16},{8,24},{16,0},{24,8},{1,17},{9,25},{17,1},{25,9},{2,18},{10... | collective-permute-start | bytes 442376 | tf_op jit(solution)/shard_map/ppermute | solution.py:280
  51.0 1.8 %collective-permute-start.13 = (f32[2,192,192]{2,1,0:T(8,128)S(1)}, f32[2,192,192]{2,1,0:T(8,128)S(1)}, u32[]{:S(2)}, u32[]{:S(2)}) collective-permute-start(f32[2,192,192]{2,1,0:T(8,128)S(1)} %convert_add_fusion), channel_id=1, source_target_pairs={{0,8},{8,0},{16,24},{24,16},{1,9},{9,1},{17,25},{25,17},{2,10},{10... | collective-permute-start | bytes 884744 | tf_op jit(solution)/shard_map/ppermute | solution.py:282

commit v10 on v7

--- a/solution.py
+++ b/solution.py
@@ -211,17 +211,36 @@
     outgoing = lax.dynamic_slice_in_dim(blocks, (1 - pair) * half, half, 2)
     mine = mine + lax.ppermute(outgoing, "dp", [(i, i ^ 1) for i in range(n_dp)]).astype(jnp.float32)
     held = mine.astype(jnp.bfloat16)
-    mine = lax.dynamic_slice_in_dim(held, slab * part, part, 1).astype(jnp.float32)
-    for k in range(1, n_seq):
-        outgoing = lax.dynamic_slice_in_dim(held, ((slab + k) % n_seq) * part, part, 1)
-        perm = [(i, (i + k) % n_seq) for i in range(n_seq)]
-        mine = mine + lax.ppermute(outgoing, "seq", perm).astype(jnp.float32)
-    bit = 2
-    while bit < n_dp:
-        held = mine.astype(jnp.bfloat16)
-        perm = [(i, i ^ bit) for i in range(n_dp)]
-        mine = held.astype(jnp.float32) + lax.ppermute(held, "dp", perm).astype(jnp.float32)
-        bit *= 2
+    group = (n_dp // 2) * n_seq
+    if group <= 4 and group & (group - 1) == 0:
+        me_g = (dp // 2) * n_seq + slab
+        pieces = [lax.dynamic_slice_in_dim(held, slab * part, part, 1)]
+        for k in range(1, group):
+            dest_part = (me_g ^ k) % n_seq
+            outgoing = lax.dynamic_slice_in_dim(held, dest_part * part, part, 1)
+            perm = []
+            for d in range(n_dp):
+                for s in range(n_seq):
+                    g = (d // 2) * n_seq + s
+                    h = g ^ k
+                    perm.append((d * n_seq + s, ((h // n_seq) * 2 + d % 2) * n_seq + h % n_seq))
+            pieces.append(lax.ppermute(outgoing, ("dp", "seq"), perm))
+        by_source = jnp.take(jnp.stack(pieces), me_g ^ jnp.arange(group, dtype=jnp.int32), axis=0)
+        mine = by_source[0].astype(jnp.float32)
+        for t in range(1, group):
+            mine = mine + by_source[t].astype(jnp.float32)
+    else:
+        mine = lax.dynamic_slice_in_dim(held, slab * part, part, 1).astype(jnp.float32)
+        for k in range(1, n_seq):
+            outgoing = lax.dynamic_slice_in_dim(held, ((slab + k) % n_seq) * part, part, 1)
+            perm = [(i, (i + k) % n_seq) for i in range(n_seq)]
+            mine = mine + lax.ppermute(outgoing, "seq", perm).astype(jnp.float32)
+        bit = 2
+        while bit < n_dp:
+            held = mine.astype(jnp.bfloat16)
+            perm = [(i, i ^ bit) for i in range(n_dp)]
+            mine = held.astype(jnp.float32) + lax.ppermute(held, "dp", perm).astype(jnp.float32)
+            bit *= 2
     other = lax.ppermute(mine, "dp", [(i, i ^ 1) for i in range(n_dp)])
     mine = jnp.where(pair == 0, jnp.concatenate([mine, other], 2), jnp.concatenate([other, mine], 2))
     mine = jnp.swapaxes(mine, 1, 2)

time: 51.2 us -> 51.6 us (level)
  local copies, waits for them, and re-layouts: 4.14 us -> 5.42 us
  waiting for transfers between devices: 18.8 us -> 17.7 us
    another operation x4 -> x6, local copies, waits for them, and re-layouts: 0.05 us -> 0.75 us  [the longest x2 0.7 us: shards(): jnp.stack(pieces)]
    ppermute x2 -> x3, waiting for transfers between devices: 9.52 us -> 8.84 us  [shards(): pieces.append(lax.ppermute(outgoing, ('dp', 'seq'), perm))]
    gather x0 -> x1, local copies, waits for them, and re-layouts: none -> 0.6 us  [shards(): jnp.take(jnp.stack(pieces), me_g ^ jnp.arange(group, dtype=jnp.int32), ax...]
    ppermute x2 -> x3, starting transfers between devices: 3.64 us -> 3.65 us  [shards(): pieces.append(lax.ppermute(outgoing, ('dp', 'seq'), perm))]
  transfers between devices with their start and end apart: 12 -> 13, of which waited for: 8 -> 8; matrix products, arithmetic and copies ran while one was open for 6% -> 6% of each run, Pallas kernels for 0% -> 0%
where the time goes in v10:
time: 51.6 us; the launch traced here: 51.4 us
  starting transfers between devices  20 us (39%)
  waiting for transfers between devices  17.7 us (34%)
  local copies, waits for them, and re-layouts  5.42 us (11%)
  matrix products  5.32 us (10%)
  other arithmetic  1.75 us (3%)
  between operations  1.31 us (3%)
    ppermute x3, waiting for transfers between devices, shards(): pieces.append(lax.ppermute(outgoing, ('dp', 'seq'), perm))  8.84 us
    ppermute x3, starting transfers between devices, shards(): lax.ppermute(outgoing, 'head', [(i, i ^ k) for i in range(n_head)])  5.75 us
    ppermute x3, starting transfers between devices, shards(): lax.ppermute(feat_quarter, 'head', [(i, i ^ k) for i in range(n_head)])  4.45 us
    ppermute x3, waiting for transfers between devices, shards(): lax.ppermute(feat_quarter, 'head', [(i, i ^ k) for i in range(n_head)])  4.17 us
    ppermute x3, starting transfers between devices, shards(): pieces.append(lax.ppermute(outgoing, ('dp', 'seq'), perm))  3.65 us
    ppermute x1, starting transfers between devices, shards(): arrived = lax.ppermute(outgoing, 'seq', perm)  3.57 us
    ppermute x1, waiting for transfers between devices, shards(): arrived = lax.ppermute(jnp.concatenate([sent, flags], axis=1), 'seq', perm)  2.55 us
    ppermute x1, starting transfers between devices, shards(): arrived = lax.ppermute(jnp.concatenate([sent, flags], axis=1), 'seq', perm)  2.38 us
  transfers between devices with their start and end apart: 13, of which 8 were waited for; matrix products, arithmetic and copies ran while one was open for 6% of the time, Pallas kernels for 0%

profile of v10, /device:TPU:0, one launch (start us, length us, event | category | flops | bytes accessed | tf_op | source)
XLA Modules:
  0.0 51.4 jit_solution(7057347087630345211)
XLA Ops:
  0.7 0.7 %copy-done.4 = s32[1,128]{1,0:T(1,128)S(1)} copy-done((s32[1,128]{1,0:T(1,128)S(1)}, s32[1,128]{1,0:T(1,128)}, u32[]{:S(2)}) %copy-start.4) | copy-done | bytes 536
  2.2 0.7 %copy-done.1 = bf16[384,384]{1,0:T(8,128)(2,1)S(1)} copy-done((bf16[384,384]{1,0:T(8,128)(2,1)S(1)}, bf16[384,384]{1,0:T(8,128)(2,1)}, u32[]{:S(2)}) %copy-start.1) | copy-done | bytes 294936
  3.8 5.1 %collective-permute-start.2 = (bf16[1,64,384]{2,1,0:T(8,128)(2,1)S(1)}, bf16[1,64,384]{2,1,0:T(8,128)(2,1)S(1)}, u32[]{:S(2)}, u32[]{:S(2)}) collective-permute-start(bf16[1,64,384]{2,1,0:T(8,128)(2,1)S(1)} %get-tuple-element.39), channel_id=1, source_target_pairs={{0,3},{1,2},{2,1},{3,0},{4,7},{5,6},{6,5},{7,4},{8,11},{9,10},{10,... | collective-permute-start | bytes 147464 | tf_op jit(solution)/shard_map/ppermute | solution.py:88
  8.9 0.6 %collective-permute-start = (bf16[1,64,384]{2,1,0:T(8,128)(2,1)S(1)}, bf16[1,64,384]{2,1,0:T(8,128)(2,1)S(1)}, u32[]{:S(2)}, u32[]{:S(2)}) collective-permute-start(bf16[1,64,384]{2,1,0:T(8,128)(2,1)S(1)} %get-tuple-element.37), channel_id=1, source_target_pairs={{0,1},{1,0},{2,3},{3,2},{4,5},{5,4},{6,7},{7,6},{8,9},{9,8},{10,11... | collective-permute-start | bytes 147464 | tf_op jit(solution)/shard_map/ppermute | solution.py:88
  9.6 3.6 %collective-permute-start.7 = (bf16[1,128,128]{2,1,0:T(8,128)(2,1)S(1)}, bf16[1,128,128]{2,1,0:T(8,128)(2,1)S(1)}, u32[]{:S(2)}, u32[]{:S(2)}) collective-permute-start(bf16[1,128,128]{2,1,0:T(8,128)(2,1)S(1)} %get-tuple-element.42), channel_id=1, source_target_pairs={{0,4},{1,5},{2,6},{3,7},{8,12},{9,13},{10,14},{11,15},{16,20},{17,... | collective-permute-start | bytes 98312 | tf_op jit(solution)/shard_map/ppermute | solution.py:60
  13.7 1.1 %collective-permute-done.7 = bf16[1,128,128]{2,1,0:T(8,128)(2,1)S(1)} collective-permute-done((bf16[1,128,128]{2,1,0:T(8,128)(2,1)S(1)}, bf16[1,128,128]{2,1,0:T(8,128)(2,1)S(1)}, u32[]{:S(2)}, u32[]{:S(2)}) %collective-permute-start.7) | collective-permute-done | bytes 32800 | tf_op jit(solution)/shard_map/ppermute | solution.py:60
  14.9 0.6 %gather_fusion.1 = bf16[4,64,384]{2,1,0:T(8,128)(2,1)S(1)} fusion(bf16[4,64,384]{2,1,0:T(8,128)(2,1)S(1)} %maximum_bitcast_fusion, s32[1024]{0:T(1024)S(1)} %pad_clamp_fusion.1), kind=kCustom, calls=%fused_computation.clone | custom fusion | bytes 393232 | tf_op jit(solution)/shard_map/jit(_take)/gather | solution.py:90
  15.6 3.7 %collective-permute-start.5 = (bf16[1,64,384]{2,1,0:T(8,128)(2,1)S(1)}, bf16[1,64,384]{2,1,0:T(8,128)(2,1)S(1)}, u32[]{:S(2)}, u32[]{:S(2)}) collective-permute-start(bf16[1,64,384]{2,1,0:T(8,128)(2,1)S(1)} %fusion.109), channel_id=1, source_target_pairs={{0,3},{1,2},{2,1},{3,0},{4,7},{5,6},{6,5},{7,4},{8,11},{9,10},{10,... | collective-permute-start | bytes 147464 | tf_op jit(solution)/shard_map/ppermute | solution.py:98
  19.3 0.8 %collective-permute-start.3 = (bf16[1,64,384]{2,1,0:T(8,128)(2,1)S(1)}, bf16[1,64,384]{2,1,0:T(8,128)(2,1)S(1)}, u32[]{:S(2)}, u32[]{:S(2)}) collective-permute-start(bf16[1,64,384]{2,1,0:T(8,128)(2,1)S(1)} %fusion.109), channel_id=1, source_target_pairs={{0,1},{1,0},{2,3},{3,2},{4,5},{5,4},{6,7},{7,6},{8,9},{9,8},{10,11... | collective-permute-start | bytes 147464 | tf_op jit(solution)/shard_map/ppermute | solution.py:98
  20.1 1.6 %collective-permute-done.5 = bf16[1,64,384]{2,1,0:T(8,128)(2,1)S(1)} collective-permute-done((bf16[1,64,384]{2,1,0:T(8,128)(2,1)S(1)}, bf16[1,64,384]{2,1,0:T(8,128)(2,1)S(1)}, u32[]{:S(2)}, u32[]{:S(2)}) %collective-permute-start.5) | collective-permute-done | bytes 49184 | tf_op jit(solution)/shard_map/ppermute | solution.py:98
  21.7 2.6 %collective-permute-done.4 = bf16[1,64,384]{2,1,0:T(8,128)(2,1)S(1)} collective-permute-done((bf16[1,64,384]{2,1,0:T(8,128)(2,1)S(1)}, bf16[1,64,384]{2,1,0:T(8,128)(2,1)S(1)}, u32[]{:S(2)}, u32[]{:S(2)}) %collective-permute-start.4) | collective-permute-done | bytes 49184 | tf_op jit(solution)/shard_map/ppermute | solution.py:98
  24.3 0.6 %gather_fusion.2 = bf16[4,64,384]{2,1,0:T(8,128)(2,1)S(1)} fusion(bf16[4,64,384]{2,1,0:T(8,128)(2,1)S(1)} %maximum_bitcast_fusion.1, s32[1024]{0:T(1024)S(1)} %pad_clamp_fusion.1), kind=kCustom, calls=%fused_computation.1.clone | custom fusion | bytes 393232 | tf_op jit(solution)/shard_map/jit(_take)/gather | solution.py:99
  25.1 2.4 %collective-permute-start.6 = (bf16[1,136,384]{2,1,0:T(8,128)(2,1)S(1)}, bf16[1,136,384]{2,1,0:T(8,128)(2,1)S(1)}, u32[]{:S(2)}, u32[]{:S(2)}) collective-permute-start(bf16[1,136,384]{2,1,0:T(8,128)(2,1)S(1)} %pad_maximum_fusion.1), channel_id=1, source_target_pairs={{0,4},{4,0},{1,5},{5,1},{2,6},{6,2},{3,7},{7,3},{8,12},{12,8},{9,1... | collective-permute-start | bytes 313352 | tf_op jit(solution)/shard_map/ppermute | solution.py:119
  27.6 2.5 %collective-permute-done.6 = bf16[1,136,384]{2,1,0:T(8,128)(2,1)S(1)} collective-permute-done((bf16[1,136,384]{2,1,0:T(8,128)(2,1)S(1)}, bf16[1,136,384]{2,1,0:T(8,128)(2,1)S(1)}, u32[]{:S(2)}, u32[]{:S(2)}) %collective-permute-start.6) | collective-permute-done | bytes 104480 | tf_op jit(solution)/shard_map/ppermute | solution.py:119
  30.3 0.5 %fusion.5 = bf16[128,384]{1,0:T(8,128)(2,1)S(1)} fusion(bf16[256,384]{1,0:T(8,128)(2,1)S(1)} %get-tuple-element.41, bf16[1,128,256]{2,1,0:T(8,128)(2,1)S(1)} %copy-done.3, bf16[1,256,384]{2,1,0:T(8,128)(2,1)S(1)} %bitcast.171, s32[256]{0:T(256)S(1)} %bitcast.188, s32[128]{0:T(128)S(1)} %bitcast.184, pred[128]{0:T(512)(128)(4,1)S(1)} %broadcast_compare_fusion.1), kind=kOutput, calls=%fused_computation.14 | convolution fusion | flops 51052544 | bytes 657408 | tf_op jit(solution)/shard_map/bij,bjp->bip/dot_general | solution.py:177
  31.4 0.5 %fusion.6 = bf16[128,384]{1,0:T(8,128)(2,1)S(1)} fusion(bf16[256,384]{1,0:T(8,128)(2,1)S(1)} %get-tuple-element.40, bf16[1,256,128]{2,1,0:T(8,128)(2,1)S(1)} %select_dynamic-update-slice_fusion, bf16[1,256,384]{2,1,0:T(8,128)(2,1)S(1)} %bitcast.172, s32[128]{0:T(128)S(1)} %bitcast.187, s32[256]{0:T(256)S(1)} %bitcast.190, ...), kind=kOutput, calls=%fused_computation.15 | convolution fusion | flops 51052544 | bytes 657408 | tf_op jit(solution)/shard_map/bij,bip->bjp/dot_general | solution.py:188
  33.1 0.8 %collective-permute-done.8 = bf16[2,384,192]{1,2,0:T(8,128)(2,1)S(1)} collective-permute-done((bf16[2,384,192]{1,2,0:T(8,128)(2,1)S(1)}, bf16[2,384,192]{1,2,0:T(8,128)(2,1)S(1)}, u32[]{:S(2)}, u32[]{:S(2)}) %collective-permute-start.8) | collective-permute-done | bytes 294944 | tf_op jit(solution)/shard_map/ppermute | solution.py:212
  34.4 3.0 %collective-permute-start.11 = (bf16[2,192,192]{1,2,0:T(8,128)(2,1)S(1)}, bf16[2,192,192]{1,2,0:T(8,128)(2,1)S(1)}, u32[]{:S(2)}, u32[]{:S(2)}) collective-permute-start(bf16[2,192,192]{1,2,0:T(8,128)(2,1)S(1)} %get-tuple-element.31), channel_id=1, source_target_pairs={{0,20},{4,16},{8,28},{12,24},{16,4},{20,0},{24,12},{28,8},{1,21},{... | collective-permute-start | bytes 442376 | tf_op jit(solution)/shard_map/ppermute | solution.py:227
  37.4 0.5 %collective-permute-start.10 = (bf16[2,192,192]{1,2,0:T(8,128)(2,1)S(1)}, bf16[2,192,192]{1,2,0:T(8,128)(2,1)S(1)}, u32[]{:S(2)}, u32[]{:S(2)}) collective-permute-start(bf16[2,192,192]{1,2,0:T(8,128)(2,1)S(1)} %get-tuple-element.32), channel_id=1, source_target_pairs={{0,16},{4,20},{8,24},{12,28},{16,0},{20,4},{24,8},{28,12},{1,17},{... | collective-permute-start | bytes 442376 | tf_op jit(solution)/shard_map/ppermute | solution.py:227
  38.3 4.9 %collective-permute-done.11 = bf16[2,192,192]{1,2,0:T(8,128)(2,1)S(1)} collective-permute-done((bf16[2,192,192]{1,2,0:T(8,128)(2,1)S(1)}, bf16[2,192,192]{1,2,0:T(8,128)(2,1)S(1)}, u32[]{:S(2)}, u32[]{:S(2)}) %collective-permute-start.11) | collective-permute-done | bytes 147488 | tf_op jit(solution)/shard_map/ppermute | solution.py:227
  43.1 4.0 %collective-permute-done.10 = bf16[2,192,192]{1,2,0:T(8,128)(2,1)S(1)} collective-permute-done((bf16[2,192,192]{1,2,0:T(8,128)(2,1)S(1)}, bf16[2,192,192]{1,2,0:T(8,128)(2,1)S(1)}, u32[]{:S(2)}, u32[]{:S(2)}) %collective-permute-start.10) | collective-permute-done | bytes 147488 | tf_op jit(solution)/shard_map/ppermute | solution.py:227
  47.6 0.6 %gather_fusion = bf16[4,2,192,192]{3,2,1,0:T(8,128)(2,1)S(1)} fusion(bf16[4,2,192,192]{3,2,1,0:T(8,128)(2,1)S(1)} %copy.13, s32[1024]{0:T(1024)S(1)} %pad_clamp_fusion), kind=kCustom, calls=%fused_computation.2 | custom fusion | bytes 1179664 | tf_op jit(solution)/shard_map/jit(_take)/gather | solution.py:228
  49.0 1.1 %fusion.2 = bf16[1,512,384]{2,1,0:T(8,128)(2,1)} fusion(f32[512,384]{1,0:T(8,128)S(1)} %convolution_add_fusion.1, f32[512,384]{1,0:T(8,128)S(1)} %fusion.14, s32[128]{0:T(128)S(1)} %get-tuple-element.44, f32[128,384]{1,0:T(8,128)S(1)} %fusion.92), kind=kOutput, calls=%fused_computation.9 | convolution fusion | flops 51183616 | bytes 2163200 | tf_op jit(solution)/shard_map/bnr,bnc->brc/dot_general | solution.py:26
  50.6 0.9 %slice_bitcast_fusion = (f32[384,192]{0,1:T(8,128)}, f32[384,192]{0,1:T(8,128)}) fusion(f32[2,384,192]{1,2,0:T(8,128)S(1)} %fusion.9), kind=kLoop, calls=%fused_computation.40 | loop fusion | bytes 1179648 | tf_op jit(solution)/shard_map/squeeze | solution.py:249
  (77 shorter events, 6.8 us)
Async XLA Ops:
  0.6 1.0 %copy-start = (bf16[1,512,384]{2,1,0:T(8,128)(2,1)S(1)}, bf16[1,512,384]{2,1,0:T(8,128)(2,1)}, u32[]{:S(2)}) copy-start(bf16[1,512,384]{2,1,0:T(8,128)(2,1)} %param.12) | copy-start | bytes 1179652
  0.7 0.7 %copy-start.4 = (s32[1,128]{1,0:T(1,128)S(1)}, s32[1,128]{1,0:T(1,128)}, u32[]{:S(2)}) copy-start(s32[1,128]{1,0:T(1,128)} %param.13) | copy-start | bytes 1540
  0.7 0.7 %copy-start.5 = (s32[1,128]{1,0:T(1,128)S(1)}, s32[1,128]{1,0:T(1,128)}, u32[]{:S(2)}) copy-start(s32[1,128]{1,0:T(1,128)} %param.14) | copy-start | bytes 1540
  1.9 1.0 %copy-start.1 = (bf16[384,384]{1,0:T(8,128)(2,1)S(1)}, bf16[384,384]{1,0:T(8,128)(2,1)}, u32[]{:S(2)}) copy-start(bf16[384,384]{1,0:T(8,128)(2,1)} %param.16) | copy-start | bytes 884740
  2.2 1.0 %copy-start.2 = (bf16[384,384]{1,0:T(8,128)(2,1)S(1)}, bf16[384,384]{1,0:T(8,128)(2,1)}, u32[]{:S(2)}) copy-start(bf16[384,384]{1,0:T(8,128)(2,1)} %param.17) | copy-start | bytes 884740
  3.8 5.8 %copy-start.3 = (bf16[1,128,256]{2,1,0:T(8,128)(2,1)S(1)}, bf16[1,128,256]{2,1,0:T(8,128)(2,1)}, u32[]{:S(2)}) copy-start(bf16[1,128,256]{2,1,0:T(8,128)(2,1)} %param.15) | copy-start | bytes 196612
  3.8 11.0 %collective-permute-start.2 = (bf16[1,64,384]{2,1,0:T(8,128)(2,1)S(1)}, bf16[1,64,384]{2,1,0:T(8,128)(2,1)S(1)}, u32[]{:S(2)}, u32[]{:S(2)}) collective-permute-start(bf16[1,64,384]{2,1,0:T(8,128)(2,1)S(1)} %get-tuple-element.39), channel_id=1, source_target_pairs={{0,3},{1,2},{2,1},{3,0},{4,7},{5,6},{6,5},{7,4},{8,11},{9,10},{10,... | collective-permute-start | bytes 147464 | tf_op jit(solution)/shard_map/ppermute | solution.py:88
  8.9 5.9 %collective-permute-start.1 = (bf16[1,64,384]{2,1,0:T(8,128)(2,1)S(1)}, bf16[1,64,384]{2,1,0:T(8,128)(2,1)S(1)}, u32[]{:S(2)}, u32[]{:S(2)}) collective-permute-start(bf16[1,64,384]{2,1,0:T(8,128)(2,1)S(1)} %get-tuple-element.38), channel_id=1, source_target_pairs={{0,2},{1,3},{2,0},{3,1},{4,6},{5,7},{6,4},{7,5},{8,10},{9,11},{10,... | collective-permute-start | bytes 147464 | tf_op jit(solution)/shard_map/ppermute | solution.py:88
  8.9 5.9 %collective-permute-start = (bf16[1,64,384]{2,1,0:T(8,128)(2,1)S(1)}, bf16[1,64,384]{2,1,0:T(8,128)(2,1)S(1)}, u32[]{:S(2)}, u32[]{:S(2)}) collective-permute-start(bf16[1,64,384]{2,1,0:T(8,128)(2,1)S(1)} %get-tuple-element.37), channel_id=1, source_target_pairs={{0,1},{1,0},{2,3},{3,2},{4,5},{5,4},{6,7},{7,6},{8,9},{9,8},{10,11... | collective-permute-start | bytes 147464 | tf_op jit(solution)/shard_map/ppermute | solution.py:88
  9.6 5.2 %collective-permute-start.7 = (bf16[1,128,128]{2,1,0:T(8,128)(2,1)S(1)}, bf16[1,128,128]{2,1,0:T(8,128)(2,1)S(1)}, u32[]{:S(2)}, u32[]{:S(2)}) collective-permute-start(bf16[1,128,128]{2,1,0:T(8,128)(2,1)S(1)} %get-tuple-element.42), channel_id=1, source_target_pairs={{0,4},{1,5},{2,6},{3,7},{8,12},{9,13},{10,14},{11,15},{16,20},{17,... | collective-permute-start | bytes 98312 | tf_op jit(solution)/shard_map/ppermute | solution.py:60
  15.6 6.1 %collective-permute-start.5 = (bf16[1,64,384]{2,1,0:T(8,128)(2,1)S(1)}, bf16[1,64,384]{2,1,0:T(8,128)(2,1)S(1)}, u32[]{:S(2)}, u32[]{:S(2)}) collective-permute-start(bf16[1,64,384]{2,1,0:T(8,128)(2,1)S(1)} %fusion.109), channel_id=1, source_target_pairs={{0,3},{1,2},{2,1},{3,0},{4,7},{5,6},{6,5},{7,4},{8,11},{9,10},{10,... | collective-permute-start | bytes 147464 | tf_op jit(solution)/shard_map/ppermute | solution.py:98
  19.3 5.0 %collective-permute-start.4 = (bf16[1,64,384]{2,1,0:T(8,128)(2,1)S(1)}, bf16[1,64,384]{2,1,0:T(8,128)(2,1)S(1)}, u32[]{:S(2)}, u32[]{:S(2)}) collective-permute-start(bf16[1,64,384]{2,1,0:T(8,128)(2,1)S(1)} %fusion.109), channel_id=1, source_target_pairs={{0,2},{1,3},{2,0},{3,1},{4,6},{5,7},{6,4},{7,5},{8,10},{9,11},{10,... | collective-permute-start | bytes 147464 | tf_op jit(solution)/shard_map/ppermute | solution.py:98
  19.3 5.0 %collective-permute-start.3 = (bf16[1,64,384]{2,1,0:T(8,128)(2,1)S(1)}, bf16[1,64,384]{2,1,0:T(8,128)(2,1)S(1)}, u32[]{:S(2)}, u32[]{:S(2)}) collective-permute-start(bf16[1,64,384]{2,1,0:T(8,128)(2,1)S(1)} %fusion.109), channel_id=1, source_target_pairs={{0,1},{1,0},{2,3},{3,2},{4,5},{5,4},{6,7},{7,6},{8,9},{9,8},{10,11... | collective-permute-start | bytes 147464 | tf_op jit(solution)/shard_map/ppermute | solution.py:98
  25.1 5.0 %collective-permute-start.6 = (bf16[1,136,384]{2,1,0:T(8,128)(2,1)S(1)}, bf16[1,136,384]{2,1,0:T(8,128)(2,1)S(1)}, u32[]{:S(2)}, u32[]{:S(2)}) collective-permute-start(bf16[1,136,384]{2,1,0:T(8,128)(2,1)S(1)} %pad_maximum_fusion.1), channel_id=1, source_target_pairs={{0,4},{4,0},{1,5},{5,1},{2,6},{6,2},{3,7},{7,3},{8,12},{12,8},{9,1... | collective-permute-start | bytes 313352 | tf_op jit(solution)/shard_map/ppermute | solution.py:119
  32.3 1.6 %collective-permute-start.8 = (bf16[2,384,192]{1,2,0:T(8,128)(2,1)S(1)}, bf16[2,384,192]{1,2,0:T(8,128)(2,1)S(1)}, u32[]{:S(2)}, u32[]{:S(2)}) collective-permute-start(bf16[2,384,192]{1,2,0:T(8,128)(2,1)S(1)} %fusion.12), channel_id=1, source_target_pairs={{0,8},{8,0},{16,24},{24,16},{1,9},{9,1},{17,25},{25,17},{2,10},{10... | collective-permute-start | bytes 884744 | tf_op jit(solution)/shard_map/ppermute | solution.py:212
  34.4 8.7 %collective-permute-start.11 = (bf16[2,192,192]{1,2,0:T(8,128)(2,1)S(1)}, bf16[2,192,192]{1,2,0:T(8,128)(2,1)S(1)}, u32[]{:S(2)}, u32[]{:S(2)}) collective-permute-start(bf16[2,192,192]{1,2,0:T(8,128)(2,1)S(1)} %get-tuple-element.31), channel_id=1, source_target_pairs={{0,20},{4,16},{8,28},{12,24},{16,4},{20,0},{24,12},{28,8},{1,21},{... | collective-permute-start | bytes 442376 | tf_op jit(solution)/shard_map/ppermute | solution.py:227
  37.4 9.7 %collective-permute-start.10 = (bf16[2,192,192]{1,2,0:T(8,128)(2,1)S(1)}, bf16[2,192,192]{1,2,0:T(8,128)(2,1)S(1)}, u32[]{:S(2)}, u32[]{:S(2)}) collective-permute-start(bf16[2,192,192]{1,2,0:T(8,128)(2,1)S(1)} %get-tuple-element.32), channel_id=1, source_target_pairs={{0,16},{4,20},{8,24},{12,28},{16,0},{20,4},{24,8},{28,12},{1,17},{... | collective-permute-start | bytes 442376 | tf_op jit(solution)/shard_map/ppermute | solution.py:227
  37.9 9.2 %collective-permute-start.9 = (bf16[2,192,192]{1,2,0:T(8,128)(2,1)S(1)}, bf16[2,192,192]{1,2,0:T(8,128)(2,1)S(1)}, u32[]{:S(2)}, u32[]{:S(2)}) collective-permute-start(bf16[2,192,192]{1,2,0:T(8,128)(2,1)S(1)} %get-tuple-element.33), channel_id=1, source_target_pairs={{0,4},{4,0},{8,12},{12,8},{16,20},{20,16},{24,28},{28,24},{1,5},{5... | collective-permute-start | bytes 442376 | tf_op jit(solution)/shard_map/ppermute | solution.py:227
  48.5 1.8 %collective-permute-start.12 = (f32[2,192,192]{2,1,0:T(8,128)S(1)}, f32[2,192,192]{2,1,0:T(8,128)S(1)}, u32[]{:S(2)}, u32[]{:S(2)}) collective-permute-start(f32[2,192,192]{2,1,0:T(8,128)S(1)} %add_bitcast_fusion), channel_id=1, source_target_pairs={{0,8},{8,0},{16,24},{24,16},{1,9},{9,1},{17,25},{25,17},{2,10},{10... | collective-permute-start | bytes 884744 | tf_op jit(solution)/shard_map/ppermute | solution.py:244

commit v11 on v8

--- a/solution.py
+++ b/solution.py
@@ -48,19 +48,6 @@
 
     head = lax.axis_index("head")
     me = slab * n_head + head
-
-    target_col = jnp.zeros((batch, sites, slab_sites), target.dtype)
-    own_cols = lax.dynamic_slice_in_dim(target, slab * slab_sites, slab_sites, 2)
-    target_col = lax.dynamic_update_slice_in_dim(target_col, own_cols, slab * slab_sites, 1)
-    for k in range(1, n_seq):
-        outgoing = lax.dynamic_slice_in_dim(
-            target, jnp.minimum(slab + k, n_seq - 1) * slab_sites, slab_sites, 2
-        )
-        perm = [(i, i + k) for i in range(n_seq - k)]
-        arrived = lax.ppermute(outgoing, "seq", perm)
-        source = jnp.maximum(slab - k, 0)
-        placed = lax.dynamic_update_slice_in_dim(target_col, arrived, source * slab_sites, 1)
-        target_col = jnp.where(slab >= k, placed, target_col)
 
     donor_match = site_match(donor_pos, slab_rows, slab).astype(jnp.bfloat16)
     acceptor_match = site_match(acceptor_pos, slab_rows, slab).astype(jnp.bfloat16)
@@ -137,10 +124,12 @@
             )
             held = kept.astype(jnp.bfloat16)
             own = lax.dynamic_slice_in_dim(held, slab * part, part, 0).astype(jnp.float32)
-            outgoing = lax.dynamic_slice_in_dim(held, (1 - slab) * part, part, 0)
-            return own, lax.ppermute(outgoing, "seq", [(0, 1), (1, 0)]).astype(jnp.float32)
-
-        own_early, from_early = to_seq_partner(rows_early, grad_early)
+            return own, lax.dynamic_slice_in_dim(held, (1 - slab) * part, part, 0)
+
+        def from_seq_partner(outgoing):
+            return lax.ppermute(outgoing, "seq", [(0, 1), (1, 0)]).astype(jnp.float32)
+
+        own_early, out_early = to_seq_partner(rows_early, grad_early)
 
     assert slab_sites <= width
     flags = jnp.zeros((batch, 8, width), jnp.bfloat16)
@@ -154,14 +143,33 @@
     )
     donor_ok_all = jnp.zeros((batch, sites), jnp.bool_)
     acceptor_ok_all = jnp.zeros((batch, sites), jnp.bool_)
+    target_col = jnp.zeros((batch, sites, slab_sites), target.dtype)
+    own_cols = lax.dynamic_slice_in_dim(target, slab * slab_sites, slab_sites, 2)
+    target_col = lax.dynamic_update_slice_in_dim(target_col, own_cols, slab * slab_sites, 1)
     for k in range(1, n_seq):
         sent = jnp.where(slab + k < n_seq, own_donor, own_acceptor)
+        target_block = lax.dynamic_slice_in_dim(
+            target, jnp.minimum(slab + k, n_seq - 1) * slab_sites, slab_sites, 2
+        ).reshape(batch, slab_sites * slab_sites)
+        target_rows = -(-(slab_sites * slab_sites) // width)
+        target_block = jnp.pad(target_block, ((0, 0), (0, target_rows * width - slab_sites * slab_sites)))
+        payload = jnp.concatenate(
+            [sent, flags, target_block.reshape(batch, target_rows, width).astype(jnp.bfloat16)], axis=1
+        )
         perm = [(i, (i + k) % n_seq) for i in range(n_seq)]
-        arrived = lax.ppermute(jnp.concatenate([sent, flags], axis=1), "seq", perm)
-        if n_seq == 2:
-            arrived, from_early = lax.optimization_barrier((arrived, from_early))
+        arrived = lax.ppermute(payload, "seq", perm)
         source = (slab - k) % n_seq
         earlier = slab >= k
+        target_in = (
+            arrived[:, slab_sites + 8 :]
+            .reshape(batch, target_rows * width)[:, : slab_sites * slab_sites]
+            .reshape(batch, slab_sites, slab_sites)
+        )
+        target_col = jnp.where(
+            earlier,
+            lax.dynamic_update_slice_in_dim(target_col, target_in, source * slab_sites, 1),
+            target_col,
+        )
         feat_in = arrived[:, :slab_sites]
         donor_feat_all = jnp.where(
             earlier,
@@ -185,6 +193,10 @@
             acceptor_ok_all,
             lax.dynamic_update_slice_in_dim(acceptor_ok_all, acceptor_in, source * slab_sites, 1),
         )
+
+    if n_seq == 2:
+        out_early, arrived = lax.optimization_barrier((out_early, arrived))
+        from_early = from_seq_partner(out_early)
 
     site_slab = jnp.arange(sites, dtype=jnp.int32) // slab_sites
     big = jnp.int32(1 << 30)
@@ -242,7 +254,8 @@
         donor_grad = jnp.where(first, grad_late, grad_early)
         acceptor_grad = jnp.where(first, grad_early, grad_late)
 
-        own_late, from_late = to_seq_partner(rows_late, grad_late)
+        own_late, out_late = to_seq_partner(rows_late, grad_late)
+        from_late = from_seq_partner(out_late)
         sum_early = own_early + from_late
         sum_late = own_late + from_early
         mine = jnp.stack(

time: 54.3 us -> 48.7 us (0.90)
  waiting for transfers between devices: 23.7 us -> 18.5 us
  starting transfers between devices: 16.8 us -> 16 us
    ppermute x4 -> x3, waiting for transfers between devices: 9.23 us -> 6.67 us  [the longest x2 4.37 us: from_seq_partner(): return lax.ppermute(outgoing, 'seq', [(0, 1), (1, 0)]).astype(jnp.float32)]
    ppermute x2, waiting for transfers between devices: 2.3 us -> 0.01 us  [to_seq_partner(): lax.ppermute(outgoing, 'dp', [(i, i ^ 1) for i in range(n_dp)])]
    ppermute x4 -> x3, starting transfers between devices: 6.12 us -> 4.03 us  [the longest x2 2.45 us: from_seq_partner(): return lax.ppermute(outgoing, 'seq', [(0, 1), (1, 0)]).astype(jnp.float32)]
    ppermute x3, waiting for transfers between devices: 5.31 us -> 3.67 us  [shards(): lax.ppermute(outgoing, 'head', [(i, i ^ k) for i in range(n_head)])]
    ppermute x3, starting transfers between devices: 4.45 us -> 5.76 us  [shards(): lax.ppermute(outgoing, 'head', [(i, i ^ k) for i in range(n_head)])]
    ppermute x3, waiting for transfers between devices: 2.26 us -> 3.12 us  [shards(): lax.ppermute(feat_quarter, 'head', [(i, i ^ k) for i in range(n_head)])]
    unnamed x14 -> x17, local copies, waits for them, and re-layouts: 2.31 us -> 2.28 us
  transfers between devices with their start and end apart: 14 -> 13, of which waited for: 10 -> 9; matrix products, arithmetic and copies ran while one was open for 8% -> 14% of each run, Pallas kernels for 0% -> 0%
where the time goes in v11:
time: 48.7 us; the launch traced here: 48.5 us
  waiting for transfers between devices  18.5 us (38%)
  starting transfers between devices  16 us (33%)
  matrix products  5.91 us (12%)
  local copies, waits for them, and re-layouts  5.29 us (11%)
  other arithmetic  1.6 us (3%)
  between operations  1.23 us (3%)
    ppermute x3, starting transfers between devices, shards(): lax.ppermute(outgoing, 'head', [(i, i ^ k) for i in range(n_head)])  5.76 us
    ppermute x1, waiting for transfers between devices, shards(): lax.ppermute(held, 'dp', perm).astype(jnp.float32)  4.8 us
    ppermute x3, starting transfers between devices, shards(): lax.ppermute(feat_quarter, 'head', [(i, i ^ k) for i in range(n_head)])  4.45 us
    ppermute x2, waiting for transfers between devices, from_seq_partner(): return lax.ppermute(outgoing, 'seq', [(0, 1), (1, 0)]).astype(jnp.float32)  4.37 us
    ppermute x3, waiting for transfers between devices, shards(): lax.ppermute(outgoing, 'head', [(i, i ^ k) for i in range(n_head)])  3.67 us
    ppermute x3, waiting for transfers between devices, shards(): lax.ppermute(feat_quarter, 'head', [(i, i ^ k) for i in range(n_head)])  3.12 us
    ppermute x2, starting transfers between devices, from_seq_partner(): return lax.ppermute(outgoing, 'seq', [(0, 1), (1, 0)]).astype(jnp.float32)  2.45 us
    ppermute x1, waiting for transfers between devices, shards(): arrived = lax.ppermute(payload, 'seq', perm)  2.31 us
  transfers between devices with their start and end apart: 13, of which 9 were waited for; matrix products, arithmetic and copies ran while one was open for 14% of the time, Pallas kernels for 0%

profile of v11, /device:TPU:0, one launch (start us, length us, event | category | flops | bytes accessed | tf_op | source)
XLA Modules:
  0.0 48.5 jit_solution(6586742491531346958)
XLA Ops:
  0.7 0.7 %copy-done.5 = s32[1,128]{1,0:T(1,128)S(1)} copy-done((s32[1,128]{1,0:T(1,128)S(1)}, s32[1,128]{1,0:T(1,128)}, u32[]{:S(2)}) %copy-start.5) | copy-done | bytes 536
  1.4 0.7 %copy-done.4 = s32[1,128]{1,0:T(1,128)S(1)} copy-done((s32[1,128]{1,0:T(1,128)S(1)}, s32[1,128]{1,0:T(1,128)}, u32[]{:S(2)}) %copy-start.4) | copy-done | bytes 536
  2.6 0.7 %copy-done.1 = bf16[384,384]{1,0:T(8,128)(2,1)S(1)} copy-done((bf16[384,384]{1,0:T(8,128)(2,1)S(1)}, bf16[384,384]{1,0:T(8,128)(2,1)}, u32[]{:S(2)}) %copy-start.1) | copy-done | bytes 294936
  4.2 5.1 %collective-permute-start.2 = (bf16[1,64,384]{2,1,0:T(8,128)(2,1)S(1)}, bf16[1,64,384]{2,1,0:T(8,128)(2,1)S(1)}, u32[]{:S(2)}, u32[]{:S(2)}) collective-permute-start(bf16[1,64,384]{2,1,0:T(8,128)(2,1)S(1)} %get-tuple-element.39), channel_id=1, source_target_pairs={{0,3},{1,2},{2,1},{3,0},{4,7},{5,6},{6,5},{7,4},{8,11},{9,10},{10,... | collective-permute-start | bytes 147464 | tf_op jit(solution)/shard_map/ppermute | solution.py:75
  9.3 0.6 %collective-permute-start = (bf16[1,64,384]{2,1,0:T(8,128)(2,1)S(1)}, bf16[1,64,384]{2,1,0:T(8,128)(2,1)S(1)}, u32[]{:S(2)}, u32[]{:S(2)}) collective-permute-start(bf16[1,64,384]{2,1,0:T(8,128)(2,1)S(1)} %get-tuple-element.37), channel_id=1, source_target_pairs={{0,1},{1,0},{2,3},{3,2},{4,5},{5,4},{6,7},{7,6},{8,9},{9,8},{10,11... | collective-permute-start | bytes 147464 | tf_op jit(solution)/shard_map/ppermute | solution.py:75
  10.6 0.9 %collective-permute-done.2 = bf16[1,64,384]{2,1,0:T(8,128)(2,1)S(1)} collective-permute-done((bf16[1,64,384]{2,1,0:T(8,128)(2,1)S(1)}, bf16[1,64,384]{2,1,0:T(8,128)(2,1)S(1)}, u32[]{:S(2)}, u32[]{:S(2)}) %collective-permute-start.2) | collective-permute-done | bytes 49184 | tf_op jit(solution)/shard_map/ppermute | solution.py:75
  11.5 2.8 %collective-permute-done.1 = bf16[1,64,384]{2,1,0:T(8,128)(2,1)S(1)} collective-permute-done((bf16[1,64,384]{2,1,0:T(8,128)(2,1)S(1)}, bf16[1,64,384]{2,1,0:T(8,128)(2,1)S(1)}, u32[]{:S(2)}, u32[]{:S(2)}) %collective-permute-start.1) | collective-permute-done | bytes 49184 | tf_op jit(solution)/shard_map/ppermute | solution.py:75
  14.3 0.6 %gather_fusion = bf16[4,64,384]{2,1,0:T(8,128)(2,1)S(1)} fusion(bf16[4,64,384]{2,1,0:T(8,128)(2,1)S(1)} %maximum_bitcast_fusion, s32[1024]{0:T(1024)S(1)} %pad_clamp_fusion), kind=kCustom, calls=%fused_computation.clone | custom fusion | bytes 393232 | tf_op jit(solution)/shard_map/jit(_take)/gather | solution.py:77
  15.1 2.2 %collective-permute-start.5 = (bf16[1,64,384]{2,1,0:T(8,128)(2,1)S(1)}, bf16[1,64,384]{2,1,0:T(8,128)(2,1)S(1)}, u32[]{:S(2)}, u32[]{:S(2)}) collective-permute-start(bf16[1,64,384]{2,1,0:T(8,128)(2,1)S(1)} %fusion.143), channel_id=1, source_target_pairs={{0,3},{1,2},{2,1},{3,0},{4,7},{5,6},{6,5},{7,4},{8,11},{9,10},{10,... | collective-permute-start | bytes 147464 | tf_op jit(solution)/shard_map/ppermute | solution.py:85
  17.2 2.3 %collective-permute-start.3 = (bf16[1,64,384]{2,1,0:T(8,128)(2,1)S(1)}, bf16[1,64,384]{2,1,0:T(8,128)(2,1)S(1)}, u32[]{:S(2)}, u32[]{:S(2)}) collective-permute-start(bf16[1,64,384]{2,1,0:T(8,128)(2,1)S(1)} %fusion.143), channel_id=1, source_target_pairs={{0,1},{1,0},{2,3},{3,2},{4,5},{5,4},{6,7},{7,6},{8,9},{9,8},{10,11... | collective-permute-start | bytes 147464 | tf_op jit(solution)/shard_map/ppermute | solution.py:85
  19.5 1.7 %collective-permute-done.5 = bf16[1,64,384]{2,1,0:T(8,128)(2,1)S(1)} collective-permute-done((bf16[1,64,384]{2,1,0:T(8,128)(2,1)S(1)}, bf16[1,64,384]{2,1,0:T(8,128)(2,1)S(1)}, u32[]{:S(2)}, u32[]{:S(2)}) %collective-permute-start.5) | collective-permute-done | bytes 49184 | tf_op jit(solution)/shard_map/ppermute | solution.py:85
  21.3 1.4 %collective-permute-done.4 = bf16[1,64,384]{2,1,0:T(8,128)(2,1)S(1)} collective-permute-done((bf16[1,64,384]{2,1,0:T(8,128)(2,1)S(1)}, bf16[1,64,384]{2,1,0:T(8,128)(2,1)S(1)}, u32[]{:S(2)}, u32[]{:S(2)}) %collective-permute-start.4) | collective-permute-done | bytes 49184 | tf_op jit(solution)/shard_map/ppermute | solution.py:85
  22.7 0.6 %gather_fusion.1 = bf16[4,64,384]{2,1,0:T(8,128)(2,1)S(1)} fusion(bf16[4,64,384]{2,1,0:T(8,128)(2,1)S(1)} %maximum_bitcast_fusion.1, s32[1024]{0:T(1024)S(1)} %pad_clamp_fusion), kind=kCustom, calls=%fused_computation.1.clone | custom fusion | bytes 393232 | tf_op jit(solution)/shard_map/jit(_take)/gather | solution.py:86
  23.5 1.6 %collective-permute-start.6 = (bf16[1,179,384]{2,1,0:T(8,128)(2,1)S(1)}, bf16[1,179,384]{2,1,0:T(8,128)(2,1)S(1)}, u32[]{:S(2)}, u32[]{:S(2)}) collective-permute-start(bf16[1,179,384]{2,1,0:T(8,128)(2,1)S(1)} %pad_maximum_fusion.1), channel_id=1, source_target_pairs={{0,4},{4,0},{1,5},{5,1},{2,6},{6,2},{3,7},{7,3},{8,12},{12,8},{9,1... | collective-permute-start | bytes 412424 | tf_op jit(solution)/shard_map/ppermute | solution.py:160
  26.3 2.3 %collective-permute-done.6 = bf16[1,179,384]{2,1,0:T(8,128)(2,1)S(1)} collective-permute-done((bf16[1,179,384]{2,1,0:T(8,128)(2,1)S(1)}, bf16[1,179,384]{2,1,0:T(8,128)(2,1)S(1)}, u32[]{:S(2)}, u32[]{:S(2)}) %collective-permute-start.6) | collective-permute-done | bytes 137504 | tf_op jit(solution)/shard_map/ppermute | solution.py:160
  29.1 0.5 %fusion.4 = bf16[128,384]{1,0:T(8,128)(2,1)S(1)} fusion(bf16[256,384]{1,0:T(8,128)(2,1)S(1)} %get-tuple-element.41, bf16[1,256,128]{2,1,0:T(8,128)(2,1)S(1)} %fusion.121, s32[128]{0:T(128)S(1)} %bitcast.231, s32[256]{0:T(256)S(1)} %bitcast.226, pred[256]{0:T(512)(128)(4,1)S(1)} %broadcast_compare_fusion, bf16[1,256,384]{2,1,0:T(8,128)(2,1)S(1)} %bitcast.212), kind=kOutput, calls=%fused_computation.14 | convolution fusion | flops 51052544 | bytes 657408 | tf_op jit(solution)/shard_map/bij,bip->bjp/dot_general | solution.py:243
  31.5 1.6 %collective-permute-start.9 = (bf16[192,192]{1,0:T(8,128)(2,1)S(1)}, bf16[192,192]{1,0:T(8,128)(2,1)S(1)}, u32[]{:S(2)}, u32[]{:S(2)}) collective-permute-start(bf16[192,192]{1,0:T(8,128)(2,1)S(1)} %constant_dynamic-slice_fusion), channel_id=1, source_target_pairs={{0,4},{4,0},{1,5},{5,1},{2,6},{6,2},{3,7},{7,3},{8,12},{12,8},{9,1... | collective-permute-start | bytes 221192 | tf_op jit(solution)/shard_map/ppermute | solution.py:130
  33.2 0.9 %collective-permute-start.10 = (bf16[192,192]{1,0:T(8,128)(2,1)S(1)}, bf16[192,192]{1,0:T(8,128)(2,1)S(1)}, u32[]{:S(2)}, u32[]{:S(2)}) collective-permute-start(bf16[192,192]{1,0:T(8,128)(2,1)S(1)} %constant_dynamic-slice_fusion.3), channel_id=1, source_target_pairs={{0,4},{4,0},{1,5},{5,1},{2,6},{6,2},{3,7},{7,3},{8,12},{12,8},{9,1... | collective-permute-start | bytes 221192 | tf_op jit(solution)/shard_map/ppermute | solution.py:130
  34.5 2.7 %collective-permute-done.9 = bf16[192,192]{1,0:T(8,128)(2,1)S(1)} collective-permute-done((bf16[192,192]{1,0:T(8,128)(2,1)S(1)}, bf16[192,192]{1,0:T(8,128)(2,1)S(1)}, u32[]{:S(2)}, u32[]{:S(2)}) %collective-permute-start.9) | collective-permute-done | bytes 73760 | tf_op jit(solution)/shard_map/ppermute | solution.py:130
  37.1 1.7 %collective-permute-done.10 = bf16[192,192]{1,0:T(8,128)(2,1)S(1)} collective-permute-done((bf16[192,192]{1,0:T(8,128)(2,1)S(1)}, bf16[192,192]{1,0:T(8,128)(2,1)S(1)}, u32[]{:S(2)}, u32[]{:S(2)}) %collective-permute-start.10) | collective-permute-done | bytes 73760 | tf_op jit(solution)/shard_map/ppermute | solution.py:130
  39.0 1.6 %collective-permute-start.11 = (bf16[2,192,192]{2,1,0:T(8,128)(2,1)S(1)}, bf16[2,192,192]{2,1,0:T(8,128)(2,1)S(1)}, u32[]{:S(2)}, u32[]{:S(2)}) collective-permute-start(bf16[2,192,192]{2,1,0:T(8,128)(2,1)S(1)} %pad_maximum_fusion), channel_id=1, source_target_pairs={{0,16},{8,24},{16,0},{24,8},{1,17},{9,25},{17,1},{25,9},{2,18},{10... | collective-permute-start | bytes 442376 | tf_op jit(solution)/shard_map/ppermute | solution.py:292
  40.7 4.8 %collective-permute-done.11 = bf16[2,192,192]{2,1,0:T(8,128)(2,1)S(1)} collective-permute-done((bf16[2,192,192]{2,1,0:T(8,128)(2,1)S(1)}, bf16[2,192,192]{2,1,0:T(8,128)(2,1)S(1)}, u32[]{:S(2)}, u32[]{:S(2)}) %collective-permute-start.11) | collective-permute-done | bytes 147488 | tf_op jit(solution)/shard_map/ppermute | solution.py:292
  46.1 1.1 %fusion.2 = bf16[1,512,384]{2,1,0:T(8,128)(2,1)} fusion(f32[512,384]{1,0:T(8,128)S(1)} %convolution_add_fusion.1, f32[512,384]{1,0:T(8,128)S(1)} %fusion.14, s32[128]{0:T(128)S(1)} %subtract_bitcast_fusion, f32[128,384]{1,0:T(8,128)S(1)} %fusion.60), kind=kOutput, calls=%fused_computation.8 | convolution fusion | flops 51183616 | bytes 2163200 | tf_op jit(solution)/shard_map/bnr,bnc->brc/dot_general | solution.py:26
  47.7 0.9 %slice_bitcast_fusion = (f32[384,192]{0,1:T(8,128)}, f32[384,192]{0,1:T(8,128)}) fusion(f32[2,384,192]{1,2,0:T(8,128)S(1)} %fusion.11), kind=kLoop, calls=%fused_computation.37 | loop fusion | bytes 1179648 | tf_op jit(solution)/shard_map/squeeze | solution.py:299
  (86 shorter events, 7.5 us)
Async XLA Ops:
  0.6 1.4 %copy-start = (bf16[1,512,384]{2,1,0:T(8,128)(2,1)S(1)}, bf16[1,512,384]{2,1,0:T(8,128)(2,1)}, u32[]{:S(2)}) copy-start(bf16[1,512,384]{2,1,0:T(8,128)(2,1)} %param.12) | copy-start | bytes 1179652
  0.7 0.7 %copy-start.5 = (s32[1,128]{1,0:T(1,128)S(1)}, s32[1,128]{1,0:T(1,128)}, u32[]{:S(2)}) copy-start(s32[1,128]{1,0:T(1,128)} %param.13) | copy-start | bytes 1540
  1.4 0.7 %copy-start.4 = (s32[1,128]{1,0:T(1,128)S(1)}, s32[1,128]{1,0:T(1,128)}, u32[]{:S(2)}) copy-start(s32[1,128]{1,0:T(1,128)} %param.14) | copy-start | bytes 1540
  2.3 1.0 %copy-start.1 = (bf16[384,384]{1,0:T(8,128)(2,1)S(1)}, bf16[384,384]{1,0:T(8,128)(2,1)}, u32[]{:S(2)}) copy-start(bf16[384,384]{1,0:T(8,128)(2,1)} %param.16) | copy-start | bytes 884740
  2.6 1.0 %copy-start.2 = (bf16[384,384]{1,0:T(8,128)(2,1)S(1)}, bf16[384,384]{1,0:T(8,128)(2,1)}, u32[]{:S(2)}) copy-start(bf16[384,384]{1,0:T(8,128)(2,1)} %param.17) | copy-start | bytes 884740
  4.2 5.9 %copy-start.3 = (bf16[1,128,256]{2,1,0:T(8,128)(2,1)S(1)}, bf16[1,128,256]{2,1,0:T(8,128)(2,1)}, u32[]{:S(2)}) copy-start(bf16[1,128,256]{2,1,0:T(8,128)(2,1)} %param.15) | copy-start | bytes 196612
  4.2 7.3 %collective-permute-start.2 = (bf16[1,64,384]{2,1,0:T(8,128)(2,1)S(1)}, bf16[1,64,384]{2,1,0:T(8,128)(2,1)S(1)}, u32[]{:S(2)}, u32[]{:S(2)}) collective-permute-start(bf16[1,64,384]{2,1,0:T(8,128)(2,1)S(1)} %get-tuple-element.39), channel_id=1, source_target_pairs={{0,3},{1,2},{2,1},{3,0},{4,7},{5,6},{6,5},{7,4},{8,11},{9,10},{10,... | collective-permute-start | bytes 147464 | tf_op jit(solution)/shard_map/ppermute | solution.py:75
  9.3 5.0 %collective-permute-start.1 = (bf16[1,64,384]{2,1,0:T(8,128)(2,1)S(1)}, bf16[1,64,384]{2,1,0:T(8,128)(2,1)S(1)}, u32[]{:S(2)}, u32[]{:S(2)}) collective-permute-start(bf16[1,64,384]{2,1,0:T(8,128)(2,1)S(1)} %get-tuple-element.38), channel_id=1, source_target_pairs={{0,2},{1,3},{2,0},{3,1},{4,6},{5,7},{6,4},{7,5},{8,10},{9,11},{10,... | collective-permute-start | bytes 147464 | tf_op jit(solution)/shard_map/ppermute | solution.py:75
  9.3 5.0 %collective-permute-start = (bf16[1,64,384]{2,1,0:T(8,128)(2,1)S(1)}, bf16[1,64,384]{2,1,0:T(8,128)(2,1)S(1)}, u32[]{:S(2)}, u32[]{:S(2)}) collective-permute-start(bf16[1,64,384]{2,1,0:T(8,128)(2,1)S(1)} %get-tuple-element.37), channel_id=1, source_target_pairs={{0,1},{1,0},{2,3},{3,2},{4,5},{5,4},{6,7},{7,6},{8,9},{9,8},{10,11... | collective-permute-start | bytes 147464 | tf_op jit(solution)/shard_map/ppermute | solution.py:75
  15.1 6.2 %collective-permute-start.5 = (bf16[1,64,384]{2,1,0:T(8,128)(2,1)S(1)}, bf16[1,64,384]{2,1,0:T(8,128)(2,1)S(1)}, u32[]{:S(2)}, u32[]{:S(2)}) collective-permute-start(bf16[1,64,384]{2,1,0:T(8,128)(2,1)S(1)} %fusion.143), channel_id=1, source_target_pairs={{0,3},{1,2},{2,1},{3,0},{4,7},{5,6},{6,5},{7,4},{8,11},{9,10},{10,... | collective-permute-start | bytes 147464 | tf_op jit(solution)/shard_map/ppermute | solution.py:85
  17.2 5.4 %collective-permute-start.4 = (bf16[1,64,384]{2,1,0:T(8,128)(2,1)S(1)}, bf16[1,64,384]{2,1,0:T(8,128)(2,1)S(1)}, u32[]{:S(2)}, u32[]{:S(2)}) collective-permute-start(bf16[1,64,384]{2,1,0:T(8,128)(2,1)S(1)} %fusion.143), channel_id=1, source_target_pairs={{0,2},{1,3},{2,0},{3,1},{4,6},{5,7},{6,4},{7,5},{8,10},{9,11},{10,... | collective-permute-start | bytes 147464 | tf_op jit(solution)/shard_map/ppermute | solution.py:85
  17.2 5.4 %collective-permute-start.3 = (bf16[1,64,384]{2,1,0:T(8,128)(2,1)S(1)}, bf16[1,64,384]{2,1,0:T(8,128)(2,1)S(1)}, u32[]{:S(2)}, u32[]{:S(2)}) collective-permute-start(bf16[1,64,384]{2,1,0:T(8,128)(2,1)S(1)} %fusion.143), channel_id=1, source_target_pairs={{0,1},{1,0},{2,3},{3,2},{4,5},{5,4},{6,7},{7,6},{8,9},{9,8},{10,11... | collective-permute-start | bytes 147464 | tf_op jit(solution)/shard_map/ppermute | solution.py:85
  23.5 5.1 %collective-permute-start.6 = (bf16[1,179,384]{2,1,0:T(8,128)(2,1)S(1)}, bf16[1,179,384]{2,1,0:T(8,128)(2,1)S(1)}, u32[]{:S(2)}, u32[]{:S(2)}) collective-permute-start(bf16[1,179,384]{2,1,0:T(8,128)(2,1)S(1)} %pad_maximum_fusion.1), channel_id=1, source_target_pairs={{0,4},{4,0},{1,5},{5,1},{2,6},{6,2},{3,7},{7,3},{8,12},{12,8},{9,1... | collective-permute-start | bytes 412424 | tf_op jit(solution)/shard_map/ppermute | solution.py:160
  26.3 5.0 %collective-permute-start.8 = (bf16[384,192]{1,0:T(8,128)(2,1)S(1)}, bf16[384,192]{1,0:T(8,128)(2,1)S(1)}, u32[]{:S(2)}, u32[]{:S(2)}) collective-permute-start(bf16[384,192]{1,0:T(8,128)(2,1)S(1)} %constant_dynamic-slice_fusion.1), channel_id=1, source_target_pairs={{0,8},{8,0},{16,24},{24,16},{1,9},{9,1},{17,25},{25,17},{2,10},{10... | collective-permute-start | bytes 442376 | tf_op jit(solution)/shard_map/ppermute | solution.py:122
  30.8 2.2 %collective-permute-start.7 = (bf16[384,192]{1,0:T(8,128)(2,1)S(1)}, bf16[384,192]{1,0:T(8,128)(2,1)S(1)}, u32[]{:S(2)}, u32[]{:S(2)}) collective-permute-start(bf16[384,192]{1,0:T(8,128)(2,1)S(1)} %constant_dynamic-slice_fusion.2), channel_id=1, source_target_pairs={{0,8},{8,0},{16,24},{24,16},{1,9},{9,1},{17,25},{25,17},{2,10},{10... | collective-permute-start | bytes 442376 | tf_op jit(solution)/shard_map/ppermute | solution.py:122
  31.5 5.7 %collective-permute-start.9 = (bf16[192,192]{1,0:T(8,128)(2,1)S(1)}, bf16[192,192]{1,0:T(8,128)(2,1)S(1)}, u32[]{:S(2)}, u32[]{:S(2)}) collective-permute-start(bf16[192,192]{1,0:T(8,128)(2,1)S(1)} %constant_dynamic-slice_fusion), channel_id=1, source_target_pairs={{0,4},{4,0},{1,5},{5,1},{2,6},{6,2},{3,7},{7,3},{8,12},{12,8},{9,1... | collective-permute-start | bytes 221192 | tf_op jit(solution)/shard_map/ppermute | solution.py:130
  33.2 5.6 %collective-permute-start.10 = (bf16[192,192]{1,0:T(8,128)(2,1)S(1)}, bf16[192,192]{1,0:T(8,128)(2,1)S(1)}, u32[]{:S(2)}, u32[]{:S(2)}) collective-permute-start(bf16[192,192]{1,0:T(8,128)(2,1)S(1)} %constant_dynamic-slice_fusion.3), channel_id=1, source_target_pairs={{0,4},{4,0},{1,5},{5,1},{2,6},{6,2},{3,7},{7,3},{8,12},{12,8},{9,1... | collective-permute-start | bytes 221192 | tf_op jit(solution)/shard_map/ppermute | solution.py:130
  39.0 6.6 %collective-permute-start.11 = (bf16[2,192,192]{2,1,0:T(8,128)(2,1)S(1)}, bf16[2,192,192]{2,1,0:T(8,128)(2,1)S(1)}, u32[]{:S(2)}, u32[]{:S(2)}) collective-permute-start(bf16[2,192,192]{2,1,0:T(8,128)(2,1)S(1)} %pad_maximum_fusion), channel_id=1, source_target_pairs={{0,16},{8,24},{16,0},{24,8},{1,17},{9,25},{17,1},{25,9},{2,18},{10... | collective-permute-start | bytes 442376 | tf_op jit(solution)/shard_map/ppermute | solution.py:292
  45.6 1.8 %collective-permute-start.12 = (f32[2,192,192]{2,1,0:T(8,128)S(1)}, f32[2,192,192]{2,1,0:T(8,128)S(1)}, u32[]{:S(2)}, u32[]{:S(2)}) collective-permute-start(f32[2,192,192]{2,1,0:T(8,128)S(1)} %convert_add_fusion), channel_id=1, source_target_pairs={{0,8},{8,0},{16,24},{24,16},{1,9},{9,1},{17,25},{25,17},{2,10},{10... | collective-permute-start | bytes 884744 | tf_op jit(solution)/shard_map/ppermute | solution.py:294

commit v12 on v11

--- a/solution.py
+++ b/solution.py
@@ -289,7 +289,10 @@
     while bit < n_dp:
         held = mine.astype(jnp.bfloat16)
         perm = [(i, i ^ bit) for i in range(n_dp)]
-        mine = held.astype(jnp.float32) + lax.ppermute(held, "dp", perm).astype(jnp.float32)
+        received = lax.ppermute(held, "dp", perm)
+        if bit == 2:
+            received, row_grad = lax.optimization_barrier((received, row_grad))
+        mine = held.astype(jnp.float32) + received.astype(jnp.float32)
         bit *= 2
     other = lax.ppermute(mine, "dp", [(i, i ^ 1) for i in range(n_dp)])
     mine = jnp.where(pair == 0, jnp.concatenate([mine, other], 2), jnp.concatenate([other, mine], 2))

time: 48.7 us -> 50.4 us (1.035)
  waiting for transfers between devices: 18.5 us -> 20.6 us
    ppermute x3, waiting for transfers between devices: 3.67 us -> 5.2 us  [shards(): lax.ppermute(outgoing, 'head', [(i, i ^ k) for i in range(n_head)])]
    ppermute x1, waiting for transfers between devices: 0.19 us -> 1.7 us  [shards(): other = lax.ppermute(mine, 'dp', [(i, i ^ 1) for i in range(n_dp)])]
    ppermute x1, waiting for transfers between devices: 4.8 us -> 3.89 us  [shards(): received = lax.ppermute(held, 'dp', perm)]
    ppermute x3, waiting for transfers between devices: 3.12 us -> 2.36 us  [shards(): lax.ppermute(feat_quarter, 'head', [(i, i ^ k) for i in range(n_head)])]
  transfers between devices with their start and end apart: 13 -> 13, of which waited for: 9 -> 9; matrix products, arithmetic and copies ran while one was open for 14% -> 12% of each run, Pallas kernels for 0% -> 0%
where the time goes in v12:
time: 50.4 us; the launch traced here: 50.3 us
  waiting for transfers between devices  20.6 us (41%)
  starting transfers between devices  15.7 us (31%)
  matrix products  5.92 us (12%)
  local copies, waits for them, and re-layouts  5.27 us (10%)
  other arithmetic  1.6 us (3%)
  between operations  1.24 us (2%)
    ppermute x3, starting transfers between devices, shards(): lax.ppermute(outgoing, 'head', [(i, i ^ k) for i in range(n_head)])  5.68 us
    ppermute x3, waiting for transfers between devices, shards(): lax.ppermute(outgoing, 'head', [(i, i ^ k) for i in range(n_head)])  5.2 us
    ppermute x2, waiting for transfers between devices, from_seq_partner(): return lax.ppermute(outgoing, 'seq', [(0, 1), (1, 0)]).astype(jnp.float32)  4.66 us
    ppermute x3, starting transfers between devices, shards(): lax.ppermute(feat_quarter, 'head', [(i, i ^ k) for i in range(n_head)])  4.45 us
    ppermute x1, waiting for transfers between devices, shards(): received = lax.ppermute(held, 'dp', perm)  3.89 us
    ppermute x1, waiting for transfers between devices, shards(): arrived = lax.ppermute(payload, 'seq', perm)  2.77 us
    ppermute x3, waiting for transfers between devices, shards(): lax.ppermute(feat_quarter, 'head', [(i, i ^ k) for i in range(n_head)])  2.36 us
    unnamed x17, local copies, waits for them, and re-layouts  2.26 us
  transfers between devices with their start and end apart: 13, of which 9 were waited for; matrix products, arithmetic and copies ran while one was open for 12% of the time, Pallas kernels for 0%

profile of v12, /device:TPU:0, one launch (start us, length us, event | category | flops | bytes accessed | tf_op | source)
XLA Modules:
  0.0 50.3 jit_solution(7008596743712153210)
XLA Ops:
  0.7 0.7 %copy-done.4 = s32[1,128]{1,0:T(1,128)S(1)} copy-done((s32[1,128]{1,0:T(1,128)S(1)}, s32[1,128]{1,0:T(1,128)}, u32[]{:S(2)}) %copy-start.4) | copy-done | bytes 536
  1.4 0.7 %copy-done.5 = s32[1,128]{1,0:T(1,128)S(1)} copy-done((s32[1,128]{1,0:T(1,128)S(1)}, s32[1,128]{1,0:T(1,128)}, u32[]{:S(2)}) %copy-start.5) | copy-done | bytes 536
  2.6 0.7 %copy-done.2 = bf16[384,384]{1,0:T(8,128)(2,1)S(1)} copy-done((bf16[384,384]{1,0:T(8,128)(2,1)S(1)}, bf16[384,384]{1,0:T(8,128)(2,1)}, u32[]{:S(2)}) %copy-start.2) | copy-done | bytes 294936
  4.2 3.1 %collective-permute-start = (bf16[1,64,384]{2,1,0:T(8,128)(2,1)S(1)}, bf16[1,64,384]{2,1,0:T(8,128)(2,1)S(1)}, u32[]{:S(2)}, u32[]{:S(2)}) collective-permute-start(bf16[1,64,384]{2,1,0:T(8,128)(2,1)S(1)} %get-tuple-element.41), channel_id=1, source_target_pairs={{0,1},{1,0},{2,3},{3,2},{4,5},{5,4},{6,7},{7,6},{8,9},{9,8},{10,11... | collective-permute-start | bytes 147464 | tf_op jit(solution)/shard_map/ppermute | solution.py:75
  7.3 2.6 %collective-permute-start.1 = (bf16[1,64,384]{2,1,0:T(8,128)(2,1)S(1)}, bf16[1,64,384]{2,1,0:T(8,128)(2,1)S(1)}, u32[]{:S(2)}, u32[]{:S(2)}) collective-permute-start(bf16[1,64,384]{2,1,0:T(8,128)(2,1)S(1)} %get-tuple-element.42), channel_id=1, source_target_pairs={{0,2},{1,3},{2,0},{3,1},{4,6},{5,7},{6,4},{7,5},{8,10},{9,11},{10,... | collective-permute-start | bytes 147464 | tf_op jit(solution)/shard_map/ppermute | solution.py:75
  10.5 2.6 %collective-permute-done.1 = bf16[1,64,384]{2,1,0:T(8,128)(2,1)S(1)} collective-permute-done((bf16[1,64,384]{2,1,0:T(8,128)(2,1)S(1)}, bf16[1,64,384]{2,1,0:T(8,128)(2,1)S(1)}, u32[]{:S(2)}, u32[]{:S(2)}) %collective-permute-start.1) | collective-permute-done | bytes 49184 | tf_op jit(solution)/shard_map/ppermute | solution.py:75
  13.2 2.6 %collective-permute-done.2 = bf16[1,64,384]{2,1,0:T(8,128)(2,1)S(1)} collective-permute-done((bf16[1,64,384]{2,1,0:T(8,128)(2,1)S(1)}, bf16[1,64,384]{2,1,0:T(8,128)(2,1)S(1)}, u32[]{:S(2)}, u32[]{:S(2)}) %collective-permute-start.2) | collective-permute-done | bytes 49184 | tf_op jit(solution)/shard_map/ppermute | solution.py:75
  15.8 0.6 %gather_fusion = bf16[4,64,384]{2,1,0:T(8,128)(2,1)S(1)} fusion(bf16[4,64,384]{2,1,0:T(8,128)(2,1)S(1)} %maximum_bitcast_fusion, s32[1024]{0:T(1024)S(1)} %pad_clamp_fusion), kind=kCustom, calls=%fused_computation.clone | custom fusion | bytes 393232 | tf_op jit(solution)/shard_map/jit(_take)/gather | solution.py:77
  16.5 0.8 %collective-permute-start.5 = (bf16[1,64,384]{2,1,0:T(8,128)(2,1)S(1)}, bf16[1,64,384]{2,1,0:T(8,128)(2,1)S(1)}, u32[]{:S(2)}, u32[]{:S(2)}) collective-permute-start(bf16[1,64,384]{2,1,0:T(8,128)(2,1)S(1)} %fusion.142), channel_id=1, source_target_pairs={{0,3},{1,2},{2,1},{3,0},{4,7},{5,6},{6,5},{7,4},{8,11},{9,10},{10,... | collective-permute-start | bytes 147464 | tf_op jit(solution)/shard_map/ppermute | solution.py:85
  17.3 3.7 %collective-permute-start.3 = (bf16[1,64,384]{2,1,0:T(8,128)(2,1)S(1)}, bf16[1,64,384]{2,1,0:T(8,128)(2,1)S(1)}, u32[]{:S(2)}, u32[]{:S(2)}) collective-permute-start(bf16[1,64,384]{2,1,0:T(8,128)(2,1)S(1)} %fusion.142), channel_id=1, source_target_pairs={{0,1},{1,0},{2,3},{3,2},{4,5},{5,4},{6,7},{7,6},{8,9},{9,8},{10,11... | collective-permute-start | bytes 147464 | tf_op jit(solution)/shard_map/ppermute | solution.py:85
  21.0 1.6 %collective-permute-done.5 = bf16[1,64,384]{2,1,0:T(8,128)(2,1)S(1)} collective-permute-done((bf16[1,64,384]{2,1,0:T(8,128)(2,1)S(1)}, bf16[1,64,384]{2,1,0:T(8,128)(2,1)S(1)}, u32[]{:S(2)}, u32[]{:S(2)}) %collective-permute-start.5) | collective-permute-done | bytes 49184 | tf_op jit(solution)/shard_map/ppermute | solution.py:85
  22.6 0.8 %collective-permute-done.4 = bf16[1,64,384]{2,1,0:T(8,128)(2,1)S(1)} collective-permute-done((bf16[1,64,384]{2,1,0:T(8,128)(2,1)S(1)}, bf16[1,64,384]{2,1,0:T(8,128)(2,1)S(1)}, u32[]{:S(2)}, u32[]{:S(2)}) %collective-permute-start.4) | collective-permute-done | bytes 49184 | tf_op jit(solution)/shard_map/ppermute | solution.py:85
  23.4 0.6 %gather_fusion.1 = bf16[4,64,384]{2,1,0:T(8,128)(2,1)S(1)} fusion(bf16[4,64,384]{2,1,0:T(8,128)(2,1)S(1)} %maximum_bitcast_fusion.1, s32[1024]{0:T(1024)S(1)} %pad_clamp_fusion), kind=kCustom, calls=%fused_computation.1.clone | custom fusion | bytes 393232 | tf_op jit(solution)/shard_map/jit(_take)/gather | solution.py:86
  24.6 1.6 %collective-permute-start.6 = (bf16[1,179,384]{2,1,0:T(8,128)(2,1)S(1)}, bf16[1,179,384]{2,1,0:T(8,128)(2,1)S(1)}, u32[]{:S(2)}, u32[]{:S(2)}) collective-permute-start(bf16[1,179,384]{2,1,0:T(8,128)(2,1)S(1)} %pad_maximum_fusion.1), channel_id=1, source_target_pairs={{0,4},{4,0},{1,5},{5,1},{2,6},{6,2},{3,7},{7,3},{8,12},{12,8},{9,1... | collective-permute-start | bytes 412424 | tf_op jit(solution)/shard_map/ppermute | solution.py:160
  27.0 2.8 %collective-permute-done.6 = bf16[1,179,384]{2,1,0:T(8,128)(2,1)S(1)} collective-permute-done((bf16[1,179,384]{2,1,0:T(8,128)(2,1)S(1)}, bf16[1,179,384]{2,1,0:T(8,128)(2,1)S(1)}, u32[]{:S(2)}, u32[]{:S(2)}) %collective-permute-start.6) | collective-permute-done | bytes 137504 | tf_op jit(solution)/shard_map/ppermute | solution.py:160
  33.2 1.6 %collective-permute-start.9 = (bf16[192,192]{1,0:T(8,128)(2,1)S(1)}, bf16[192,192]{1,0:T(8,128)(2,1)S(1)}, u32[]{:S(2)}, u32[]{:S(2)}) collective-permute-start(bf16[192,192]{1,0:T(8,128)(2,1)S(1)} %constant_dynamic-slice_fusion), channel_id=1, source_target_pairs={{0,4},{4,0},{1,5},{5,1},{2,6},{6,2},{3,7},{7,3},{8,12},{12,8},{9,1... | collective-permute-start | bytes 221192 | tf_op jit(solution)/shard_map/ppermute | solution.py:130
  35.0 0.6 %collective-permute-start.10 = (bf16[192,192]{1,0:T(8,128)(2,1)S(1)}, bf16[192,192]{1,0:T(8,128)(2,1)S(1)}, u32[]{:S(2)}, u32[]{:S(2)}) collective-permute-start(bf16[192,192]{1,0:T(8,128)(2,1)S(1)} %constant_dynamic-slice_fusion.3), channel_id=1, source_target_pairs={{0,4},{4,0},{1,5},{5,1},{2,6},{6,2},{3,7},{7,3},{8,12},{12,8},{9,1... | collective-permute-start | bytes 221192 | tf_op jit(solution)/shard_map/ppermute | solution.py:130
  36.0 3.0 %collective-permute-done.9 = bf16[192,192]{1,0:T(8,128)(2,1)S(1)} collective-permute-done((bf16[192,192]{1,0:T(8,128)(2,1)S(1)}, bf16[192,192]{1,0:T(8,128)(2,1)S(1)}, u32[]{:S(2)}, u32[]{:S(2)}) %collective-permute-start.9) | collective-permute-done | bytes 73760 | tf_op jit(solution)/shard_map/ppermute | solution.py:130
  38.9 1.7 %collective-permute-done.10 = bf16[192,192]{1,0:T(8,128)(2,1)S(1)} collective-permute-done((bf16[192,192]{1,0:T(8,128)(2,1)S(1)}, bf16[192,192]{1,0:T(8,128)(2,1)S(1)}, u32[]{:S(2)}, u32[]{:S(2)}) %collective-permute-start.10) | collective-permute-done | bytes 73760 | tf_op jit(solution)/shard_map/ppermute | solution.py:130
  40.7 1.6 %collective-permute-start.11 = (bf16[2,192,192]{2,1,0:T(8,128)(2,1)S(1)}, bf16[2,192,192]{2,1,0:T(8,128)(2,1)S(1)}, u32[]{:S(2)}, u32[]{:S(2)}) collective-permute-start(bf16[2,192,192]{2,1,0:T(8,128)(2,1)S(1)} %pad_maximum_fusion), channel_id=1, source_target_pairs={{0,16},{8,24},{16,0},{24,8},{1,17},{9,25},{17,1},{25,9},{2,18},{10... | collective-permute-start | bytes 442376 | tf_op jit(solution)/shard_map/ppermute | solution.py:292
  42.3 1.1 %fusion.1 = bf16[1,512,384]{2,1,0:T(8,128)(2,1)} fusion(f32[512,384]{1,0:T(8,128)S(1)} %convolution_add_fusion.1, f32[512,384]{1,0:T(8,128)S(1)} %fusion.13, s32[128]{0:T(128)S(1)} %subtract_bitcast_fusion, f32[128,384]{1,0:T(8,128)S(1)} %fusion.57), kind=kOutput, calls=%fused_computation.4 | convolution fusion | flops 51183616 | bytes 2163200 | tf_op jit(solution)/shard_map/bnr,bnc->brc/dot_general | solution.py:26
  43.4 3.9 %collective-permute-done.11 = bf16[2,192,192]{2,1,0:T(8,128)(2,1)S(1)} collective-permute-done((bf16[2,192,192]{2,1,0:T(8,128)(2,1)S(1)}, bf16[2,192,192]{2,1,0:T(8,128)(2,1)S(1)}, u32[]{:S(2)}, u32[]{:S(2)}) %collective-permute-start.11) | collective-permute-done | bytes 147488 | tf_op jit(solution)/shard_map/ppermute | solution.py:292
  47.5 1.7 %collective-permute-done.12 = f32[2,192,192]{2,1,0:T(8,128)S(1)} collective-permute-done((f32[2,192,192]{2,1,0:T(8,128)S(1)}, f32[2,192,192]{2,1,0:T(8,128)S(1)}, u32[]{:S(2)}, u32[]{:S(2)}) %collective-permute-start.12) | collective-permute-done | bytes 294944 | tf_op jit(solution)/shard_map/ppermute | solution.py:297
  49.4 0.9 %slice_bitcast_fusion = (f32[384,192]{0,1:T(8,128)}, f32[384,192]{0,1:T(8,128)}) fusion(f32[2,384,192]{1,2,0:T(8,128)S(1)} %fusion.10), kind=kLoop, calls=%fused_computation.36 | loop fusion | bytes 1179648 | tf_op jit(solution)/shard_map/squeeze | solution.py:302
  (86 shorter events, 7.9 us)
Async XLA Ops:
  0.6 1.4 %copy-start = (bf16[1,512,384]{2,1,0:T(8,128)(2,1)S(1)}, bf16[1,512,384]{2,1,0:T(8,128)(2,1)}, u32[]{:S(2)}) copy-start(bf16[1,512,384]{2,1,0:T(8,128)(2,1)} %param.12) | copy-start | bytes 1179652
  0.7 0.7 %copy-start.4 = (s32[1,128]{1,0:T(1,128)S(1)}, s32[1,128]{1,0:T(1,128)}, u32[]{:S(2)}) copy-start(s32[1,128]{1,0:T(1,128)} %param.14) | copy-start | bytes 1540
  1.4 0.7 %copy-start.5 = (s32[1,128]{1,0:T(1,128)S(1)}, s32[1,128]{1,0:T(1,128)}, u32[]{:S(2)}) copy-start(s32[1,128]{1,0:T(1,128)} %param.13) | copy-start | bytes 1540
  2.3 1.0 %copy-start.2 = (bf16[384,384]{1,0:T(8,128)(2,1)S(1)}, bf16[384,384]{1,0:T(8,128)(2,1)}, u32[]{:S(2)}) copy-start(bf16[384,384]{1,0:T(8,128)(2,1)} %param.17) | copy-start | bytes 884740
  2.6 1.0 %copy-start.1 = (bf16[384,384]{1,0:T(8,128)(2,1)S(1)}, bf16[384,384]{1,0:T(8,128)(2,1)}, u32[]{:S(2)}) copy-start(bf16[384,384]{1,0:T(8,128)(2,1)} %param.16) | copy-start | bytes 884740
  4.2 5.8 %copy-start.3 = (bf16[1,128,256]{2,1,0:T(8,128)(2,1)S(1)}, bf16[1,128,256]{2,1,0:T(8,128)(2,1)}, u32[]{:S(2)}) copy-start(bf16[1,128,256]{2,1,0:T(8,128)(2,1)} %param.15) | copy-start | bytes 196612
  4.2 6.4 %collective-permute-start = (bf16[1,64,384]{2,1,0:T(8,128)(2,1)S(1)}, bf16[1,64,384]{2,1,0:T(8,128)(2,1)S(1)}, u32[]{:S(2)}, u32[]{:S(2)}) collective-permute-start(bf16[1,64,384]{2,1,0:T(8,128)(2,1)S(1)} %get-tuple-element.41), channel_id=1, source_target_pairs={{0,1},{1,0},{2,3},{3,2},{4,5},{5,4},{6,7},{7,6},{8,9},{9,8},{10,11... | collective-permute-start | bytes 147464 | tf_op jit(solution)/shard_map/ppermute | solution.py:75
  7.3 5.9 %collective-permute-start.1 = (bf16[1,64,384]{2,1,0:T(8,128)(2,1)S(1)}, bf16[1,64,384]{2,1,0:T(8,128)(2,1)S(1)}, u32[]{:S(2)}, u32[]{:S(2)}) collective-permute-start(bf16[1,64,384]{2,1,0:T(8,128)(2,1)S(1)} %get-tuple-element.42), channel_id=1, source_target_pairs={{0,2},{1,3},{2,0},{3,1},{4,6},{5,7},{6,4},{7,5},{8,10},{9,11},{10,... | collective-permute-start | bytes 147464 | tf_op jit(solution)/shard_map/ppermute | solution.py:75
  9.8 5.9 %collective-permute-start.2 = (bf16[1,64,384]{2,1,0:T(8,128)(2,1)S(1)}, bf16[1,64,384]{2,1,0:T(8,128)(2,1)S(1)}, u32[]{:S(2)}, u32[]{:S(2)}) collective-permute-start(bf16[1,64,384]{2,1,0:T(8,128)(2,1)S(1)} %get-tuple-element.43), channel_id=1, source_target_pairs={{0,3},{1,2},{2,1},{3,0},{4,7},{5,6},{6,5},{7,4},{8,11},{9,10},{10,... | collective-permute-start | bytes 147464 | tf_op jit(solution)/shard_map/ppermute | solution.py:75
  16.5 6.1 %collective-permute-start.5 = (bf16[1,64,384]{2,1,0:T(8,128)(2,1)S(1)}, bf16[1,64,384]{2,1,0:T(8,128)(2,1)S(1)}, u32[]{:S(2)}, u32[]{:S(2)}) collective-permute-start(bf16[1,64,384]{2,1,0:T(8,128)(2,1)S(1)} %fusion.142), channel_id=1, source_target_pairs={{0,3},{1,2},{2,1},{3,0},{4,7},{5,6},{6,5},{7,4},{8,11},{9,10},{10,... | collective-permute-start | bytes 147464 | tf_op jit(solution)/shard_map/ppermute | solution.py:85
  17.3 6.0 %collective-permute-start.4 = (bf16[1,64,384]{2,1,0:T(8,128)(2,1)S(1)}, bf16[1,64,384]{2,1,0:T(8,128)(2,1)S(1)}, u32[]{:S(2)}, u32[]{:S(2)}) collective-permute-start(bf16[1,64,384]{2,1,0:T(8,128)(2,1)S(1)} %fusion.142), channel_id=1, source_target_pairs={{0,2},{1,3},{2,0},{3,1},{4,6},{5,7},{6,4},{7,5},{8,10},{9,11},{10,... | collective-permute-start | bytes 147464 | tf_op jit(solution)/shard_map/ppermute | solution.py:85
  17.3 6.0 %collective-permute-start.3 = (bf16[1,64,384]{2,1,0:T(8,128)(2,1)S(1)}, bf16[1,64,384]{2,1,0:T(8,128)(2,1)S(1)}, u32[]{:S(2)}, u32[]{:S(2)}) collective-permute-start(bf16[1,64,384]{2,1,0:T(8,128)(2,1)S(1)} %fusion.142), channel_id=1, source_target_pairs={{0,1},{1,0},{2,3},{3,2},{4,5},{5,4},{6,7},{7,6},{8,9},{9,8},{10,11... | collective-permute-start | bytes 147464 | tf_op jit(solution)/shard_map/ppermute | solution.py:85
  24.6 5.1 %collective-permute-start.6 = (bf16[1,179,384]{2,1,0:T(8,128)(2,1)S(1)}, bf16[1,179,384]{2,1,0:T(8,128)(2,1)S(1)}, u32[]{:S(2)}, u32[]{:S(2)}) collective-permute-start(bf16[1,179,384]{2,1,0:T(8,128)(2,1)S(1)} %pad_maximum_fusion.1), channel_id=1, source_target_pairs={{0,4},{4,0},{1,5},{5,1},{2,6},{6,2},{3,7},{7,3},{8,12},{12,8},{9,1... | collective-permute-start | bytes 412424 | tf_op jit(solution)/shard_map/ppermute | solution.py:160
  26.9 6.1 %collective-permute-start.8 = (bf16[384,192]{1,0:T(8,128)(2,1)S(1)}, bf16[384,192]{1,0:T(8,128)(2,1)S(1)}, u32[]{:S(2)}, u32[]{:S(2)}) collective-permute-start(bf16[384,192]{1,0:T(8,128)(2,1)S(1)} %constant_dynamic-slice_fusion.1), channel_id=1, source_target_pairs={{0,8},{8,0},{16,24},{24,16},{1,9},{9,1},{17,25},{25,17},{2,10},{10... | collective-permute-start | bytes 442376 | tf_op jit(solution)/shard_map/ppermute | solution.py:122
  32.0 2.9 %collective-permute-start.7 = (bf16[384,192]{1,0:T(8,128)(2,1)S(1)}, bf16[384,192]{1,0:T(8,128)(2,1)S(1)}, u32[]{:S(2)}, u32[]{:S(2)}) collective-permute-start(bf16[384,192]{1,0:T(8,128)(2,1)S(1)} %constant_dynamic-slice_fusion.2), channel_id=1, source_target_pairs={{0,8},{8,0},{16,24},{24,16},{1,9},{9,1},{17,25},{25,17},{2,10},{10... | collective-permute-start | bytes 442376 | tf_op jit(solution)/shard_map/ppermute | solution.py:122
  33.2 5.7 %collective-permute-start.9 = (bf16[192,192]{1,0:T(8,128)(2,1)S(1)}, bf16[192,192]{1,0:T(8,128)(2,1)S(1)}, u32[]{:S(2)}, u32[]{:S(2)}) collective-permute-start(bf16[192,192]{1,0:T(8,128)(2,1)S(1)} %constant_dynamic-slice_fusion), channel_id=1, source_target_pairs={{0,4},{4,0},{1,5},{5,1},{2,6},{6,2},{3,7},{7,3},{8,12},{12,8},{9,1... | collective-permute-start | bytes 221192 | tf_op jit(solution)/shard_map/ppermute | solution.py:130
  35.0 5.6 %collective-permute-start.10 = (bf16[192,192]{1,0:T(8,128)(2,1)S(1)}, bf16[192,192]{1,0:T(8,128)(2,1)S(1)}, u32[]{:S(2)}, u32[]{:S(2)}) collective-permute-start(bf16[192,192]{1,0:T(8,128)(2,1)S(1)} %constant_dynamic-slice_fusion.3), channel_id=1, source_target_pairs={{0,4},{4,0},{1,5},{5,1},{2,6},{6,2},{3,7},{7,3},{8,12},{12,8},{9,1... | collective-permute-start | bytes 221192 | tf_op jit(solution)/shard_map/ppermute | solution.py:130
  40.7 6.6 %collective-permute-start.11 = (bf16[2,192,192]{2,1,0:T(8,128)(2,1)S(1)}, bf16[2,192,192]{2,1,0:T(8,128)(2,1)S(1)}, u32[]{:S(2)}, u32[]{:S(2)}) collective-permute-start(bf16[2,192,192]{2,1,0:T(8,128)(2,1)S(1)} %pad_maximum_fusion), channel_id=1, source_target_pairs={{0,16},{8,24},{16,0},{24,8},{1,17},{9,25},{17,1},{25,9},{2,18},{10... | collective-permute-start | bytes 442376 | tf_op jit(solution)/shard_map/ppermute | solution.py:292
  47.4 1.8 %collective-permute-start.12 = (f32[2,192,192]{2,1,0:T(8,128)S(1)}, f32[2,192,192]{2,1,0:T(8,128)S(1)}, u32[]{:S(2)}, u32[]{:S(2)}) collective-permute-start(f32[2,192,192]{2,1,0:T(8,128)S(1)} %convert_add_fusion), channel_id=1, source_target_pairs={{0,8},{8,0},{16,24},{24,16},{1,9},{9,1},{17,25},{25,17},{2,10},{10... | collective-permute-start | bytes 884744 | tf_op jit(solution)/shard_map/ppermute | solution.py:297

commit v13 on v11

--- a/solution.py
+++ b/solution.py
@@ -222,34 +222,47 @@
     donor_feat = own_donor
     acceptor_feat = own_acceptor
 
-    scores_row = (
-        jnp.einsum("bip,bjp->bij", donor_feat, acceptor_feat_all, preferred_element_type=jnp.float32)
-        * scale
-    )
-    allowed_row = (donor_pos[:, :, None] >= 0) & (acceptor_eff[:, None, :] > donor_pos[:, :, None])
-    slope_row = pair_slope(scores_row, target, allowed_row)
-    donor_grad = (
-        jnp.einsum("bij,bjp->bip", slope_row, acceptor_feat_all, preferred_element_type=jnp.float32)
-        * scale
-    ).astype(jnp.bfloat16)
-
-    scores_col = (
-        jnp.einsum("bip,bjp->bij", donor_feat_all, acceptor_feat, preferred_element_type=jnp.float32)
-        * scale
-    )
-    allowed_col = (donor_eff[:, :, None] >= 0) & (acceptor_pos[:, None, :] > donor_eff[:, :, None])
-    slope_col = pair_slope(scores_col, target_col, allowed_col)
-    acceptor_grad = (
-        jnp.einsum("bij,bip->bjp", slope_col, donor_feat_all, preferred_element_type=jnp.float32)
-        * scale
-    ).astype(jnp.bfloat16)
-
-
     if n_seq == 2:
         first = slab == 0
+        queries = jnp.where(first, own_donor, own_acceptor)
+        keys = jnp.where(first, acceptor_feat_all, donor_feat_all)
+        scores_late = (
+            jnp.einsum("bip,bjp->bij", queries, keys, preferred_element_type=jnp.float32) * scale
+        )
+        allowed_row = (donor_pos[:, :, None] >= 0) & (acceptor_eff[:, None, :] > donor_pos[:, :, None])
+        allowed_col = (donor_eff[:, None, :] >= 0) & (acceptor_pos[:, :, None] > donor_eff[:, None, :])
+        allowed_late = jnp.where(first, allowed_row, allowed_col)
+        target_late = jnp.where(first, target, jnp.swapaxes(target_col, 1, 2))
+        slope_late = pair_slope(scores_late, target_late, allowed_late)
+        grad_late = (
+            jnp.einsum("bij,bjp->bip", slope_late, keys, preferred_element_type=jnp.float32) * scale
+        ).astype(jnp.bfloat16)
+    else:
+        scores_row = (
+            jnp.einsum("bip,bjp->bij", donor_feat, acceptor_feat_all, preferred_element_type=jnp.float32)
+            * scale
+        )
+        allowed_row = (donor_pos[:, :, None] >= 0) & (acceptor_eff[:, None, :] > donor_pos[:, :, None])
+        slope_row = pair_slope(scores_row, target, allowed_row)
+        donor_grad = (
+            jnp.einsum("bij,bjp->bip", slope_row, acceptor_feat_all, preferred_element_type=jnp.float32)
+            * scale
+        ).astype(jnp.bfloat16)
+
+        scores_col = (
+            jnp.einsum("bip,bjp->bij", donor_feat_all, acceptor_feat, preferred_element_type=jnp.float32)
+            * scale
+        )
+        allowed_col = (donor_eff[:, :, None] >= 0) & (acceptor_pos[:, None, :] > donor_eff[:, :, None])
+        slope_col = pair_slope(scores_col, target_col, allowed_col)
+        acceptor_grad = (
+            jnp.einsum("bij,bip->bjp", slope_col, donor_feat_all, preferred_element_type=jnp.float32)
+            * scale
+        ).astype(jnp.bfloat16)
+
+    if n_seq == 2:
         grad_early = jnp.where(first, early_acceptor, early_donor)
         rows_early = jnp.where(first, acceptor_rows, donor_rows)
-        grad_late = jnp.where(first, donor_grad, acceptor_grad)
         rows_late = jnp.where(first, donor_rows, acceptor_rows)
         donor_grad = jnp.where(first, grad_late, grad_early)
         acceptor_grad = jnp.where(first, grad_early, grad_late)

time: 48.7 us -> 48.3 us (level)
  matrix products: 5.91 us -> 5.38 us
    dot_general x2 -> x1, matrix products: 1.07 us -> 0.56 us  [shards(): jnp.einsum('bij,bjp->bip', slope_late, keys, preferred_element_type=jnp.f...]
    unnamed x17 -> x16, local copies, waits for them, and re-layouts: 2.28 us -> 2.35 us
  transfers between devices with their start and end apart: 13 -> 13, of which waited for: 9 -> 9; matrix products, arithmetic and copies ran while one was open for 14% -> 13% of each run, Pallas kernels for 0% -> 0%
where the time goes in v13:
time: 48.3 us; the launch traced here: 48.1 us
  waiting for transfers between devices  18.4 us (38%)
  starting transfers between devices  16 us (33%)
  local copies, waits for them, and re-layouts  5.48 us (11%)
  matrix products  5.38 us (11%)
  other arithmetic  1.61 us (3%)
  between operations  1.23 us (3%)
    ppermute x3, starting transfers between devices, shards(): lax.ppermute(outgoing, 'head', [(i, i ^ k) for i in range(n_head)])  5.76 us
    ppermute x1, waiting for transfers between devices, shards(): lax.ppermute(held, 'dp', perm).astype(jnp.float32)  4.79 us
    ppermute x3, starting transfers between devices, shards(): lax.ppermute(feat_quarter, 'head', [(i, i ^ k) for i in range(n_head)])  4.45 us
    ppermute x2, waiting for transfers between devices, from_seq_partner(): return lax.ppermute(outgoing, 'seq', [(0, 1), (1, 0)]).astype(jnp.float32)  4.36 us
    ppermute x3, waiting for transfers between devices, shards(): lax.ppermute(outgoing, 'head', [(i, i ^ k) for i in range(n_head)])  3.54 us
    ppermute x3, waiting for transfers between devices, shards(): lax.ppermute(feat_quarter, 'head', [(i, i ^ k) for i in range(n_head)])  3.12 us
    ppermute x2, starting transfers between devices, from_seq_partner(): return lax.ppermute(outgoing, 'seq', [(0, 1), (1, 0)]).astype(jnp.float32)  2.46 us
    ppermute x1, waiting for transfers between devices, shards(): arrived = lax.ppermute(payload, 'seq', perm)  2.37 us
  transfers between devices with their start and end apart: 13, of which 9 were waited for; matrix products, arithmetic and copies ran while one was open for 13% of the time, Pallas kernels for 0%

profile of v13, /device:TPU:0, one launch (start us, length us, event | category | flops | bytes accessed | tf_op | source)
XLA Modules:
  0.0 48.1 jit_solution(847795987910448484)
XLA Ops:
  0.7 0.7 %copy-done.4 = s32[1,128]{1,0:T(1,128)S(1)} copy-done((s32[1,128]{1,0:T(1,128)S(1)}, s32[1,128]{1,0:T(1,128)}, u32[]{:S(2)}) %copy-start.4) | copy-done | bytes 536
  1.4 0.7 %copy-done.5 = s32[1,128]{1,0:T(1,128)S(1)} copy-done((s32[1,128]{1,0:T(1,128)S(1)}, s32[1,128]{1,0:T(1,128)}, u32[]{:S(2)}) %copy-start.5) | copy-done | bytes 536
  2.6 0.7 %copy-done.1 = bf16[384,384]{1,0:T(8,128)(2,1)S(1)} copy-done((bf16[384,384]{1,0:T(8,128)(2,1)S(1)}, bf16[384,384]{1,0:T(8,128)(2,1)}, u32[]{:S(2)}) %copy-start.1) | copy-done | bytes 294936
  4.2 5.1 %collective-permute-start.2 = (bf16[1,64,384]{2,1,0:T(8,128)(2,1)S(1)}, bf16[1,64,384]{2,1,0:T(8,128)(2,1)S(1)}, u32[]{:S(2)}, u32[]{:S(2)}) collective-permute-start(bf16[1,64,384]{2,1,0:T(8,128)(2,1)S(1)} %get-tuple-element.39), channel_id=1, source_target_pairs={{0,3},{1,2},{2,1},{3,0},{4,7},{5,6},{6,5},{7,4},{8,11},{9,10},{10,... | collective-permute-start | bytes 147464 | tf_op jit(solution)/shard_map/ppermute | solution.py:75
  9.3 0.6 %collective-permute-start = (bf16[1,64,384]{2,1,0:T(8,128)(2,1)S(1)}, bf16[1,64,384]{2,1,0:T(8,128)(2,1)S(1)}, u32[]{:S(2)}, u32[]{:S(2)}) collective-permute-start(bf16[1,64,384]{2,1,0:T(8,128)(2,1)S(1)} %get-tuple-element.37), channel_id=1, source_target_pairs={{0,1},{1,0},{2,3},{3,2},{4,5},{5,4},{6,7},{7,6},{8,9},{9,8},{10,11... | collective-permute-start | bytes 147464 | tf_op jit(solution)/shard_map/ppermute | solution.py:75
  10.7 0.8 %collective-permute-done.2 = bf16[1,64,384]{2,1,0:T(8,128)(2,1)S(1)} collective-permute-done((bf16[1,64,384]{2,1,0:T(8,128)(2,1)S(1)}, bf16[1,64,384]{2,1,0:T(8,128)(2,1)S(1)}, u32[]{:S(2)}, u32[]{:S(2)}) %collective-permute-start.2) | collective-permute-done | bytes 49184 | tf_op jit(solution)/shard_map/ppermute | solution.py:75
  11.5 2.8 %collective-permute-done.1 = bf16[1,64,384]{2,1,0:T(8,128)(2,1)S(1)} collective-permute-done((bf16[1,64,384]{2,1,0:T(8,128)(2,1)S(1)}, bf16[1,64,384]{2,1,0:T(8,128)(2,1)S(1)}, u32[]{:S(2)}, u32[]{:S(2)}) %collective-permute-start.1) | collective-permute-done | bytes 49184 | tf_op jit(solution)/shard_map/ppermute | solution.py:75
  14.3 0.6 %gather_fusion = bf16[4,64,384]{2,1,0:T(8,128)(2,1)S(1)} fusion(bf16[4,64,384]{2,1,0:T(8,128)(2,1)S(1)} %maximum_bitcast_fusion, s32[1024]{0:T(1024)S(1)} %pad_clamp_fusion), kind=kCustom, calls=%fused_computation.clone | custom fusion | bytes 393232 | tf_op jit(solution)/shard_map/jit(_take)/gather | solution.py:77
  15.1 2.2 %collective-permute-start.5 = (bf16[1,64,384]{2,1,0:T(8,128)(2,1)S(1)}, bf16[1,64,384]{2,1,0:T(8,128)(2,1)S(1)}, u32[]{:S(2)}, u32[]{:S(2)}) collective-permute-start(bf16[1,64,384]{2,1,0:T(8,128)(2,1)S(1)} %fusion.133), channel_id=1, source_target_pairs={{0,3},{1,2},{2,1},{3,0},{4,7},{5,6},{6,5},{7,4},{8,11},{9,10},{10,... | collective-permute-start | bytes 147464 | tf_op jit(solution)/shard_map/ppermute | solution.py:85
  17.2 2.3 %collective-permute-start.3 = (bf16[1,64,384]{2,1,0:T(8,128)(2,1)S(1)}, bf16[1,64,384]{2,1,0:T(8,128)(2,1)S(1)}, u32[]{:S(2)}, u32[]{:S(2)}) collective-permute-start(bf16[1,64,384]{2,1,0:T(8,128)(2,1)S(1)} %fusion.133), channel_id=1, source_target_pairs={{0,1},{1,0},{2,3},{3,2},{4,5},{5,4},{6,7},{7,6},{8,9},{9,8},{10,11... | collective-permute-start | bytes 147464 | tf_op jit(solution)/shard_map/ppermute | solution.py:85
  19.5 1.7 %collective-permute-done.5 = bf16[1,64,384]{2,1,0:T(8,128)(2,1)S(1)} collective-permute-done((bf16[1,64,384]{2,1,0:T(8,128)(2,1)S(1)}, bf16[1,64,384]{2,1,0:T(8,128)(2,1)S(1)}, u32[]{:S(2)}, u32[]{:S(2)}) %collective-permute-start.5) | collective-permute-done | bytes 49184 | tf_op jit(solution)/shard_map/ppermute | solution.py:85
  21.3 1.4 %collective-permute-done.4 = bf16[1,64,384]{2,1,0:T(8,128)(2,1)S(1)} collective-permute-done((bf16[1,64,384]{2,1,0:T(8,128)(2,1)S(1)}, bf16[1,64,384]{2,1,0:T(8,128)(2,1)S(1)}, u32[]{:S(2)}, u32[]{:S(2)}) %collective-permute-start.4) | collective-permute-done | bytes 49184 | tf_op jit(solution)/shard_map/ppermute | solution.py:85
  22.7 0.6 %gather_fusion.1 = bf16[4,64,384]{2,1,0:T(8,128)(2,1)S(1)} fusion(bf16[4,64,384]{2,1,0:T(8,128)(2,1)S(1)} %maximum_bitcast_fusion.1, s32[1024]{0:T(1024)S(1)} %pad_clamp_fusion), kind=kCustom, calls=%fused_computation.1.clone | custom fusion | bytes 393232 | tf_op jit(solution)/shard_map/jit(_take)/gather | solution.py:86
  23.5 1.6 %collective-permute-start.6 = (bf16[1,179,384]{2,1,0:T(8,128)(2,1)S(1)}, bf16[1,179,384]{2,1,0:T(8,128)(2,1)S(1)}, u32[]{:S(2)}, u32[]{:S(2)}) collective-permute-start(bf16[1,179,384]{2,1,0:T(8,128)(2,1)S(1)} %pad_maximum_fusion.1), channel_id=1, source_target_pairs={{0,4},{4,0},{1,5},{5,1},{2,6},{6,2},{3,7},{7,3},{8,12},{12,8},{9,1... | collective-permute-start | bytes 412424 | tf_op jit(solution)/shard_map/ppermute | solution.py:160
  26.3 2.4 %collective-permute-done.6 = bf16[1,179,384]{2,1,0:T(8,128)(2,1)S(1)} collective-permute-done((bf16[1,179,384]{2,1,0:T(8,128)(2,1)S(1)}, bf16[1,179,384]{2,1,0:T(8,128)(2,1)S(1)}, u32[]{:S(2)}, u32[]{:S(2)}) %collective-permute-start.6) | collective-permute-done | bytes 137504 | tf_op jit(solution)/shard_map/ppermute | solution.py:160
  29.2 0.6 %fusion.3 = bf16[128,384]{1,0:T(8,128)(2,1)S(1)} fusion(bf16[1,256,384]{2,1,0:T(8,128)(2,1)S(1)} %get-tuple-element.41, bf16[1,256,384]{2,1,0:T(8,128)(2,1)S(1)} %get-tuple-element.40, pred[]{:T(512)S(6)} %eq.114, bf16[1,128,256]{2,1,0:T(8,128)(2,1)S(1)} %copy-done.3, bf16[1,256,128]{1,2,0:T(8,128)(2,1)S(1)} %select_dynamic-update-slice_fusion.2, ...), kind=kOutput, calls=%fused_computation.12 | convolution fusion | flops 51429376 | bytes 1218560 | tf_op jit(solution)/shard_map/bij,bjp->bip/dot_general | solution.py:238
  31.1 1.6 %collective-permute-start.9 = (bf16[192,192]{1,0:T(8,128)(2,1)S(1)}, bf16[192,192]{1,0:T(8,128)(2,1)S(1)}, u32[]{:S(2)}, u32[]{:S(2)}) collective-permute-start(bf16[192,192]{1,0:T(8,128)(2,1)S(1)} %constant_dynamic-slice_fusion), channel_id=1, source_target_pairs={{0,4},{4,0},{1,5},{5,1},{2,6},{6,2},{3,7},{7,3},{8,12},{12,8},{9,1... | collective-permute-start | bytes 221192 | tf_op jit(solution)/shard_map/ppermute | solution.py:130
  32.8 0.9 %collective-permute-start.10 = (bf16[192,192]{1,0:T(8,128)(2,1)S(1)}, bf16[192,192]{1,0:T(8,128)(2,1)S(1)}, u32[]{:S(2)}, u32[]{:S(2)}) collective-permute-start(bf16[192,192]{1,0:T(8,128)(2,1)S(1)} %constant_dynamic-slice_fusion.4), channel_id=1, source_target_pairs={{0,4},{4,0},{1,5},{5,1},{2,6},{6,2},{3,7},{7,3},{8,12},{12,8},{9,1... | collective-permute-start | bytes 221192 | tf_op jit(solution)/shard_map/ppermute | solution.py:130
  34.1 2.6 %collective-permute-done.9 = bf16[192,192]{1,0:T(8,128)(2,1)S(1)} collective-permute-done((bf16[192,192]{1,0:T(8,128)(2,1)S(1)}, bf16[192,192]{1,0:T(8,128)(2,1)S(1)}, u32[]{:S(2)}, u32[]{:S(2)}) %collective-permute-start.9) | collective-permute-done | bytes 73760 | tf_op jit(solution)/shard_map/ppermute | solution.py:130
  36.7 1.7 %collective-permute-done.10 = bf16[192,192]{1,0:T(8,128)(2,1)S(1)} collective-permute-done((bf16[192,192]{1,0:T(8,128)(2,1)S(1)}, bf16[192,192]{1,0:T(8,128)(2,1)S(1)}, u32[]{:S(2)}, u32[]{:S(2)}) %collective-permute-start.10) | collective-permute-done | bytes 73760 | tf_op jit(solution)/shard_map/ppermute | solution.py:130
  38.6 1.6 %collective-permute-start.11 = (bf16[2,192,192]{2,1,0:T(8,128)(2,1)S(1)}, bf16[2,192,192]{2,1,0:T(8,128)(2,1)S(1)}, u32[]{:S(2)}, u32[]{:S(2)}) collective-permute-start(bf16[2,192,192]{2,1,0:T(8,128)(2,1)S(1)} %pad_maximum_fusion), channel_id=1, source_target_pairs={{0,16},{8,24},{16,0},{24,8},{1,17},{9,25},{17,1},{25,9},{2,18},{10... | collective-permute-start | bytes 442376 | tf_op jit(solution)/shard_map/ppermute | solution.py:305
  40.3 4.8 %collective-permute-done.11 = bf16[2,192,192]{2,1,0:T(8,128)(2,1)S(1)} collective-permute-done((bf16[2,192,192]{2,1,0:T(8,128)(2,1)S(1)}, bf16[2,192,192]{2,1,0:T(8,128)(2,1)S(1)}, u32[]{:S(2)}, u32[]{:S(2)}) %collective-permute-start.11) | collective-permute-done | bytes 147488 | tf_op jit(solution)/shard_map/ppermute | solution.py:305
  45.7 1.1 %fusion.2 = bf16[1,512,384]{2,1,0:T(8,128)(2,1)} fusion(f32[512,384]{1,0:T(8,128)S(1)} %convolution_add_fusion.1, f32[512,384]{1,0:T(8,128)S(1)} %fusion.12, s32[128]{0:T(128)S(1)} %subtract_bitcast_fusion, f32[128,384]{1,0:T(8,128)S(1)} %fusion.58), kind=kOutput, calls=%fused_computation.8 | convolution fusion | flops 51183616 | bytes 2163200 | tf_op jit(solution)/shard_map/bnr,bnc->brc/dot_general | solution.py:26
  47.3 0.9 %slice_bitcast_fusion = (f32[384,192]{0,1:T(8,128)}, f32[384,192]{0,1:T(8,128)}) fusion(f32[2,384,192]{1,2,0:T(8,128)S(1)} %fusion.9), kind=kLoop, calls=%fused_computation.32 | loop fusion | bytes 1179648 | tf_op jit(solution)/shard_map/squeeze | solution.py:312
  (86 shorter events, 7.2 us)
Async XLA Ops:
  0.6 1.4 %copy-start = (bf16[1,512,384]{2,1,0:T(8,128)(2,1)S(1)}, bf16[1,512,384]{2,1,0:T(8,128)(2,1)}, u32[]{:S(2)}) copy-start(bf16[1,512,384]{2,1,0:T(8,128)(2,1)} %param.12) | copy-start | bytes 1179652
  0.7 0.7 %copy-start.4 = (s32[1,128]{1,0:T(1,128)S(1)}, s32[1,128]{1,0:T(1,128)}, u32[]{:S(2)}) copy-start(s32[1,128]{1,0:T(1,128)} %param.13) | copy-start | bytes 1540
  1.4 0.7 %copy-start.5 = (s32[1,128]{1,0:T(1,128)S(1)}, s32[1,128]{1,0:T(1,128)}, u32[]{:S(2)}) copy-start(s32[1,128]{1,0:T(1,128)} %param.14) | copy-start | bytes 1540
  2.3 1.0 %copy-start.1 = (bf16[384,384]{1,0:T(8,128)(2,1)S(1)}, bf16[384,384]{1,0:T(8,128)(2,1)}, u32[]{:S(2)}) copy-start(bf16[384,384]{1,0:T(8,128)(2,1)} %param.16) | copy-start | bytes 884740
  2.6 1.0 %copy-start.2 = (bf16[384,384]{1,0:T(8,128)(2,1)S(1)}, bf16[384,384]{1,0:T(8,128)(2,1)}, u32[]{:S(2)}) copy-start(bf16[384,384]{1,0:T(8,128)(2,1)} %param.17) | copy-start | bytes 884740
  3.8 6.2 %copy-start.3 = (bf16[1,128,256]{2,1,0:T(8,128)(2,1)S(1)}, bf16[1,128,256]{2,1,0:T(8,128)(2,1)}, u32[]{:S(2)}) copy-start(bf16[1,128,256]{2,1,0:T(8,128)(2,1)} %param.15) | copy-start | bytes 196612
  4.2 7.3 %collective-permute-start.2 = (bf16[1,64,384]{2,1,0:T(8,128)(2,1)S(1)}, bf16[1,64,384]{2,1,0:T(8,128)(2,1)S(1)}, u32[]{:S(2)}, u32[]{:S(2)}) collective-permute-start(bf16[1,64,384]{2,1,0:T(8,128)(2,1)S(1)} %get-tuple-element.39), channel_id=1, source_target_pairs={{0,3},{1,2},{2,1},{3,0},{4,7},{5,6},{6,5},{7,4},{8,11},{9,10},{10,... | collective-permute-start | bytes 147464 | tf_op jit(solution)/shard_map/ppermute | solution.py:75
  9.3 5.0 %collective-permute-start.1 = (bf16[1,64,384]{2,1,0:T(8,128)(2,1)S(1)}, bf16[1,64,384]{2,1,0:T(8,128)(2,1)S(1)}, u32[]{:S(2)}, u32[]{:S(2)}) collective-permute-start(bf16[1,64,384]{2,1,0:T(8,128)(2,1)S(1)} %get-tuple-element.38), channel_id=1, source_target_pairs={{0,2},{1,3},{2,0},{3,1},{4,6},{5,7},{6,4},{7,5},{8,10},{9,11},{10,... | collective-permute-start | bytes 147464 | tf_op jit(solution)/shard_map/ppermute | solution.py:75
  9.3 5.0 %collective-permute-start = (bf16[1,64,384]{2,1,0:T(8,128)(2,1)S(1)}, bf16[1,64,384]{2,1,0:T(8,128)(2,1)S(1)}, u32[]{:S(2)}, u32[]{:S(2)}) collective-permute-start(bf16[1,64,384]{2,1,0:T(8,128)(2,1)S(1)} %get-tuple-element.37), channel_id=1, source_target_pairs={{0,1},{1,0},{2,3},{3,2},{4,5},{5,4},{6,7},{7,6},{8,9},{9,8},{10,11... | collective-permute-start | bytes 147464 | tf_op jit(solution)/shard_map/ppermute | solution.py:75
  15.1 6.2 %collective-permute-start.5 = (bf16[1,64,384]{2,1,0:T(8,128)(2,1)S(1)}, bf16[1,64,384]{2,1,0:T(8,128)(2,1)S(1)}, u32[]{:S(2)}, u32[]{:S(2)}) collective-permute-start(bf16[1,64,384]{2,1,0:T(8,128)(2,1)S(1)} %fusion.133), channel_id=1, source_target_pairs={{0,3},{1,2},{2,1},{3,0},{4,7},{5,6},{6,5},{7,4},{8,11},{9,10},{10,... | collective-permute-start | bytes 147464 | tf_op jit(solution)/shard_map/ppermute | solution.py:85
  17.2 5.4 %collective-permute-start.4 = (bf16[1,64,384]{2,1,0:T(8,128)(2,1)S(1)}, bf16[1,64,384]{2,1,0:T(8,128)(2,1)S(1)}, u32[]{:S(2)}, u32[]{:S(2)}) collective-permute-start(bf16[1,64,384]{2,1,0:T(8,128)(2,1)S(1)} %fusion.133), channel_id=1, source_target_pairs={{0,2},{1,3},{2,0},{3,1},{4,6},{5,7},{6,4},{7,5},{8,10},{9,11},{10,... | collective-permute-start | bytes 147464 | tf_op jit(solution)/shard_map/ppermute | solution.py:85
  17.2 5.4 %collective-permute-start.3 = (bf16[1,64,384]{2,1,0:T(8,128)(2,1)S(1)}, bf16[1,64,384]{2,1,0:T(8,128)(2,1)S(1)}, u32[]{:S(2)}, u32[]{:S(2)}) collective-permute-start(bf16[1,64,384]{2,1,0:T(8,128)(2,1)S(1)} %fusion.133), channel_id=1, source_target_pairs={{0,1},{1,0},{2,3},{3,2},{4,5},{5,4},{6,7},{7,6},{8,9},{9,8},{10,11... | collective-permute-start | bytes 147464 | tf_op jit(solution)/shard_map/ppermute | solution.py:85
  23.5 5.1 %collective-permute-start.6 = (bf16[1,179,384]{2,1,0:T(8,128)(2,1)S(1)}, bf16[1,179,384]{2,1,0:T(8,128)(2,1)S(1)}, u32[]{:S(2)}, u32[]{:S(2)}) collective-permute-start(bf16[1,179,384]{2,1,0:T(8,128)(2,1)S(1)} %pad_maximum_fusion.1), channel_id=1, source_target_pairs={{0,4},{4,0},{1,5},{5,1},{2,6},{6,2},{3,7},{7,3},{8,12},{12,8},{9,1... | collective-permute-start | bytes 412424 | tf_op jit(solution)/shard_map/ppermute | solution.py:160
  26.1 4.8 %collective-permute-start.8 = (bf16[384,192]{1,0:T(8,128)(2,1)S(1)}, bf16[384,192]{1,0:T(8,128)(2,1)S(1)}, u32[]{:S(2)}, u32[]{:S(2)}) collective-permute-start(bf16[384,192]{1,0:T(8,128)(2,1)S(1)} %constant_dynamic-slice_fusion.1), channel_id=1, source_target_pairs={{0,8},{8,0},{16,24},{24,16},{1,9},{9,1},{17,25},{25,17},{2,10},{10... | collective-permute-start | bytes 442376 | tf_op jit(solution)/shard_map/ppermute | solution.py:122
  30.4 2.2 %collective-permute-start.7 = (bf16[384,192]{1,0:T(8,128)(2,1)S(1)}, bf16[384,192]{1,0:T(8,128)(2,1)S(1)}, u32[]{:S(2)}, u32[]{:S(2)}) collective-permute-start(bf16[384,192]{1,0:T(8,128)(2,1)S(1)} %constant_dynamic-slice_fusion.2), channel_id=1, source_target_pairs={{0,8},{8,0},{16,24},{24,16},{1,9},{9,1},{17,25},{25,17},{2,10},{10... | collective-permute-start | bytes 442376 | tf_op jit(solution)/shard_map/ppermute | solution.py:122
  31.1 5.7 %collective-permute-start.9 = (bf16[192,192]{1,0:T(8,128)(2,1)S(1)}, bf16[192,192]{1,0:T(8,128)(2,1)S(1)}, u32[]{:S(2)}, u32[]{:S(2)}) collective-permute-start(bf16[192,192]{1,0:T(8,128)(2,1)S(1)} %constant_dynamic-slice_fusion), channel_id=1, source_target_pairs={{0,4},{4,0},{1,5},{5,1},{2,6},{6,2},{3,7},{7,3},{8,12},{12,8},{9,1... | collective-permute-start | bytes 221192 | tf_op jit(solution)/shard_map/ppermute | solution.py:130
  32.8 5.6 %collective-permute-start.10 = (bf16[192,192]{1,0:T(8,128)(2,1)S(1)}, bf16[192,192]{1,0:T(8,128)(2,1)S(1)}, u32[]{:S(2)}, u32[]{:S(2)}) collective-permute-start(bf16[192,192]{1,0:T(8,128)(2,1)S(1)} %constant_dynamic-slice_fusion.4), channel_id=1, source_target_pairs={{0,4},{4,0},{1,5},{5,1},{2,6},{6,2},{3,7},{7,3},{8,12},{12,8},{9,1... | collective-permute-start | bytes 221192 | tf_op jit(solution)/shard_map/ppermute | solution.py:130
  38.6 6.6 %collective-permute-start.11 = (bf16[2,192,192]{2,1,0:T(8,128)(2,1)S(1)}, bf16[2,192,192]{2,1,0:T(8,128)(2,1)S(1)}, u32[]{:S(2)}, u32[]{:S(2)}) collective-permute-start(bf16[2,192,192]{2,1,0:T(8,128)(2,1)S(1)} %pad_maximum_fusion), channel_id=1, source_target_pairs={{0,16},{8,24},{16,0},{24,8},{1,17},{9,25},{17,1},{25,9},{2,18},{10... | collective-permute-start | bytes 442376 | tf_op jit(solution)/shard_map/ppermute | solution.py:305
  45.2 1.8 %collective-permute-start.12 = (f32[2,192,192]{2,1,0:T(8,128)S(1)}, f32[2,192,192]{2,1,0:T(8,128)S(1)}, u32[]{:S(2)}, u32[]{:S(2)}) collective-permute-start(f32[2,192,192]{2,1,0:T(8,128)S(1)} %convert_add_fusion), channel_id=1, source_target_pairs={{0,8},{8,0},{16,24},{24,16},{1,9},{9,1},{17,25},{25,17},{2,10},{10... | collective-permute-start | bytes 884744 | tf_op jit(solution)/shard_map/ppermute | solution.py:307

commit v14 on v13

--- a/solution.py
+++ b/solution.py
@@ -95,6 +95,15 @@
     channels = embed.shape[2]
     half = channels // 2
     part = width // n_seq
+    def over_dp_bits(value):
+        bit = 2
+        while bit < n_dp:
+            held = value.astype(jnp.bfloat16)
+            perm = [(i, i ^ bit) for i in range(n_dp)]
+            value = held.astype(jnp.float32) + lax.ppermute(held, "dp", perm).astype(jnp.float32)
+            bit *= 2
+        return value
+
     if n_seq == 2:
         target_own = lax.dynamic_slice_in_dim(target, slab * slab_sites, slab_sites, 2)
         scores_own = (
@@ -271,6 +280,8 @@
         from_late = from_seq_partner(out_late)
         sum_early = own_early + from_late
         sum_late = own_late + from_early
+        sum_late = over_dp_bits(sum_late)
+        sum_early = over_dp_bits(sum_early)
         mine = jnp.stack(
             [jnp.where(first, sum_late, sum_early), jnp.where(first, sum_early, sum_late)]
         )
@@ -298,12 +309,8 @@
         "bnp,cp->bnc", acceptor_grad, acceptor_w, preferred_element_type=jnp.float32
     )
     row_grad = place_rows(donor_match, donor_site) + place_rows(acceptor_match, acceptor_site)
-    bit = 2
-    while bit < n_dp:
-        held = mine.astype(jnp.bfloat16)
-        perm = [(i, i ^ bit) for i in range(n_dp)]
-        mine = held.astype(jnp.float32) + lax.ppermute(held, "dp", perm).astype(jnp.float32)
-        bit *= 2
+    if n_seq != 2:
+        mine = over_dp_bits(mine)
     other = lax.ppermute(mine, "dp", [(i, i ^ 1) for i in range(n_dp)])
     mine = jnp.where(pair == 0, jnp.concatenate([mine, other], 2), jnp.concatenate([other, mine], 2))
     mine = jnp.swapaxes(mine, 1, 2)

time: 48.3 us -> 47.1 us (0.975)
  waiting for transfers between devices: 18.4 us -> 15.7 us
  starting transfers between devices: 16 us -> 17.6 us
    ppermute x1 -> x2, starting transfers between devices: 1.56 us -> 3.13 us  [over_dp_bits(): lax.ppermute(held, 'dp', perm).astype(jnp.float32)]
    ppermute x1 -> x2, waiting for transfers between devices: 4.79 us -> 3.28 us  [over_dp_bits(): lax.ppermute(held, 'dp', perm).astype(jnp.float32)]
    ppermute x2, waiting for transfers between devices: 4.36 us -> 3.16 us  [from_seq_partner(): return lax.ppermute(outgoing, 'seq', [(0, 1), (1, 0)]).astype(jnp.float32)]
  transfers between devices with their start and end apart: 13 -> 14, of which waited for: 9 -> 10; matrix products, arithmetic and copies ran while one was open for 13% -> 13% of each run, Pallas kernels for 0% -> 0%
where the time goes in v14:
time: 47.1 us; the launch traced here: 46.9 us
  starting transfers between devices  17.6 us (37%)
  waiting for transfers between devices  15.7 us (33%)
  local copies, waits for them, and re-layouts  5.48 us (12%)
  matrix products  5.39 us (11%)
  other arithmetic  1.6 us (3%)
  between operations  1.23 us (3%)
    ppermute x3, starting transfers between devices, shards(): lax.ppermute(outgoing, 'head', [(i, i ^ k) for i in range(n_head)])  5.76 us
    ppermute x3, starting transfers between devices, shards(): lax.ppermute(feat_quarter, 'head', [(i, i ^ k) for i in range(n_head)])  4.45 us
    ppermute x3, waiting for transfers between devices, shards(): lax.ppermute(outgoing, 'head', [(i, i ^ k) for i in range(n_head)])  3.54 us
    ppermute x2, waiting for transfers between devices, over_dp_bits(): lax.ppermute(held, 'dp', perm).astype(jnp.float32)  3.28 us
    ppermute x2, waiting for transfers between devices, from_seq_partner(): return lax.ppermute(outgoing, 'seq', [(0, 1), (1, 0)]).astype(jnp.float32)  3.16 us
    ppermute x2, starting transfers between devices, over_dp_bits(): lax.ppermute(held, 'dp', perm).astype(jnp.float32)  3.13 us
    ppermute x3, waiting for transfers between devices, shards(): lax.ppermute(feat_quarter, 'head', [(i, i ^ k) for i in range(n_head)])  3.12 us
    ppermute x2, starting transfers between devices, from_seq_partner(): return lax.ppermute(outgoing, 'seq', [(0, 1), (1, 0)]).astype(jnp.float32)  2.45 us
  transfers between devices with their start and end apart: 14, of which 10 were waited for; matrix products, arithmetic and copies ran while one was open for 13% of the time, Pallas kernels for 0%

profile of v14, /device:TPU:0, one launch (start us, length us, event | category | flops | bytes accessed | tf_op | source)
XLA Modules:
  0.0 46.9 jit_solution(3382700112196800128)
XLA Ops:
  0.7 0.7 %copy-done.4 = s32[1,128]{1,0:T(1,128)S(1)} copy-done((s32[1,128]{1,0:T(1,128)S(1)}, s32[1,128]{1,0:T(1,128)}, u32[]{:S(2)}) %copy-start.4) | copy-done | bytes 536
  1.4 0.7 %copy-done.5 = s32[1,128]{1,0:T(1,128)S(1)} copy-done((s32[1,128]{1,0:T(1,128)S(1)}, s32[1,128]{1,0:T(1,128)}, u32[]{:S(2)}) %copy-start.5) | copy-done | bytes 536
  2.6 0.7 %copy-done.1 = bf16[384,384]{1,0:T(8,128)(2,1)S(1)} copy-done((bf16[384,384]{1,0:T(8,128)(2,1)S(1)}, bf16[384,384]{1,0:T(8,128)(2,1)}, u32[]{:S(2)}) %copy-start.1) | copy-done | bytes 294936
  4.2 5.1 %collective-permute-start.2 = (bf16[1,64,384]{2,1,0:T(8,128)(2,1)S(1)}, bf16[1,64,384]{2,1,0:T(8,128)(2,1)S(1)}, u32[]{:S(2)}, u32[]{:S(2)}) collective-permute-start(bf16[1,64,384]{2,1,0:T(8,128)(2,1)S(1)} %get-tuple-element.39), channel_id=1, source_target_pairs={{0,3},{1,2},{2,1},{3,0},{4,7},{5,6},{6,5},{7,4},{8,11},{9,10},{10,... | collective-permute-start | bytes 147464 | tf_op jit(solution)/shard_map/ppermute | solution.py:75
  9.3 0.6 %collective-permute-start = (bf16[1,64,384]{2,1,0:T(8,128)(2,1)S(1)}, bf16[1,64,384]{2,1,0:T(8,128)(2,1)S(1)}, u32[]{:S(2)}, u32[]{:S(2)}) collective-permute-start(bf16[1,64,384]{2,1,0:T(8,128)(2,1)S(1)} %get-tuple-element.37), channel_id=1, source_target_pairs={{0,1},{1,0},{2,3},{3,2},{4,5},{5,4},{6,7},{7,6},{8,9},{9,8},{10,11... | collective-permute-start | bytes 147464 | tf_op jit(solution)/shard_map/ppermute | solution.py:75
  10.7 0.8 %collective-permute-done.2 = bf16[1,64,384]{2,1,0:T(8,128)(2,1)S(1)} collective-permute-done((bf16[1,64,384]{2,1,0:T(8,128)(2,1)S(1)}, bf16[1,64,384]{2,1,0:T(8,128)(2,1)S(1)}, u32[]{:S(2)}, u32[]{:S(2)}) %collective-permute-start.2) | collective-permute-done | bytes 49184 | tf_op jit(solution)/shard_map/ppermute | solution.py:75
  11.5 2.8 %collective-permute-done.1 = bf16[1,64,384]{2,1,0:T(8,128)(2,1)S(1)} collective-permute-done((bf16[1,64,384]{2,1,0:T(8,128)(2,1)S(1)}, bf16[1,64,384]{2,1,0:T(8,128)(2,1)S(1)}, u32[]{:S(2)}, u32[]{:S(2)}) %collective-permute-start.1) | collective-permute-done | bytes 49184 | tf_op jit(solution)/shard_map/ppermute | solution.py:75
  14.3 0.6 %gather_fusion = bf16[4,64,384]{2,1,0:T(8,128)(2,1)S(1)} fusion(bf16[4,64,384]{2,1,0:T(8,128)(2,1)S(1)} %maximum_bitcast_fusion, s32[1024]{0:T(1024)S(1)} %pad_clamp_fusion), kind=kCustom, calls=%fused_computation.clone | custom fusion | bytes 393232 | tf_op jit(solution)/shard_map/jit(_take)/gather | solution.py:77
  15.1 2.2 %collective-permute-start.5 = (bf16[1,64,384]{2,1,0:T(8,128)(2,1)S(1)}, bf16[1,64,384]{2,1,0:T(8,128)(2,1)S(1)}, u32[]{:S(2)}, u32[]{:S(2)}) collective-permute-start(bf16[1,64,384]{2,1,0:T(8,128)(2,1)S(1)} %fusion.131), channel_id=1, source_target_pairs={{0,3},{1,2},{2,1},{3,0},{4,7},{5,6},{6,5},{7,4},{8,11},{9,10},{10,... | collective-permute-start | bytes 147464 | tf_op jit(solution)/shard_map/ppermute | solution.py:85
  17.2 2.3 %collective-permute-start.3 = (bf16[1,64,384]{2,1,0:T(8,128)(2,1)S(1)}, bf16[1,64,384]{2,1,0:T(8,128)(2,1)S(1)}, u32[]{:S(2)}, u32[]{:S(2)}) collective-permute-start(bf16[1,64,384]{2,1,0:T(8,128)(2,1)S(1)} %fusion.131), channel_id=1, source_target_pairs={{0,1},{1,0},{2,3},{3,2},{4,5},{5,4},{6,7},{7,6},{8,9},{9,8},{10,11... | collective-permute-start | bytes 147464 | tf_op jit(solution)/shard_map/ppermute | solution.py:85
  19.5 1.7 %collective-permute-done.5 = bf16[1,64,384]{2,1,0:T(8,128)(2,1)S(1)} collective-permute-done((bf16[1,64,384]{2,1,0:T(8,128)(2,1)S(1)}, bf16[1,64,384]{2,1,0:T(8,128)(2,1)S(1)}, u32[]{:S(2)}, u32[]{:S(2)}) %collective-permute-start.5) | collective-permute-done | bytes 49184 | tf_op jit(solution)/shard_map/ppermute | solution.py:85
  21.3 1.4 %collective-permute-done.4 = bf16[1,64,384]{2,1,0:T(8,128)(2,1)S(1)} collective-permute-done((bf16[1,64,384]{2,1,0:T(8,128)(2,1)S(1)}, bf16[1,64,384]{2,1,0:T(8,128)(2,1)S(1)}, u32[]{:S(2)}, u32[]{:S(2)}) %collective-permute-start.4) | collective-permute-done | bytes 49184 | tf_op jit(solution)/shard_map/ppermute | solution.py:85
  22.7 0.6 %gather_fusion.1 = bf16[4,64,384]{2,1,0:T(8,128)(2,1)S(1)} fusion(bf16[4,64,384]{2,1,0:T(8,128)(2,1)S(1)} %maximum_bitcast_fusion.1, s32[1024]{0:T(1024)S(1)} %pad_clamp_fusion), kind=kCustom, calls=%fused_computation.1.clone | custom fusion | bytes 393232 | tf_op jit(solution)/shard_map/jit(_take)/gather | solution.py:86
  23.5 1.6 %collective-permute-start.6 = (bf16[1,179,384]{2,1,0:T(8,128)(2,1)S(1)}, bf16[1,179,384]{2,1,0:T(8,128)(2,1)S(1)}, u32[]{:S(2)}, u32[]{:S(2)}) collective-permute-start(bf16[1,179,384]{2,1,0:T(8,128)(2,1)S(1)} %pad_maximum_fusion.1), channel_id=1, source_target_pairs={{0,4},{4,0},{1,5},{5,1},{2,6},{6,2},{3,7},{7,3},{8,12},{12,8},{9,1... | collective-permute-start | bytes 412424 | tf_op jit(solution)/shard_map/ppermute | solution.py:169
  26.3 2.4 %collective-permute-done.6 = bf16[1,179,384]{2,1,0:T(8,128)(2,1)S(1)} collective-permute-done((bf16[1,179,384]{2,1,0:T(8,128)(2,1)S(1)}, bf16[1,179,384]{2,1,0:T(8,128)(2,1)S(1)}, u32[]{:S(2)}, u32[]{:S(2)}) %collective-permute-start.6) | collective-permute-done | bytes 137504 | tf_op jit(solution)/shard_map/ppermute | solution.py:169
  31.5 1.6 %collective-permute-start.9 = (bf16[192,192]{1,0:T(8,128)(2,1)S(1)}, bf16[192,192]{1,0:T(8,128)(2,1)S(1)}, u32[]{:S(2)}, u32[]{:S(2)}) collective-permute-start(bf16[192,192]{1,0:T(8,128)(2,1)S(1)} %constant_dynamic-slice_fusion), channel_id=1, source_target_pairs={{0,4},{4,0},{1,5},{5,1},{2,6},{6,2},{3,7},{7,3},{8,12},{12,8},{9,1... | collective-permute-start | bytes 221192 | tf_op jit(solution)/shard_map/ppermute | solution.py:139
  33.2 0.9 %collective-permute-start.11 = (bf16[192,192]{1,0:T(8,128)(2,1)S(1)}, bf16[192,192]{1,0:T(8,128)(2,1)S(1)}, u32[]{:S(2)}, u32[]{:S(2)}) collective-permute-start(bf16[192,192]{1,0:T(8,128)(2,1)S(1)} %constant_dynamic-slice_fusion.4), channel_id=1, source_target_pairs={{0,4},{4,0},{1,5},{5,1},{2,6},{6,2},{3,7},{7,3},{8,12},{12,8},{9,1... | collective-permute-start | bytes 221192 | tf_op jit(solution)/shard_map/ppermute | solution.py:139
  34.1 3.0 %collective-permute-done.9 = bf16[192,192]{1,0:T(8,128)(2,1)S(1)} collective-permute-done((bf16[192,192]{1,0:T(8,128)(2,1)S(1)}, bf16[192,192]{1,0:T(8,128)(2,1)S(1)}, u32[]{:S(2)}, u32[]{:S(2)}) %collective-permute-start.9) | collective-permute-done | bytes 73760 | tf_op jit(solution)/shard_map/ppermute | solution.py:139
  37.2 1.6 %collective-permute-start.10 = (bf16[192,192]{1,0:T(8,128)(2,1)S(1)}, bf16[192,192]{1,0:T(8,128)(2,1)S(1)}, u32[]{:S(2)}, u32[]{:S(2)}) collective-permute-start(bf16[192,192]{1,0:T(8,128)(2,1)S(1)} %add_convert_fusion.3), channel_id=1, source_target_pairs={{0,16},{8,24},{16,0},{24,8},{1,17},{9,25},{17,1},{25,9},{2,18},{10... | collective-permute-start | bytes 221192 | tf_op jit(solution)/shard_map/ppermute | solution.py:103
  38.9 1.6 %collective-permute-start.12 = (bf16[192,192]{1,0:T(8,128)(2,1)S(1)}, bf16[192,192]{1,0:T(8,128)(2,1)S(1)}, u32[]{:S(2)}, u32[]{:S(2)}) collective-permute-start(bf16[192,192]{1,0:T(8,128)(2,1)S(1)} %add_convert_fusion.2), channel_id=1, source_target_pairs={{0,16},{8,24},{16,0},{24,8},{1,17},{9,25},{17,1},{25,9},{2,18},{10... | collective-permute-start | bytes 221192 | tf_op jit(solution)/shard_map/ppermute | solution.py:103
  40.7 1.8 %collective-permute-done.10 = bf16[192,192]{1,0:T(8,128)(2,1)S(1)} collective-permute-done((bf16[192,192]{1,0:T(8,128)(2,1)S(1)}, bf16[192,192]{1,0:T(8,128)(2,1)S(1)}, u32[]{:S(2)}, u32[]{:S(2)}) %collective-permute-start.10) | collective-permute-done | bytes 73760 | tf_op jit(solution)/shard_map/ppermute | solution.py:103
  42.5 1.4 %collective-permute-done.12 = bf16[192,192]{1,0:T(8,128)(2,1)S(1)} collective-permute-done((bf16[192,192]{1,0:T(8,128)(2,1)S(1)}, bf16[192,192]{1,0:T(8,128)(2,1)S(1)}, u32[]{:S(2)}, u32[]{:S(2)}) %collective-permute-start.12) | collective-permute-done | bytes 73760 | tf_op jit(solution)/shard_map/ppermute | solution.py:103
  44.5 1.1 %fusion.2 = bf16[1,512,384]{2,1,0:T(8,128)(2,1)} fusion(f32[512,384]{1,0:T(8,128)S(1)} %convolution_add_fusion.1, f32[512,384]{1,0:T(8,128)S(1)} %fusion.12, s32[128]{0:T(128)S(1)} %subtract_bitcast_fusion, f32[128,384]{1,0:T(8,128)S(1)} %fusion.56), kind=kOutput, calls=%fused_computation.8 | convolution fusion | flops 51183616 | bytes 2163200 | tf_op jit(solution)/shard_map/bnr,bnc->brc/dot_general | solution.py:26
  46.1 0.9 %slice_bitcast_fusion = (f32[384,192]{0,1:T(8,128)}, f32[384,192]{0,1:T(8,128)}) fusion(f32[2,384,192]{1,2,0:T(8,128)S(1)} %fusion.9), kind=kLoop, calls=%fused_computation.32 | loop fusion | bytes 1179648 | tf_op jit(solution)/shard_map/squeeze | solution.py:319
  (89 shorter events, 7.8 us)
Async XLA Ops:
  0.6 1.4 %copy-start = (bf16[1,512,384]{2,1,0:T(8,128)(2,1)S(1)}, bf16[1,512,384]{2,1,0:T(8,128)(2,1)}, u32[]{:S(2)}) copy-start(bf16[1,512,384]{2,1,0:T(8,128)(2,1)} %param.12) | copy-start | bytes 1179652
  0.7 0.7 %copy-start.4 = (s32[1,128]{1,0:T(1,128)S(1)}, s32[1,128]{1,0:T(1,128)}, u32[]{:S(2)}) copy-start(s32[1,128]{1,0:T(1,128)} %param.13) | copy-start | bytes 1540
  1.4 0.7 %copy-start.5 = (s32[1,128]{1,0:T(1,128)S(1)}, s32[1,128]{1,0:T(1,128)}, u32[]{:S(2)}) copy-start(s32[1,128]{1,0:T(1,128)} %param.14) | copy-start | bytes 1540
  2.3 1.0 %copy-start.1 = (bf16[384,384]{1,0:T(8,128)(2,1)S(1)}, bf16[384,384]{1,0:T(8,128)(2,1)}, u32[]{:S(2)}) copy-start(bf16[384,384]{1,0:T(8,128)(2,1)} %param.16) | copy-start | bytes 884740
  2.6 1.0 %copy-start.2 = (bf16[384,384]{1,0:T(8,128)(2,1)S(1)}, bf16[384,384]{1,0:T(8,128)(2,1)}, u32[]{:S(2)}) copy-start(bf16[384,384]{1,0:T(8,128)(2,1)} %param.17) | copy-start | bytes 884740
  3.8 6.2 %copy-start.3 = (bf16[1,128,256]{2,1,0:T(8,128)(2,1)S(1)}, bf16[1,128,256]{2,1,0:T(8,128)(2,1)}, u32[]{:S(2)}) copy-start(bf16[1,128,256]{2,1,0:T(8,128)(2,1)} %param.15) | copy-start | bytes 196612
  4.2 7.3 %collective-permute-start.2 = (bf16[1,64,384]{2,1,0:T(8,128)(2,1)S(1)}, bf16[1,64,384]{2,1,0:T(8,128)(2,1)S(1)}, u32[]{:S(2)}, u32[]{:S(2)}) collective-permute-start(bf16[1,64,384]{2,1,0:T(8,128)(2,1)S(1)} %get-tuple-element.39), channel_id=1, source_target_pairs={{0,3},{1,2},{2,1},{3,0},{4,7},{5,6},{6,5},{7,4},{8,11},{9,10},{10,... | collective-permute-start | bytes 147464 | tf_op jit(solution)/shard_map/ppermute | solution.py:75
  9.3 5.0 %collective-permute-start.1 = (bf16[1,64,384]{2,1,0:T(8,128)(2,1)S(1)}, bf16[1,64,384]{2,1,0:T(8,128)(2,1)S(1)}, u32[]{:S(2)}, u32[]{:S(2)}) collective-permute-start(bf16[1,64,384]{2,1,0:T(8,128)(2,1)S(1)} %get-tuple-element.38), channel_id=1, source_target_pairs={{0,2},{1,3},{2,0},{3,1},{4,6},{5,7},{6,4},{7,5},{8,10},{9,11},{10,... | collective-permute-start | bytes 147464 | tf_op jit(solution)/shard_map/ppermute | solution.py:75
  9.3 5.0 %collective-permute-start = (bf16[1,64,384]{2,1,0:T(8,128)(2,1)S(1)}, bf16[1,64,384]{2,1,0:T(8,128)(2,1)S(1)}, u32[]{:S(2)}, u32[]{:S(2)}) collective-permute-start(bf16[1,64,384]{2,1,0:T(8,128)(2,1)S(1)} %get-tuple-element.37), channel_id=1, source_target_pairs={{0,1},{1,0},{2,3},{3,2},{4,5},{5,4},{6,7},{7,6},{8,9},{9,8},{10,11... | collective-permute-start | bytes 147464 | tf_op jit(solution)/shard_map/ppermute | solution.py:75
  15.1 6.2 %collective-permute-start.5 = (bf16[1,64,384]{2,1,0:T(8,128)(2,1)S(1)}, bf16[1,64,384]{2,1,0:T(8,128)(2,1)S(1)}, u32[]{:S(2)}, u32[]{:S(2)}) collective-permute-start(bf16[1,64,384]{2,1,0:T(8,128)(2,1)S(1)} %fusion.131), channel_id=1, source_target_pairs={{0,3},{1,2},{2,1},{3,0},{4,7},{5,6},{6,5},{7,4},{8,11},{9,10},{10,... | collective-permute-start | bytes 147464 | tf_op jit(solution)/shard_map/ppermute | solution.py:85
  17.2 5.4 %collective-permute-start.4 = (bf16[1,64,384]{2,1,0:T(8,128)(2,1)S(1)}, bf16[1,64,384]{2,1,0:T(8,128)(2,1)S(1)}, u32[]{:S(2)}, u32[]{:S(2)}) collective-permute-start(bf16[1,64,384]{2,1,0:T(8,128)(2,1)S(1)} %fusion.131), channel_id=1, source_target_pairs={{0,2},{1,3},{2,0},{3,1},{4,6},{5,7},{6,4},{7,5},{8,10},{9,11},{10,... | collective-permute-start | bytes 147464 | tf_op jit(solution)/shard_map/ppermute | solution.py:85
  17.2 5.4 %collective-permute-start.3 = (bf16[1,64,384]{2,1,0:T(8,128)(2,1)S(1)}, bf16[1,64,384]{2,1,0:T(8,128)(2,1)S(1)}, u32[]{:S(2)}, u32[]{:S(2)}) collective-permute-start(bf16[1,64,384]{2,1,0:T(8,128)(2,1)S(1)} %fusion.131), channel_id=1, source_target_pairs={{0,1},{1,0},{2,3},{3,2},{4,5},{5,4},{6,7},{7,6},{8,9},{9,8},{10,11... | collective-permute-start | bytes 147464 | tf_op jit(solution)/shard_map/ppermute | solution.py:85
  23.5 5.1 %collective-permute-start.6 = (bf16[1,179,384]{2,1,0:T(8,128)(2,1)S(1)}, bf16[1,179,384]{2,1,0:T(8,128)(2,1)S(1)}, u32[]{:S(2)}, u32[]{:S(2)}) collective-permute-start(bf16[1,179,384]{2,1,0:T(8,128)(2,1)S(1)} %pad_maximum_fusion.1), channel_id=1, source_target_pairs={{0,4},{4,0},{1,5},{5,1},{2,6},{6,2},{3,7},{7,3},{8,12},{12,8},{9,1... | collective-permute-start | bytes 412424 | tf_op jit(solution)/shard_map/ppermute | solution.py:169
  26.1 5.2 %collective-permute-start.8 = (bf16[384,192]{1,0:T(8,128)(2,1)S(1)}, bf16[384,192]{1,0:T(8,128)(2,1)S(1)}, u32[]{:S(2)}, u32[]{:S(2)}) collective-permute-start(bf16[384,192]{1,0:T(8,128)(2,1)S(1)} %constant_dynamic-slice_fusion.1), channel_id=1, source_target_pairs={{0,8},{8,0},{16,24},{24,16},{1,9},{9,1},{17,25},{25,17},{2,10},{10... | collective-permute-start | bytes 442376 | tf_op jit(solution)/shard_map/ppermute | solution.py:131
  30.8 2.2 %collective-permute-start.7 = (bf16[384,192]{1,0:T(8,128)(2,1)S(1)}, bf16[384,192]{1,0:T(8,128)(2,1)S(1)}, u32[]{:S(2)}, u32[]{:S(2)}) collective-permute-start(bf16[384,192]{1,0:T(8,128)(2,1)S(1)} %constant_dynamic-slice_fusion.2), channel_id=1, source_target_pairs={{0,8},{8,0},{16,24},{24,16},{1,9},{9,1},{17,25},{25,17},{2,10},{10... | collective-permute-start | bytes 442376 | tf_op jit(solution)/shard_map/ppermute | solution.py:131
  31.5 5.7 %collective-permute-start.9 = (bf16[192,192]{1,0:T(8,128)(2,1)S(1)}, bf16[192,192]{1,0:T(8,128)(2,1)S(1)}, u32[]{:S(2)}, u32[]{:S(2)}) collective-permute-start(bf16[192,192]{1,0:T(8,128)(2,1)S(1)} %constant_dynamic-slice_fusion), channel_id=1, source_target_pairs={{0,4},{4,0},{1,5},{5,1},{2,6},{6,2},{3,7},{7,3},{8,12},{12,8},{9,1... | collective-permute-start | bytes 221192 | tf_op jit(solution)/shard_map/ppermute | solution.py:139
  33.2 5.6 %collective-permute-start.11 = (bf16[192,192]{1,0:T(8,128)(2,1)S(1)}, bf16[192,192]{1,0:T(8,128)(2,1)S(1)}, u32[]{:S(2)}, u32[]{:S(2)}) collective-permute-start(bf16[192,192]{1,0:T(8,128)(2,1)S(1)} %constant_dynamic-slice_fusion.4), channel_id=1, source_target_pairs={{0,4},{4,0},{1,5},{5,1},{2,6},{6,2},{3,7},{7,3},{8,12},{12,8},{9,1... | collective-permute-start | bytes 221192 | tf_op jit(solution)/shard_map/ppermute | solution.py:139
  37.2 5.4 %collective-permute-start.10 = (bf16[192,192]{1,0:T(8,128)(2,1)S(1)}, bf16[192,192]{1,0:T(8,128)(2,1)S(1)}, u32[]{:S(2)}, u32[]{:S(2)}) collective-permute-start(bf16[192,192]{1,0:T(8,128)(2,1)S(1)} %add_convert_fusion.3), channel_id=1, source_target_pairs={{0,16},{8,24},{16,0},{24,8},{1,17},{9,25},{17,1},{25,9},{2,18},{10... | collective-permute-start | bytes 221192 | tf_op jit(solution)/shard_map/ppermute | solution.py:103
  38.9 5.1 %collective-permute-start.12 = (bf16[192,192]{1,0:T(8,128)(2,1)S(1)}, bf16[192,192]{1,0:T(8,128)(2,1)S(1)}, u32[]{:S(2)}, u32[]{:S(2)}) collective-permute-start(bf16[192,192]{1,0:T(8,128)(2,1)S(1)} %add_convert_fusion.2), channel_id=1, source_target_pairs={{0,16},{8,24},{16,0},{24,8},{1,17},{9,25},{17,1},{25,9},{2,18},{10... | collective-permute-start | bytes 221192 | tf_op jit(solution)/shard_map/ppermute | solution.py:103
  44.0 1.8 %collective-permute-start.13 = (f32[2,192,192]{2,1,0:T(8,128)S(1)}, f32[2,192,192]{2,1,0:T(8,128)S(1)}, u32[]{:S(2)}, u32[]{:S(2)}) collective-permute-start(f32[2,192,192]{2,1,0:T(8,128)S(1)} %pad_maximum_fusion), channel_id=1, source_target_pairs={{0,8},{8,0},{16,24},{24,16},{1,9},{9,1},{17,25},{25,17},{2,10},{10... | collective-permute-start | bytes 884744 | tf_op jit(solution)/shard_map/ppermute | solution.py:314

commit v15 on v14

--- a/solution.py
+++ b/solution.py
@@ -281,10 +281,6 @@
         sum_early = own_early + from_late
         sum_late = own_late + from_early
         sum_late = over_dp_bits(sum_late)
-        sum_early = over_dp_bits(sum_early)
-        mine = jnp.stack(
-            [jnp.where(first, sum_late, sum_early), jnp.where(first, sum_early, sum_late)]
-        )
     else:
         local_dw = jnp.einsum(
             "bnc,bnp->pc", donor_rows, donor_grad, preferred_element_type=jnp.float32
@@ -309,10 +305,23 @@
         "bnp,cp->bnc", acceptor_grad, acceptor_w, preferred_element_type=jnp.float32
     )
     row_grad = place_rows(donor_match, donor_site) + place_rows(acceptor_match, acceptor_site)
-    if n_seq != 2:
-        mine = over_dp_bits(mine)
-    other = lax.ppermute(mine, "dp", [(i, i ^ 1) for i in range(n_dp)])
-    mine = jnp.where(pair == 0, jnp.concatenate([mine, other], 2), jnp.concatenate([other, mine], 2))
+
+    def with_partner_half(value):
+        other = lax.ppermute(value, "dp", [(i, i ^ 1) for i in range(n_dp)])
+        axis = value.ndim - 1
+        return jnp.where(
+            pair == 0, jnp.concatenate([value, other], axis), jnp.concatenate([other, value], axis)
+        )
+
+    if n_seq == 2:
+        late_full = with_partner_half(sum_late)
+        sum_early, row_grad = lax.optimization_barrier((sum_early, row_grad))
+        early_full = with_partner_half(over_dp_bits(sum_early))
+        mine = jnp.stack(
+            [jnp.where(first, late_full, early_full), jnp.where(first, early_full, late_full)]
+        )
+    else:
+        mine = with_partner_half(over_dp_bits(mine))
     mine = jnp.swapaxes(mine, 1, 2)
     column_major = Layout(major_to_minor=(1, 0))
     grad_dw = with_layout_constraint(mine[0], column_major)

time: 47.1 us -> 50.8 us (1.079)
  waiting for transfers between devices: 15.7 us -> 18.7 us
  starting transfers between devices: 17.6 us -> 18.2 us
    ppermute x3, waiting for transfers between devices: 3.54 us -> 5.07 us  [shards(): lax.ppermute(outgoing, 'head', [(i, i ^ k) for i in range(n_head)])]
    ppermute x1 -> x2, waiting for transfers between devices: 0.19 us -> 1.42 us  [with_partner_half(): other = lax.ppermute(value, 'dp', [(i, i ^ 1) for i in range(n_dp)])]
    ppermute x3, waiting for transfers between devices: 3.12 us -> 2.36 us  [shards(): lax.ppermute(feat_quarter, 'head', [(i, i ^ k) for i in range(n_head)])]
    ppermute x2, starting transfers between devices: 2.45 us -> 3.18 us  [from_seq_partner(): return lax.ppermute(outgoing, 'seq', [(0, 1), (1, 0)]).astype(jnp.float32)]
    ppermute x2, waiting for transfers between devices: 3.16 us -> 3.75 us  [from_seq_partner(): return lax.ppermute(outgoing, 'seq', [(0, 1), (1, 0)]).astype(jnp.float32)]
    unnamed x16 -> x15, local copies, waits for them, and re-layouts: 2.35 us -> 2.22 us
  transfers between devices with their start and end apart: 14 -> 15, of which waited for: 10 -> 11; matrix products, arithmetic and copies ran while one was open for 13% -> 12% of each run, Pallas kernels for 0% -> 0%
where the time goes in v15:
time: 50.8 us; the launch traced here: 50.6 us
  waiting for transfers between devices  18.7 us (37%)
  starting transfers between devices  18.2 us (36%)
  local copies, waits for them, and re-layouts  5.45 us (11%)
  matrix products  5.4 us (11%)
  other arithmetic  1.61 us (3%)
  between operations  1.25 us (2%)
    ppermute x3, starting transfers between devices, shards(): lax.ppermute(outgoing, 'head', [(i, i ^ k) for i in range(n_head)])  5.68 us
    ppermute x3, waiting for transfers between devices, shards(): lax.ppermute(outgoing, 'head', [(i, i ^ k) for i in range(n_head)])  5.07 us
    ppermute x3, starting transfers between devices, shards(): lax.ppermute(feat_quarter, 'head', [(i, i ^ k) for i in range(n_head)])  4.45 us
    ppermute x2, waiting for transfers between devices, from_seq_partner(): return lax.ppermute(outgoing, 'seq', [(0, 1), (1, 0)]).astype(jnp.float32)  3.75 us
    ppermute x2, starting transfers between devices, from_seq_partner(): return lax.ppermute(outgoing, 'seq', [(0, 1), (1, 0)]).astype(jnp.float32)  3.18 us
    ppermute x2, starting transfers between devices, over_dp_bits(): lax.ppermute(held, 'dp', perm).astype(jnp.float32)  3.05 us
    ppermute x2, waiting for transfers between devices, over_dp_bits(): lax.ppermute(held, 'dp', perm).astype(jnp.float32)  3.01 us
    ppermute x1, waiting for transfers between devices, shards(): arrived = lax.ppermute(payload, 'seq', perm)  2.83 us
  transfers between devices with their start and end apart: 15, of which 11 were waited for; matrix products, arithmetic and copies ran while one was open for 12% of the time, Pallas kernels for 0%

profile of v15, /device:TPU:0, one launch (start us, length us, event | category | flops | bytes accessed | tf_op | source)
XLA Modules:
  0.0 50.6 jit_solution(14223842279538550204)
XLA Ops:
  0.7 0.7 %copy-done.5 = s32[1,128]{1,0:T(1,128)S(1)} copy-done((s32[1,128]{1,0:T(1,128)S(1)}, s32[1,128]{1,0:T(1,128)}, u32[]{:S(2)}) %copy-start.5) | copy-done | bytes 536
  1.4 0.7 %copy-done.4 = s32[1,128]{1,0:T(1,128)S(1)} copy-done((s32[1,128]{1,0:T(1,128)S(1)}, s32[1,128]{1,0:T(1,128)}, u32[]{:S(2)}) %copy-start.4) | copy-done | bytes 536
  2.6 0.6 %copy-done.1 = bf16[384,384]{1,0:T(8,128)(2,1)S(1)} copy-done((bf16[384,384]{1,0:T(8,128)(2,1)S(1)}, bf16[384,384]{1,0:T(8,128)(2,1)}, u32[]{:S(2)}) %copy-start.1) | copy-done | bytes 294936
  4.2 3.1 %collective-permute-start = (bf16[1,64,384]{2,1,0:T(8,128)(2,1)S(1)}, bf16[1,64,384]{2,1,0:T(8,128)(2,1)S(1)}, u32[]{:S(2)}, u32[]{:S(2)}) collective-permute-start(bf16[1,64,384]{2,1,0:T(8,128)(2,1)S(1)} %get-tuple-element.47), channel_id=1, source_target_pairs={{0,1},{1,0},{2,3},{3,2},{4,5},{5,4},{6,7},{7,6},{8,9},{9,8},{10,11... | collective-permute-start | bytes 147464 | tf_op jit(solution)/shard_map/ppermute | solution.py:75
  7.3 2.6 %collective-permute-start.1 = (bf16[1,64,384]{2,1,0:T(8,128)(2,1)S(1)}, bf16[1,64,384]{2,1,0:T(8,128)(2,1)S(1)}, u32[]{:S(2)}, u32[]{:S(2)}) collective-permute-start(bf16[1,64,384]{2,1,0:T(8,128)(2,1)S(1)} %get-tuple-element.48), channel_id=1, source_target_pairs={{0,2},{1,3},{2,0},{3,1},{4,6},{5,7},{6,4},{7,5},{8,10},{9,11},{10,... | collective-permute-start | bytes 147464 | tf_op jit(solution)/shard_map/ppermute | solution.py:75
  10.7 2.5 %collective-permute-done.1 = bf16[1,64,384]{2,1,0:T(8,128)(2,1)S(1)} collective-permute-done((bf16[1,64,384]{2,1,0:T(8,128)(2,1)S(1)}, bf16[1,64,384]{2,1,0:T(8,128)(2,1)S(1)}, u32[]{:S(2)}, u32[]{:S(2)}) %collective-permute-start.1) | collective-permute-done | bytes 49184 | tf_op jit(solution)/shard_map/ppermute | solution.py:75
  13.2 2.6 %collective-permute-done.2 = bf16[1,64,384]{2,1,0:T(8,128)(2,1)S(1)} collective-permute-done((bf16[1,64,384]{2,1,0:T(8,128)(2,1)S(1)}, bf16[1,64,384]{2,1,0:T(8,128)(2,1)S(1)}, u32[]{:S(2)}, u32[]{:S(2)}) %collective-permute-start.2) | collective-permute-done | bytes 49184 | tf_op jit(solution)/shard_map/ppermute | solution.py:75
  15.8 0.6 %gather_fusion = bf16[4,64,384]{2,1,0:T(8,128)(2,1)S(1)} fusion(bf16[4,64,384]{2,1,0:T(8,128)(2,1)S(1)} %maximum_bitcast_fusion.1, s32[1024]{0:T(1024)S(1)} %pad_clamp_fusion), kind=kCustom, calls=%fused_computation.clone | custom fusion | bytes 393232 | tf_op jit(solution)/shard_map/jit(_take)/gather | solution.py:77
  16.5 0.8 %collective-permute-start.5 = (bf16[1,64,384]{2,1,0:T(8,128)(2,1)S(1)}, bf16[1,64,384]{2,1,0:T(8,128)(2,1)S(1)}, u32[]{:S(2)}, u32[]{:S(2)}) collective-permute-start(bf16[1,64,384]{2,1,0:T(8,128)(2,1)S(1)} %fusion.131), channel_id=1, source_target_pairs={{0,3},{1,2},{2,1},{3,0},{4,7},{5,6},{6,5},{7,4},{8,11},{9,10},{10,... | collective-permute-start | bytes 147464 | tf_op jit(solution)/shard_map/ppermute | solution.py:85
  17.3 3.6 %collective-permute-start.3 = (bf16[1,64,384]{2,1,0:T(8,128)(2,1)S(1)}, bf16[1,64,384]{2,1,0:T(8,128)(2,1)S(1)}, u32[]{:S(2)}, u32[]{:S(2)}) collective-permute-start(bf16[1,64,384]{2,1,0:T(8,128)(2,1)S(1)} %fusion.131), channel_id=1, source_target_pairs={{0,1},{1,0},{2,3},{3,2},{4,5},{5,4},{6,7},{7,6},{8,9},{9,8},{10,11... | collective-permute-start | bytes 147464 | tf_op jit(solution)/shard_map/ppermute | solution.py:85
  21.0 1.6 %collective-permute-done.5 = bf16[1,64,384]{2,1,0:T(8,128)(2,1)S(1)} collective-permute-done((bf16[1,64,384]{2,1,0:T(8,128)(2,1)S(1)}, bf16[1,64,384]{2,1,0:T(8,128)(2,1)S(1)}, u32[]{:S(2)}, u32[]{:S(2)}) %collective-permute-start.5) | collective-permute-done | bytes 49184 | tf_op jit(solution)/shard_map/ppermute | solution.py:85
  22.6 0.8 %collective-permute-done.4 = bf16[1,64,384]{2,1,0:T(8,128)(2,1)S(1)} collective-permute-done((bf16[1,64,384]{2,1,0:T(8,128)(2,1)S(1)}, bf16[1,64,384]{2,1,0:T(8,128)(2,1)S(1)}, u32[]{:S(2)}, u32[]{:S(2)}) %collective-permute-start.4) | collective-permute-done | bytes 49184 | tf_op jit(solution)/shard_map/ppermute | solution.py:85
  24.6 1.6 %collective-permute-start.7 = (bf16[1,179,384]{2,1,0:T(8,128)(2,1)S(1)}, bf16[1,179,384]{2,1,0:T(8,128)(2,1)S(1)}, u32[]{:S(2)}, u32[]{:S(2)}) collective-permute-start(bf16[1,179,384]{2,1,0:T(8,128)(2,1)S(1)} %pad_maximum_fusion), channel_id=1, source_target_pairs={{0,4},{4,0},{1,5},{5,1},{2,6},{6,2},{3,7},{7,3},{8,12},{12,8},{9,1... | collective-permute-start | bytes 412424 | tf_op jit(solution)/shard_map/ppermute | solution.py:169
  27.0 2.8 %collective-permute-done.7 = bf16[1,179,384]{2,1,0:T(8,128)(2,1)S(1)} collective-permute-done((bf16[1,179,384]{2,1,0:T(8,128)(2,1)S(1)}, bf16[1,179,384]{2,1,0:T(8,128)(2,1)S(1)}, u32[]{:S(2)}, u32[]{:S(2)}) %collective-permute-start.7) | collective-permute-done | bytes 137504 | tf_op jit(solution)/shard_map/ppermute | solution.py:169
  33.5 1.6 %collective-permute-start.9 = (bf16[192,192]{1,0:T(8,128)(2,1)S(1)}, bf16[192,192]{1,0:T(8,128)(2,1)S(1)}, u32[]{:S(2)}, u32[]{:S(2)}) collective-permute-start(bf16[192,192]{1,0:T(8,128)(2,1)S(1)} %constant_dynamic-slice_fusion), channel_id=1, source_target_pairs={{0,4},{4,0},{1,5},{5,1},{2,6},{6,2},{3,7},{7,3},{8,12},{12,8},{9,1... | collective-permute-start | bytes 221192 | tf_op jit(solution)/shard_map/ppermute | solution.py:139
  35.2 3.3 %collective-permute-done.9 = bf16[192,192]{1,0:T(8,128)(2,1)S(1)} collective-permute-done((bf16[192,192]{1,0:T(8,128)(2,1)S(1)}, bf16[192,192]{1,0:T(8,128)(2,1)S(1)}, u32[]{:S(2)}, u32[]{:S(2)}) %collective-permute-start.9) | collective-permute-done | bytes 73760 | tf_op jit(solution)/shard_map/ppermute | solution.py:139
  38.5 1.6 %collective-permute-start.10 = (bf16[192,192]{1,0:T(8,128)(2,1)S(1)}, bf16[192,192]{1,0:T(8,128)(2,1)S(1)}, u32[]{:S(2)}, u32[]{:S(2)}) collective-permute-start(bf16[192,192]{1,0:T(8,128)(2,1)S(1)} %get-tuple-element.32), channel_id=1, source_target_pairs={{0,4},{4,0},{1,5},{5,1},{2,6},{6,2},{3,7},{7,3},{8,12},{12,8},{9,1... | collective-permute-start | bytes 221192 | tf_op jit(solution)/shard_map/ppermute | solution.py:139
  40.1 1.1 %fusion.1 = bf16[1,512,384]{2,1,0:T(8,128)(2,1)} fusion(f32[512,384]{1,0:T(8,128)S(1)} %convolution_add_fusion.1, f32[512,384]{1,0:T(8,128)S(1)} %fusion.10, s32[128]{0:T(128)S(1)} %subtract_bitcast_fusion, f32[128,384]{1,0:T(8,128)S(1)} %fusion.52), kind=kOutput, calls=%fused_computation.4 | convolution fusion | flops 51183616 | bytes 2163200 | tf_op jit(solution)/shard_map/bnr,bnc->brc/dot_general | solution.py:26
  41.3 1.5 %collective-permute-start.13 = (bf16[192,192]{1,0:T(8,128)(2,1)S(1)}, bf16[192,192]{1,0:T(8,128)(2,1)S(1)}, u32[]{:S(2)}, u32[]{:S(2)}) collective-permute-start(bf16[192,192]{1,0:T(8,128)(2,1)S(1)} %get-tuple-element.33), channel_id=1, source_target_pairs={{0,16},{8,24},{16,0},{24,8},{1,17},{9,25},{17,1},{25,9},{2,18},{10... | collective-permute-start | bytes 221192 | tf_op jit(solution)/shard_map/ppermute | solution.py:103
  43.2 1.6 %collective-permute-start.11 = (bf16[192,192]{1,0:T(8,128)(2,1)S(1)}, bf16[192,192]{1,0:T(8,128)(2,1)S(1)}, u32[]{:S(2)}, u32[]{:S(2)}) collective-permute-start(bf16[192,192]{1,0:T(8,128)(2,1)S(1)} %add_convert_fusion.2), channel_id=1, source_target_pairs={{0,16},{8,24},{16,0},{24,8},{1,17},{9,25},{17,1},{25,9},{2,18},{10... | collective-permute-start | bytes 221192 | tf_op jit(solution)/shard_map/ppermute | solution.py:103
  44.8 1.6 %collective-permute-done.13 = bf16[192,192]{1,0:T(8,128)(2,1)S(1)} collective-permute-done((bf16[192,192]{1,0:T(8,128)(2,1)S(1)}, bf16[192,192]{1,0:T(8,128)(2,1)S(1)}, u32[]{:S(2)}, u32[]{:S(2)}) %collective-permute-start.13) | collective-permute-done | bytes 73760 | tf_op jit(solution)/shard_map/ppermute | solution.py:103
  46.5 1.4 %collective-permute-done.11 = bf16[192,192]{1,0:T(8,128)(2,1)S(1)} collective-permute-done((bf16[192,192]{1,0:T(8,128)(2,1)S(1)}, bf16[192,192]{1,0:T(8,128)(2,1)S(1)}, u32[]{:S(2)}, u32[]{:S(2)}) %collective-permute-start.11) | collective-permute-done | bytes 73760 | tf_op jit(solution)/shard_map/ppermute | solution.py:103
  48.1 1.4 %collective-permute-done.12 = f32[192,192]{1,0:T(8,128)S(1)} collective-permute-done((f32[192,192]{1,0:T(8,128)S(1)}, f32[192,192]{1,0:T(8,128)S(1)}, u32[]{:S(2)}, u32[]{:S(2)}) %collective-permute-start.12) | collective-permute-done | bytes 147488 | tf_op jit(solution)/shard_map/ppermute | solution.py:310
  49.8 0.9 %slice_bitcast_fusion = (f32[384,192]{0,1:T(8,128)}, f32[384,192]{0,1:T(8,128)}) fusion(f32[2,384,192]{1,2,0:T(8,128)S(1)} %maximum_bitcast_fusion), kind=kLoop, calls=%fused_computation.29 | loop fusion | bytes 1179648 | tf_op jit(solution)/shard_map/squeeze | solution.py:328
  (91 shorter events, 8.9 us)
Async XLA Ops:
  0.6 1.4 %copy-start = (bf16[1,512,384]{2,1,0:T(8,128)(2,1)S(1)}, bf16[1,512,384]{2,1,0:T(8,128)(2,1)}, u32[]{:S(2)}) copy-start(bf16[1,512,384]{2,1,0:T(8,128)(2,1)} %param.12) | copy-start | bytes 1179652
  0.7 0.7 %copy-start.5 = (s32[1,128]{1,0:T(1,128)S(1)}, s32[1,128]{1,0:T(1,128)}, u32[]{:S(2)}) copy-start(s32[1,128]{1,0:T(1,128)} %param.14) | copy-start | bytes 1540
  1.4 0.7 %copy-start.4 = (s32[1,128]{1,0:T(1,128)S(1)}, s32[1,128]{1,0:T(1,128)}, u32[]{:S(2)}) copy-start(s32[1,128]{1,0:T(1,128)} %param.13) | copy-start | bytes 1540
  2.3 1.0 %copy-start.1 = (bf16[384,384]{1,0:T(8,128)(2,1)S(1)}, bf16[384,384]{1,0:T(8,128)(2,1)}, u32[]{:S(2)}) copy-start(bf16[384,384]{1,0:T(8,128)(2,1)} %param.17) | copy-start | bytes 884740
  2.6 1.0 %copy-start.2 = (bf16[384,384]{1,0:T(8,128)(2,1)S(1)}, bf16[384,384]{1,0:T(8,128)(2,1)}, u32[]{:S(2)}) copy-start(bf16[384,384]{1,0:T(8,128)(2,1)} %param.16) | copy-start | bytes 884740
  3.8 6.1 %copy-start.3 = (bf16[1,128,256]{2,1,0:T(8,128)(2,1)S(1)}, bf16[1,128,256]{2,1,0:T(8,128)(2,1)}, u32[]{:S(2)}) copy-start(bf16[1,128,256]{2,1,0:T(8,128)(2,1)} %param.15) | copy-start | bytes 196612
  4.2 6.5 %collective-permute-start = (bf16[1,64,384]{2,1,0:T(8,128)(2,1)S(1)}, bf16[1,64,384]{2,1,0:T(8,128)(2,1)S(1)}, u32[]{:S(2)}, u32[]{:S(2)}) collective-permute-start(bf16[1,64,384]{2,1,0:T(8,128)(2,1)S(1)} %get-tuple-element.47), channel_id=1, source_target_pairs={{0,1},{1,0},{2,3},{3,2},{4,5},{5,4},{6,7},{7,6},{8,9},{9,8},{10,11... | collective-permute-start | bytes 147464 | tf_op jit(solution)/shard_map/ppermute | solution.py:75
  7.3 5.9 %collective-permute-start.1 = (bf16[1,64,384]{2,1,0:T(8,128)(2,1)S(1)}, bf16[1,64,384]{2,1,0:T(8,128)(2,1)S(1)}, u32[]{:S(2)}, u32[]{:S(2)}) collective-permute-start(bf16[1,64,384]{2,1,0:T(8,128)(2,1)S(1)} %get-tuple-element.48), channel_id=1, source_target_pairs={{0,2},{1,3},{2,0},{3,1},{4,6},{5,7},{6,4},{7,5},{8,10},{9,11},{10,... | collective-permute-start | bytes 147464 | tf_op jit(solution)/shard_map/ppermute | solution.py:75
  9.8 5.9 %collective-permute-start.2 = (bf16[1,64,384]{2,1,0:T(8,128)(2,1)S(1)}, bf16[1,64,384]{2,1,0:T(8,128)(2,1)S(1)}, u32[]{:S(2)}, u32[]{:S(2)}) collective-permute-start(bf16[1,64,384]{2,1,0:T(8,128)(2,1)S(1)} %get-tuple-element.49), channel_id=1, source_target_pairs={{0,3},{1,2},{2,1},{3,0},{4,7},{5,6},{6,5},{7,4},{8,11},{9,10},{10,... | collective-permute-start | bytes 147464 | tf_op jit(solution)/shard_map/ppermute | solution.py:75
  16.5 6.1 %collective-permute-start.5 = (bf16[1,64,384]{2,1,0:T(8,128)(2,1)S(1)}, bf16[1,64,384]{2,1,0:T(8,128)(2,1)S(1)}, u32[]{:S(2)}, u32[]{:S(2)}) collective-permute-start(bf16[1,64,384]{2,1,0:T(8,128)(2,1)S(1)} %fusion.131), channel_id=1, source_target_pairs={{0,3},{1,2},{2,1},{3,0},{4,7},{5,6},{6,5},{7,4},{8,11},{9,10},{10,... | collective-permute-start | bytes 147464 | tf_op jit(solution)/shard_map/ppermute | solution.py:85
  17.3 6.0 %collective-permute-start.4 = (bf16[1,64,384]{2,1,0:T(8,128)(2,1)S(1)}, bf16[1,64,384]{2,1,0:T(8,128)(2,1)S(1)}, u32[]{:S(2)}, u32[]{:S(2)}) collective-permute-start(bf16[1,64,384]{2,1,0:T(8,128)(2,1)S(1)} %fusion.131), channel_id=1, source_target_pairs={{0,2},{1,3},{2,0},{3,1},{4,6},{5,7},{6,4},{7,5},{8,10},{9,11},{10,... | collective-permute-start | bytes 147464 | tf_op jit(solution)/shard_map/ppermute | solution.py:85
  17.3 6.0 %collective-permute-start.3 = (bf16[1,64,384]{2,1,0:T(8,128)(2,1)S(1)}, bf16[1,64,384]{2,1,0:T(8,128)(2,1)S(1)}, u32[]{:S(2)}, u32[]{:S(2)}) collective-permute-start(bf16[1,64,384]{2,1,0:T(8,128)(2,1)S(1)} %fusion.131), channel_id=1, source_target_pairs={{0,1},{1,0},{2,3},{3,2},{4,5},{5,4},{6,7},{7,6},{8,9},{9,8},{10,11... | collective-permute-start | bytes 147464 | tf_op jit(solution)/shard_map/ppermute | solution.py:85
  24.6 5.1 %collective-permute-start.7 = (bf16[1,179,384]{2,1,0:T(8,128)(2,1)S(1)}, bf16[1,179,384]{2,1,0:T(8,128)(2,1)S(1)}, u32[]{:S(2)}, u32[]{:S(2)}) collective-permute-start(bf16[1,179,384]{2,1,0:T(8,128)(2,1)S(1)} %pad_maximum_fusion), channel_id=1, source_target_pairs={{0,4},{4,0},{1,5},{5,1},{2,6},{6,2},{3,7},{7,3},{8,12},{12,8},{9,1... | collective-permute-start | bytes 412424 | tf_op jit(solution)/shard_map/ppermute | solution.py:169
  26.8 8.3 %collective-permute-start.6 = (bf16[384,192]{1,0:T(8,128)(2,1)S(1)}, bf16[384,192]{1,0:T(8,128)(2,1)S(1)}, u32[]{:S(2)}, u32[]{:S(2)}) collective-permute-start(bf16[384,192]{1,0:T(8,128)(2,1)S(1)} %constant_dynamic-slice_fusion.2), channel_id=1, source_target_pairs={{0,8},{8,0},{16,24},{24,16},{1,9},{9,1},{17,25},{25,17},{2,10},{10... | collective-permute-start | bytes 442376 | tf_op jit(solution)/shard_map/ppermute | solution.py:131
  31.8 1.5 %collective-permute-start.8 = (bf16[384,192]{1,0:T(8,128)(2,1)S(1)}, bf16[384,192]{1,0:T(8,128)(2,1)S(1)}, u32[]{:S(2)}, u32[]{:S(2)}) collective-permute-start(bf16[384,192]{1,0:T(8,128)(2,1)S(1)} %constant_dynamic-slice_fusion.1), channel_id=1, source_target_pairs={{0,8},{8,0},{16,24},{24,16},{1,9},{9,1},{17,25},{25,17},{2,10},{10... | collective-permute-start | bytes 442376 | tf_op jit(solution)/shard_map/ppermute | solution.py:131
  33.5 5.0 %collective-permute-start.9 = (bf16[192,192]{1,0:T(8,128)(2,1)S(1)}, bf16[192,192]{1,0:T(8,128)(2,1)S(1)}, u32[]{:S(2)}, u32[]{:S(2)}) collective-permute-start(bf16[192,192]{1,0:T(8,128)(2,1)S(1)} %constant_dynamic-slice_fusion), channel_id=1, source_target_pairs={{0,4},{4,0},{1,5},{5,1},{2,6},{6,2},{3,7},{7,3},{8,12},{12,8},{9,1... | collective-permute-start | bytes 221192 | tf_op jit(solution)/shard_map/ppermute | solution.py:139
  38.5 4.7 %collective-permute-start.10 = (bf16[192,192]{1,0:T(8,128)(2,1)S(1)}, bf16[192,192]{1,0:T(8,128)(2,1)S(1)}, u32[]{:S(2)}, u32[]{:S(2)}) collective-permute-start(bf16[192,192]{1,0:T(8,128)(2,1)S(1)} %get-tuple-element.32), channel_id=1, source_target_pairs={{0,4},{4,0},{1,5},{5,1},{2,6},{6,2},{3,7},{7,3},{8,12},{12,8},{9,1... | collective-permute-start | bytes 221192 | tf_op jit(solution)/shard_map/ppermute | solution.py:139
  41.3 5.2 %collective-permute-start.13 = (bf16[192,192]{1,0:T(8,128)(2,1)S(1)}, bf16[192,192]{1,0:T(8,128)(2,1)S(1)}, u32[]{:S(2)}, u32[]{:S(2)}) collective-permute-start(bf16[192,192]{1,0:T(8,128)(2,1)S(1)} %get-tuple-element.33), channel_id=1, source_target_pairs={{0,16},{8,24},{16,0},{24,8},{1,17},{9,25},{17,1},{25,9},{2,18},{10... | collective-permute-start | bytes 221192 | tf_op jit(solution)/shard_map/ppermute | solution.py:103
  43.2 4.7 %collective-permute-start.11 = (bf16[192,192]{1,0:T(8,128)(2,1)S(1)}, bf16[192,192]{1,0:T(8,128)(2,1)S(1)}, u32[]{:S(2)}, u32[]{:S(2)}) collective-permute-start(bf16[192,192]{1,0:T(8,128)(2,1)S(1)} %add_convert_fusion.2), channel_id=1, source_target_pairs={{0,16},{8,24},{16,0},{24,8},{1,17},{9,25},{17,1},{25,9},{2,18},{10... | collective-permute-start | bytes 221192 | tf_op jit(solution)/shard_map/ppermute | solution.py:103
  46.4 1.6 %collective-permute-start.14 = (f32[192,192]{1,0:T(8,128)S(1)}, f32[192,192]{1,0:T(8,128)S(1)}, u32[]{:S(2)}, u32[]{:S(2)}) collective-permute-start(f32[192,192]{1,0:T(8,128)S(1)} %get-tuple-element.42), channel_id=1, source_target_pairs={{0,8},{8,0},{16,24},{24,16},{1,9},{9,1},{17,25},{25,17},{2,10},{10... | collective-permute-start | bytes 442376 | tf_op jit(solution)/shard_map/ppermute | solution.py:310
  48.0 1.5 %collective-permute-start.12 = (f32[192,192]{1,0:T(8,128)S(1)}, f32[192,192]{1,0:T(8,128)S(1)}, u32[]{:S(2)}, u32[]{:S(2)}) collective-permute-start(f32[192,192]{1,0:T(8,128)S(1)} %get-tuple-element.38), channel_id=1, source_target_pairs={{0,8},{8,0},{16,24},{24,16},{1,9},{9,1},{17,25},{25,17},{2,10},{10... | collective-permute-start | bytes 442376 | tf_op jit(solution)/shard_map/ppermute | solution.py:310

commit v16 on v14

--- a/solution.py
+++ b/solution.py
@@ -126,14 +126,17 @@
         def to_seq_partner(rows, grad):
             local = jnp.einsum("bnc,bnp->pc", rows, grad, preferred_element_type=jnp.float32)
             local = local.astype(jnp.bfloat16)
-            kept = lax.dynamic_slice_in_dim(local, pair * half, half, 1).astype(jnp.float32)
-            outgoing = lax.dynamic_slice_in_dim(local, (1 - pair) * half, half, 1)
-            kept = kept + lax.ppermute(outgoing, "dp", [(i, i ^ 1) for i in range(n_dp)]).astype(
-                jnp.float32
-            )
-            held = kept.astype(jnp.bfloat16)
-            own = lax.dynamic_slice_in_dim(held, slab * part, part, 0).astype(jnp.float32)
-            return own, lax.dynamic_slice_in_dim(held, (1 - slab) * part, part, 0)
+
+            def chip_sum(width_part):
+                block = lax.dynamic_slice_in_dim(local, width_part * part, part, 0)
+                kept = lax.dynamic_slice_in_dim(block, pair * half, half, 1).astype(jnp.float32)
+                outgoing = lax.dynamic_slice_in_dim(block, (1 - pair) * half, half, 1)
+                received = lax.ppermute(outgoing, "dp", [(i, i ^ 1) for i in range(n_dp)])
+                return (kept + received.astype(jnp.float32)).astype(jnp.bfloat16)
+
+            for_partner = chip_sum(1 - slab)
+            own = chip_sum(slab).astype(jnp.float32)
+            return own, for_partner
 
         def from_seq_partner(outgoing):
             return lax.ppermute(outgoing, "seq", [(0, 1), (1, 0)]).astype(jnp.float32)

time: 47.1 us -> 49.5 us (1.051)
  starting transfers between devices: 17.6 us -> 18.9 us
  waiting for transfers between devices: 15.7 us -> 16.6 us
    ppermute x2 -> x4, waiting for transfers between devices: 0.01 us -> 1.06 us  [chip_sum(): received = lax.ppermute(outgoing, 'dp', [(i, i ^ 1) for i in range(n_dp)])]
    ppermute x2, waiting for transfers between devices: 3.16 us -> 3.99 us  [from_seq_partner(): return lax.ppermute(outgoing, 'seq', [(0, 1), (1, 0)]).astype(jnp.float32)]
    ppermute x2, starting transfers between devices: 2.45 us -> 3.18 us  [from_seq_partner(): return lax.ppermute(outgoing, 'seq', [(0, 1), (1, 0)]).astype(jnp.float32)]
    ppermute x2 -> x4, starting transfers between devices: 0.14 us -> 0.71 us  [chip_sum(): received = lax.ppermute(outgoing, 'dp', [(i, i ^ 1) for i in range(n_dp)])]
    ppermute x1, waiting for transfers between devices: 2.37 us -> 1.84 us  [shards(): arrived = lax.ppermute(payload, 'seq', perm)]
  transfers between devices with their start and end apart: 14 -> 16, of which waited for: 10 -> 11; matrix products, arithmetic and copies ran while one was open for 13% -> 13% of each run, Pallas kernels for 0% -> 0%
where the time goes in v16:
time: 49.5 us; the launch traced here: 49.3 us
  starting transfers between devices  18.9 us (38%)
  waiting for transfers between devices  16.6 us (34%)
  local copies, waits for them, and re-layouts  5.52 us (11%)
  matrix products  5.39 us (11%)
  other arithmetic  1.68 us (3%)
  between operations  1.23 us (2%)
    ppermute x3, starting transfers between devices, shards(): lax.ppermute(outgoing, 'head', [(i, i ^ k) for i in range(n_head)])  5.76 us
    ppermute x3, starting transfers between devices, shards(): lax.ppermute(feat_quarter, 'head', [(i, i ^ k) for i in range(n_head)])  4.45 us
    ppermute x2, waiting for transfers between devices, from_seq_partner(): return lax.ppermute(outgoing, 'seq', [(0, 1), (1, 0)]).astype(jnp.float32)  3.99 us
    ppermute x3, waiting for transfers between devices, shards(): lax.ppermute(outgoing, 'head', [(i, i ^ k) for i in range(n_head)])  3.52 us
    ppermute x2, starting transfers between devices, from_seq_partner(): return lax.ppermute(outgoing, 'seq', [(0, 1), (1, 0)]).astype(jnp.float32)  3.18 us
    ppermute x3, waiting for transfers between devices, shards(): lax.ppermute(feat_quarter, 'head', [(i, i ^ k) for i in range(n_head)])  3.12 us
    ppermute x2, starting transfers between devices, over_dp_bits(): lax.ppermute(held, 'dp', perm).astype(jnp.float32)  3.11 us
    ppermute x2, waiting for transfers between devices, over_dp_bits(): lax.ppermute(held, 'dp', perm).astype(jnp.float32)  2.89 us
  transfers between devices with their start and end apart: 16, of which 11 were waited for; matrix products, arithmetic and copies ran while one was open for 13% of the time, Pallas kernels for 0%

profile of v16, /device:TPU:0, one launch (start us, length us, event | category | flops | bytes accessed | tf_op | source)
XLA Modules:
  0.0 49.3 jit_solution(5596321532785744370)
XLA Ops:
  0.7 0.7 %copy-done.4 = s32[1,128]{1,0:T(1,128)S(1)} copy-done((s32[1,128]{1,0:T(1,128)S(1)}, s32[1,128]{1,0:T(1,128)}, u32[]{:S(2)}) %copy-start.4) | copy-done | bytes 536
  1.4 0.7 %copy-done.5 = s32[1,128]{1,0:T(1,128)S(1)} copy-done((s32[1,128]{1,0:T(1,128)S(1)}, s32[1,128]{1,0:T(1,128)}, u32[]{:S(2)}) %copy-start.5) | copy-done | bytes 536
  2.6 0.7 %copy-done.1 = bf16[384,384]{1,0:T(8,128)(2,1)S(1)} copy-done((bf16[384,384]{1,0:T(8,128)(2,1)S(1)}, bf16[384,384]{1,0:T(8,128)(2,1)}, u32[]{:S(2)}) %copy-start.1) | copy-done | bytes 294936
  4.2 5.1 %collective-permute-start.2 = (bf16[1,64,384]{2,1,0:T(8,128)(2,1)S(1)}, bf16[1,64,384]{2,1,0:T(8,128)(2,1)S(1)}, u32[]{:S(2)}, u32[]{:S(2)}) collective-permute-start(bf16[1,64,384]{2,1,0:T(8,128)(2,1)S(1)} %get-tuple-element.45), channel_id=1, source_target_pairs={{0,3},{1,2},{2,1},{3,0},{4,7},{5,6},{6,5},{7,4},{8,11},{9,10},{10,... | collective-permute-start | bytes 147464 | tf_op jit(solution)/shard_map/ppermute | solution.py:75
  9.3 0.6 %collective-permute-start = (bf16[1,64,384]{2,1,0:T(8,128)(2,1)S(1)}, bf16[1,64,384]{2,1,0:T(8,128)(2,1)S(1)}, u32[]{:S(2)}, u32[]{:S(2)}) collective-permute-start(bf16[1,64,384]{2,1,0:T(8,128)(2,1)S(1)} %get-tuple-element.43), channel_id=1, source_target_pairs={{0,1},{1,0},{2,3},{3,2},{4,5},{5,4},{6,7},{7,6},{8,9},{9,8},{10,11... | collective-permute-start | bytes 147464 | tf_op jit(solution)/shard_map/ppermute | solution.py:75
  10.8 0.8 %collective-permute-done.2 = bf16[1,64,384]{2,1,0:T(8,128)(2,1)S(1)} collective-permute-done((bf16[1,64,384]{2,1,0:T(8,128)(2,1)S(1)}, bf16[1,64,384]{2,1,0:T(8,128)(2,1)S(1)}, u32[]{:S(2)}, u32[]{:S(2)}) %collective-permute-start.2) | collective-permute-done | bytes 49184 | tf_op jit(solution)/shard_map/ppermute | solution.py:75
  11.5 2.8 %collective-permute-done.1 = bf16[1,64,384]{2,1,0:T(8,128)(2,1)S(1)} collective-permute-done((bf16[1,64,384]{2,1,0:T(8,128)(2,1)S(1)}, bf16[1,64,384]{2,1,0:T(8,128)(2,1)S(1)}, u32[]{:S(2)}, u32[]{:S(2)}) %collective-permute-start.1) | collective-permute-done | bytes 49184 | tf_op jit(solution)/shard_map/ppermute | solution.py:75
  15.1 2.2 %collective-permute-start.5 = (bf16[1,64,384]{2,1,0:T(8,128)(2,1)S(1)}, bf16[1,64,384]{2,1,0:T(8,128)(2,1)S(1)}, u32[]{:S(2)}, u32[]{:S(2)}) collective-permute-start(bf16[1,64,384]{2,1,0:T(8,128)(2,1)S(1)} %fusion.133), channel_id=1, source_target_pairs={{0,3},{1,2},{2,1},{3,0},{4,7},{5,6},{6,5},{7,4},{8,11},{9,10},{10,... | collective-permute-start | bytes 147464 | tf_op jit(solution)/shard_map/ppermute | solution.py:85
  17.2 2.3 %collective-permute-start.3 = (bf16[1,64,384]{2,1,0:T(8,128)(2,1)S(1)}, bf16[1,64,384]{2,1,0:T(8,128)(2,1)S(1)}, u32[]{:S(2)}, u32[]{:S(2)}) collective-permute-start(bf16[1,64,384]{2,1,0:T(8,128)(2,1)S(1)} %fusion.133), channel_id=1, source_target_pairs={{0,1},{1,0},{2,3},{3,2},{4,5},{5,4},{6,7},{7,6},{8,9},{9,8},{10,11... | collective-permute-start | bytes 147464 | tf_op jit(solution)/shard_map/ppermute | solution.py:85
  19.5 1.7 %collective-permute-done.5 = bf16[1,64,384]{2,1,0:T(8,128)(2,1)S(1)} collective-permute-done((bf16[1,64,384]{2,1,0:T(8,128)(2,1)S(1)}, bf16[1,64,384]{2,1,0:T(8,128)(2,1)S(1)}, u32[]{:S(2)}, u32[]{:S(2)}) %collective-permute-start.5) | collective-permute-done | bytes 49184 | tf_op jit(solution)/shard_map/ppermute | solution.py:85
  21.3 1.4 %collective-permute-done.4 = bf16[1,64,384]{2,1,0:T(8,128)(2,1)S(1)} collective-permute-done((bf16[1,64,384]{2,1,0:T(8,128)(2,1)S(1)}, bf16[1,64,384]{2,1,0:T(8,128)(2,1)S(1)}, u32[]{:S(2)}, u32[]{:S(2)}) %collective-permute-start.4) | collective-permute-done | bytes 49184 | tf_op jit(solution)/shard_map/ppermute | solution.py:85
  23.5 1.6 %collective-permute-start.6 = (bf16[1,179,384]{2,1,0:T(8,128)(2,1)S(1)}, bf16[1,179,384]{2,1,0:T(8,128)(2,1)S(1)}, u32[]{:S(2)}, u32[]{:S(2)}) collective-permute-start(bf16[1,179,384]{2,1,0:T(8,128)(2,1)S(1)} %pad_maximum_fusion.1), channel_id=1, source_target_pairs={{0,4},{4,0},{1,5},{5,1},{2,6},{6,2},{3,7},{7,3},{8,12},{12,8},{9,1... | collective-permute-start | bytes 412424 | tf_op jit(solution)/shard_map/ppermute | solution.py:172
  26.8 1.8 %collective-permute-done.6 = bf16[1,179,384]{2,1,0:T(8,128)(2,1)S(1)} collective-permute-done((bf16[1,179,384]{2,1,0:T(8,128)(2,1)S(1)}, bf16[1,179,384]{2,1,0:T(8,128)(2,1)S(1)}, u32[]{:S(2)}, u32[]{:S(2)}) %collective-permute-start.6) | collective-permute-done | bytes 137504 | tf_op jit(solution)/shard_map/ppermute | solution.py:172
  30.6 1.1 %collective-permute-done.12 = bf16[192,192]{1,0:T(8,128)(2,1)S(1)} collective-permute-done((bf16[192,192]{1,0:T(8,128)(2,1)S(1)}, bf16[192,192]{1,0:T(8,128)(2,1)S(1)}, u32[]{:S(2)}, u32[]{:S(2)}) %collective-permute-start.12) | collective-permute-done | bytes 73760 | tf_op jit(solution)/shard_map/ppermute | solution.py:134
  31.7 1.6 %collective-permute-start.13 = (bf16[192,192]{1,0:T(8,128)(2,1)S(1)}, bf16[192,192]{1,0:T(8,128)(2,1)S(1)}, u32[]{:S(2)}, u32[]{:S(2)}) collective-permute-start(bf16[192,192]{1,0:T(8,128)(2,1)S(1)} %add_convert_fusion.1), channel_id=1, source_target_pairs={{0,4},{4,0},{1,5},{5,1},{2,6},{6,2},{3,7},{7,3},{8,12},{12,8},{9,1... | collective-permute-start | bytes 221192 | tf_op jit(solution)/shard_map/ppermute | solution.py:142
  33.8 2.8 %collective-permute-done.13 = bf16[192,192]{1,0:T(8,128)(2,1)S(1)} collective-permute-done((bf16[192,192]{1,0:T(8,128)(2,1)S(1)}, bf16[192,192]{1,0:T(8,128)(2,1)S(1)}, u32[]{:S(2)}, u32[]{:S(2)}) %collective-permute-start.13) | collective-permute-done | bytes 73760 | tf_op jit(solution)/shard_map/ppermute | solution.py:142
  36.8 1.6 %collective-permute-start.9 = (bf16[192,192]{1,0:T(8,128)(2,1)S(1)}, bf16[192,192]{1,0:T(8,128)(2,1)S(1)}, u32[]{:S(2)}, u32[]{:S(2)}) collective-permute-start(bf16[192,192]{1,0:T(8,128)(2,1)S(1)} %get-tuple-element.29), channel_id=1, source_target_pairs={{0,4},{4,0},{1,5},{5,1},{2,6},{6,2},{3,7},{7,3},{8,12},{12,8},{9,1... | collective-permute-start | bytes 221192 | tf_op jit(solution)/shard_map/ppermute | solution.py:142
  38.8 1.6 %collective-permute-start.14 = (bf16[192,192]{1,0:T(8,128)(2,1)S(1)}, bf16[192,192]{1,0:T(8,128)(2,1)S(1)}, u32[]{:S(2)}, u32[]{:S(2)}) collective-permute-start(bf16[192,192]{1,0:T(8,128)(2,1)S(1)} %get-tuple-element.34), channel_id=1, source_target_pairs={{0,16},{8,24},{16,0},{24,8},{1,17},{9,25},{17,1},{25,9},{2,18},{10... | collective-permute-start | bytes 221192 | tf_op jit(solution)/shard_map/ppermute | solution.py:103
  40.3 1.1 %collective-permute-done.9 = bf16[192,192]{1,0:T(8,128)(2,1)S(1)} collective-permute-done((bf16[192,192]{1,0:T(8,128)(2,1)S(1)}, bf16[192,192]{1,0:T(8,128)(2,1)S(1)}, u32[]{:S(2)}, u32[]{:S(2)}) %collective-permute-start.9) | collective-permute-done | bytes 73760 | tf_op jit(solution)/shard_map/ppermute | solution.py:142
  41.6 1.6 %collective-permute-start.10 = (bf16[192,192]{1,0:T(8,128)(2,1)S(1)}, bf16[192,192]{1,0:T(8,128)(2,1)S(1)}, u32[]{:S(2)}, u32[]{:S(2)}) collective-permute-start(bf16[192,192]{1,0:T(8,128)(2,1)S(1)} %add_convert_fusion.3), channel_id=1, source_target_pairs={{0,16},{8,24},{16,0},{24,8},{1,17},{9,25},{17,1},{25,9},{2,18},{10... | collective-permute-start | bytes 221192 | tf_op jit(solution)/shard_map/ppermute | solution.py:103
  43.4 1.1 %collective-permute-done.14 = bf16[192,192]{1,0:T(8,128)(2,1)S(1)} collective-permute-done((bf16[192,192]{1,0:T(8,128)(2,1)S(1)}, bf16[192,192]{1,0:T(8,128)(2,1)S(1)}, u32[]{:S(2)}, u32[]{:S(2)}) %collective-permute-start.14) | collective-permute-done | bytes 73760 | tf_op jit(solution)/shard_map/ppermute | solution.py:103
  44.5 1.8 %collective-permute-done.10 = bf16[192,192]{1,0:T(8,128)(2,1)S(1)} collective-permute-done((bf16[192,192]{1,0:T(8,128)(2,1)S(1)}, bf16[192,192]{1,0:T(8,128)(2,1)S(1)}, u32[]{:S(2)}, u32[]{:S(2)}) %collective-permute-start.10) | collective-permute-done | bytes 73760 | tf_op jit(solution)/shard_map/ppermute | solution.py:103
  46.9 1.1 %fusion.2 = bf16[1,512,384]{2,1,0:T(8,128)(2,1)} fusion(f32[512,384]{1,0:T(8,128)S(1)} %convolution_add_fusion.1, f32[512,384]{1,0:T(8,128)S(1)} %fusion.12, s32[128]{0:T(128)S(1)} %subtract_bitcast_fusion, f32[128,384]{1,0:T(8,128)S(1)} %fusion.56), kind=kOutput, calls=%fused_computation.8 | convolution fusion | flops 51183616 | bytes 2163200 | tf_op jit(solution)/shard_map/bnr,bnc->brc/dot_general | solution.py:26
  48.4 0.9 %slice_bitcast_fusion = (f32[384,192]{0,1:T(8,128)}, f32[384,192]{0,1:T(8,128)}) fusion(f32[2,384,192]{1,2,0:T(8,128)S(1)} %fusion.9), kind=kLoop, calls=%fused_computation.30 | loop fusion | bytes 1179648 | tf_op jit(solution)/shard_map/squeeze | solution.py:322
  (90 shorter events, 9.6 us)
Async XLA Ops:
  0.6 1.4 %copy-start = (bf16[1,512,384]{2,1,0:T(8,128)(2,1)S(1)}, bf16[1,512,384]{2,1,0:T(8,128)(2,1)}, u32[]{:S(2)}) copy-start(bf16[1,512,384]{2,1,0:T(8,128)(2,1)} %param.12) | copy-start | bytes 1179652
  0.7 0.7 %copy-start.4 = (s32[1,128]{1,0:T(1,128)S(1)}, s32[1,128]{1,0:T(1,128)}, u32[]{:S(2)}) copy-start(s32[1,128]{1,0:T(1,128)} %param.13) | copy-start | bytes 1540
  1.4 0.7 %copy-start.5 = (s32[1,128]{1,0:T(1,128)S(1)}, s32[1,128]{1,0:T(1,128)}, u32[]{:S(2)}) copy-start(s32[1,128]{1,0:T(1,128)} %param.14) | copy-start | bytes 1540
  2.3 1.0 %copy-start.1 = (bf16[384,384]{1,0:T(8,128)(2,1)S(1)}, bf16[384,384]{1,0:T(8,128)(2,1)}, u32[]{:S(2)}) copy-start(bf16[384,384]{1,0:T(8,128)(2,1)} %param.16) | copy-start | bytes 884740
  2.6 1.0 %copy-start.2 = (bf16[384,384]{1,0:T(8,128)(2,1)S(1)}, bf16[384,384]{1,0:T(8,128)(2,1)}, u32[]{:S(2)}) copy-start(bf16[384,384]{1,0:T(8,128)(2,1)} %param.17) | copy-start | bytes 884740
  3.8 6.2 %copy-start.3 = (bf16[1,128,256]{2,1,0:T(8,128)(2,1)S(1)}, bf16[1,128,256]{2,1,0:T(8,128)(2,1)}, u32[]{:S(2)}) copy-start(bf16[1,128,256]{2,1,0:T(8,128)(2,1)} %param.15) | copy-start | bytes 196612
  4.2 7.3 %collective-permute-start.2 = (bf16[1,64,384]{2,1,0:T(8,128)(2,1)S(1)}, bf16[1,64,384]{2,1,0:T(8,128)(2,1)S(1)}, u32[]{:S(2)}, u32[]{:S(2)}) collective-permute-start(bf16[1,64,384]{2,1,0:T(8,128)(2,1)S(1)} %get-tuple-element.45), channel_id=1, source_target_pairs={{0,3},{1,2},{2,1},{3,0},{4,7},{5,6},{6,5},{7,4},{8,11},{9,10},{10,... | collective-permute-start | bytes 147464 | tf_op jit(solution)/shard_map/ppermute | solution.py:75
  9.3 5.0 %collective-permute-start.1 = (bf16[1,64,384]{2,1,0:T(8,128)(2,1)S(1)}, bf16[1,64,384]{2,1,0:T(8,128)(2,1)S(1)}, u32[]{:S(2)}, u32[]{:S(2)}) collective-permute-start(bf16[1,64,384]{2,1,0:T(8,128)(2,1)S(1)} %get-tuple-element.44), channel_id=1, source_target_pairs={{0,2},{1,3},{2,0},{3,1},{4,6},{5,7},{6,4},{7,5},{8,10},{9,11},{10,... | collective-permute-start | bytes 147464 | tf_op jit(solution)/shard_map/ppermute | solution.py:75
  9.3 5.0 %collective-permute-start = (bf16[1,64,384]{2,1,0:T(8,128)(2,1)S(1)}, bf16[1,64,384]{2,1,0:T(8,128)(2,1)S(1)}, u32[]{:S(2)}, u32[]{:S(2)}) collective-permute-start(bf16[1,64,384]{2,1,0:T(8,128)(2,1)S(1)} %get-tuple-element.43), channel_id=1, source_target_pairs={{0,1},{1,0},{2,3},{3,2},{4,5},{5,4},{6,7},{7,6},{8,9},{9,8},{10,11... | collective-permute-start | bytes 147464 | tf_op jit(solution)/shard_map/ppermute | solution.py:75
  15.1 6.2 %collective-permute-start.5 = (bf16[1,64,384]{2,1,0:T(8,128)(2,1)S(1)}, bf16[1,64,384]{2,1,0:T(8,128)(2,1)S(1)}, u32[]{:S(2)}, u32[]{:S(2)}) collective-permute-start(bf16[1,64,384]{2,1,0:T(8,128)(2,1)S(1)} %fusion.133), channel_id=1, source_target_pairs={{0,3},{1,2},{2,1},{3,0},{4,7},{5,6},{6,5},{7,4},{8,11},{9,10},{10,... | collective-permute-start | bytes 147464 | tf_op jit(solution)/shard_map/ppermute | solution.py:85
  17.2 5.4 %collective-permute-start.4 = (bf16[1,64,384]{2,1,0:T(8,128)(2,1)S(1)}, bf16[1,64,384]{2,1,0:T(8,128)(2,1)S(1)}, u32[]{:S(2)}, u32[]{:S(2)}) collective-permute-start(bf16[1,64,384]{2,1,0:T(8,128)(2,1)S(1)} %fusion.133), channel_id=1, source_target_pairs={{0,2},{1,3},{2,0},{3,1},{4,6},{5,7},{6,4},{7,5},{8,10},{9,11},{10,... | collective-permute-start | bytes 147464 | tf_op jit(solution)/shard_map/ppermute | solution.py:85
  17.2 5.4 %collective-permute-start.3 = (bf16[1,64,384]{2,1,0:T(8,128)(2,1)S(1)}, bf16[1,64,384]{2,1,0:T(8,128)(2,1)S(1)}, u32[]{:S(2)}, u32[]{:S(2)}) collective-permute-start(bf16[1,64,384]{2,1,0:T(8,128)(2,1)S(1)} %fusion.133), channel_id=1, source_target_pairs={{0,1},{1,0},{2,3},{3,2},{4,5},{5,4},{6,7},{7,6},{8,9},{9,8},{10,11... | collective-permute-start | bytes 147464 | tf_op jit(solution)/shard_map/ppermute | solution.py:85
  23.5 5.1 %collective-permute-start.6 = (bf16[1,179,384]{2,1,0:T(8,128)(2,1)S(1)}, bf16[1,179,384]{2,1,0:T(8,128)(2,1)S(1)}, u32[]{:S(2)}, u32[]{:S(2)}) collective-permute-start(bf16[1,179,384]{2,1,0:T(8,128)(2,1)S(1)} %pad_maximum_fusion.1), channel_id=1, source_target_pairs={{0,4},{4,0},{1,5},{5,1},{2,6},{6,2},{3,7},{7,3},{8,12},{12,8},{9,1... | collective-permute-start | bytes 412424 | tf_op jit(solution)/shard_map/ppermute | solution.py:172
  26.2 7.6 %collective-permute-start.11 = (bf16[192,192]{1,0:T(8,128)(2,1)S(1)}, bf16[192,192]{1,0:T(8,128)(2,1)S(1)}, u32[]{:S(2)}, u32[]{:S(2)}) collective-permute-start(bf16[192,192]{1,0:T(8,128)(2,1)S(1)} %get-tuple-element.36), channel_id=1, source_target_pairs={{0,8},{8,0},{16,24},{24,16},{1,9},{9,1},{17,25},{25,17},{2,10},{10... | collective-permute-start | bytes 221192 | tf_op jit(solution)/shard_map/ppermute | solution.py:134
  26.2 7.5 %collective-permute-start.8 = (bf16[192,192]{1,0:T(8,128)(2,1)S(1)}, bf16[192,192]{1,0:T(8,128)(2,1)S(1)}, u32[]{:S(2)}, u32[]{:S(2)}) collective-permute-start(bf16[192,192]{1,0:T(8,128)(2,1)S(1)} %get-tuple-element.37), channel_id=1, source_target_pairs={{0,8},{8,0},{16,24},{24,16},{1,9},{9,1},{17,25},{25,17},{2,10},{10... | collective-permute-start | bytes 221192 | tf_op jit(solution)/shard_map/ppermute | solution.py:134
  30.2 1.4 %collective-permute-start.12 = (bf16[192,192]{1,0:T(8,128)(2,1)S(1)}, bf16[192,192]{1,0:T(8,128)(2,1)S(1)}, u32[]{:S(2)}, u32[]{:S(2)}) collective-permute-start(bf16[192,192]{1,0:T(8,128)(2,1)S(1)} %get-tuple-element.38), channel_id=1, source_target_pairs={{0,8},{8,0},{16,24},{24,16},{1,9},{9,1},{17,25},{25,17},{2,10},{10... | collective-permute-start | bytes 221192 | tf_op jit(solution)/shard_map/ppermute | solution.py:134
  31.7 4.9 %collective-permute-start.13 = (bf16[192,192]{1,0:T(8,128)(2,1)S(1)}, bf16[192,192]{1,0:T(8,128)(2,1)S(1)}, u32[]{:S(2)}, u32[]{:S(2)}) collective-permute-start(bf16[192,192]{1,0:T(8,128)(2,1)S(1)} %add_convert_fusion.1), channel_id=1, source_target_pairs={{0,4},{4,0},{1,5},{5,1},{2,6},{6,2},{3,7},{7,3},{8,12},{12,8},{9,1... | collective-permute-start | bytes 221192 | tf_op jit(solution)/shard_map/ppermute | solution.py:142
  33.7 6.6 %collective-permute-start.7 = (bf16[192,192]{1,0:T(8,128)(2,1)S(1)}, bf16[192,192]{1,0:T(8,128)(2,1)S(1)}, u32[]{:S(2)}, u32[]{:S(2)}) collective-permute-start(bf16[192,192]{1,0:T(8,128)(2,1)S(1)} %get-tuple-element.39), channel_id=1, source_target_pairs={{0,8},{8,0},{16,24},{24,16},{1,9},{9,1},{17,25},{25,17},{2,10},{10... | collective-permute-start | bytes 221192 | tf_op jit(solution)/shard_map/ppermute | solution.py:134
  36.8 4.7 %collective-permute-start.9 = (bf16[192,192]{1,0:T(8,128)(2,1)S(1)}, bf16[192,192]{1,0:T(8,128)(2,1)S(1)}, u32[]{:S(2)}, u32[]{:S(2)}) collective-permute-start(bf16[192,192]{1,0:T(8,128)(2,1)S(1)} %get-tuple-element.29), channel_id=1, source_target_pairs={{0,4},{4,0},{1,5},{5,1},{2,6},{6,2},{3,7},{7,3},{8,12},{12,8},{9,1... | collective-permute-start | bytes 221192 | tf_op jit(solution)/shard_map/ppermute | solution.py:142
  38.8 5.7 %collective-permute-start.14 = (bf16[192,192]{1,0:T(8,128)(2,1)S(1)}, bf16[192,192]{1,0:T(8,128)(2,1)S(1)}, u32[]{:S(2)}, u32[]{:S(2)}) collective-permute-start(bf16[192,192]{1,0:T(8,128)(2,1)S(1)} %get-tuple-element.34), channel_id=1, source_target_pairs={{0,16},{8,24},{16,0},{24,8},{1,17},{9,25},{17,1},{25,9},{2,18},{10... | collective-permute-start | bytes 221192 | tf_op jit(solution)/shard_map/ppermute | solution.py:103
  41.6 4.7 %collective-permute-start.10 = (bf16[192,192]{1,0:T(8,128)(2,1)S(1)}, bf16[192,192]{1,0:T(8,128)(2,1)S(1)}, u32[]{:S(2)}, u32[]{:S(2)}) collective-permute-start(bf16[192,192]{1,0:T(8,128)(2,1)S(1)} %add_convert_fusion.3), channel_id=1, source_target_pairs={{0,16},{8,24},{16,0},{24,8},{1,17},{9,25},{17,1},{25,9},{2,18},{10... | collective-permute-start | bytes 221192 | tf_op jit(solution)/shard_map/ppermute | solution.py:103
  46.4 1.8 %collective-permute-start.15 = (f32[2,192,192]{2,1,0:T(8,128)S(1)}, f32[2,192,192]{2,1,0:T(8,128)S(1)}, u32[]{:S(2)}, u32[]{:S(2)}) collective-permute-start(f32[2,192,192]{2,1,0:T(8,128)S(1)} %pad_maximum_fusion), channel_id=1, source_target_pairs={{0,8},{8,0},{16,24},{24,16},{1,9},{9,1},{17,25},{25,17},{2,10},{10... | collective-permute-start | bytes 884744 | tf_op jit(solution)/shard_map/ppermute | solution.py:317

commit v17 on v14

--- a/solution.py
+++ b/solution.py
@@ -34,6 +34,13 @@
     by_offset = jnp.stack(pieces)
     order = (me - jnp.arange(count, dtype=jnp.int32)) % count
     return jnp.take(by_offset, order, axis=0)
+
+
+def from_head(pieces, head, source):
+    chosen = pieces[0]
+    for k in range(1, len(pieces)):
+        chosen = jnp.where((head ^ k) == source, pieces[k], chosen)
+    return chosen
 
 
 def shards(embed, donor_pos, acceptor_pos, target, donor_w, acceptor_w):
@@ -73,18 +80,15 @@
     for k in range(1, n_head):
         outgoing = lax.dynamic_slice_in_dim(parts, (head ^ k) * quarter, quarter, 1)
         pieces.append(lax.ppermute(outgoing, "head", [(i, i ^ k) for i in range(n_head)]))
-    by_partner = jnp.stack(pieces)
-    by_head = jnp.take(by_partner, head ^ jnp.arange(n_head, dtype=jnp.int32), axis=0)
     total = jnp.zeros((batch, quarter, width), jnp.float32)
     for h in range(n_head):
-        total = total + by_head[h].astype(jnp.float32)
+        total = total + from_head(pieces, head, h).astype(jnp.float32)
     feat_quarter = total.astype(jnp.bfloat16)
 
     pieces = [feat_quarter]
     for k in range(1, n_head):
         pieces.append(lax.ppermute(feat_quarter, "head", [(i, i ^ k) for i in range(n_head)]))
-    slab_feats = jnp.take(jnp.stack(pieces), head ^ jnp.arange(n_head, dtype=jnp.int32), axis=0)
-    slab_feats = jnp.moveaxis(slab_feats, 0, 1).reshape(batch, both, width)
+    slab_feats = jnp.concatenate([from_head(pieces, head, h) for h in range(n_head)], axis=1)
     own_donor = slab_feats[:, :slab_sites]
     own_acceptor = slab_feats[:, slab_sites:]
 

time: 47.1 us -> 45.7 us (0.970)
  local copies, waits for them, and re-layouts: 5.48 us -> 4.27 us
    gather x2 -> x0, local copies, waits for them, and re-layouts: 1.18 us -> none  [the longest x1 0.59 us: shards(): jnp.take(by_partner, head ^ jnp.arange(n_head, dtype=jnp.int32), axis=0)]
    ppermute x3, waiting for transfers between devices: 3.54 us -> 4.1 us  [shards(): lax.ppermute(outgoing, 'head', [(i, i ^ k) for i in range(n_head)])]
  transfers between devices with their start and end apart: 14 -> 14, of which waited for: 10 -> 10; matrix products, arithmetic and copies ran while one was open for 13% -> 14% of each run, Pallas kernels for 0% -> 0%
where the time goes in v17:
time: 45.7 us; the launch traced here: 45.5 us
  starting transfers between devices  17.6 us (39%)
  waiting for transfers between devices  15.8 us (35%)
  matrix products  5.4 us (12%)
  local copies, waits for them, and re-layouts  4.27 us (9%)
  other arithmetic  1.32 us (3%)
  between operations  1.15 us (3%)
    ppermute x3, starting transfers between devices, shards(): lax.ppermute(outgoing, 'head', [(i, i ^ k) for i in range(n_head)])  5.76 us
    ppermute x3, starting transfers between devices, shards(): lax.ppermute(feat_quarter, 'head', [(i, i ^ k) for i in range(n_head)])  4.45 us
    ppermute x3, waiting for transfers between devices, shards(): lax.ppermute(outgoing, 'head', [(i, i ^ k) for i in range(n_head)])  4.1 us
    ppermute x2, waiting for transfers between devices, over_dp_bits(): lax.ppermute(held, 'dp', perm).astype(jnp.float32)  3.29 us
    ppermute x2, waiting for transfers between devices, from_seq_partner(): return lax.ppermute(outgoing, 'seq', [(0, 1), (1, 0)]).astype(jnp.float32)  3.17 us
    ppermute x2, starting transfers between devices, over_dp_bits(): lax.ppermute(held, 'dp', perm).astype(jnp.float32)  3.11 us
    ppermute x3, waiting for transfers between devices, shards(): lax.ppermute(feat_quarter, 'head', [(i, i ^ k) for i in range(n_head)])  2.66 us
    ppermute x2, starting transfers between devices, from_seq_partner(): return lax.ppermute(outgoing, 'seq', [(0, 1), (1, 0)]).astype(jnp.float32)  2.45 us
  transfers between devices with their start and end apart: 14, of which 10 were waited for; matrix products, arithmetic and copies ran while one was open for 14% of the time, Pallas kernels for 0%

profile of v17, /device:TPU:0, one launch (start us, length us, event | category | flops | bytes accessed | tf_op | source)
XLA Modules:
  0.0 45.5 jit_solution(3210969136107523655)
XLA Ops:
  0.7 0.7 %copy-done.4 = s32[1,128]{1,0:T(1,128)S(1)} copy-done((s32[1,128]{1,0:T(1,128)S(1)}, s32[1,128]{1,0:T(1,128)}, u32[]{:S(2)}) %copy-start.4) | copy-done | bytes 536
  1.4 0.7 %copy-done.5 = s32[1,128]{1,0:T(1,128)S(1)} copy-done((s32[1,128]{1,0:T(1,128)S(1)}, s32[1,128]{1,0:T(1,128)}, u32[]{:S(2)}) %copy-start.5) | copy-done | bytes 536
  2.6 0.7 %copy-done.1 = bf16[384,384]{1,0:T(8,128)(2,1)S(1)} copy-done((bf16[384,384]{1,0:T(8,128)(2,1)S(1)}, bf16[384,384]{1,0:T(8,128)(2,1)}, u32[]{:S(2)}) %copy-start.1) | copy-done | bytes 294936
  4.1 5.1 %collective-permute-start = (bf16[1,64,384]{2,1,0:T(8,128)(2,1)S(1)}, bf16[1,64,384]{2,1,0:T(8,128)(2,1)S(1)}, u32[]{:S(2)}, u32[]{:S(2)}) collective-permute-start(bf16[1,64,384]{2,1,0:T(8,128)(2,1)S(1)} %get-tuple-element.38), channel_id=1, source_target_pairs={{0,3},{1,2},{2,1},{3,0},{4,7},{5,6},{6,5},{7,4},{8,11},{9,10},{10,... | collective-permute-start | bytes 147464 | tf_op jit(solution)/shard_map/ppermute | solution.py:82
  9.2 0.6 %collective-permute-start.2 = (bf16[1,64,384]{2,1,0:T(8,128)(2,1)S(1)}, bf16[1,64,384]{2,1,0:T(8,128)(2,1)S(1)}, u32[]{:S(2)}, u32[]{:S(2)}) collective-permute-start(bf16[1,64,384]{2,1,0:T(8,128)(2,1)S(1)} %get-tuple-element.37), channel_id=1, source_target_pairs={{0,1},{1,0},{2,3},{3,2},{4,5},{5,4},{6,7},{7,6},{8,9},{9,8},{10,11... | collective-permute-start | bytes 147464 | tf_op jit(solution)/shard_map/ppermute | solution.py:82
  10.1 1.3 %collective-permute-done = bf16[1,64,384]{2,1,0:T(8,128)(2,1)S(1)} collective-permute-done((bf16[1,64,384]{2,1,0:T(8,128)(2,1)S(1)}, bf16[1,64,384]{2,1,0:T(8,128)(2,1)S(1)}, u32[]{:S(2)}, u32[]{:S(2)}) %collective-permute-start) | collective-permute-done | bytes 49184 | tf_op jit(solution)/shard_map/ppermute | solution.py:82
  11.4 2.8 %collective-permute-done.1 = bf16[1,64,384]{2,1,0:T(8,128)(2,1)S(1)} collective-permute-done((bf16[1,64,384]{2,1,0:T(8,128)(2,1)S(1)}, bf16[1,64,384]{2,1,0:T(8,128)(2,1)S(1)}, u32[]{:S(2)}, u32[]{:S(2)}) %collective-permute-start.1) | collective-permute-done | bytes 49184 | tf_op jit(solution)/shard_map/ppermute | solution.py:82
  14.3 2.2 %collective-permute-start.3 = (bf16[1,64,384]{2,1,0:T(8,128)(2,1)S(1)}, bf16[1,64,384]{2,1,0:T(8,128)(2,1)S(1)}, u32[]{:S(2)}, u32[]{:S(2)}) collective-permute-start(bf16[1,64,384]{2,1,0:T(8,128)(2,1)S(1)} %add_convert_fusion.4), channel_id=1, source_target_pairs={{0,3},{1,2},{2,1},{3,0},{4,7},{5,6},{6,5},{7,4},{8,11},{9,10},{10,... | collective-permute-start | bytes 147464 | tf_op jit(solution)/shard_map/ppermute | solution.py:90
  16.4 2.3 %collective-permute-start.5 = (bf16[1,64,384]{2,1,0:T(8,128)(2,1)S(1)}, bf16[1,64,384]{2,1,0:T(8,128)(2,1)S(1)}, u32[]{:S(2)}, u32[]{:S(2)}) collective-permute-start(bf16[1,64,384]{2,1,0:T(8,128)(2,1)S(1)} %add_convert_fusion.4), channel_id=1, source_target_pairs={{0,1},{1,0},{2,3},{3,2},{4,5},{5,4},{6,7},{7,6},{8,9},{9,8},{10,11... | collective-permute-start | bytes 147464 | tf_op jit(solution)/shard_map/ppermute | solution.py:90
  19.2 1.3 %collective-permute-done.3 = bf16[1,64,384]{2,1,0:T(8,128)(2,1)S(1)} collective-permute-done((bf16[1,64,384]{2,1,0:T(8,128)(2,1)S(1)}, bf16[1,64,384]{2,1,0:T(8,128)(2,1)S(1)}, u32[]{:S(2)}, u32[]{:S(2)}) %collective-permute-start.3) | collective-permute-done | bytes 49184 | tf_op jit(solution)/shard_map/ppermute | solution.py:90
  20.5 1.4 %collective-permute-done.4 = bf16[1,64,384]{2,1,0:T(8,128)(2,1)S(1)} collective-permute-done((bf16[1,64,384]{2,1,0:T(8,128)(2,1)S(1)}, bf16[1,64,384]{2,1,0:T(8,128)(2,1)S(1)}, u32[]{:S(2)}, u32[]{:S(2)}) %collective-permute-start.4) | collective-permute-done | bytes 49184 | tf_op jit(solution)/shard_map/ppermute | solution.py:90
  22.0 1.6 %collective-permute-start.6 = (bf16[1,179,384]{2,1,0:T(8,128)(2,1)S(1)}, bf16[1,179,384]{2,1,0:T(8,128)(2,1)S(1)}, u32[]{:S(2)}, u32[]{:S(2)}) collective-permute-start(bf16[1,179,384]{2,1,0:T(8,128)(2,1)S(1)} %pad_maximum_fusion.1), channel_id=1, source_target_pairs={{0,4},{4,0},{1,5},{5,1},{2,6},{6,2},{3,7},{7,3},{8,12},{12,8},{9,1... | collective-permute-start | bytes 412424 | tf_op jit(solution)/shard_map/ppermute | solution.py:173
  24.8 2.4 %collective-permute-done.6 = bf16[1,179,384]{2,1,0:T(8,128)(2,1)S(1)} collective-permute-done((bf16[1,179,384]{2,1,0:T(8,128)(2,1)S(1)}, bf16[1,179,384]{2,1,0:T(8,128)(2,1)S(1)}, u32[]{:S(2)}, u32[]{:S(2)}) %collective-permute-start.6) | collective-permute-done | bytes 137504 | tf_op jit(solution)/shard_map/ppermute | solution.py:173
  27.8 0.6 %fusion.3 = bf16[128,384]{1,0:T(8,128)(2,1)S(1)} fusion(bf16[1,256,384]{2,1,0:T(8,128)(2,1)S(1)} %get-tuple-element.41, bf16[1,256,384]{2,1,0:T(8,128)(2,1)S(1)} %get-tuple-element.40, pred[]{:T(512)S(6)} %eq.162, bf16[64,384]{1,0:T(8,128)(2,1)S(1)} %bitcast.164, bf16[64,384]{1,0:T(8,128)(2,1)S(1)} %bitcast.163, bf16[64,384]{1,0:T(8,128)(2,1)S(1)} %bitcast.159, ...), kind=kOutput, calls=%fused_computation.10 | convolution fusion | flops 51822592 | bytes 822657 | tf_op jit(solution)/shard_map/bij,bjp->bip/dot_general | solution.py:251
  28.8 0.4 fusion.13
  30.0 1.6 %collective-permute-start.9 = (bf16[192,192]{1,0:T(8,128)(2,1)S(1)}, bf16[192,192]{1,0:T(8,128)(2,1)S(1)}, u32[]{:S(2)}, u32[]{:S(2)}) collective-permute-start(bf16[192,192]{1,0:T(8,128)(2,1)S(1)} %constant_dynamic-slice_fusion.2), channel_id=1, source_target_pairs={{0,4},{4,0},{1,5},{5,1},{2,6},{6,2},{3,7},{7,3},{8,12},{12,8},{9,1... | collective-permute-start | bytes 221192 | tf_op jit(solution)/shard_map/ppermute | solution.py:143
  31.7 0.9 %collective-permute-start.11 = (bf16[192,192]{1,0:T(8,128)(2,1)S(1)}, bf16[192,192]{1,0:T(8,128)(2,1)S(1)}, u32[]{:S(2)}, u32[]{:S(2)}) collective-permute-start(bf16[192,192]{1,0:T(8,128)(2,1)S(1)} %constant_dynamic-slice_fusion.4), channel_id=1, source_target_pairs={{0,4},{4,0},{1,5},{5,1},{2,6},{6,2},{3,7},{7,3},{8,12},{12,8},{9,1... | collective-permute-start | bytes 221192 | tf_op jit(solution)/shard_map/ppermute | solution.py:143
  32.6 3.0 %collective-permute-done.9 = bf16[192,192]{1,0:T(8,128)(2,1)S(1)} collective-permute-done((bf16[192,192]{1,0:T(8,128)(2,1)S(1)}, bf16[192,192]{1,0:T(8,128)(2,1)S(1)}, u32[]{:S(2)}, u32[]{:S(2)}) %collective-permute-start.9) | collective-permute-done | bytes 73760 | tf_op jit(solution)/shard_map/ppermute | solution.py:143
  35.7 1.6 %collective-permute-start.10 = (bf16[192,192]{1,0:T(8,128)(2,1)S(1)}, bf16[192,192]{1,0:T(8,128)(2,1)S(1)}, u32[]{:S(2)}, u32[]{:S(2)}) collective-permute-start(bf16[192,192]{1,0:T(8,128)(2,1)S(1)} %add_convert_fusion.3), channel_id=1, source_target_pairs={{0,16},{8,24},{16,0},{24,8},{1,17},{9,25},{17,1},{25,9},{2,18},{10... | collective-permute-start | bytes 221192 | tf_op jit(solution)/shard_map/ppermute | solution.py:107
  37.4 1.6 %collective-permute-start.12 = (bf16[192,192]{1,0:T(8,128)(2,1)S(1)}, bf16[192,192]{1,0:T(8,128)(2,1)S(1)}, u32[]{:S(2)}, u32[]{:S(2)}) collective-permute-start(bf16[192,192]{1,0:T(8,128)(2,1)S(1)} %add_convert_fusion.2), channel_id=1, source_target_pairs={{0,16},{8,24},{16,0},{24,8},{1,17},{9,25},{17,1},{25,9},{2,18},{10... | collective-permute-start | bytes 221192 | tf_op jit(solution)/shard_map/ppermute | solution.py:107
  39.2 1.9 %collective-permute-done.10 = bf16[192,192]{1,0:T(8,128)(2,1)S(1)} collective-permute-done((bf16[192,192]{1,0:T(8,128)(2,1)S(1)}, bf16[192,192]{1,0:T(8,128)(2,1)S(1)}, u32[]{:S(2)}, u32[]{:S(2)}) %collective-permute-start.10) | collective-permute-done | bytes 73760 | tf_op jit(solution)/shard_map/ppermute | solution.py:107
  41.0 1.4 %collective-permute-done.12 = bf16[192,192]{1,0:T(8,128)(2,1)S(1)} collective-permute-done((bf16[192,192]{1,0:T(8,128)(2,1)S(1)}, bf16[192,192]{1,0:T(8,128)(2,1)S(1)}, u32[]{:S(2)}, u32[]{:S(2)}) %collective-permute-start.12) | collective-permute-done | bytes 73760 | tf_op jit(solution)/shard_map/ppermute | solution.py:107
  43.0 1.1 %fusion.2 = bf16[1,512,384]{2,1,0:T(8,128)(2,1)} fusion(f32[512,384]{1,0:T(8,128)S(1)} %convolution_add_fusion.1, f32[512,384]{1,0:T(8,128)S(1)} %fusion.12, s32[128]{0:T(128)S(1)} %subtract_bitcast_fusion, f32[128,384]{1,0:T(8,128)S(1)} %fusion.64), kind=kOutput, calls=%fused_computation.6 | convolution fusion | flops 51183616 | bytes 2163200 | tf_op jit(solution)/shard_map/bnr,bnc->brc/dot_general | solution.py:26
  44.6 0.9 %slice_bitcast_fusion = (f32[384,192]{0,1:T(8,128)}, f32[384,192]{0,1:T(8,128)}) fusion(f32[2,384,192]{1,2,0:T(8,128)S(1)} %fusion.9), kind=kLoop, calls=%fused_computation.30 | loop fusion | bytes 1179648 | tf_op jit(solution)/shard_map/squeeze | solution.py:323
  (80 shorter events, 6.6 us)
Async XLA Ops:
  0.6 1.4 %copy-start = (bf16[1,512,384]{2,1,0:T(8,128)(2,1)S(1)}, bf16[1,512,384]{2,1,0:T(8,128)(2,1)}, u32[]{:S(2)}) copy-start(bf16[1,512,384]{2,1,0:T(8,128)(2,1)} %param.10) | copy-start | bytes 1179652
  0.7 0.7 %copy-start.4 = (s32[1,128]{1,0:T(1,128)S(1)}, s32[1,128]{1,0:T(1,128)}, u32[]{:S(2)}) copy-start(s32[1,128]{1,0:T(1,128)} %param.11) | copy-start | bytes 1540
  1.4 0.7 %copy-start.5 = (s32[1,128]{1,0:T(1,128)S(1)}, s32[1,128]{1,0:T(1,128)}, u32[]{:S(2)}) copy-start(s32[1,128]{1,0:T(1,128)} %param.12) | copy-start | bytes 1540
  2.3 1.0 %copy-start.1 = (bf16[384,384]{1,0:T(8,128)(2,1)S(1)}, bf16[384,384]{1,0:T(8,128)(2,1)}, u32[]{:S(2)}) copy-start(bf16[384,384]{1,0:T(8,128)(2,1)} %param.14) | copy-start | bytes 884740
  2.6 1.0 %copy-start.2 = (bf16[384,384]{1,0:T(8,128)(2,1)S(1)}, bf16[384,384]{1,0:T(8,128)(2,1)}, u32[]{:S(2)}) copy-start(bf16[384,384]{1,0:T(8,128)(2,1)} %param.15) | copy-start | bytes 884740
  3.8 6.0 %copy-start.3 = (bf16[1,128,256]{2,1,0:T(8,128)(2,1)S(1)}, bf16[1,128,256]{2,1,0:T(8,128)(2,1)}, u32[]{:S(2)}) copy-start(bf16[1,128,256]{2,1,0:T(8,128)(2,1)} %param.13) | copy-start | bytes 196612
  4.1 7.3 %collective-permute-start = (bf16[1,64,384]{2,1,0:T(8,128)(2,1)S(1)}, bf16[1,64,384]{2,1,0:T(8,128)(2,1)S(1)}, u32[]{:S(2)}, u32[]{:S(2)}) collective-permute-start(bf16[1,64,384]{2,1,0:T(8,128)(2,1)S(1)} %get-tuple-element.38), channel_id=1, source_target_pairs={{0,3},{1,2},{2,1},{3,0},{4,7},{5,6},{6,5},{7,4},{8,11},{9,10},{10,... | collective-permute-start | bytes 147464 | tf_op jit(solution)/shard_map/ppermute | solution.py:82
  9.2 5.0 %collective-permute-start.1 = (bf16[1,64,384]{2,1,0:T(8,128)(2,1)S(1)}, bf16[1,64,384]{2,1,0:T(8,128)(2,1)S(1)}, u32[]{:S(2)}, u32[]{:S(2)}) collective-permute-start(bf16[1,64,384]{2,1,0:T(8,128)(2,1)S(1)} %get-tuple-element.39), channel_id=1, source_target_pairs={{0,2},{1,3},{2,0},{3,1},{4,6},{5,7},{6,4},{7,5},{8,10},{9,11},{10,... | collective-permute-start | bytes 147464 | tf_op jit(solution)/shard_map/ppermute | solution.py:82
  9.2 5.0 %collective-permute-start.2 = (bf16[1,64,384]{2,1,0:T(8,128)(2,1)S(1)}, bf16[1,64,384]{2,1,0:T(8,128)(2,1)S(1)}, u32[]{:S(2)}, u32[]{:S(2)}) collective-permute-start(bf16[1,64,384]{2,1,0:T(8,128)(2,1)S(1)} %get-tuple-element.37), channel_id=1, source_target_pairs={{0,1},{1,0},{2,3},{3,2},{4,5},{5,4},{6,7},{7,6},{8,9},{9,8},{10,11... | collective-permute-start | bytes 147464 | tf_op jit(solution)/shard_map/ppermute | solution.py:82
  14.3 6.2 %collective-permute-start.3 = (bf16[1,64,384]{2,1,0:T(8,128)(2,1)S(1)}, bf16[1,64,384]{2,1,0:T(8,128)(2,1)S(1)}, u32[]{:S(2)}, u32[]{:S(2)}) collective-permute-start(bf16[1,64,384]{2,1,0:T(8,128)(2,1)S(1)} %add_convert_fusion.4), channel_id=1, source_target_pairs={{0,3},{1,2},{2,1},{3,0},{4,7},{5,6},{6,5},{7,4},{8,11},{9,10},{10,... | collective-permute-start | bytes 147464 | tf_op jit(solution)/shard_map/ppermute | solution.py:90
  16.4 5.4 %collective-permute-start.4 = (bf16[1,64,384]{2,1,0:T(8,128)(2,1)S(1)}, bf16[1,64,384]{2,1,0:T(8,128)(2,1)S(1)}, u32[]{:S(2)}, u32[]{:S(2)}) collective-permute-start(bf16[1,64,384]{2,1,0:T(8,128)(2,1)S(1)} %add_convert_fusion.4), channel_id=1, source_target_pairs={{0,2},{1,3},{2,0},{3,1},{4,6},{5,7},{6,4},{7,5},{8,10},{9,11},{10,... | collective-permute-start | bytes 147464 | tf_op jit(solution)/shard_map/ppermute | solution.py:90
  16.4 5.4 %collective-permute-start.5 = (bf16[1,64,384]{2,1,0:T(8,128)(2,1)S(1)}, bf16[1,64,384]{2,1,0:T(8,128)(2,1)S(1)}, u32[]{:S(2)}, u32[]{:S(2)}) collective-permute-start(bf16[1,64,384]{2,1,0:T(8,128)(2,1)S(1)} %add_convert_fusion.4), channel_id=1, source_target_pairs={{0,1},{1,0},{2,3},{3,2},{4,5},{5,4},{6,7},{7,6},{8,9},{9,8},{10,11... | collective-permute-start | bytes 147464 | tf_op jit(solution)/shard_map/ppermute | solution.py:90
  22.0 5.1 %collective-permute-start.6 = (bf16[1,179,384]{2,1,0:T(8,128)(2,1)S(1)}, bf16[1,179,384]{2,1,0:T(8,128)(2,1)S(1)}, u32[]{:S(2)}, u32[]{:S(2)}) collective-permute-start(bf16[1,179,384]{2,1,0:T(8,128)(2,1)S(1)} %pad_maximum_fusion.1), channel_id=1, source_target_pairs={{0,4},{4,0},{1,5},{5,1},{2,6},{6,2},{3,7},{7,3},{8,12},{12,8},{9,1... | collective-permute-start | bytes 412424 | tf_op jit(solution)/shard_map/ppermute | solution.py:173
  24.7 5.2 %collective-permute-start.8 = (bf16[384,192]{1,0:T(8,128)(2,1)S(1)}, bf16[384,192]{1,0:T(8,128)(2,1)S(1)}, u32[]{:S(2)}, u32[]{:S(2)}) collective-permute-start(bf16[384,192]{1,0:T(8,128)(2,1)S(1)} %constant_dynamic-slice_fusion), channel_id=1, source_target_pairs={{0,8},{8,0},{16,24},{24,16},{1,9},{9,1},{17,25},{25,17},{2,10},{10... | collective-permute-start | bytes 442376 | tf_op jit(solution)/shard_map/ppermute | solution.py:135
  29.4 2.2 %collective-permute-start.7 = (bf16[384,192]{1,0:T(8,128)(2,1)S(1)}, bf16[384,192]{1,0:T(8,128)(2,1)S(1)}, u32[]{:S(2)}, u32[]{:S(2)}) collective-permute-start(bf16[384,192]{1,0:T(8,128)(2,1)S(1)} %constant_dynamic-slice_fusion.1), channel_id=1, source_target_pairs={{0,8},{8,0},{16,24},{24,16},{1,9},{9,1},{17,25},{25,17},{2,10},{10... | collective-permute-start | bytes 442376 | tf_op jit(solution)/shard_map/ppermute | solution.py:135
  30.0 5.7 %collective-permute-start.9 = (bf16[192,192]{1,0:T(8,128)(2,1)S(1)}, bf16[192,192]{1,0:T(8,128)(2,1)S(1)}, u32[]{:S(2)}, u32[]{:S(2)}) collective-permute-start(bf16[192,192]{1,0:T(8,128)(2,1)S(1)} %constant_dynamic-slice_fusion.2), channel_id=1, source_target_pairs={{0,4},{4,0},{1,5},{5,1},{2,6},{6,2},{3,7},{7,3},{8,12},{12,8},{9,1... | collective-permute-start | bytes 221192 | tf_op jit(solution)/shard_map/ppermute | solution.py:143
  31.7 5.6 %collective-permute-start.11 = (bf16[192,192]{1,0:T(8,128)(2,1)S(1)}, bf16[192,192]{1,0:T(8,128)(2,1)S(1)}, u32[]{:S(2)}, u32[]{:S(2)}) collective-permute-start(bf16[192,192]{1,0:T(8,128)(2,1)S(1)} %constant_dynamic-slice_fusion.4), channel_id=1, source_target_pairs={{0,4},{4,0},{1,5},{5,1},{2,6},{6,2},{3,7},{7,3},{8,12},{12,8},{9,1... | collective-permute-start | bytes 221192 | tf_op jit(solution)/shard_map/ppermute | solution.py:143
  35.7 5.4 %collective-permute-start.10 = (bf16[192,192]{1,0:T(8,128)(2,1)S(1)}, bf16[192,192]{1,0:T(8,128)(2,1)S(1)}, u32[]{:S(2)}, u32[]{:S(2)}) collective-permute-start(bf16[192,192]{1,0:T(8,128)(2,1)S(1)} %add_convert_fusion.3), channel_id=1, source_target_pairs={{0,16},{8,24},{16,0},{24,8},{1,17},{9,25},{17,1},{25,9},{2,18},{10... | collective-permute-start | bytes 221192 | tf_op jit(solution)/shard_map/ppermute | solution.py:107
  37.4 5.1 %collective-permute-start.12 = (bf16[192,192]{1,0:T(8,128)(2,1)S(1)}, bf16[192,192]{1,0:T(8,128)(2,1)S(1)}, u32[]{:S(2)}, u32[]{:S(2)}) collective-permute-start(bf16[192,192]{1,0:T(8,128)(2,1)S(1)} %add_convert_fusion.2), channel_id=1, source_target_pairs={{0,16},{8,24},{16,0},{24,8},{1,17},{9,25},{17,1},{25,9},{2,18},{10... | collective-permute-start | bytes 221192 | tf_op jit(solution)/shard_map/ppermute | solution.py:107
  42.6 1.8 %collective-permute-start.13 = (f32[2,192,192]{2,1,0:T(8,128)S(1)}, f32[2,192,192]{2,1,0:T(8,128)S(1)}, u32[]{:S(2)}, u32[]{:S(2)}) collective-permute-start(f32[2,192,192]{2,1,0:T(8,128)S(1)} %pad_maximum_fusion), channel_id=1, source_target_pairs={{0,8},{8,0},{16,24},{24,16},{1,9},{9,1},{17,25},{25,17},{2,10},{10... | collective-permute-start | bytes 884744 | tf_op jit(solution)/shard_map/ppermute | solution.py:318

commit v18 on v17

--- a/solution.py
+++ b/solution.py
@@ -316,7 +316,9 @@
     if n_seq != 2:
         mine = over_dp_bits(mine)
     other = lax.ppermute(mine, "dp", [(i, i ^ 1) for i in range(n_dp)])
-    mine = jnp.where(pair == 0, jnp.concatenate([mine, other], 2), jnp.concatenate([other, mine], 2))
+    full = jnp.zeros(mine.shape[:2] + (2 * half,), jnp.float32)
+    full = lax.dynamic_update_slice_in_dim(full, mine, pair * half, 2)
+    mine = lax.dynamic_update_slice_in_dim(full, other, (1 - pair) * half, 2)
     mine = jnp.swapaxes(mine, 1, 2)
     column_major = Layout(major_to_minor=(1, 0))
     grad_dw = with_layout_constraint(mine[0], column_major)

time: 45.7 us -> 48 us (1.050)
  local copies, waits for them, and re-layouts: 4.27 us -> 7.04 us
    dynamic_update_slice x0 -> x2, local copies, waits for them, and re-layouts: none -> 2.74 us  [the longest x1 1.47 us: shards(): mine = lax.dynamic_update_slice_in_dim(full, other, (1 - pair) * half, 2)]
  transfers between devices with their start and end apart: 14 -> 14, of which waited for: 10 -> 9; matrix products, arithmetic and copies ran while one was open for 14% -> 16% of each run, Pallas kernels for 0% -> 0%
where the time goes in v18:
time: 48 us; the launch traced here: 47.8 us
  starting transfers between devices  17.6 us (37%)
  waiting for transfers between devices  15.6 us (32%)
  local copies, waits for them, and re-layouts  7.04 us (15%)
  matrix products  5.4 us (11%)
  between operations  1.17 us (2%)
  other arithmetic  1.05 us (2%)
    ppermute x3, starting transfers between devices, shards(): lax.ppermute(outgoing, 'head', [(i, i ^ k) for i in range(n_head)])  5.76 us
    ppermute x3, starting transfers between devices, shards(): lax.ppermute(feat_quarter, 'head', [(i, i ^ k) for i in range(n_head)])  4.45 us
    ppermute x3, waiting for transfers between devices, shards(): lax.ppermute(outgoing, 'head', [(i, i ^ k) for i in range(n_head)])  4.1 us
    ppermute x2, waiting for transfers between devices, over_dp_bits(): lax.ppermute(held, 'dp', perm).astype(jnp.float32)  3.29 us
    ppermute x2, waiting for transfers between devices, from_seq_partner(): return lax.ppermute(outgoing, 'seq', [(0, 1), (1, 0)]).astype(jnp.float32)  3.17 us
    ppermute x2, starting transfers between devices, over_dp_bits(): lax.ppermute(held, 'dp', perm).astype(jnp.float32)  3.11 us
    ppermute x3, waiting for transfers between devices, shards(): lax.ppermute(feat_quarter, 'head', [(i, i ^ k) for i in range(n_head)])  2.66 us
    ppermute x2, starting transfers between devices, from_seq_partner(): return lax.ppermute(outgoing, 'seq', [(0, 1), (1, 0)]).astype(jnp.float32)  2.45 us
  transfers between devices with their start and end apart: 14, of which 9 were waited for; matrix products, arithmetic and copies ran while one was open for 16% of the time, Pallas kernels for 0%

profile of v18, /device:TPU:0, one launch (start us, length us, event | category | flops | bytes accessed | tf_op | source)
XLA Modules:
  0.0 47.8 jit_solution(16944376432626648717)
XLA Ops:
  0.7 0.7 %copy-done.4 = s32[1,128]{1,0:T(1,128)S(1)} copy-done((s32[1,128]{1,0:T(1,128)S(1)}, s32[1,128]{1,0:T(1,128)}, u32[]{:S(2)}) %copy-start.4) | copy-done | bytes 536
  1.4 0.7 %copy-done.5 = s32[1,128]{1,0:T(1,128)S(1)} copy-done((s32[1,128]{1,0:T(1,128)S(1)}, s32[1,128]{1,0:T(1,128)}, u32[]{:S(2)}) %copy-start.5) | copy-done | bytes 536
  2.6 0.7 %copy-done.1 = bf16[384,384]{1,0:T(8,128)(2,1)S(1)} copy-done((bf16[384,384]{1,0:T(8,128)(2,1)S(1)}, bf16[384,384]{1,0:T(8,128)(2,1)}, u32[]{:S(2)}) %copy-start.1) | copy-done | bytes 294936
  4.1 5.1 %collective-permute-start = (bf16[1,64,384]{2,1,0:T(8,128)(2,1)S(1)}, bf16[1,64,384]{2,1,0:T(8,128)(2,1)S(1)}, u32[]{:S(2)}, u32[]{:S(2)}) collective-permute-start(bf16[1,64,384]{2,1,0:T(8,128)(2,1)S(1)} %get-tuple-element.38), channel_id=1, source_target_pairs={{0,3},{1,2},{2,1},{3,0},{4,7},{5,6},{6,5},{7,4},{8,11},{9,10},{10,... | collective-permute-start | bytes 147464 | tf_op jit(solution)/shard_map/ppermute | solution.py:82
  9.2 0.6 %collective-permute-start.2 = (bf16[1,64,384]{2,1,0:T(8,128)(2,1)S(1)}, bf16[1,64,384]{2,1,0:T(8,128)(2,1)S(1)}, u32[]{:S(2)}, u32[]{:S(2)}) collective-permute-start(bf16[1,64,384]{2,1,0:T(8,128)(2,1)S(1)} %get-tuple-element.37), channel_id=1, source_target_pairs={{0,1},{1,0},{2,3},{3,2},{4,5},{5,4},{6,7},{7,6},{8,9},{9,8},{10,11... | collective-permute-start | bytes 147464 | tf_op jit(solution)/shard_map/ppermute | solution.py:82
  10.1 1.3 %collective-permute-done = bf16[1,64,384]{2,1,0:T(8,128)(2,1)S(1)} collective-permute-done((bf16[1,64,384]{2,1,0:T(8,128)(2,1)S(1)}, bf16[1,64,384]{2,1,0:T(8,128)(2,1)S(1)}, u32[]{:S(2)}, u32[]{:S(2)}) %collective-permute-start) | collective-permute-done | bytes 49184 | tf_op jit(solution)/shard_map/ppermute | solution.py:82
  11.4 2.8 %collective-permute-done.1 = bf16[1,64,384]{2,1,0:T(8,128)(2,1)S(1)} collective-permute-done((bf16[1,64,384]{2,1,0:T(8,128)(2,1)S(1)}, bf16[1,64,384]{2,1,0:T(8,128)(2,1)S(1)}, u32[]{:S(2)}, u32[]{:S(2)}) %collective-permute-start.1) | collective-permute-done | bytes 49184 | tf_op jit(solution)/shard_map/ppermute | solution.py:82
  14.3 2.2 %collective-permute-start.3 = (bf16[1,64,384]{2,1,0:T(8,128)(2,1)S(1)}, bf16[1,64,384]{2,1,0:T(8,128)(2,1)S(1)}, u32[]{:S(2)}, u32[]{:S(2)}) collective-permute-start(bf16[1,64,384]{2,1,0:T(8,128)(2,1)S(1)} %add_convert_fusion.4), channel_id=1, source_target_pairs={{0,3},{1,2},{2,1},{3,0},{4,7},{5,6},{6,5},{7,4},{8,11},{9,10},{10,... | collective-permute-start | bytes 147464 | tf_op jit(solution)/shard_map/ppermute | solution.py:90
  16.4 2.3 %collective-permute-start.5 = (bf16[1,64,384]{2,1,0:T(8,128)(2,1)S(1)}, bf16[1,64,384]{2,1,0:T(8,128)(2,1)S(1)}, u32[]{:S(2)}, u32[]{:S(2)}) collective-permute-start(bf16[1,64,384]{2,1,0:T(8,128)(2,1)S(1)} %add_convert_fusion.4), channel_id=1, source_target_pairs={{0,1},{1,0},{2,3},{3,2},{4,5},{5,4},{6,7},{7,6},{8,9},{9,8},{10,11... | collective-permute-start | bytes 147464 | tf_op jit(solution)/shard_map/ppermute | solution.py:90
  19.2 1.3 %collective-permute-done.3 = bf16[1,64,384]{2,1,0:T(8,128)(2,1)S(1)} collective-permute-done((bf16[1,64,384]{2,1,0:T(8,128)(2,1)S(1)}, bf16[1,64,384]{2,1,0:T(8,128)(2,1)S(1)}, u32[]{:S(2)}, u32[]{:S(2)}) %collective-permute-start.3) | collective-permute-done | bytes 49184 | tf_op jit(solution)/shard_map/ppermute | solution.py:90
  20.5 1.4 %collective-permute-done.4 = bf16[1,64,384]{2,1,0:T(8,128)(2,1)S(1)} collective-permute-done((bf16[1,64,384]{2,1,0:T(8,128)(2,1)S(1)}, bf16[1,64,384]{2,1,0:T(8,128)(2,1)S(1)}, u32[]{:S(2)}, u32[]{:S(2)}) %collective-permute-start.4) | collective-permute-done | bytes 49184 | tf_op jit(solution)/shard_map/ppermute | solution.py:90
  22.0 1.6 %collective-permute-start.6 = (bf16[1,179,384]{2,1,0:T(8,128)(2,1)S(1)}, bf16[1,179,384]{2,1,0:T(8,128)(2,1)S(1)}, u32[]{:S(2)}, u32[]{:S(2)}) collective-permute-start(bf16[1,179,384]{2,1,0:T(8,128)(2,1)S(1)} %pad_maximum_fusion.1), channel_id=1, source_target_pairs={{0,4},{4,0},{1,5},{5,1},{2,6},{6,2},{3,7},{7,3},{8,12},{12,8},{9,1... | collective-permute-start | bytes 412424 | tf_op jit(solution)/shard_map/ppermute | solution.py:173
  24.8 2.4 %collective-permute-done.6 = bf16[1,179,384]{2,1,0:T(8,128)(2,1)S(1)} collective-permute-done((bf16[1,179,384]{2,1,0:T(8,128)(2,1)S(1)}, bf16[1,179,384]{2,1,0:T(8,128)(2,1)S(1)}, u32[]{:S(2)}, u32[]{:S(2)}) %collective-permute-start.6) | collective-permute-done | bytes 137504 | tf_op jit(solution)/shard_map/ppermute | solution.py:173
  30.0 1.6 %collective-permute-start.9 = (bf16[192,192]{1,0:T(8,128)(2,1)S(1)}, bf16[192,192]{1,0:T(8,128)(2,1)S(1)}, u32[]{:S(2)}, u32[]{:S(2)}) collective-permute-start(bf16[192,192]{1,0:T(8,128)(2,1)S(1)} %constant_dynamic-slice_fusion), channel_id=1, source_target_pairs={{0,4},{4,0},{1,5},{5,1},{2,6},{6,2},{3,7},{7,3},{8,12},{12,8},{9,1... | collective-permute-start | bytes 221192 | tf_op jit(solution)/shard_map/ppermute | solution.py:143
  31.7 0.9 %collective-permute-start.11 = (bf16[192,192]{1,0:T(8,128)(2,1)S(1)}, bf16[192,192]{1,0:T(8,128)(2,1)S(1)}, u32[]{:S(2)}, u32[]{:S(2)}) collective-permute-start(bf16[192,192]{1,0:T(8,128)(2,1)S(1)} %constant_dynamic-slice_fusion.3), channel_id=1, source_target_pairs={{0,4},{4,0},{1,5},{5,1},{2,6},{6,2},{3,7},{7,3},{8,12},{12,8},{9,1... | collective-permute-start | bytes 221192 | tf_op jit(solution)/shard_map/ppermute | solution.py:143
  32.6 3.0 %collective-permute-done.9 = bf16[192,192]{1,0:T(8,128)(2,1)S(1)} collective-permute-done((bf16[192,192]{1,0:T(8,128)(2,1)S(1)}, bf16[192,192]{1,0:T(8,128)(2,1)S(1)}, u32[]{:S(2)}, u32[]{:S(2)}) %collective-permute-start.9) | collective-permute-done | bytes 73760 | tf_op jit(solution)/shard_map/ppermute | solution.py:143
  35.7 1.6 %collective-permute-start.10 = (bf16[192,192]{1,0:T(8,128)(2,1)S(1)}, bf16[192,192]{1,0:T(8,128)(2,1)S(1)}, u32[]{:S(2)}, u32[]{:S(2)}) collective-permute-start(bf16[192,192]{1,0:T(8,128)(2,1)S(1)} %add_convert_fusion.3), channel_id=1, source_target_pairs={{0,16},{8,24},{16,0},{24,8},{1,17},{9,25},{17,1},{25,9},{2,18},{10... | collective-permute-start | bytes 221192 | tf_op jit(solution)/shard_map/ppermute | solution.py:107
  37.4 1.6 %collective-permute-start.12 = (bf16[192,192]{1,0:T(8,128)(2,1)S(1)}, bf16[192,192]{1,0:T(8,128)(2,1)S(1)}, u32[]{:S(2)}, u32[]{:S(2)}) collective-permute-start(bf16[192,192]{1,0:T(8,128)(2,1)S(1)} %add_convert_fusion.2), channel_id=1, source_target_pairs={{0,16},{8,24},{16,0},{24,8},{1,17},{9,25},{17,1},{25,9},{2,18},{10... | collective-permute-start | bytes 221192 | tf_op jit(solution)/shard_map/ppermute | solution.py:107
  39.2 1.9 %collective-permute-done.10 = bf16[192,192]{1,0:T(8,128)(2,1)S(1)} collective-permute-done((bf16[192,192]{1,0:T(8,128)(2,1)S(1)}, bf16[192,192]{1,0:T(8,128)(2,1)S(1)}, u32[]{:S(2)}, u32[]{:S(2)}) %collective-permute-start.10) | collective-permute-done | bytes 73760 | tf_op jit(solution)/shard_map/ppermute | solution.py:107
  41.0 1.4 %collective-permute-done.12 = bf16[192,192]{1,0:T(8,128)(2,1)S(1)} collective-permute-done((bf16[192,192]{1,0:T(8,128)(2,1)S(1)}, bf16[192,192]{1,0:T(8,128)(2,1)S(1)}, u32[]{:S(2)}, u32[]{:S(2)}) %collective-permute-start.12) | collective-permute-done | bytes 73760 | tf_op jit(solution)/shard_map/ppermute | solution.py:107
  43.0 1.1 %fusion.2 = bf16[1,512,384]{2,1,0:T(8,128)(2,1)} fusion(f32[512,384]{1,0:T(8,128)S(1)} %convolution_add_fusion.1, f32[512,384]{1,0:T(8,128)S(1)} %fusion.11, s32[128]{0:T(128)S(1)} %subtract_bitcast_fusion, f32[128,384]{1,0:T(8,128)S(1)} %fusion.63), kind=kOutput, calls=%fused_computation.6 | convolution fusion | flops 51183616 | bytes 2163200 | tf_op jit(solution)/shard_map/bnr,bnc->brc/dot_general | solution.py:26
  44.2 1.3 %dynamic_update_slice.23 = f32[2,192,384]{2,1,0:T(8,128)S(1)} dynamic-update-slice(f32[2,192,384]{2,1,0:T(8,128)S(1)} %broadcast_in_dim.52, f32[2,192,192]{2,1,0:T(8,128)S(1)} %pad_maximum_fusion, s32[]{:T(128)} %constant.133.clone.1, s32[]{:T(128)} %constant.133.clone.1, s32[]{:T(128)S(6)} %select_n.468) | dynamic-update-slice | bytes 589828 | tf_op jit(solution)/shard_map/dynamic_update_slice | solution.py:320
  45.5 1.5 %dynamic_update_slice.24 = f32[2,192,384]{2,1,0:T(8,128)S(1)} dynamic-update-slice(f32[2,192,384]{2,1,0:T(8,128)S(1)} %dynamic_update_slice.23, f32[2,192,192]{2,1,0:T(8,128)S(1)} %collective-permute-done.13, s32[]{:T(128)} %constant.133.clone.1, s32[]{:T(128)} %constant.133.clone.1, s32[]{:T(128)S(6)} %select_n.469) | dynamic-update-slice | bytes 589828 | tf_op jit(solution)/shard_map/dynamic_update_slice | solution.py:321
  47.0 0.9 %slice_bitcast_fusion = (f32[384,192]{0,1:T(8,128)}, f32[384,192]{0,1:T(8,128)}) fusion(f32[2,384,192]{1,2,0:T(8,128)S(1)} %bitcast.158), kind=kLoop, calls=%fused_computation.28 | loop fusion | bytes 1179648 | tf_op jit(solution)/shard_map/squeeze | solution.py:325
  (82 shorter events, 7.1 us)
Async XLA Ops:
  0.6 1.4 %copy-start = (bf16[1,512,384]{2,1,0:T(8,128)(2,1)S(1)}, bf16[1,512,384]{2,1,0:T(8,128)(2,1)}, u32[]{:S(2)}) copy-start(bf16[1,512,384]{2,1,0:T(8,128)(2,1)} %param.10) | copy-start | bytes 1179652
  0.7 0.7 %copy-start.4 = (s32[1,128]{1,0:T(1,128)S(1)}, s32[1,128]{1,0:T(1,128)}, u32[]{:S(2)}) copy-start(s32[1,128]{1,0:T(1,128)} %param.11) | copy-start | bytes 1540
  1.4 0.7 %copy-start.5 = (s32[1,128]{1,0:T(1,128)S(1)}, s32[1,128]{1,0:T(1,128)}, u32[]{:S(2)}) copy-start(s32[1,128]{1,0:T(1,128)} %param.12) | copy-start | bytes 1540
  2.3 1.0 %copy-start.1 = (bf16[384,384]{1,0:T(8,128)(2,1)S(1)}, bf16[384,384]{1,0:T(8,128)(2,1)}, u32[]{:S(2)}) copy-start(bf16[384,384]{1,0:T(8,128)(2,1)} %param.14) | copy-start | bytes 884740
  2.6 1.0 %copy-start.2 = (bf16[384,384]{1,0:T(8,128)(2,1)S(1)}, bf16[384,384]{1,0:T(8,128)(2,1)}, u32[]{:S(2)}) copy-start(bf16[384,384]{1,0:T(8,128)(2,1)} %param.15) | copy-start | bytes 884740
  3.8 6.0 %copy-start.3 = (bf16[1,128,256]{2,1,0:T(8,128)(2,1)S(1)}, bf16[1,128,256]{2,1,0:T(8,128)(2,1)}, u32[]{:S(2)}) copy-start(bf16[1,128,256]{2,1,0:T(8,128)(2,1)} %param.13) | copy-start | bytes 196612
  4.1 7.3 %collective-permute-start = (bf16[1,64,384]{2,1,0:T(8,128)(2,1)S(1)}, bf16[1,64,384]{2,1,0:T(8,128)(2,1)S(1)}, u32[]{:S(2)}, u32[]{:S(2)}) collective-permute-start(bf16[1,64,384]{2,1,0:T(8,128)(2,1)S(1)} %get-tuple-element.38), channel_id=1, source_target_pairs={{0,3},{1,2},{2,1},{3,0},{4,7},{5,6},{6,5},{7,4},{8,11},{9,10},{10,... | collective-permute-start | bytes 147464 | tf_op jit(solution)/shard_map/ppermute | solution.py:82
  9.2 5.0 %collective-permute-start.1 = (bf16[1,64,384]{2,1,0:T(8,128)(2,1)S(1)}, bf16[1,64,384]{2,1,0:T(8,128)(2,1)S(1)}, u32[]{:S(2)}, u32[]{:S(2)}) collective-permute-start(bf16[1,64,384]{2,1,0:T(8,128)(2,1)S(1)} %get-tuple-element.39), channel_id=1, source_target_pairs={{0,2},{1,3},{2,0},{3,1},{4,6},{5,7},{6,4},{7,5},{8,10},{9,11},{10,... | collective-permute-start | bytes 147464 | tf_op jit(solution)/shard_map/ppermute | solution.py:82
  9.2 5.0 %collective-permute-start.2 = (bf16[1,64,384]{2,1,0:T(8,128)(2,1)S(1)}, bf16[1,64,384]{2,1,0:T(8,128)(2,1)S(1)}, u32[]{:S(2)}, u32[]{:S(2)}) collective-permute-start(bf16[1,64,384]{2,1,0:T(8,128)(2,1)S(1)} %get-tuple-element.37), channel_id=1, source_target_pairs={{0,1},{1,0},{2,3},{3,2},{4,5},{5,4},{6,7},{7,6},{8,9},{9,8},{10,11... | collective-permute-start | bytes 147464 | tf_op jit(solution)/shard_map/ppermute | solution.py:82
  14.3 6.2 %collective-permute-start.3 = (bf16[1,64,384]{2,1,0:T(8,128)(2,1)S(1)}, bf16[1,64,384]{2,1,0:T(8,128)(2,1)S(1)}, u32[]{:S(2)}, u32[]{:S(2)}) collective-permute-start(bf16[1,64,384]{2,1,0:T(8,128)(2,1)S(1)} %add_convert_fusion.4), channel_id=1, source_target_pairs={{0,3},{1,2},{2,1},{3,0},{4,7},{5,6},{6,5},{7,4},{8,11},{9,10},{10,... | collective-permute-start | bytes 147464 | tf_op jit(solution)/shard_map/ppermute | solution.py:90
  16.4 5.4 %collective-permute-start.4 = (bf16[1,64,384]{2,1,0:T(8,128)(2,1)S(1)}, bf16[1,64,384]{2,1,0:T(8,128)(2,1)S(1)}, u32[]{:S(2)}, u32[]{:S(2)}) collective-permute-start(bf16[1,64,384]{2,1,0:T(8,128)(2,1)S(1)} %add_convert_fusion.4), channel_id=1, source_target_pairs={{0,2},{1,3},{2,0},{3,1},{4,6},{5,7},{6,4},{7,5},{8,10},{9,11},{10,... | collective-permute-start | bytes 147464 | tf_op jit(solution)/shard_map/ppermute | solution.py:90
  16.4 5.4 %collective-permute-start.5 = (bf16[1,64,384]{2,1,0:T(8,128)(2,1)S(1)}, bf16[1,64,384]{2,1,0:T(8,128)(2,1)S(1)}, u32[]{:S(2)}, u32[]{:S(2)}) collective-permute-start(bf16[1,64,384]{2,1,0:T(8,128)(2,1)S(1)} %add_convert_fusion.4), channel_id=1, source_target_pairs={{0,1},{1,0},{2,3},{3,2},{4,5},{5,4},{6,7},{7,6},{8,9},{9,8},{10,11... | collective-permute-start | bytes 147464 | tf_op jit(solution)/shard_map/ppermute | solution.py:90
  22.0 5.1 %collective-permute-start.6 = (bf16[1,179,384]{2,1,0:T(8,128)(2,1)S(1)}, bf16[1,179,384]{2,1,0:T(8,128)(2,1)S(1)}, u32[]{:S(2)}, u32[]{:S(2)}) collective-permute-start(bf16[1,179,384]{2,1,0:T(8,128)(2,1)S(1)} %pad_maximum_fusion.1), channel_id=1, source_target_pairs={{0,4},{4,0},{1,5},{5,1},{2,6},{6,2},{3,7},{7,3},{8,12},{12,8},{9,1... | collective-permute-start | bytes 412424 | tf_op jit(solution)/shard_map/ppermute | solution.py:173
  24.7 5.2 %collective-permute-start.8 = (bf16[384,192]{1,0:T(8,128)(2,1)S(1)}, bf16[384,192]{1,0:T(8,128)(2,1)S(1)}, u32[]{:S(2)}, u32[]{:S(2)}) collective-permute-start(bf16[384,192]{1,0:T(8,128)(2,1)S(1)} %constant_dynamic-slice_fusion.1), channel_id=1, source_target_pairs={{0,8},{8,0},{16,24},{24,16},{1,9},{9,1},{17,25},{25,17},{2,10},{10... | collective-permute-start | bytes 442376 | tf_op jit(solution)/shard_map/ppermute | solution.py:135
  29.4 2.2 %collective-permute-start.7 = (bf16[384,192]{1,0:T(8,128)(2,1)S(1)}, bf16[384,192]{1,0:T(8,128)(2,1)S(1)}, u32[]{:S(2)}, u32[]{:S(2)}) collective-permute-start(bf16[384,192]{1,0:T(8,128)(2,1)S(1)} %constant_dynamic-slice_fusion.2), channel_id=1, source_target_pairs={{0,8},{8,0},{16,24},{24,16},{1,9},{9,1},{17,25},{25,17},{2,10},{10... | collective-permute-start | bytes 442376 | tf_op jit(solution)/shard_map/ppermute | solution.py:135
  30.0 5.7 %collective-permute-start.9 = (bf16[192,192]{1,0:T(8,128)(2,1)S(1)}, bf16[192,192]{1,0:T(8,128)(2,1)S(1)}, u32[]{:S(2)}, u32[]{:S(2)}) collective-permute-start(bf16[192,192]{1,0:T(8,128)(2,1)S(1)} %constant_dynamic-slice_fusion), channel_id=1, source_target_pairs={{0,4},{4,0},{1,5},{5,1},{2,6},{6,2},{3,7},{7,3},{8,12},{12,8},{9,1... | collective-permute-start | bytes 221192 | tf_op jit(solution)/shard_map/ppermute | solution.py:143
  31.7 5.6 %collective-permute-start.11 = (bf16[192,192]{1,0:T(8,128)(2,1)S(1)}, bf16[192,192]{1,0:T(8,128)(2,1)S(1)}, u32[]{:S(2)}, u32[]{:S(2)}) collective-permute-start(bf16[192,192]{1,0:T(8,128)(2,1)S(1)} %constant_dynamic-slice_fusion.3), channel_id=1, source_target_pairs={{0,4},{4,0},{1,5},{5,1},{2,6},{6,2},{3,7},{7,3},{8,12},{12,8},{9,1... | collective-permute-start | bytes 221192 | tf_op jit(solution)/shard_map/ppermute | solution.py:143
  35.7 5.4 %collective-permute-start.10 = (bf16[192,192]{1,0:T(8,128)(2,1)S(1)}, bf16[192,192]{1,0:T(8,128)(2,1)S(1)}, u32[]{:S(2)}, u32[]{:S(2)}) collective-permute-start(bf16[192,192]{1,0:T(8,128)(2,1)S(1)} %add_convert_fusion.3), channel_id=1, source_target_pairs={{0,16},{8,24},{16,0},{24,8},{1,17},{9,25},{17,1},{25,9},{2,18},{10... | collective-permute-start | bytes 221192 | tf_op jit(solution)/shard_map/ppermute | solution.py:107
  37.4 5.1 %collective-permute-start.12 = (bf16[192,192]{1,0:T(8,128)(2,1)S(1)}, bf16[192,192]{1,0:T(8,128)(2,1)S(1)}, u32[]{:S(2)}, u32[]{:S(2)}) collective-permute-start(bf16[192,192]{1,0:T(8,128)(2,1)S(1)} %add_convert_fusion.2), channel_id=1, source_target_pairs={{0,16},{8,24},{16,0},{24,8},{1,17},{9,25},{17,1},{25,9},{2,18},{10... | collective-permute-start | bytes 221192 | tf_op jit(solution)/shard_map/ppermute | solution.py:107
  42.6 2.9 %collective-permute-start.13 = (f32[2,192,192]{2,1,0:T(8,128)S(1)}, f32[2,192,192]{2,1,0:T(8,128)S(1)}, u32[]{:S(2)}, u32[]{:S(2)}) collective-permute-start(f32[2,192,192]{2,1,0:T(8,128)S(1)} %pad_maximum_fusion), channel_id=1, source_target_pairs={{0,8},{8,0},{16,24},{24,16},{1,9},{9,1},{17,25},{25,17},{2,10},{10... | collective-permute-start | bytes 884744 | tf_op jit(solution)/shard_map/ppermute | solution.py:318

commit v19 on v17

--- a/solution.py
+++ b/solution.py
@@ -116,14 +116,16 @@
         )
         allowed_own = (donor_pos[:, :, None] >= 0) & (acceptor_pos[:, None, :] > donor_pos[:, :, None])
         slope_own = pair_slope(scores_own, target_own, allowed_own)
-        early_acceptor = (
-            jnp.einsum("bij,bip->bjp", slope_own, own_donor, preferred_element_type=jnp.float32) * scale
-        ).astype(jnp.bfloat16)
-        early_donor = (
-            jnp.einsum("bij,bjp->bip", slope_own, own_acceptor, preferred_element_type=jnp.float32)
-            * scale
-        ).astype(jnp.bfloat16)
+        own_part_acceptor = jnp.einsum(
+            "bij,bip->bjp", slope_own, own_donor, preferred_element_type=jnp.float32
+        )
+        own_part_donor = jnp.einsum(
+            "bij,bjp->bip", slope_own, own_acceptor, preferred_element_type=jnp.float32
+        )
+        early_acceptor = (own_part_acceptor * scale).astype(jnp.bfloat16)
+        early_donor = (own_part_donor * scale).astype(jnp.bfloat16)
         first = slab == 0
+        own_part_late = jnp.where(first, own_part_donor, own_part_acceptor)
         grad_early = jnp.where(first, early_acceptor, early_donor)
         rows_early = jnp.where(first, acceptor_rows, donor_rows)
 
@@ -238,18 +240,20 @@
     if n_seq == 2:
         first = slab == 0
         queries = jnp.where(first, own_donor, own_acceptor)
-        keys = jnp.where(first, acceptor_feat_all, donor_feat_all)
-        scores_late = (
-            jnp.einsum("bip,bjp->bij", queries, keys, preferred_element_type=jnp.float32) * scale
-        )
-        allowed_row = (donor_pos[:, :, None] >= 0) & (acceptor_eff[:, None, :] > donor_pos[:, :, None])
-        allowed_col = (donor_eff[:, None, :] >= 0) & (acceptor_pos[:, :, None] > donor_eff[:, None, :])
-        allowed_late = jnp.where(first, allowed_row, allowed_col)
-        target_late = jnp.where(first, target, jnp.swapaxes(target_col, 1, 2))
-        slope_late = pair_slope(scores_late, target_late, allowed_late)
-        grad_late = (
-            jnp.einsum("bij,bjp->bip", slope_late, keys, preferred_element_type=jnp.float32) * scale
-        ).astype(jnp.bfloat16)
+        scores_cross = (
+            jnp.einsum("bip,bjp->bij", queries, feat_in, preferred_element_type=jnp.float32) * scale
+        )
+        own_ok = jnp.where(first, donor_pos >= 0, acceptor_pos >= 0)
+        other_ok = jnp.where(first, acceptor_in, donor_in)
+        allowed_cross = own_ok[:, :, None] & other_ok[:, None, :]
+        target_cross = jnp.where(
+            first,
+            lax.dynamic_slice_in_dim(target, (1 - slab) * slab_sites, slab_sites, 2),
+            jnp.swapaxes(target_in, 1, 2),
+        )
+        slope_cross = pair_slope(scores_cross, target_cross, allowed_cross)
+        cross = jnp.einsum("bij,bjp->bip", slope_cross, feat_in, preferred_element_type=jnp.float32)
+        grad_late = ((own_part_late + cross) * scale).astype(jnp.bfloat16)
     else:
         scores_row = (
             jnp.einsum("bip,bjp->bij", donor_feat, acceptor_feat_all, preferred_element_type=jnp.float32)

time: 45.7 us -> 45.5 us (level)
  waiting for transfers between devices: 15.8 us -> 16.7 us
  local copies, waits for them, and re-layouts: 4.27 us -> 3.69 us
    ppermute x1, waiting for transfers between devices: 2.37 us -> 3.08 us  [shards(): arrived = lax.ppermute(payload, 'seq', perm)]
    unnamed x16, local copies, waits for them, and re-layouts: 2.34 us -> 1.87 us
  transfers between devices with their start and end apart: 14 -> 14, of which waited for: 10 -> 10; matrix products, arithmetic and copies ran while one was open for 14% -> 11% of each run, Pallas kernels for 0% -> 0%
where the time goes in v19:
time: 45.5 us; the launch traced here: 45.3 us
  starting transfers between devices  17.6 us (39%)
  waiting for transfers between devices  16.7 us (37%)
  matrix products  5.2 us (11%)
  local copies, waits for them, and re-layouts  3.69 us (8%)
  other arithmetic  1.13 us (2%)
  between operations  1.06 us (2%)
    ppermute x3, starting transfers between devices, shards(): lax.ppermute(outgoing, 'head', [(i, i ^ k) for i in range(n_head)])  5.75 us
    ppermute x3, starting transfers between devices, shards(): lax.ppermute(feat_quarter, 'head', [(i, i ^ k) for i in range(n_head)])  4.45 us
    ppermute x3, waiting for transfers between devices, shards(): lax.ppermute(outgoing, 'head', [(i, i ^ k) for i in range(n_head)])  4.27 us
    ppermute x2, waiting for transfers between devices, over_dp_bits(): lax.ppermute(held, 'dp', perm).astype(jnp.float32)  3.29 us
    ppermute x2, waiting for transfers between devices, from_seq_partner(): return lax.ppermute(outgoing, 'seq', [(0, 1), (1, 0)]).astype(jnp.float32)  3.17 us
    ppermute x2, starting transfers between devices, over_dp_bits(): lax.ppermute(held, 'dp', perm).astype(jnp.float32)  3.11 us
    ppermute x1, waiting for transfers between devices, shards(): arrived = lax.ppermute(payload, 'seq', perm)  3.08 us
    ppermute x3, waiting for transfers between devices, shards(): lax.ppermute(feat_quarter, 'head', [(i, i ^ k) for i in range(n_head)])  2.67 us
  transfers between devices with their start and end apart: 14, of which 10 were waited for; matrix products, arithmetic and copies ran while one was open for 11% of the time, Pallas kernels for 0%

profile of v19, /device:TPU:0, one launch (start us, length us, event | category | flops | bytes accessed | tf_op | source)
XLA Modules:
  0.0 45.3 jit_solution(4223657880100876871)
XLA Ops:
  0.7 0.7 %copy-done.4 = s32[1,128]{1,0:T(1,128)S(1)} copy-done((s32[1,128]{1,0:T(1,128)S(1)}, s32[1,128]{1,0:T(1,128)}, u32[]{:S(2)}) %copy-start.4) | copy-done | bytes 536
  2.2 0.7 %copy-done.1 = bf16[384,384]{1,0:T(8,128)(2,1)S(1)} copy-done((bf16[384,384]{1,0:T(8,128)(2,1)S(1)}, bf16[384,384]{1,0:T(8,128)(2,1)}, u32[]{:S(2)}) %copy-start.1) | copy-done | bytes 294936
  3.7 5.1 %collective-permute-start = (bf16[1,64,384]{2,1,0:T(8,128)(2,1)S(1)}, bf16[1,64,384]{2,1,0:T(8,128)(2,1)S(1)}, u32[]{:S(2)}, u32[]{:S(2)}) collective-permute-start(bf16[1,64,384]{2,1,0:T(8,128)(2,1)S(1)} %get-tuple-element.38), channel_id=1, source_target_pairs={{0,3},{1,2},{2,1},{3,0},{4,7},{5,6},{6,5},{7,4},{8,11},{9,10},{10,... | collective-permute-start | bytes 147464 | tf_op jit(solution)/shard_map/ppermute | solution.py:82
  8.8 0.6 %collective-permute-start.2 = (bf16[1,64,384]{2,1,0:T(8,128)(2,1)S(1)}, bf16[1,64,384]{2,1,0:T(8,128)(2,1)S(1)}, u32[]{:S(2)}, u32[]{:S(2)}) collective-permute-start(bf16[1,64,384]{2,1,0:T(8,128)(2,1)S(1)} %get-tuple-element.37), channel_id=1, source_target_pairs={{0,1},{1,0},{2,3},{3,2},{4,5},{5,4},{6,7},{7,6},{8,9},{9,8},{10,11... | collective-permute-start | bytes 147464 | tf_op jit(solution)/shard_map/ppermute | solution.py:82
  9.5 1.5 %collective-permute-done = bf16[1,64,384]{2,1,0:T(8,128)(2,1)S(1)} collective-permute-done((bf16[1,64,384]{2,1,0:T(8,128)(2,1)S(1)}, bf16[1,64,384]{2,1,0:T(8,128)(2,1)S(1)}, u32[]{:S(2)}, u32[]{:S(2)}) %collective-permute-start) | collective-permute-done | bytes 49184 | tf_op jit(solution)/shard_map/ppermute | solution.py:82
  11.0 2.8 %collective-permute-done.1 = bf16[1,64,384]{2,1,0:T(8,128)(2,1)S(1)} collective-permute-done((bf16[1,64,384]{2,1,0:T(8,128)(2,1)S(1)}, bf16[1,64,384]{2,1,0:T(8,128)(2,1)S(1)}, u32[]{:S(2)}, u32[]{:S(2)}) %collective-permute-start.1) | collective-permute-done | bytes 49184 | tf_op jit(solution)/shard_map/ppermute | solution.py:82
  13.9 2.2 %collective-permute-start.3 = (bf16[1,64,384]{2,1,0:T(8,128)(2,1)S(1)}, bf16[1,64,384]{2,1,0:T(8,128)(2,1)S(1)}, u32[]{:S(2)}, u32[]{:S(2)}) collective-permute-start(bf16[1,64,384]{2,1,0:T(8,128)(2,1)S(1)} %add_convert_fusion.4), channel_id=1, source_target_pairs={{0,3},{1,2},{2,1},{3,0},{4,7},{5,6},{6,5},{7,4},{8,11},{9,10},{10,... | collective-permute-start | bytes 147464 | tf_op jit(solution)/shard_map/ppermute | solution.py:90
  16.1 2.3 %collective-permute-start.5 = (bf16[1,64,384]{2,1,0:T(8,128)(2,1)S(1)}, bf16[1,64,384]{2,1,0:T(8,128)(2,1)S(1)}, u32[]{:S(2)}, u32[]{:S(2)}) collective-permute-start(bf16[1,64,384]{2,1,0:T(8,128)(2,1)S(1)} %add_convert_fusion.4), channel_id=1, source_target_pairs={{0,1},{1,0},{2,3},{3,2},{4,5},{5,4},{6,7},{7,6},{8,9},{9,8},{10,11... | collective-permute-start | bytes 147464 | tf_op jit(solution)/shard_map/ppermute | solution.py:90
  18.8 1.3 %collective-permute-done.3 = bf16[1,64,384]{2,1,0:T(8,128)(2,1)S(1)} collective-permute-done((bf16[1,64,384]{2,1,0:T(8,128)(2,1)S(1)}, bf16[1,64,384]{2,1,0:T(8,128)(2,1)S(1)}, u32[]{:S(2)}, u32[]{:S(2)}) %collective-permute-start.3) | collective-permute-done | bytes 49184 | tf_op jit(solution)/shard_map/ppermute | solution.py:90
  20.1 1.4 %collective-permute-done.4 = bf16[1,64,384]{2,1,0:T(8,128)(2,1)S(1)} collective-permute-done((bf16[1,64,384]{2,1,0:T(8,128)(2,1)S(1)}, bf16[1,64,384]{2,1,0:T(8,128)(2,1)S(1)}, u32[]{:S(2)}, u32[]{:S(2)}) %collective-permute-start.4) | collective-permute-done | bytes 49184 | tf_op jit(solution)/shard_map/ppermute | solution.py:90
  22.3 1.6 %collective-permute-start.6 = (bf16[1,179,384]{2,1,0:T(8,128)(2,1)S(1)}, bf16[1,179,384]{2,1,0:T(8,128)(2,1)S(1)}, u32[]{:S(2)}, u32[]{:S(2)}) collective-permute-start(bf16[1,179,384]{2,1,0:T(8,128)(2,1)S(1)} %pad_maximum_fusion.1), channel_id=1, source_target_pairs={{0,4},{4,0},{1,5},{5,1},{2,6},{6,2},{3,7},{7,3},{8,12},{12,8},{9,1... | collective-permute-start | bytes 412424 | tf_op jit(solution)/shard_map/ppermute | solution.py:175
  24.3 3.1 %collective-permute-done.6 = bf16[1,179,384]{2,1,0:T(8,128)(2,1)S(1)} collective-permute-done((bf16[1,179,384]{2,1,0:T(8,128)(2,1)S(1)}, bf16[1,179,384]{2,1,0:T(8,128)(2,1)S(1)}, u32[]{:S(2)}, u32[]{:S(2)}) %collective-permute-start.6) | collective-permute-done | bytes 137504 | tf_op jit(solution)/shard_map/ppermute | solution.py:175
  28.7 0.4 fusion.11
  29.3 0.4 convolution_add_fusion.1
  29.8 1.6 %collective-permute-start.9 = (bf16[192,192]{1,0:T(8,128)(2,1)S(1)}, bf16[192,192]{1,0:T(8,128)(2,1)S(1)}, u32[]{:S(2)}, u32[]{:S(2)}) collective-permute-start(bf16[192,192]{1,0:T(8,128)(2,1)S(1)} %constant_dynamic-slice_fusion.1), channel_id=1, source_target_pairs={{0,4},{4,0},{1,5},{5,1},{2,6},{6,2},{3,7},{7,3},{8,12},{12,8},{9,1... | collective-permute-start | bytes 221192 | tf_op jit(solution)/shard_map/ppermute | solution.py:145
  31.6 0.9 %collective-permute-start.11 = (bf16[192,192]{1,0:T(8,128)(2,1)S(1)}, bf16[192,192]{1,0:T(8,128)(2,1)S(1)}, u32[]{:S(2)}, u32[]{:S(2)}) collective-permute-start(bf16[192,192]{1,0:T(8,128)(2,1)S(1)} %constant_dynamic-slice_fusion), channel_id=1, source_target_pairs={{0,4},{4,0},{1,5},{5,1},{2,6},{6,2},{3,7},{7,3},{8,12},{12,8},{9,1... | collective-permute-start | bytes 221192 | tf_op jit(solution)/shard_map/ppermute | solution.py:145
  32.4 3.0 %collective-permute-done.9 = bf16[192,192]{1,0:T(8,128)(2,1)S(1)} collective-permute-done((bf16[192,192]{1,0:T(8,128)(2,1)S(1)}, bf16[192,192]{1,0:T(8,128)(2,1)S(1)}, u32[]{:S(2)}, u32[]{:S(2)}) %collective-permute-start.9) | collective-permute-done | bytes 73760 | tf_op jit(solution)/shard_map/ppermute | solution.py:145
  35.5 1.6 %collective-permute-start.10 = (bf16[192,192]{1,0:T(8,128)(2,1)S(1)}, bf16[192,192]{1,0:T(8,128)(2,1)S(1)}, u32[]{:S(2)}, u32[]{:S(2)}) collective-permute-start(bf16[192,192]{1,0:T(8,128)(2,1)S(1)} %add_convert_fusion.3), channel_id=1, source_target_pairs={{0,16},{8,24},{16,0},{24,8},{1,17},{9,25},{17,1},{25,9},{2,18},{10... | collective-permute-start | bytes 221192 | tf_op jit(solution)/shard_map/ppermute | solution.py:107
  37.2 1.6 %collective-permute-start.12 = (bf16[192,192]{1,0:T(8,128)(2,1)S(1)}, bf16[192,192]{1,0:T(8,128)(2,1)S(1)}, u32[]{:S(2)}, u32[]{:S(2)}) collective-permute-start(bf16[192,192]{1,0:T(8,128)(2,1)S(1)} %add_convert_fusion.2), channel_id=1, source_target_pairs={{0,16},{8,24},{16,0},{24,8},{1,17},{9,25},{17,1},{25,9},{2,18},{10... | collective-permute-start | bytes 221192 | tf_op jit(solution)/shard_map/ppermute | solution.py:107
  39.0 1.9 %collective-permute-done.10 = bf16[192,192]{1,0:T(8,128)(2,1)S(1)} collective-permute-done((bf16[192,192]{1,0:T(8,128)(2,1)S(1)}, bf16[192,192]{1,0:T(8,128)(2,1)S(1)}, u32[]{:S(2)}, u32[]{:S(2)}) %collective-permute-start.10) | collective-permute-done | bytes 73760 | tf_op jit(solution)/shard_map/ppermute | solution.py:107
  40.9 1.4 %collective-permute-done.12 = bf16[192,192]{1,0:T(8,128)(2,1)S(1)} collective-permute-done((bf16[192,192]{1,0:T(8,128)(2,1)S(1)}, bf16[192,192]{1,0:T(8,128)(2,1)S(1)}, u32[]{:S(2)}, u32[]{:S(2)}) %collective-permute-start.12) | collective-permute-done | bytes 73760 | tf_op jit(solution)/shard_map/ppermute | solution.py:107
  42.5 0.4 fusion.10
  42.9 1.1 %fusion.2 = bf16[1,512,384]{2,1,0:T(8,128)(2,1)} fusion(f32[512,384]{1,0:T(8,128)S(1)} %convolution_add_fusion.1, f32[512,384]{1,0:T(8,128)S(1)} %fusion.10, s32[128]{0:T(128)S(1)} %get-tuple-element.45, f32[128,384]{1,0:T(8,128)S(1)} %fusion.36), kind=kOutput, calls=%fused_computation.6 | convolution fusion | flops 51183616 | bytes 2163200 | tf_op jit(solution)/shard_map/bnr,bnc->brc/dot_general | solution.py:26
  44.5 0.9 %slice_bitcast_fusion = (f32[384,192]{0,1:T(8,128)}, f32[384,192]{0,1:T(8,128)}) fusion(f32[2,384,192]{1,2,0:T(8,128)S(1)} %fusion.7), kind=kLoop, calls=%fused_computation.25 | loop fusion | bytes 1179648 | tf_op jit(solution)/shard_map/squeeze | solution.py:327
  (63 shorter events, 6.1 us)
Async XLA Ops:
  0.6 1.0 %copy-start = (bf16[1,512,384]{2,1,0:T(8,128)(2,1)S(1)}, bf16[1,512,384]{2,1,0:T(8,128)(2,1)}, u32[]{:S(2)}) copy-start(bf16[1,512,384]{2,1,0:T(8,128)(2,1)} %param.10) | copy-start | bytes 1179652
  0.7 0.7 %copy-start.4 = (s32[1,128]{1,0:T(1,128)S(1)}, s32[1,128]{1,0:T(1,128)}, u32[]{:S(2)}) copy-start(s32[1,128]{1,0:T(1,128)} %param.12) | copy-start | bytes 1540
  0.7 0.7 %copy-start.5 = (s32[1,128]{1,0:T(1,128)S(1)}, s32[1,128]{1,0:T(1,128)}, u32[]{:S(2)}) copy-start(s32[1,128]{1,0:T(1,128)} %param.11) | copy-start | bytes 1540
  1.9 1.0 %copy-start.1 = (bf16[384,384]{1,0:T(8,128)(2,1)S(1)}, bf16[384,384]{1,0:T(8,128)(2,1)}, u32[]{:S(2)}) copy-start(bf16[384,384]{1,0:T(8,128)(2,1)} %param.14) | copy-start | bytes 884740
  2.2 1.0 %copy-start.2 = (bf16[384,384]{1,0:T(8,128)(2,1)S(1)}, bf16[384,384]{1,0:T(8,128)(2,1)}, u32[]{:S(2)}) copy-start(bf16[384,384]{1,0:T(8,128)(2,1)} %param.15) | copy-start | bytes 884740
  3.4 6.0 %copy-start.3 = (bf16[1,128,256]{2,1,0:T(8,128)(2,1)S(1)}, bf16[1,128,256]{2,1,0:T(8,128)(2,1)}, u32[]{:S(2)}) copy-start(bf16[1,128,256]{2,1,0:T(8,128)(2,1)} %param.13) | copy-start | bytes 196612
  3.7 7.3 %collective-permute-start = (bf16[1,64,384]{2,1,0:T(8,128)(2,1)S(1)}, bf16[1,64,384]{2,1,0:T(8,128)(2,1)S(1)}, u32[]{:S(2)}, u32[]{:S(2)}) collective-permute-start(bf16[1,64,384]{2,1,0:T(8,128)(2,1)S(1)} %get-tuple-element.38), channel_id=1, source_target_pairs={{0,3},{1,2},{2,1},{3,0},{4,7},{5,6},{6,5},{7,4},{8,11},{9,10},{10,... | collective-permute-start | bytes 147464 | tf_op jit(solution)/shard_map/ppermute | solution.py:82
  8.8 5.0 %collective-permute-start.1 = (bf16[1,64,384]{2,1,0:T(8,128)(2,1)S(1)}, bf16[1,64,384]{2,1,0:T(8,128)(2,1)S(1)}, u32[]{:S(2)}, u32[]{:S(2)}) collective-permute-start(bf16[1,64,384]{2,1,0:T(8,128)(2,1)S(1)} %get-tuple-element.39), channel_id=1, source_target_pairs={{0,2},{1,3},{2,0},{3,1},{4,6},{5,7},{6,4},{7,5},{8,10},{9,11},{10,... | collective-permute-start | bytes 147464 | tf_op jit(solution)/shard_map/ppermute | solution.py:82
  8.8 5.0 %collective-permute-start.2 = (bf16[1,64,384]{2,1,0:T(8,128)(2,1)S(1)}, bf16[1,64,384]{2,1,0:T(8,128)(2,1)S(1)}, u32[]{:S(2)}, u32[]{:S(2)}) collective-permute-start(bf16[1,64,384]{2,1,0:T(8,128)(2,1)S(1)} %get-tuple-element.37), channel_id=1, source_target_pairs={{0,1},{1,0},{2,3},{3,2},{4,5},{5,4},{6,7},{7,6},{8,9},{9,8},{10,11... | collective-permute-start | bytes 147464 | tf_op jit(solution)/shard_map/ppermute | solution.py:82
  13.9 6.2 %collective-permute-start.3 = (bf16[1,64,384]{2,1,0:T(8,128)(2,1)S(1)}, bf16[1,64,384]{2,1,0:T(8,128)(2,1)S(1)}, u32[]{:S(2)}, u32[]{:S(2)}) collective-permute-start(bf16[1,64,384]{2,1,0:T(8,128)(2,1)S(1)} %add_convert_fusion.4), channel_id=1, source_target_pairs={{0,3},{1,2},{2,1},{3,0},{4,7},{5,6},{6,5},{7,4},{8,11},{9,10},{10,... | collective-permute-start | bytes 147464 | tf_op jit(solution)/shard_map/ppermute | solution.py:90
  16.1 5.4 %collective-permute-start.4 = (bf16[1,64,384]{2,1,0:T(8,128)(2,1)S(1)}, bf16[1,64,384]{2,1,0:T(8,128)(2,1)S(1)}, u32[]{:S(2)}, u32[]{:S(2)}) collective-permute-start(bf16[1,64,384]{2,1,0:T(8,128)(2,1)S(1)} %add_convert_fusion.4), channel_id=1, source_target_pairs={{0,2},{1,3},{2,0},{3,1},{4,6},{5,7},{6,4},{7,5},{8,10},{9,11},{10,... | collective-permute-start | bytes 147464 | tf_op jit(solution)/shard_map/ppermute | solution.py:90
  16.1 5.4 %collective-permute-start.5 = (bf16[1,64,384]{2,1,0:T(8,128)(2,1)S(1)}, bf16[1,64,384]{2,1,0:T(8,128)(2,1)S(1)}, u32[]{:S(2)}, u32[]{:S(2)}) collective-permute-start(bf16[1,64,384]{2,1,0:T(8,128)(2,1)S(1)} %add_convert_fusion.4), channel_id=1, source_target_pairs={{0,1},{1,0},{2,3},{3,2},{4,5},{5,4},{6,7},{7,6},{8,9},{9,8},{10,11... | collective-permute-start | bytes 147464 | tf_op jit(solution)/shard_map/ppermute | solution.py:90
  22.3 5.1 %collective-permute-start.6 = (bf16[1,179,384]{2,1,0:T(8,128)(2,1)S(1)}, bf16[1,179,384]{2,1,0:T(8,128)(2,1)S(1)}, u32[]{:S(2)}, u32[]{:S(2)}) collective-permute-start(bf16[1,179,384]{2,1,0:T(8,128)(2,1)S(1)} %pad_maximum_fusion.1), channel_id=1, source_target_pairs={{0,4},{4,0},{1,5},{5,1},{2,6},{6,2},{3,7},{7,3},{8,12},{12,8},{9,1... | collective-permute-start | bytes 412424 | tf_op jit(solution)/shard_map/ppermute | solution.py:175
  24.3 5.4 %collective-permute-start.8 = (bf16[384,192]{1,0:T(8,128)(2,1)S(1)}, bf16[384,192]{1,0:T(8,128)(2,1)S(1)}, u32[]{:S(2)}, u32[]{:S(2)}) collective-permute-start(bf16[384,192]{1,0:T(8,128)(2,1)S(1)} %constant_dynamic-slice_fusion.2), channel_id=1, source_target_pairs={{0,8},{8,0},{16,24},{24,16},{1,9},{9,1},{17,25},{25,17},{2,10},{10... | collective-permute-start | bytes 442376 | tf_op jit(solution)/shard_map/ppermute | solution.py:137
  29.2 2.2 %collective-permute-start.7 = (bf16[384,192]{1,0:T(8,128)(2,1)S(1)}, bf16[384,192]{1,0:T(8,128)(2,1)S(1)}, u32[]{:S(2)}, u32[]{:S(2)}) collective-permute-start(bf16[384,192]{1,0:T(8,128)(2,1)S(1)} %constant_dynamic-slice_fusion.3), channel_id=1, source_target_pairs={{0,8},{8,0},{16,24},{24,16},{1,9},{9,1},{17,25},{25,17},{2,10},{10... | collective-permute-start | bytes 442376 | tf_op jit(solution)/shard_map/ppermute | solution.py:137
  29.8 5.7 %collective-permute-start.9 = (bf16[192,192]{1,0:T(8,128)(2,1)S(1)}, bf16[192,192]{1,0:T(8,128)(2,1)S(1)}, u32[]{:S(2)}, u32[]{:S(2)}) collective-permute-start(bf16[192,192]{1,0:T(8,128)(2,1)S(1)} %constant_dynamic-slice_fusion.1), channel_id=1, source_target_pairs={{0,4},{4,0},{1,5},{5,1},{2,6},{6,2},{3,7},{7,3},{8,12},{12,8},{9,1... | collective-permute-start | bytes 221192 | tf_op jit(solution)/shard_map/ppermute | solution.py:145
  31.6 5.6 %collective-permute-start.11 = (bf16[192,192]{1,0:T(8,128)(2,1)S(1)}, bf16[192,192]{1,0:T(8,128)(2,1)S(1)}, u32[]{:S(2)}, u32[]{:S(2)}) collective-permute-start(bf16[192,192]{1,0:T(8,128)(2,1)S(1)} %constant_dynamic-slice_fusion), channel_id=1, source_target_pairs={{0,4},{4,0},{1,5},{5,1},{2,6},{6,2},{3,7},{7,3},{8,12},{12,8},{9,1... | collective-permute-start | bytes 221192 | tf_op jit(solution)/shard_map/ppermute | solution.py:145
  35.5 5.4 %collective-permute-start.10 = (bf16[192,192]{1,0:T(8,128)(2,1)S(1)}, bf16[192,192]{1,0:T(8,128)(2,1)S(1)}, u32[]{:S(2)}, u32[]{:S(2)}) collective-permute-start(bf16[192,192]{1,0:T(8,128)(2,1)S(1)} %add_convert_fusion.3), channel_id=1, source_target_pairs={{0,16},{8,24},{16,0},{24,8},{1,17},{9,25},{17,1},{25,9},{2,18},{10... | collective-permute-start | bytes 221192 | tf_op jit(solution)/shard_map/ppermute | solution.py:107
  37.2 5.1 %collective-permute-start.12 = (bf16[192,192]{1,0:T(8,128)(2,1)S(1)}, bf16[192,192]{1,0:T(8,128)(2,1)S(1)}, u32[]{:S(2)}, u32[]{:S(2)}) collective-permute-start(bf16[192,192]{1,0:T(8,128)(2,1)S(1)} %add_convert_fusion.2), channel_id=1, source_target_pairs={{0,16},{8,24},{16,0},{24,8},{1,17},{9,25},{17,1},{25,9},{2,18},{10... | collective-permute-start | bytes 221192 | tf_op jit(solution)/shard_map/ppermute | solution.py:107
  42.4 1.8 %collective-permute-start.13 = (f32[2,192,192]{2,1,0:T(8,128)S(1)}, f32[2,192,192]{2,1,0:T(8,128)S(1)}, u32[]{:S(2)}, u32[]{:S(2)}) collective-permute-start(f32[2,192,192]{2,1,0:T(8,128)S(1)} %pad_maximum_fusion), channel_id=1, source_target_pairs={{0,8},{8,0},{16,24},{24,16},{1,9},{9,1},{17,25},{25,17},{2,10},{10... | collective-permute-start | bytes 884744 | tf_op jit(solution)/shard_map/ppermute | solution.py:322

commit v20 on v19

--- a/solution.py
+++ b/solution.py
@@ -84,6 +84,19 @@
     for h in range(n_head):
         total = total + from_head(pieces, head, h).astype(jnp.float32)
     feat_quarter = total.astype(jnp.bfloat16)
+
+    target_col = jnp.zeros((batch, sites, slab_sites), target.dtype)
+    own_cols = lax.dynamic_slice_in_dim(target, slab * slab_sites, slab_sites, 2)
+    target_col = lax.dynamic_update_slice_in_dim(target_col, own_cols, slab * slab_sites, 1)
+    for k in range(1, n_seq):
+        outgoing = lax.dynamic_slice_in_dim(
+            target, jnp.minimum(slab + k, n_seq - 1) * slab_sites, slab_sites, 2
+        )
+        target_in = lax.ppermute(outgoing, "seq", [(i, i + k) for i in range(n_seq - k)])
+        placed = lax.dynamic_update_slice_in_dim(
+            target_col, target_in, jnp.maximum(slab - k, 0) * slab_sites, 1
+        )
+        target_col = jnp.where(slab >= k, placed, target_col)
 
     pieces = [feat_quarter]
     for k in range(1, n_head):
@@ -158,33 +171,13 @@
     )
     donor_ok_all = jnp.zeros((batch, sites), jnp.bool_)
     acceptor_ok_all = jnp.zeros((batch, sites), jnp.bool_)
-    target_col = jnp.zeros((batch, sites, slab_sites), target.dtype)
-    own_cols = lax.dynamic_slice_in_dim(target, slab * slab_sites, slab_sites, 2)
-    target_col = lax.dynamic_update_slice_in_dim(target_col, own_cols, slab * slab_sites, 1)
     for k in range(1, n_seq):
         sent = jnp.where(slab + k < n_seq, own_donor, own_acceptor)
-        target_block = lax.dynamic_slice_in_dim(
-            target, jnp.minimum(slab + k, n_seq - 1) * slab_sites, slab_sites, 2
-        ).reshape(batch, slab_sites * slab_sites)
-        target_rows = -(-(slab_sites * slab_sites) // width)
-        target_block = jnp.pad(target_block, ((0, 0), (0, target_rows * width - slab_sites * slab_sites)))
-        payload = jnp.concatenate(
-            [sent, flags, target_block.reshape(batch, target_rows, width).astype(jnp.bfloat16)], axis=1
-        )
+        payload = jnp.concatenate([sent, flags], axis=1)
         perm = [(i, (i + k) % n_seq) for i in range(n_seq)]
         arrived = lax.ppermute(payload, "seq", perm)
         source = (slab - k) % n_seq
         earlier = slab >= k
-        target_in = (
-            arrived[:, slab_sites + 8 :]
-            .reshape(batch, target_rows * width)[:, : slab_sites * slab_sites]
-            .reshape(batch, slab_sites, slab_sites)
-        )
-        target_col = jnp.where(
-            earlier,
-            lax.dynamic_update_slice_in_dim(target_col, target_in, source * slab_sites, 1),
-            target_col,
-        )
         feat_in = arrived[:, :slab_sites]
         donor_feat_all = jnp.where(
             earlier,

time: 45.5 us -> 45.2 us (level)
  starting transfers between devices: 17.6 us -> 20.3 us
  waiting for transfers between devices: 16.7 us -> 14.2 us
  local copies, waits for them, and re-layouts: 3.69 us -> 3.11 us
    ppermute x3, waiting for transfers between devices: 4.27 us -> 0.57 us  [shards(): lax.ppermute(outgoing, 'head', [(i, i ^ k) for i in range(n_head)])]
    ppermute x0 -> x1, starting transfers between devices: none -> 3.57 us  [shards(): lax.ppermute(outgoing, 'seq', [(i, i + k) for i in range(n_seq - k)])]
    ppermute x3, waiting for transfers between devices: 2.67 us -> 3.54 us  [shards(): lax.ppermute(feat_quarter, 'head', [(i, i ^ k) for i in range(n_head)])]
    ppermute x1, starting transfers between devices: 1.58 us -> 1.08 us  [shards(): arrived = lax.ppermute(payload, 'seq', perm)]
    unnamed x16 -> x13, local copies, waits for them, and re-layouts: 1.87 us -> 1.86 us
  transfers between devices with their start and end apart: 14 -> 15, of which waited for: 10 -> 9; matrix products, arithmetic and copies ran while one was open for 11% -> 12% of each run, Pallas kernels for 0% -> 0%
where the time goes in v20:
time: 45.2 us; the launch traced here: 45.1 us
  starting transfers between devices  20.3 us (45%)
  waiting for transfers between devices  14.2 us (31%)
  matrix products  5.2 us (12%)
  local copies, waits for them, and re-layouts  3.11 us (7%)
  other arithmetic  1.13 us (2%)
  between operations  1.06 us (2%)
    ppermute x3, starting transfers between devices, shards(): lax.ppermute(outgoing, 'head', [(i, i ^ k) for i in range(n_head)])  5.76 us
    ppermute x3, starting transfers between devices, shards(): lax.ppermute(feat_quarter, 'head', [(i, i ^ k) for i in range(n_head)])  4.45 us
    ppermute x1, starting transfers between devices, shards(): lax.ppermute(outgoing, 'seq', [(i, i + k) for i in range(n_seq - k)])  3.57 us
    ppermute x3, waiting for transfers between devices, shards(): lax.ppermute(feat_quarter, 'head', [(i, i ^ k) for i in range(n_head)])  3.54 us
    ppermute x2, waiting for transfers between devices, from_seq_partner(): return lax.ppermute(outgoing, 'seq', [(0, 1), (1, 0)]).astype(jnp.float32)  3.45 us
    ppermute x2, waiting for transfers between devices, over_dp_bits(): lax.ppermute(held, 'dp', perm).astype(jnp.float32)  3.28 us
    ppermute x1, waiting for transfers between devices, shards(): arrived = lax.ppermute(payload, 'seq', perm)  3.19 us
    ppermute x2, starting transfers between devices, over_dp_bits(): lax.ppermute(held, 'dp', perm).astype(jnp.float32)  3.13 us
  transfers between devices with their start and end apart: 15, of which 9 were waited for; matrix products, arithmetic and copies ran while one was open for 12% of the time, Pallas kernels for 0%

profile of v20, /device:TPU:0, one launch (start us, length us, event | category | flops | bytes accessed | tf_op | source)
XLA Modules:
  0.0 45.1 jit_solution(5510873257881256469)
XLA Ops:
  0.7 0.7 %copy-done.4 = s32[1,128]{1,0:T(1,128)S(1)} copy-done((s32[1,128]{1,0:T(1,128)S(1)}, s32[1,128]{1,0:T(1,128)}, u32[]{:S(2)}) %copy-start.4) | copy-done | bytes 536
  2.2 0.7 %copy-done.1 = bf16[384,384]{1,0:T(8,128)(2,1)S(1)} copy-done((bf16[384,384]{1,0:T(8,128)(2,1)S(1)}, bf16[384,384]{1,0:T(8,128)(2,1)}, u32[]{:S(2)}) %copy-start.1) | copy-done | bytes 294936
  3.7 5.1 %collective-permute-start = (bf16[1,64,384]{2,1,0:T(8,128)(2,1)S(1)}, bf16[1,64,384]{2,1,0:T(8,128)(2,1)S(1)}, u32[]{:S(2)}, u32[]{:S(2)}) collective-permute-start(bf16[1,64,384]{2,1,0:T(8,128)(2,1)S(1)} %get-tuple-element.38), channel_id=1, source_target_pairs={{0,3},{1,2},{2,1},{3,0},{4,7},{5,6},{6,5},{7,4},{8,11},{9,10},{10,... | collective-permute-start | bytes 147464 | tf_op jit(solution)/shard_map/ppermute | solution.py:82
  8.8 0.6 %collective-permute-start.2 = (bf16[1,64,384]{2,1,0:T(8,128)(2,1)S(1)}, bf16[1,64,384]{2,1,0:T(8,128)(2,1)S(1)}, u32[]{:S(2)}, u32[]{:S(2)}) collective-permute-start(bf16[1,64,384]{2,1,0:T(8,128)(2,1)S(1)} %get-tuple-element.37), channel_id=1, source_target_pairs={{0,1},{1,0},{2,3},{3,2},{4,5},{5,4},{6,7},{7,6},{8,9},{9,8},{10,11... | collective-permute-start | bytes 147464 | tf_op jit(solution)/shard_map/ppermute | solution.py:82
  9.6 3.6 %collective-permute-start.7 = (bf16[1,128,128]{1,2,0:T(8,128)(2,1)S(1)}, bf16[1,128,128]{1,2,0:T(8,128)(2,1)S(1)}, u32[]{:S(2)}, u32[]{:S(2)}) collective-permute-start(bf16[1,128,128]{1,2,0:T(8,128)(2,1)S(1)} %copy.17), channel_id=1, source_target_pairs={{0,4},{1,5},{2,6},{3,7},{8,12},{9,13},{10,14},{11,15},{16,20},{17,... | collective-permute-start | bytes 98312 | tf_op jit(solution)/shard_map/ppermute | solution.py:95
  13.2 0.6 %collective-permute-done.1 = bf16[1,64,384]{2,1,0:T(8,128)(2,1)S(1)} collective-permute-done((bf16[1,64,384]{2,1,0:T(8,128)(2,1)S(1)}, bf16[1,64,384]{2,1,0:T(8,128)(2,1)S(1)}, u32[]{:S(2)}, u32[]{:S(2)}) %collective-permute-start.1) | collective-permute-done | bytes 49184 | tf_op jit(solution)/shard_map/ppermute | solution.py:82
  13.9 3.1 %collective-permute-start.3 = (bf16[1,64,384]{2,1,0:T(8,128)(2,1)S(1)}, bf16[1,64,384]{2,1,0:T(8,128)(2,1)S(1)}, u32[]{:S(2)}, u32[]{:S(2)}) collective-permute-start(bf16[1,64,384]{2,1,0:T(8,128)(2,1)S(1)} %add_convert_fusion.4), channel_id=1, source_target_pairs={{0,3},{1,2},{2,1},{3,0},{4,7},{5,6},{6,5},{7,4},{8,11},{9,10},{10,... | collective-permute-start | bytes 147464 | tf_op jit(solution)/shard_map/ppermute | solution.py:103
  17.0 1.3 %collective-permute-start.5 = (bf16[1,64,384]{2,1,0:T(8,128)(2,1)S(1)}, bf16[1,64,384]{2,1,0:T(8,128)(2,1)S(1)}, u32[]{:S(2)}, u32[]{:S(2)}) collective-permute-start(bf16[1,64,384]{2,1,0:T(8,128)(2,1)S(1)} %add_convert_fusion.4), channel_id=1, source_target_pairs={{0,1},{1,0},{2,3},{3,2},{4,5},{5,4},{6,7},{7,6},{8,9},{9,8},{10,11... | collective-permute-start | bytes 147464 | tf_op jit(solution)/shard_map/ppermute | solution.py:103
  18.5 1.5 %collective-permute-done.3 = bf16[1,64,384]{2,1,0:T(8,128)(2,1)S(1)} collective-permute-done((bf16[1,64,384]{2,1,0:T(8,128)(2,1)S(1)}, bf16[1,64,384]{2,1,0:T(8,128)(2,1)S(1)}, u32[]{:S(2)}, u32[]{:S(2)}) %collective-permute-start.3) | collective-permute-done | bytes 49184 | tf_op jit(solution)/shard_map/ppermute | solution.py:103
  20.0 2.1 %collective-permute-done.4 = bf16[1,64,384]{2,1,0:T(8,128)(2,1)S(1)} collective-permute-done((bf16[1,64,384]{2,1,0:T(8,128)(2,1)S(1)}, bf16[1,64,384]{2,1,0:T(8,128)(2,1)S(1)}, u32[]{:S(2)}, u32[]{:S(2)}) %collective-permute-start.4) | collective-permute-done | bytes 49184 | tf_op jit(solution)/shard_map/ppermute | solution.py:103
  22.8 1.1 %collective-permute-start.6 = (bf16[1,136,384]{2,1,0:T(8,128)(2,1)S(1)}, bf16[1,136,384]{2,1,0:T(8,128)(2,1)S(1)}, u32[]{:S(2)}, u32[]{:S(2)}) collective-permute-start(bf16[1,136,384]{2,1,0:T(8,128)(2,1)S(1)} %pad_maximum_fusion.1), channel_id=1, source_target_pairs={{0,4},{4,0},{1,5},{5,1},{2,6},{6,2},{3,7},{7,3},{8,12},{12,8},{9,1... | collective-permute-start | bytes 313352 | tf_op jit(solution)/shard_map/ppermute | solution.py:178
  24.3 3.2 %collective-permute-done.6 = bf16[1,136,384]{2,1,0:T(8,128)(2,1)S(1)} collective-permute-done((bf16[1,136,384]{2,1,0:T(8,128)(2,1)S(1)}, bf16[1,136,384]{2,1,0:T(8,128)(2,1)S(1)}, u32[]{:S(2)}, u32[]{:S(2)}) %collective-permute-start.6) | collective-permute-done | bytes 104480 | tf_op jit(solution)/shard_map/ppermute | solution.py:178
  28.4 0.4 fusion.11
  29.0 0.4 convolution_add_fusion.1
  29.6 1.1 %collective-permute-start.10 = (bf16[192,192]{1,0:T(8,128)(2,1)S(1)}, bf16[192,192]{1,0:T(8,128)(2,1)S(1)}, u32[]{:S(2)}, u32[]{:S(2)}) collective-permute-start(bf16[192,192]{1,0:T(8,128)(2,1)S(1)} %constant_dynamic-slice_fusion.1), channel_id=1, source_target_pairs={{0,4},{4,0},{1,5},{5,1},{2,6},{6,2},{3,7},{7,3},{8,12},{12,8},{9,1... | collective-permute-start | bytes 221192 | tf_op jit(solution)/shard_map/ppermute | solution.py:158
  30.8 1.1 %collective-permute-start.12 = (bf16[192,192]{1,0:T(8,128)(2,1)S(1)}, bf16[192,192]{1,0:T(8,128)(2,1)S(1)}, u32[]{:S(2)}, u32[]{:S(2)}) collective-permute-start(bf16[192,192]{1,0:T(8,128)(2,1)S(1)} %constant_dynamic-slice_fusion), channel_id=1, source_target_pairs={{0,4},{4,0},{1,5},{5,1},{2,6},{6,2},{3,7},{7,3},{8,12},{12,8},{9,1... | collective-permute-start | bytes 221192 | tf_op jit(solution)/shard_map/ppermute | solution.py:158
  31.9 3.3 %collective-permute-done.10 = bf16[192,192]{1,0:T(8,128)(2,1)S(1)} collective-permute-done((bf16[192,192]{1,0:T(8,128)(2,1)S(1)}, bf16[192,192]{1,0:T(8,128)(2,1)S(1)}, u32[]{:S(2)}, u32[]{:S(2)}) %collective-permute-start.10) | collective-permute-done | bytes 73760 | tf_op jit(solution)/shard_map/ppermute | solution.py:158
  35.3 1.6 %collective-permute-start.11 = (bf16[192,192]{1,0:T(8,128)(2,1)S(1)}, bf16[192,192]{1,0:T(8,128)(2,1)S(1)}, u32[]{:S(2)}, u32[]{:S(2)}) collective-permute-start(bf16[192,192]{1,0:T(8,128)(2,1)S(1)} %add_convert_fusion.3), channel_id=1, source_target_pairs={{0,16},{8,24},{16,0},{24,8},{1,17},{9,25},{17,1},{25,9},{2,18},{10... | collective-permute-start | bytes 221192 | tf_op jit(solution)/shard_map/ppermute | solution.py:120
  37.0 1.6 %collective-permute-start.13 = (bf16[192,192]{1,0:T(8,128)(2,1)S(1)}, bf16[192,192]{1,0:T(8,128)(2,1)S(1)}, u32[]{:S(2)}, u32[]{:S(2)}) collective-permute-start(bf16[192,192]{1,0:T(8,128)(2,1)S(1)} %add_convert_fusion.2), channel_id=1, source_target_pairs={{0,16},{8,24},{16,0},{24,8},{1,17},{9,25},{17,1},{25,9},{2,18},{10... | collective-permute-start | bytes 221192 | tf_op jit(solution)/shard_map/ppermute | solution.py:120
  38.8 1.8 %collective-permute-done.11 = bf16[192,192]{1,0:T(8,128)(2,1)S(1)} collective-permute-done((bf16[192,192]{1,0:T(8,128)(2,1)S(1)}, bf16[192,192]{1,0:T(8,128)(2,1)S(1)}, u32[]{:S(2)}, u32[]{:S(2)}) %collective-permute-start.11) | collective-permute-done | bytes 73760 | tf_op jit(solution)/shard_map/ppermute | solution.py:120
  40.6 1.4 %collective-permute-done.13 = bf16[192,192]{1,0:T(8,128)(2,1)S(1)} collective-permute-done((bf16[192,192]{1,0:T(8,128)(2,1)S(1)}, bf16[192,192]{1,0:T(8,128)(2,1)S(1)}, u32[]{:S(2)}, u32[]{:S(2)}) %collective-permute-start.13) | collective-permute-done | bytes 73760 | tf_op jit(solution)/shard_map/ppermute | solution.py:120
  42.2 0.4 fusion.10
  42.6 1.1 %fusion.2 = bf16[1,512,384]{2,1,0:T(8,128)(2,1)} fusion(f32[512,384]{1,0:T(8,128)S(1)} %convolution_add_fusion.1, f32[512,384]{1,0:T(8,128)S(1)} %fusion.10, s32[128]{0:T(128)S(1)} %get-tuple-element.45, f32[128,384]{1,0:T(8,128)S(1)} %fusion.36), kind=kOutput, calls=%fused_computation.6 | convolution fusion | flops 51183616 | bytes 2163200 | tf_op jit(solution)/shard_map/bnr,bnc->brc/dot_general | solution.py:26
  44.2 0.9 %slice_bitcast_fusion = (f32[384,192]{0,1:T(8,128)}, f32[384,192]{0,1:T(8,128)}) fusion(f32[2,384,192]{1,2,0:T(8,128)S(1)} %fusion.7), kind=kLoop, calls=%fused_computation.25 | loop fusion | bytes 1179648 | tf_op jit(solution)/shard_map/squeeze | solution.py:320
  (59 shorter events, 5.5 us)
Async XLA Ops:
  0.6 1.0 %copy-start = (bf16[1,512,384]{2,1,0:T(8,128)(2,1)S(1)}, bf16[1,512,384]{2,1,0:T(8,128)(2,1)}, u32[]{:S(2)}) copy-start(bf16[1,512,384]{2,1,0:T(8,128)(2,1)} %param.10) | copy-start | bytes 1179652
  0.7 0.7 %copy-start.4 = (s32[1,128]{1,0:T(1,128)S(1)}, s32[1,128]{1,0:T(1,128)}, u32[]{:S(2)}) copy-start(s32[1,128]{1,0:T(1,128)} %param.12) | copy-start | bytes 1540
  0.7 0.7 %copy-start.5 = (s32[1,128]{1,0:T(1,128)S(1)}, s32[1,128]{1,0:T(1,128)}, u32[]{:S(2)}) copy-start(s32[1,128]{1,0:T(1,128)} %param.11) | copy-start | bytes 1540
  1.9 1.0 %copy-start.1 = (bf16[384,384]{1,0:T(8,128)(2,1)S(1)}, bf16[384,384]{1,0:T(8,128)(2,1)}, u32[]{:S(2)}) copy-start(bf16[384,384]{1,0:T(8,128)(2,1)} %param.14) | copy-start | bytes 884740
  2.2 1.0 %copy-start.2 = (bf16[384,384]{1,0:T(8,128)(2,1)S(1)}, bf16[384,384]{1,0:T(8,128)(2,1)}, u32[]{:S(2)}) copy-start(bf16[384,384]{1,0:T(8,128)(2,1)} %param.15) | copy-start | bytes 884740
  3.4 6.0 %copy-start.3 = (bf16[1,128,256]{2,1,0:T(8,128)(2,1)S(1)}, bf16[1,128,256]{2,1,0:T(8,128)(2,1)}, u32[]{:S(2)}) copy-start(bf16[1,128,256]{2,1,0:T(8,128)(2,1)} %param.13) | copy-start | bytes 196612
  3.7 9.5 %collective-permute-start = (bf16[1,64,384]{2,1,0:T(8,128)(2,1)S(1)}, bf16[1,64,384]{2,1,0:T(8,128)(2,1)S(1)}, u32[]{:S(2)}, u32[]{:S(2)}) collective-permute-start(bf16[1,64,384]{2,1,0:T(8,128)(2,1)S(1)} %get-tuple-element.38), channel_id=1, source_target_pairs={{0,3},{1,2},{2,1},{3,0},{4,7},{5,6},{6,5},{7,4},{8,11},{9,10},{10,... | collective-permute-start | bytes 147464 | tf_op jit(solution)/shard_map/ppermute | solution.py:82
  8.8 5.0 %collective-permute-start.1 = (bf16[1,64,384]{2,1,0:T(8,128)(2,1)S(1)}, bf16[1,64,384]{2,1,0:T(8,128)(2,1)S(1)}, u32[]{:S(2)}, u32[]{:S(2)}) collective-permute-start(bf16[1,64,384]{2,1,0:T(8,128)(2,1)S(1)} %get-tuple-element.39), channel_id=1, source_target_pairs={{0,2},{1,3},{2,0},{3,1},{4,6},{5,7},{6,4},{7,5},{8,10},{9,11},{10,... | collective-permute-start | bytes 147464 | tf_op jit(solution)/shard_map/ppermute | solution.py:82
  8.8 5.0 %collective-permute-start.2 = (bf16[1,64,384]{2,1,0:T(8,128)(2,1)S(1)}, bf16[1,64,384]{2,1,0:T(8,128)(2,1)S(1)}, u32[]{:S(2)}, u32[]{:S(2)}) collective-permute-start(bf16[1,64,384]{2,1,0:T(8,128)(2,1)S(1)} %get-tuple-element.37), channel_id=1, source_target_pairs={{0,1},{1,0},{2,3},{3,2},{4,5},{5,4},{6,7},{7,6},{8,9},{9,8},{10,11... | collective-permute-start | bytes 147464 | tf_op jit(solution)/shard_map/ppermute | solution.py:82
  9.6 18.0 %collective-permute-start.7 = (bf16[1,128,128]{1,2,0:T(8,128)(2,1)S(1)}, bf16[1,128,128]{1,2,0:T(8,128)(2,1)S(1)}, u32[]{:S(2)}, u32[]{:S(2)}) collective-permute-start(bf16[1,128,128]{1,2,0:T(8,128)(2,1)S(1)} %copy.17), channel_id=1, source_target_pairs={{0,4},{1,5},{2,6},{3,7},{8,12},{9,13},{10,14},{11,15},{16,20},{17,... | collective-permute-start | bytes 98312 | tf_op jit(solution)/shard_map/ppermute | solution.py:95
  13.9 6.1 %collective-permute-start.3 = (bf16[1,64,384]{2,1,0:T(8,128)(2,1)S(1)}, bf16[1,64,384]{2,1,0:T(8,128)(2,1)S(1)}, u32[]{:S(2)}, u32[]{:S(2)}) collective-permute-start(bf16[1,64,384]{2,1,0:T(8,128)(2,1)S(1)} %add_convert_fusion.4), channel_id=1, source_target_pairs={{0,3},{1,2},{2,1},{3,0},{4,7},{5,6},{6,5},{7,4},{8,11},{9,10},{10,... | collective-permute-start | bytes 147464 | tf_op jit(solution)/shard_map/ppermute | solution.py:103
  17.0 5.0 %collective-permute-start.4 = (bf16[1,64,384]{2,1,0:T(8,128)(2,1)S(1)}, bf16[1,64,384]{2,1,0:T(8,128)(2,1)S(1)}, u32[]{:S(2)}, u32[]{:S(2)}) collective-permute-start(bf16[1,64,384]{2,1,0:T(8,128)(2,1)S(1)} %add_convert_fusion.4), channel_id=1, source_target_pairs={{0,2},{1,3},{2,0},{3,1},{4,6},{5,7},{6,4},{7,5},{8,10},{9,11},{10,... | collective-permute-start | bytes 147464 | tf_op jit(solution)/shard_map/ppermute | solution.py:103
  17.0 5.0 %collective-permute-start.5 = (bf16[1,64,384]{2,1,0:T(8,128)(2,1)S(1)}, bf16[1,64,384]{2,1,0:T(8,128)(2,1)S(1)}, u32[]{:S(2)}, u32[]{:S(2)}) collective-permute-start(bf16[1,64,384]{2,1,0:T(8,128)(2,1)S(1)} %add_convert_fusion.4), channel_id=1, source_target_pairs={{0,1},{1,0},{2,3},{3,2},{4,5},{5,4},{6,7},{7,6},{8,9},{9,8},{10,11... | collective-permute-start | bytes 147464 | tf_op jit(solution)/shard_map/ppermute | solution.py:103
  22.8 4.7 %collective-permute-start.6 = (bf16[1,136,384]{2,1,0:T(8,128)(2,1)S(1)}, bf16[1,136,384]{2,1,0:T(8,128)(2,1)S(1)}, u32[]{:S(2)}, u32[]{:S(2)}) collective-permute-start(bf16[1,136,384]{2,1,0:T(8,128)(2,1)S(1)} %pad_maximum_fusion.1), channel_id=1, source_target_pairs={{0,4},{4,0},{1,5},{5,1},{2,6},{6,2},{3,7},{7,3},{8,12},{12,8},{9,1... | collective-permute-start | bytes 313352 | tf_op jit(solution)/shard_map/ppermute | solution.py:178
  24.3 5.2 %collective-permute-start.9 = (bf16[384,192]{1,0:T(8,128)(2,1)S(1)}, bf16[384,192]{1,0:T(8,128)(2,1)S(1)}, u32[]{:S(2)}, u32[]{:S(2)}) collective-permute-start(bf16[384,192]{1,0:T(8,128)(2,1)S(1)} %constant_dynamic-slice_fusion.2), channel_id=1, source_target_pairs={{0,8},{8,0},{16,24},{24,16},{1,9},{9,1},{17,25},{25,17},{2,10},{10... | collective-permute-start | bytes 442376 | tf_op jit(solution)/shard_map/ppermute | solution.py:150
  28.9 1.7 %collective-permute-start.8 = (bf16[384,192]{1,0:T(8,128)(2,1)S(1)}, bf16[384,192]{1,0:T(8,128)(2,1)S(1)}, u32[]{:S(2)}, u32[]{:S(2)}) collective-permute-start(bf16[384,192]{1,0:T(8,128)(2,1)S(1)} %constant_dynamic-slice_fusion.3), channel_id=1, source_target_pairs={{0,8},{8,0},{16,24},{24,16},{1,9},{9,1},{17,25},{25,17},{2,10},{10... | collective-permute-start | bytes 442376 | tf_op jit(solution)/shard_map/ppermute | solution.py:150
  29.6 5.7 %collective-permute-start.10 = (bf16[192,192]{1,0:T(8,128)(2,1)S(1)}, bf16[192,192]{1,0:T(8,128)(2,1)S(1)}, u32[]{:S(2)}, u32[]{:S(2)}) collective-permute-start(bf16[192,192]{1,0:T(8,128)(2,1)S(1)} %constant_dynamic-slice_fusion.1), channel_id=1, source_target_pairs={{0,4},{4,0},{1,5},{5,1},{2,6},{6,2},{3,7},{7,3},{8,12},{12,8},{9,1... | collective-permute-start | bytes 221192 | tf_op jit(solution)/shard_map/ppermute | solution.py:158
  30.8 6.1 %collective-permute-start.12 = (bf16[192,192]{1,0:T(8,128)(2,1)S(1)}, bf16[192,192]{1,0:T(8,128)(2,1)S(1)}, u32[]{:S(2)}, u32[]{:S(2)}) collective-permute-start(bf16[192,192]{1,0:T(8,128)(2,1)S(1)} %constant_dynamic-slice_fusion), channel_id=1, source_target_pairs={{0,4},{4,0},{1,5},{5,1},{2,6},{6,2},{3,7},{7,3},{8,12},{12,8},{9,1... | collective-permute-start | bytes 221192 | tf_op jit(solution)/shard_map/ppermute | solution.py:158
  35.3 5.4 %collective-permute-start.11 = (bf16[192,192]{1,0:T(8,128)(2,1)S(1)}, bf16[192,192]{1,0:T(8,128)(2,1)S(1)}, u32[]{:S(2)}, u32[]{:S(2)}) collective-permute-start(bf16[192,192]{1,0:T(8,128)(2,1)S(1)} %add_convert_fusion.3), channel_id=1, source_target_pairs={{0,16},{8,24},{16,0},{24,8},{1,17},{9,25},{17,1},{25,9},{2,18},{10... | collective-permute-start | bytes 221192 | tf_op jit(solution)/shard_map/ppermute | solution.py:120
  37.0 5.1 %collective-permute-start.13 = (bf16[192,192]{1,0:T(8,128)(2,1)S(1)}, bf16[192,192]{1,0:T(8,128)(2,1)S(1)}, u32[]{:S(2)}, u32[]{:S(2)}) collective-permute-start(bf16[192,192]{1,0:T(8,128)(2,1)S(1)} %add_convert_fusion.2), channel_id=1, source_target_pairs={{0,16},{8,24},{16,0},{24,8},{1,17},{9,25},{17,1},{25,9},{2,18},{10... | collective-permute-start | bytes 221192 | tf_op jit(solution)/shard_map/ppermute | solution.py:120
  42.2 1.8 %collective-permute-start.14 = (f32[2,192,192]{2,1,0:T(8,128)S(1)}, f32[2,192,192]{2,1,0:T(8,128)S(1)}, u32[]{:S(2)}, u32[]{:S(2)}) collective-permute-start(f32[2,192,192]{2,1,0:T(8,128)S(1)} %pad_maximum_fusion), channel_id=1, source_target_pairs={{0,8},{8,0},{16,24},{24,16},{1,9},{9,1},{17,25},{25,17},{2,10},{10... | collective-permute-start | bytes 884744 | tf_op jit(solution)/shard_map/ppermute | solution.py:315
